TPU v7x, 32 devices: a whole 2x2x4 slice. The times are simulated.
32 devices in a mesh: section: 2 (over x), mp: 4 (over z), dp: 4 (over y, core).
Axes of the slice: x: 2, y: 2, z: 4, core: 2. Of those that a mesh axis runs over, the one named last changes fastest.
Arguments:
- text_in: bfloat16 [4, 2, 512, 8192], P('dp', 'section', None, 'mp'), may hold values from -6 to 6
- vision: bfloat16 [4, 2, 256, 8192], P('dp', 'section', None, 'mp'), may hold values from -6 to 6
- tile_counts: int32 [4, 2], P('dp'), may hold values from 1 to 4, as said below
- lengths: int32 [4, 2], P('dp', 'section'), may hold values from 128 to 512, as said below
- image_of: int32 [4, 2], P('dp'), may hold values from 0 to 1, each once within a row
- norm_gain: float32 [2, 8192], P('section'), may hold values from 0.5 to 1.5
- query_weight: bfloat16 [2, 8192, 4096], P('section', 'dp', 'mp'), may hold values from -0.0625 to 0.0625
- key_weight: bfloat16 [2, 8192, 1024], P('section', 'dp', 'mp'), may hold values from -0.0625 to 0.0625
- value_weight: bfloat16 [2, 8192, 1024], P('section', 'dp', 'mp'), may hold values from -0.0625 to 0.0625
- query_gain: float32 [2, 128], P('section')
- key_gain: float32 [2, 128], P('section')
- cross_gate: float32 [2], P('section'), may hold values from 0.4 to 1.5
- context_grad: bfloat16 [4, 2, 512, 4096], P('dp', 'section', None, 'mp'), may hold values from -6 to 6
Outputs:
- gated_context: bfloat16 [4, 2, 512, 4096], P('dp', 'section', None, 'mp')
- vision_grad: bfloat16 [4, 2, 256, 8192], P('dp', 'section', None, 'mp')
- key_weight_grad: bfloat16 [2, 8192, 1024], P('section', 'dp', 'mp')
- value_weight_grad: bfloat16 [2, 8192, 1024], P('section', 'dp', 'mp')
Inputs may be any that keep to these rules, and one draw needn't show every extreme that they name: `tile_counts`: some image has 4 tiles and some has one. `lengths`: some sample has the full 512 tokens. `image_of`: each row is a permutation of the sections.
All inputs are finite; a program needn't handle non-finite values.
Results may differ from a plain program's by a relative error of at most 0.018.
Values may be sent and summed in bfloat16 or wider, within the bound.
No kernel may reach another device: no remote copies, remote signals or barrier semaphores. Data moves between devices by JAX's collectives and lax.ppermute only.
A program may use at most 192 MiB of HBM per device.

v0:
```python
import jax
import jax.numpy as jnp
from jax import lax
from jax.sharding import PartitionSpec as P

HD = 128
TILE_ROWS = 64


def shifted(value, axis, steps):
    count = lax.axis_size(axis)
    pairs = [(source, (source + steps) % count) for source in range(count)]
    return lax.ppermute(value, axis, pairs)


def norm_rows(values, gain):
    values = values.astype(jnp.float32)
    scaled = values * lax.rsqrt(jnp.mean(values * values, axis=-1, keepdims=True) + 1e-05)
    return scaled * gain


def rounded(values):
    return lax.optimization_barrier(values.astype(jnp.bfloat16)).astype(jnp.float32)


def attend(queries, keys_raw, values_raw, key_norm, usable, present, gate_value):
    keys = rounded(norm_rows(keys_raw, key_norm))
    values = rounded(values_raw)
    text_rows, heads, depth = queries.shape
    groups = keys.shape[1]
    grouped = queries.astype(jnp.float32).reshape(text_rows, groups, heads // groups, depth)
    scores = jnp.einsum("tgjd,vgd->gjtv", grouped, keys) * depth ** (-0.5)
    scores = jnp.where(usable[None, None, None, :], scores, -1e30)
    highest = lax.stop_gradient(jnp.max(scores, axis=-1, keepdims=True))
    weights = jnp.exp(scores - highest)
    probs = rounded(weights / jnp.sum(weights, axis=-1, keepdims=True))
    context = jnp.einsum("gjtv,vgd->tgjd", probs, values).reshape(text_rows, heads * depth)
    return jnp.where(present[:, None], jnp.tanh(gate_value) * context, 0.0)


def per_device(
    text_in,
    vision,
    tile_counts,
    lengths,
    image_of,
    norm_gain,
    query_weight,
    key_weight,
    value_weight,
    query_gain,
    key_gain,
    cross_gate,
    context_grad,
):
    arrived = shifted(text_in, "section", 1)
    full_text = lax.all_gather(arrived, "mp", axis=3, tiled=True)[0, 0]
    text_rows = full_text.shape[0]
    normed = norm_rows(full_text, norm_gain[0]).astype(jnp.bfloat16)
    width_q = query_weight.shape[2]
    columns = normed
    query_raw = jnp.dot(
        columns,
        lax.all_gather(query_weight, "dp", axis=1, tiled=True)[0],
        preferred_element_type=jnp.float32,
    )
    queries = norm_rows(query_raw.reshape(text_rows, width_q // HD, HD), query_gain[0]).astype(
        jnp.bfloat16
    )
    key_full, value_full = (
        lax.all_gather(key_weight, "dp", axis=1, tiled=True),
        lax.all_gather(value_weight, "dp", axis=1, tiled=True),
    )
    key_full = key_full[0]
    value_full = value_full[0]
    slot_rows = vision.shape[2]
    part_width = vision.shape[3]
    wanted = image_of[0, lax.axis_index("section")]
    shard_piece = lax.all_gather(vision, "section", axis=1, tiled=True)
    owners = jnp.arange(shard_piece.shape[1])
    chosen = (owners == wanted)[:, None, None]
    taken = jnp.where(chosen, shard_piece[0], jnp.zeros_like(shard_piece[0]))
    image_part = jnp.sum(taken.astype(jnp.float32), axis=0).astype(jnp.bfloat16)
    image = lax.all_gather(image_part, "mp", axis=1, tiled=True)
    width_k = key_full.shape[1]
    keys_raw = jnp.dot(image, key_full, preferred_element_type=jnp.float32).reshape(
        slot_rows, width_k // HD, HD
    )
    values_raw = jnp.dot(image, value_full, preferred_element_type=jnp.float32).reshape(
        slot_rows, width_k // HD, HD
    )
    usable = jnp.arange(slot_rows) < tile_counts[0, wanted] * TILE_ROWS
    present = jnp.arange(text_rows) < lengths[0, 0]

    def forward(keys_in, values_in):
        return attend(queries, keys_in, values_in, key_gain[0], usable, present, cross_gate[0])

    context, pullback = jax.vjp(forward, keys_raw, values_raw)
    gated_context = context.astype(jnp.bfloat16).reshape(1, 1, text_rows, width_q)
    key_back, value_back = pullback(context_grad[0, 0].astype(jnp.float32))
    key_flat = key_back.reshape(slot_rows, width_k).astype(jnp.bfloat16)
    value_flat = value_back.reshape(slot_rows, width_k).astype(jnp.bfloat16)
    contract = (((1,), (1,)), ((), ()))
    partial_sum = lax.dot_general(key_flat, key_full, contract, preferred_element_type=jnp.float32)
    partial_sum = partial_sum + lax.dot_general(
        value_flat, value_full, contract, preferred_element_type=jnp.float32
    )
    partial_bf = partial_sum.astype(jnp.bfloat16)
    summed = lax.psum_scatter(
        partial_bf.astype(jnp.float32).astype(jnp.bfloat16), "mp", scatter_dimension=1, tiled=True
    )
    row_ids = jnp.arange(slot_rows * lax.axis_size("section"))
    taken = jnp.take(summed, row_ids % slot_rows, axis=0).astype(jnp.float32)
    routed = lax.psum_scatter(
        jnp.where((row_ids // slot_rows == wanted)[:, None], taken, 0.0).astype(jnp.bfloat16),
        "section",
        scatter_dimension=0,
        tiled=True,
    )
    vision_grad = routed.reshape(1, 1, slot_rows, part_width)
    columns = image
    inner = (((0,), (0,)), ((), ()))
    key_part = lax.dot_general(columns, key_flat, inner, preferred_element_type=jnp.float32).astype(
        jnp.bfloat16
    )
    value_part = lax.dot_general(
        columns, value_flat, inner, preferred_element_type=jnp.float32
    ).astype(jnp.bfloat16)
    both_grads = lax.psum_scatter(
        jnp.concatenate([key_part, value_part], axis=1).astype(jnp.float32).astype(jnp.bfloat16),
        "dp",
        scatter_dimension=0,
        tiled=True,
    )
    key_weight_grad = both_grads[:, :width_k][None]
    value_weight_grad = both_grads[:, width_k:][None]
    return (gated_context, vision_grad, key_weight_grad, value_weight_grad)


def solution(mesh):
    return jax.shard_map(
        per_device,
        mesh=mesh,
        in_specs=(
            P("dp", "section", None, "mp"),
            P("dp", "section", None, "mp"),
            P("dp", None),
            P("dp", "section"),
            P("dp", None),
            P("section", None),
            P("section", "dp", "mp"),
            P("section", "dp", "mp"),
            P("section", "dp", "mp"),
            P("section", None),
            P("section", None),
            P("section"),
            P("dp", "section", None, "mp"),
        ),
        out_specs=(
            P("dp", "section", None, "mp"),
            P("dp", "section", None, "mp"),
            P("section", "dp", "mp"),
            P("section", "dp", "mp"),
        ),
        check_vma=False,
    )
```

profile of v0, /device:TPU:0, one launch (start us, length us, event | category | flops | bytes accessed | tf_op | source)
XLA Modules:
  0.0 705.0 jit_solution(10474390815657424555)
XLA Ops:
  7.2 0.7 all-gather.7.cloned.1.call-update
  7.9 0.0 all-gather.13.cloned.1.call-start
  8.0 0.7 all-gather.13.cloned.1.call-update
  8.7 0.0 all-gather.11.cloned.1.call-start
  8.7 0.7 all-gather.11.cloned.1.call-update
  9.4 0.0 all-gather.9.cloned.1.call-start
  9.5 0.6 constant_dynamic-slice_fusion.1
  10.0 0.6 iota_compare_fusion.2
  10.7 34.7 %all-gather.7.cloned.1.call-done = bf16[1,2,256,2048]{3,2,0,1:T(8,128)(2,1)} async-done(((bf16[1,1,256,2048]{3,2,0,1:T(8,128)(2,1)}), bf16[1,2,256,2048]{3,2,0,1:T(8,128)(2,1)}) %all-gather.7.cloned.1.call-update) | async-done | bytes 2097168 | tf_op jit(solution)/shard_map/all_gather | solution.py:79
  45.4 3.4 fusion.34
  48.8 0.0 all-gather.15.cloned.1.call-start
  48.9 0.4 collective-permute-start
  49.3 47.3 %collective-permute-done = bf16[1,1,512,2048]{3,2,1,0:T(8,128)(2,1)S(1)} collective-permute-done((bf16[1,1,512,2048]{3,2,1,0:T(8,128)(2,1)}, bf16[1,1,512,2048]{3,2,1,0:T(8,128)(2,1)S(1)}, u32[]{:S(2)}, u32[]{:S(2)}) %collective-permute-start) | collective-permute-done | bytes 2097184 | tf_op jit(solution)/shard_map/ppermute | solution.py:13
  96.5 1.4 copy-done.11
  98.0 0.0 all-gather.17.cloned.1.call-start
  98.0 0.5 all-gather.17.cloned.1.call-update
  98.5 0.0 reduce-scatter.4.cloned.1.call-start
  99.9 0.5 copy.81
  102.4 0.6 fusion.100
  103.0 1.2 iota_compare_fusion.1
  104.2 6.4 copy.51
  110.6 7.0 all-gather.11.cloned.1.call-done
  117.6 6.4 copy.50
  123.9 76.4 %all-gather.9.cloned.1.call-done = bf16[256,8192]{1,0:T(8,128)(2,1)} async-done(((bf16[256,2048]{1,0:T(8,128)(2,1)}), bf16[256,8192]{1,0:T(8,128)(2,1)}) %all-gather.9.cloned.1.call-update) | async-done | bytes 4194320 | tf_op jit(solution)/shard_map/all_gather | solution.py:84
  200.4 4.9 multiply_reduce_fusion.2
  205.3 0.7 multiply_convert_fusion.1
  206.0 0.3 copy-done.10
  206.3 1.3 fusion.60
  207.6 2.0 fusion.43
  209.6 140.3 %all-gather.15.cloned.1.call-done = bf16[1,1,512,8192]{3,2,1,0:T(8,128)(2,1)} async-done(((bf16[1,1,512,2048]{3,2,1,0:T(8,128)(2,1)}), bf16[1,1,512,8192]{3,2,1,0:T(8,128)(2,1)}) %all-gather.15.cloned.1.call-update) | async-done | bytes 8388624 | tf_op jit(solution)/shard_map/all_gather | solution.py:57
  350.0 5.1 fusion.1
  355.1 100.4 %all-gather.17.cloned.1.call-done = bf16[1,8192,1024]{2,1,0:T(8,128)(2,1)} async-done(((bf16[1,2048,1024]{2,1,0:T(8,128)(2,1)}), bf16[1,8192,1024]{2,1,0:T(8,128)(2,1)}) %all-gather.17.cloned.1.call-update) | async-done | bytes 16777232 | tf_op jit(solution)/shard_map/all_gather | solution.py:64
  455.5 21.4 %copy.52 = bf16[1024,8192]{1,0:T(8,128)(2,1)} copy(bf16[1024,8192]{0,1:T(8,128)(2,1)} %bitcast.150) | data formatting | bytes 33554432 | tf_op jit(solution)/shard_map/dot_general | solution.py:62
  477.0 14.8 %multiply_reduce_fusion = (f32[512,8]{0,1:T(8,128)S(1)}, f32[512,8,128]{0,2,1:T(8,128)S(1)}) fusion(bf16[8,128,8192]{2,1,0:T(8,128)(2,1)} %bitcast.151, bf16[1,1,512,8192]{3,2,1,0:T(8,128)(2,1)} %all-gather.15.cloned.1.call-done, f32[8192]{0:T(1024)S(1)} %bitcast.169, f32[512]{0:T(512)S(1)} %add_rsqrt_fusion.1), kind=kOutput, calls=%fused_computation.55 | convolution fusion | flops 8607756288 | bytes 27314176 | tf_op jit(solution)/shard_map/dot_general | solution.py:62
  491.8 0.5 multiply_convert_fusion
  492.3 5.1 fusion.101
  497.4 0.7 multiply_divide_fusion
  498.1 3.9 fusion.16
  502.0 0.7 copy-done.9
  502.8 1.2 fusion.66
  504.0 0.1 multiply_reduce_fusion.1
  504.1 0.1 fusion.75
  504.3 0.8 fusion.63
  505.1 1.1 copy-done.4
  506.2 1.3 fusion.19
  507.5 0.9 copy-done.7
  508.4 3.4 fusion.4
  511.8 0.0 reduce-scatter.8.cloned.1.call-start
  511.9 5.5 convolution_convert_fusion
  517.4 3.2 convolution_convert_fusion.1
  520.6 7.7 %pad_maximum_fusion = bf16[8192,512]{0,1:T(8,128)(2,1)} fusion(bf16[8192,256]{0,1:T(8,128)(2,1)} %convolution_convert_fusion, bf16[8192,256]{0,1:T(8,128)(2,1)} %convolution_convert_fusion.1), kind=kLoop, calls=%fused_computation.13 | loop fusion | flops 16777216 | bytes 16777216 | tf_op jit(solution)/shard_map/concatenate | solution.py:130
  528.3 0.0 reduce-scatter.6.cloned.1.call-start
  528.4 0.7 fusion.89
  529.1 59.6 %reduce-scatter.4.cloned.1.call-done = bf16[256,2048]{1,0:T(8,128)(2,1)} async-done(((bf16[256,8192]{1,0:T(8,128)(2,1)}), bf16[256,2048]{1,0:T(8,128)(2,1)}) %reduce-scatter.4.cloned.1.call-update) | async-done | bytes 1048592 | tf_op jit(solution)/shard_map/reduce_scatter | solution.py:109
  588.7 6.8 gather_fusion
  595.5 3.7 select_convert_fusion
  599.3 0.5 convolution_multiply_fusion
  599.8 0.5 copy.57
  600.3 1.2 select_convert_fusion.1
  601.6 62.2 %reduce-scatter.8.cloned.1.call-done = bf16[2048,512]{0,1:T(8,128)(2,1)} async-done(((bf16[8192,512]{0,1:T(8,128)(2,1)}), bf16[2048,512]{0,1:T(8,128)(2,1)}) %reduce-scatter.8.cloned.1.call-update) | async-done | bytes 2097168 | tf_op jit(solution)/shard_map/reduce_scatter | solution.py:129
  663.8 1.7 slice_bitcast_fusion
  665.4 1.3 copy.64
  666.7 1.3 copy.65
  668.0 30.4 %reduce-scatter.6.cloned.1.call-done = bf16[256,2048]{1,0:T(8,128)(2,1)} async-done(((bf16[512,2048]{1,0:T(8,128)(2,1)}), bf16[256,2048]{1,0:T(8,128)(2,1)}) %reduce-scatter.6.cloned.1.call-update) | async-done | bytes 1048592 | tf_op jit(solution)/shard_map/reduce_scatter | solution.py:114
  (49 shorter events, 0.3 us)
Async XLA Ops:
  7.2 2.3 copy-start
  7.2 38.2 %all-gather.7.cloned.1.call-start = ((), (), s32[]{:S(2)}) async-start(), calls=%async_computation.3 | async-start | bytes 3145728 | tf_op jit(solution)/shard_map/all_gather | solution.py:79
  7.9 96.3 %all-gather.13.cloned.1.call-start = ((), (), s32[]{:S(2)}) async-start(), calls=%async_computation.6 | async-start | bytes 5242880 | tf_op jit(solution)/shard_map/all_gather | solution.py:71
  8.7 108.9 %all-gather.11.cloned.1.call-start = ((), (), s32[]{:S(2)}) async-start(), calls=%async_computation.5 | async-start | bytes 5242880 | tf_op jit(solution)/shard_map/all_gather | solution.py:72
  9.4 191.0 %all-gather.9.cloned.1.call-start = ((), (), s32[]{:S(2)}) async-start(), calls=%async_computation.4 | async-start | bytes 5242880 | tf_op jit(solution)/shard_map/all_gather | solution.py:84
  48.8 51.1 %copy-start.12 = (bf16[1,1,512,1024]{3,2,1,0:T(8,128)(2,1)S(1)}, bf16[1,1,512,1024]{3,2,1,0:T(8,128)(2,1)}, u32[]{:S(2)}) copy-start(bf16[1,1,512,1024]{3,2,1,0:T(8,128)(2,1)} %param.25) | copy-start | bytes 3145732
  48.8 301.2 %all-gather.15.cloned.1.call-start = ((), (), s32[]{:S(2)}) async-start(), calls=%async_computation.7 | async-start | bytes 10485760 | tf_op jit(solution)/shard_map/all_gather | solution.py:57
  48.9 47.6 %collective-permute-start = (bf16[1,1,512,2048]{3,2,1,0:T(8,128)(2,1)}, bf16[1,1,512,2048]{3,2,1,0:T(8,128)(2,1)S(1)}, u32[]{:S(2)}, u32[]{:S(2)}) collective-permute-start(bf16[1,1,512,2048]{3,2,1,0:T(8,128)(2,1)} %param.13), channel_id=1, source_target_pairs={{0,16},{16,0},{1,17},{17,1},{2,18},{18,2},{3,19},{19,3},{4,20},{20... | collective-permute-start | bytes 6291464 | tf_op jit(solution)/shard_map/ppermute | solution.py:13
  96.5 1.4 copy-start.11
  97.9 4.5 copy-start.17
  98.0 357.6 %all-gather.17.cloned.1.call-start = ((), (), s32[]{:S(2)}) async-start(), calls=%async_computation.8 | async-start | bytes 20971520 | tf_op jit(solution)/shard_map/all_gather | solution.py:64
  98.5 490.2 %reduce-scatter.4.cloned.1.call-start = ((), (), s32[]{:S(2)}) async-start(), calls=%async_computation.9 | async-start | bytes 5242880 | tf_op jit(solution)/shard_map/reduce_scatter | solution.py:109
  200.4 4.9 copy-start.14
  200.4 5.7 copy-start.5
  200.4 5.9 copy-start.10
  455.5 21.4 %copy-start.16 = (f32[1,8192]{1,0:T(1,128)S(1)}, f32[1,8192]{1,0:T(1,128)}, u32[]{:S(2)}) copy-start(f32[1,8192]{1,0:T(1,128)} %param.18) | copy-start | bytes 98308
  477.0 14.8 %copy-start.15 = (f32[1,128]{1,0:T(1,128)S(1)}, f32[1,128]{1,0:T(1,128)}, u32[]{:S(2)}) copy-start(f32[1,128]{1,0:T(1,128)} %param.22) | copy-start | bytes 1540
  498.1 3.9 copy-start.8
  498.1 4.7 copy-start.9
  498.1 4.7 copy-start.13
  498.1 4.7 copy-start.18
  502.0 2.3 copy-start.2
  504.0 2.2 copy-start.4
  506.2 2.2 copy-start.7
  511.8 151.9 %reduce-scatter.8.cloned.1.call-start = ((), (), s32[]{:S(2)}) async-start(), calls=%async_computation.11 | async-start | bytes 10485760 | tf_op jit(solution)/shard_map/reduce_scatter | solution.py:129
  511.9 5.5 copy-start.6
  528.3 170.1 %reduce-scatter.6.cloned.1.call-start = ((), (), s32[]{:S(2)}) async-start(), calls=%async_computation.10 | async-start | bytes 3145728 | tf_op jit(solution)/shard_map/reduce_scatter | solution.py:114
  595.5 3.7 copy-start.3
  600.3 98.1 %copy-start.1 = (s32[1,2]{1,0:T(1,128)S(1)}, s32[1,2]{1,0:T(1,128)}, u32[]{:S(2)}) copy-start(s32[1,2]{1,0:T(1,128)} %param.17) | copy-start | bytes 28
Sparse Core Ops, SparseCore 0:
  9.6 35.7 all-gather.6
  47.0 34.4 all-gather.12
  83.1 34.4 all-gather.10
  119.6 80.7 all-gather.8
  201.8 148.1 all-gather.14
  351.4 104.1 all-gather.16
  511.9 76.7 reduce-scatter.3
  591.5 72.2 reduce-scatter.7
  666.6 31.8 reduce-scatter.5
where the time goes:
time: 706 us; the launch traced here: 705 us
  waiting for transfers between devices  561 us (79%)
  local copies, waits for them, and re-layouts  51.3 us (7%)
  matrix products  44.1 us (6%)
  other arithmetic  30.3 us (4%)
  between operations  17.4 us (2%)
    all_gather x1, waiting for transfers between devices, per_device(): full_text = lax.all_gather(arrived, 'mp', axis=3, tiled=True)[0, 0]  140 us
    all_gather x1, waiting for transfers between devices, per_device(): lax.all_gather(query_weight, 'dp', axis=1, tiled=True)[0]  100 us
    all_gather x1, waiting for transfers between devices, per_device(): image = lax.all_gather(image_part, 'mp', axis=1, tiled=True)  76.4 us
    reduce_scatter x1, waiting for transfers between devices, per_device(): lax.psum_scatter(jnp.concatenate([key_part, value_part], axis=1).astype(j...  62.2 us
    reduce_scatter x1, waiting for transfers between devices, per_device(): lax.psum_scatter(partial_bf.astype(jnp.float32).astype(jnp.bfloat16), 'mp...  59.6 us
    ppermute x1, waiting for transfers between devices, shifted(): return lax.ppermute(value, axis, pairs)  47.3 us
    all_gather x1, waiting for transfers between devices, per_device(): shard_piece = lax.all_gather(vision, 'section', axis=1, tiled=True)  34.7 us
    reduce_scatter x1, waiting for transfers between devices, per_device(): lax.psum_scatter(jnp.where((row_ids // slot_rows == wanted)[:, None], tak...  30.4 us
  transfers between devices with their start and end apart: 10, of which 9 were waited for; matrix products, arithmetic and copies ran while one was open for 10% of the time, Pallas kernels for 0%

commit v1 on v0

v1 whole, which is shorter than its diff:
```python
import jax
import jax.numpy as jnp
from jax import lax
from jax.sharding import PartitionSpec as P

HD = 128
TILE_ROWS = 64


def shifted(value, axis, steps):
    count = lax.axis_size(axis)
    pairs = [(source, (source + steps) % count) for source in range(count)]
    return lax.ppermute(value, axis, pairs)


def swapped(value, axis, mask):
    count = lax.axis_size(axis)
    pairs = [(source, source ^ mask) for source in range(count)]
    return lax.ppermute(value, axis, pairs)


def bit_order(count, high_first):
    bits = []
    step = 1
    while step < count:
        bits.append(step)
        step *= 2
    return bits[::-1] if high_first else bits


def gather_blocks(block, axis):
    count = lax.axis_size(axis)
    held = {0: block}
    for mask in bit_order(count, True):
        codes = sorted(held)
        arrived = swapped(jnp.stack([held[c] for c in codes]), axis, mask)
        for position, code in enumerate(codes):
            held[code ^ mask] = arrived[position]
    return held


def scatter_blocks(by_code, axis):
    count = lax.axis_size(axis)
    held = {code: value.astype(jnp.float32) for code, value in by_code.items()}
    for mask in bit_order(count, False):
        sent = sorted(c for c in held if c & mask)
        kept = [c ^ mask for c in sent]
        arrived = swapped(jnp.stack([held[c].astype(jnp.bfloat16) for c in sent]), axis, mask)
        held = {c: held[c] + arrived[position].astype(jnp.float32) for position, c in enumerate(kept)}
    return held[0]


def norm_rows(values, gain):
    values = values.astype(jnp.float32)
    scaled = values * lax.rsqrt(jnp.mean(values * values, axis=-1, keepdims=True) + 1e-05)
    return scaled * gain


def rounded(values):
    return lax.optimization_barrier(values.astype(jnp.bfloat16)).astype(jnp.float32)


def attend(queries, keys_raw, values_raw, key_norm, usable, present, gate_value):
    keys = rounded(norm_rows(keys_raw, key_norm))
    values = rounded(values_raw)
    text_rows, heads, depth = queries.shape
    groups = keys.shape[1]
    grouped = queries.astype(jnp.float32).reshape(text_rows, groups, heads // groups, depth)
    scores = jnp.einsum("tgjd,vgd->gjtv", grouped, keys) * depth ** (-0.5)
    scores = jnp.where(usable[None, None, None, :], scores, -1e30)
    highest = lax.stop_gradient(jnp.max(scores, axis=-1, keepdims=True))
    weights = jnp.exp(scores - highest)
    probs = rounded(weights / jnp.sum(weights, axis=-1, keepdims=True))
    context = jnp.einsum("gjtv,vgd->tgjd", probs, values).reshape(text_rows, heads * depth)
    return jnp.where(present[:, None], jnp.tanh(gate_value) * context, 0.0)


def columns_of(values, start, width):
    return lax.dynamic_slice_in_dim(values, start, width, axis=1)


def per_device(
    text_in,
    vision,
    tile_counts,
    lengths,
    image_of,
    norm_gain,
    query_weight,
    key_weight,
    value_weight,
    query_gain,
    key_gain,
    cross_gate,
    context_grad,
):
    sections = lax.axis_size("section")
    section = lax.axis_index("section")
    dp_index = lax.axis_index("dp")
    block_rows = query_weight.shape[1]

    query_blocks = gather_blocks(query_weight[0], "dp")
    key_blocks = gather_blocks(key_weight[0], "dp")
    value_blocks = gather_blocks(value_weight[0], "dp")

    arrived = shifted(text_in, "section", 1)
    full_text = lax.all_gather(arrived, "mp", axis=3, tiled=True)[0, 0]
    text_rows = full_text.shape[0]
    normed = norm_rows(full_text, norm_gain[0]).astype(jnp.bfloat16)
    width_q = query_weight.shape[2]
    query_raw = None
    for code, block in query_blocks.items():
        part = jnp.dot(
            columns_of(normed, (dp_index ^ code) * block_rows, block_rows),
            block,
            preferred_element_type=jnp.float32,
        )
        query_raw = part if query_raw is None else query_raw + part
    queries = norm_rows(query_raw.reshape(text_rows, width_q // HD, HD), query_gain[0]).astype(
        jnp.bfloat16
    )

    slot_rows = vision.shape[2]
    part_width = vision.shape[3]
    wanted = image_of[0, section]
    image_part = vision[0, 0]
    for steps in range(1, sections):
        moved = shifted(vision, "section", steps)[0, 0]
        image_part = jnp.where((section - steps) % sections == wanted, moved, image_part)
    image = lax.all_gather(image_part, "mp", axis=1, tiled=True)

    width_k = key_weight.shape[2]
    keys_raw = None
    values_raw = None
    for code in key_blocks:
        piece = columns_of(image, (dp_index ^ code) * block_rows, block_rows)
        key_part = jnp.dot(piece, key_blocks[code], preferred_element_type=jnp.float32)
        value_part = jnp.dot(piece, value_blocks[code], preferred_element_type=jnp.float32)
        keys_raw = key_part if keys_raw is None else keys_raw + key_part
        values_raw = value_part if values_raw is None else values_raw + value_part
    keys_raw = keys_raw.reshape(slot_rows, width_k // HD, HD)
    values_raw = values_raw.reshape(slot_rows, width_k // HD, HD)
    usable = jnp.arange(slot_rows) < tile_counts[0, wanted] * TILE_ROWS
    present = jnp.arange(text_rows) < lengths[0, 0]

    def forward(keys_in, values_in):
        return attend(queries, keys_in, values_in, key_gain[0], usable, present, cross_gate[0])

    context, pullback = jax.vjp(forward, keys_raw, values_raw)
    gated_context = context.astype(jnp.bfloat16).reshape(1, 1, text_rows, width_q)
    key_back, value_back = pullback(context_grad[0, 0].astype(jnp.float32))
    key_flat = key_back.reshape(slot_rows, width_k).astype(jnp.bfloat16)
    value_flat = value_back.reshape(slot_rows, width_k).astype(jnp.bfloat16)

    contract = (((1,), (1,)), ((), ()))
    partial_sum = jnp.zeros((slot_rows, image.shape[1]), jnp.bfloat16)
    for code in key_blocks:
        term = lax.dot_general(key_flat, key_blocks[code], contract, preferred_element_type=jnp.float32)
        term = term + lax.dot_general(
            value_flat, value_blocks[code], contract, preferred_element_type=jnp.float32
        )
        partial_sum = lax.dynamic_update_slice_in_dim(
            partial_sum, term.astype(jnp.bfloat16), (dp_index ^ code) * block_rows, axis=1
        )
    summed = lax.psum_scatter(partial_sum, "mp", scatter_dimension=1, tiled=True)

    routed = summed
    for steps in range(1, sections):
        moved = shifted(summed, "section", steps)
        source = (section - steps) % sections
        routed = jnp.where(image_of[0, source] == section, moved, routed)
    vision_grad = routed.reshape(1, 1, slot_rows, part_width)

    inner = (((0,), (0,)), ((), ()))
    grad_blocks = {}
    for code in key_blocks:
        piece = columns_of(image, (dp_index ^ code) * block_rows, block_rows)
        key_part = lax.dot_general(piece, key_flat, inner, preferred_element_type=jnp.float32)
        value_part = lax.dot_general(piece, value_flat, inner, preferred_element_type=jnp.float32)
        grad_blocks[code] = jnp.concatenate(
            [key_part.astype(jnp.bfloat16), value_part.astype(jnp.bfloat16)], axis=1
        )
    both_grads = scatter_blocks(grad_blocks, "dp").astype(jnp.bfloat16)
    key_weight_grad = both_grads[:, :width_k][None]
    value_weight_grad = both_grads[:, width_k:][None]
    return (gated_context, vision_grad, key_weight_grad, value_weight_grad)


def solution(mesh):
    return jax.shard_map(
        per_device,
        mesh=mesh,
        in_specs=(
            P("dp", "section", None, "mp"),
            P("dp", "section", None, "mp"),
            P("dp", None),
            P("dp", "section"),
            P("dp", None),
            P("section", None),
            P("section", "dp", "mp"),
            P("section", "dp", "mp"),
            P("section", "dp", "mp"),
            P("section", None),
            P("section", None),
            P("section"),
            P("dp", "section", None, "mp"),
        ),
        out_specs=(
            P("dp", "section", None, "mp"),
            P("dp", "section", None, "mp"),
            P("section", "dp", "mp"),
            P("section", "dp", "mp"),
        ),
        check_vma=False,
    )
```

time: 706 us -> 468 us (0.66); the launches traced: 705 us -> 459 us
  waiting for transfers between devices: 561 us -> 285 us
  local copies, waits for them, and re-layouts: 51.3 us -> 19.7 us
  matrix products: 44.1 us -> 70.6 us
  other arithmetic: 30.3 us -> 51.5 us
  starting transfers between devices: 0.74 us -> 12.8 us
    all_gather x4 -> x0, waiting for transfers between devices: 142 us -> none  [the longest x1 100 us: per_device(): lax.all_gather(query_weight, 'dp', axis=1, tiled=True)[0]]
    ppermute x0 -> x8, waiting for transfers between devices: none -> 134 us  [swapped(): return lax.ppermute(value, axis, pairs)]
    all_gather x1, waiting for transfers between devices: 140 us -> 15.4 us  [per_device(): full_text = lax.all_gather(arrived, 'mp', axis=3, tiled=True)[0, 0]]
    reduce_scatter x3 -> x1, waiting for transfers between devices: 152 us -> 51.9 us  [per_device(): lax.psum_scatter(partial_sum, 'mp', scatter_dimension=1, tiled=True)]
    all_gather x1, waiting for transfers between devices: 76.4 us -> 0.01 us  [per_device(): image = lax.all_gather(image_part, 'mp', axis=1, tiled=True)]
    ppermute x1 -> x3, waiting for transfers between devices: 47.3 us -> 84.3 us  [shifted(): return lax.ppermute(value, axis, pairs)]
    dot_general x3 -> x0, local copies, waits for them, and re-layouts: 34.2 us -> none  [the longest x1 21.4 us: per_device(): jnp.dot(columns, lax.all_gather(query_weight, 'dp', axis=1, tiled=True)[0...]
    dot_general x7 -> x28, matrix products: 34.4 us -> 59.9 us  [the longest x4 20.8 us: per_device(): jnp.dot(columns_of(normed, (dp_index ^ code) * block_rows, block_rows), b...]
  transfers between devices with their start and end apart: 10 -> 14, of which waited for: 9 -> 8; matrix products, arithmetic and copies ran while one was open for 10% -> 18% of each run, Pallas kernels for 0% -> 0%
where the time goes in v1:
time: 468 us; the launch traced here: 459 us
  waiting for transfers between devices  285 us (61%)
  matrix products  70.6 us (15%)
  other arithmetic  51.5 us (11%)
  local copies, waits for them, and re-layouts  19.7 us (4%)
  between operations  19.1 us (4%)
  starting transfers between devices  12.8 us (3%)
    ppermute x8, waiting for transfers between devices, swapped(): return lax.ppermute(value, axis, pairs)  134 us
    ppermute x3, waiting for transfers between devices, shifted(): return lax.ppermute(value, axis, pairs)  84.3 us
    reduce_scatter x1, waiting for transfers between devices, per_device(): lax.psum_scatter(partial_sum, 'mp', scatter_dimension=1, tiled=True)  51.9 us
    dot_general x4, matrix products, per_device(): jnp.dot(columns_of(normed, (dp_index ^ code) * block_rows, block_rows), b...  20.8 us
    all_gather x1, waiting for transfers between devices, per_device(): full_text = lax.all_gather(arrived, 'mp', axis=3, tiled=True)[0, 0]  15.4 us
    another operation x3, other arithmetic, gather_blocks(): arrived = swapped(jnp.stack([held[c] for c in codes]), axis, mask)  10.7 us
    convert_element_type x1, other arithmetic, per_device(): normed = norm_rows(full_text, norm_gain[0]).astype(jnp.bfloat16)  9.86 us
  transfers between devices with their start and end apart: 14, of which 8 were waited for; matrix products, arithmetic and copies ran while one was open for 18% of the time, Pallas kernels for 0%

profile of v1, /device:TPU:0, one launch (start us, length us, event | category | flops | bytes accessed | tf_op | source)
XLA Modules:
  0.0 459.1 jit_solution(15175115956844189335)
XLA Ops:
  7.2 3.0 collective-permute-start
  10.2 1.3 constant_dynamic-slice_fusion
  12.2 21.4 %collective-permute-done = bf16[1,1,256,2048]{3,2,1,0:T(8,128)(2,1)S(1)} collective-permute-done((bf16[1,1,256,2048]{3,2,1,0:T(8,128)(2,1)}, bf16[1,1,256,2048]{3,2,1,0:T(8,128)(2,1)S(1)}, u32[]{:S(2)}, u32[]{:S(2)}) %collective-permute-start) | collective-permute-done | bytes 1048608 | tf_op jit(solution)/shard_map/ppermute | solution.py:13
  33.6 1.1 broadcast_select_fusion
  34.7 1.8 collective-permute-start.5
  36.5 45.4 %collective-permute-done.5 = bf16[1,1,512,2048]{3,2,1,0:T(8,128)(2,1)} collective-permute-done((bf16[1,1,512,2048]{3,2,1,0:T(8,128)(2,1)}, bf16[1,1,512,2048]{3,2,1,0:T(8,128)(2,1)}, u32[]{:S(2)}, u32[]{:S(2)}) %collective-permute-start.5) | collective-permute-done | bytes 2097184 | tf_op jit(solution)/shard_map/ppermute | solution.py:13
  82.0 2.7 collective-permute-start.6
  84.9 111.4 %collective-permute-done.3 = bf16[1,2048,256]{2,1,0:T(8,128)(2,1)S(1)} collective-permute-done((bf16[1,2048,256]{2,1,0:T(8,128)(2,1)S(1)}, bf16[1,2048,256]{2,1,0:T(8,128)(2,1)S(1)}, u32[]{:S(2)}, u32[]{:S(2)}) %collective-permute-start.3) | collective-permute-done | bytes 1048608 | tf_op jit(solution)/shard_map/ppermute | solution.py:19
  196.2 1.5 pad_maximum_fusion.3
  197.8 1.7 collective-permute-start.1
  199.5 7.5 %pad_maximum_fusion = bf16[2,2048,1024]{2,1,0:T(8,128)(2,1)} fusion(bf16[1,2048,1024]{2,1,0:T(8,128)(2,1)} %collective-permute-done.6, bf16[1,2048,1024]{2,1,0:T(8,128)(2,1)} %param.19), kind=kLoop, calls=%fused_computation.6 | loop fusion | flops 4194304 | bytes 16777216 | tf_op jit(solution)/shard_map/stack | solution.py:36
  207.3 16.1 %collective-permute-done.1 = bf16[1,2048,256]{2,1,0:T(8,128)(2,1)S(1)} collective-permute-done((bf16[1,2048,256]{2,1,0:T(8,128)(2,1)S(1)}, bf16[1,2048,256]{2,1,0:T(8,128)(2,1)S(1)}, u32[]{:S(2)}, u32[]{:S(2)}) %collective-permute-start.1) | collective-permute-done | bytes 1048608 | tf_op jit(solution)/shard_map/ppermute | solution.py:19
  223.3 1.7 pad_maximum_fusion.2
  226.3 1.7 copy.98
  230.6 1.2 iota_compare_fusion.1
  231.9 1.9 fusion.79
  233.8 2.1 fusion.86
  235.9 1.8 convolution_add_fusion.5
  237.7 2.5 multiply_reduce_fusion.1
  240.2 1.1 copy.74
  242.6 2.2 fusion.96
  244.8 2.1 fusion.88
  246.9 1.8 convolution_add_fusion.7
  248.7 1.8 fusion.65
  250.5 2.1 fusion.52
  252.7 15.4 %all-gather.4.cloned.1.call-done = bf16[1,1,512,8192]{3,2,1,0:T(8,128)(2,1)} async-done(((bf16[1,1,512,2048]{3,2,1,0:T(8,128)(2,1)}), bf16[1,1,512,8192]{3,2,1,0:T(8,128)(2,1)}) %all-gather.4.cloned.1.call-update) | async-done | bytes 8388624 | tf_op jit(solution)/shard_map/all_gather | solution.py:107
  268.1 5.1 %fusion.1 = f32[512]{0:T(512)S(1)} fusion(bf16[1,1,512,8192]{3,2,1,0:T(8,128)(2,1)} %all-gather.4.cloned.1.call-done), kind=kLoop, calls=%fused_computation.3 | loop fusion | flops 12582400 | bytes 8390656 | tf_op jit(solution)/shard_map/reduce_sum | solution.py:55
  273.2 9.9 %fusion.3 = bf16[512,8192]{1,0:T(8,128)(2,1)} fusion(bf16[1,1,512,8192]{3,2,1,0:T(8,128)(2,1)} %all-gather.4.cloned.1.call-done, f32[8192]{0:T(1024)S(1)} %bitcast.256, f32[512]{0:T(512)S(1)} %add_rsqrt_fusion.1), kind=kLoop, calls=%fused_computation.5 | loop fusion | flops 16777216 | bytes 16812032 | tf_op jit(solution)/shard_map/convert_element_type | solution.py:109
  283.1 5.3 %fusion.18 = f32[512,1024]{1,0:T(8,128)S(1)} fusion(bf16[1,2048,1024]{2,1,0:T(8,128)(2,1)} %param.19, bf16[512,8192]{1,0:T(8,128)(2,1)} %fusion.3, s32[]{:T(128)S(6)} %select_n.91), kind=kOutput, calls=%fused_computation.30 | convolution fusion | flops 2147483648 | bytes 8388612 | tf_op jit(solution)/shard_map/dot_general | solution.py:113
  288.4 5.0 %fusion.16 = f32[512,1024]{1,0:T(8,128)S(1)} fusion(bf16[1,2048,1024]{2,1,0:T(8,128)(2,1)} %collective-permute-done.6, bf16[512,8192]{1,0:T(8,128)(2,1)S(1)} %copy-done.10, s32[]{:T(128)S(6)} %select_n.92), kind=kOutput, calls=%fused_computation.28 | convolution fusion | flops 2147483648 | bytes 8388612 | tf_op jit(solution)/shard_map/dot_general | solution.py:113
  293.4 4.6 fusion.12
  298.0 5.9 %add_add_fusion = f32[512,1024]{1,0:T(8,128)} fusion(f32[512,1024]{1,0:T(8,128)S(1)} %fusion.12, f32[512,1024]{1,0:T(8,128)S(1)} %fusion.18, f32[512,1024]{1,0:T(8,128)S(1)} %fusion.16, bf16[2,2048,1024]{2,1,0:T(8,128)(2,1)} %collective-permute-done.7, bf16[512,8192]{1,0:T(8,128)(2,1)S(1)} %copy-done.10, s32[]{:T(128)S(6)} %select_n.94), kind=kOutput, calls=%fused_computation.80 | convolution fusion | flops 2149056512 | bytes 14680068 | tf_op jit(solution)/shard_map/dot_general | solution.py:113
  303.9 3.2 reshape.185
  307.2 1.8 multiply_bitcast_fusion
  308.9 1.8 copy.101
  310.7 2.9 reduce_sum.64
  313.6 1.0 copy.75
  315.3 1.3 rsqrt.32
  316.6 5.6 %fusion.172 = (f32[2,4,512]{2,1,0:T(4,128)S(1)}, f32[2,4,512,256]{2,3,1,0:T(8,128)}) fusion(pred[256]{0:T(512)(128)(4,1)} %iota_compare_fusion.1, bf16[256,2,128]{2,0,1:T(8,128)(2,1)} %multiply_convert_fusion, f32[512,2,4,128]{3,2,1,0:T(4,128)} %reshape.185, f32[128]{0:T(128)} %bitcast.260, f32[512,2,4]{0,2,1:T(4,128)} %rsqrt.32), kind=kOutput, calls=%fused_computation.213 | convolution fusion | flops 274202880 | bytes 6456064 | tf_op jit(solution)/shard_map/jvp()/sub | solution.py:72
  322.3 5.2 %fusion.10 = (f32[2,4,512]{2,1,0:T(4,128)S(1)}, bf16[2,4,512,256]{2,3,1,0:T(8,128)(2,1)}) fusion(f32[2,4,512,256]{2,3,1,0:T(8,128)} %get-tuple-element.33, bf16[2,4,512,256]{2,3,1,0:T(8,128)(2,1)} %fusion.52, f32[2,4,512]{2,1,0:T(4,128)S(1)} %multiply_divide_fusion, f32[2,4,512]{2,1,0:T(4,128)S(1)} %get-tuple-element.32), kind=kLoop, calls=%fused_computation.15 | loop fusion | flops 6287360 | bytes 8437760 | tf_op jit(solution)/shard_map/transpose(jvp())/reduce_sum | solution.py:73
  328.3 1.7 fusion.75
  332.1 1.9 fusion.81
  334.9 2.5 broadcast_in_dim.65
  337.4 1.5 fusion.25
  339.3 1.7 fusion.114
  341.0 1.7 fusion.115
  342.8 1.5 fusion.27
  344.3 2.7 fusion.29
  347.0 2.7 fusion.31
  349.7 1.8 convolution_convert_fusion.4
  351.6 1.7 convolution_convert_fusion.5
  356.4 6.2 %collective-permute-done.9 = bf16[2,2048,512]{1,2,0:T(8,128)(2,1)S(1)} collective-permute-done((bf16[2,2048,512]{1,2,0:T(8,128)(2,1)S(1)}, bf16[2,2048,512]{1,2,0:T(8,128)(2,1)S(1)}, u32[]{:S(2)}, u32[]{:S(2)}) %collective-permute-start.9) | collective-permute-done | bytes 4194336 | tf_op jit(solution)/shard_map/ppermute | solution.py:19
  362.6 2.6 add_convert_fusion
  365.2 1.5 collective-permute-start.10
  368.3 1.7 convolution_convert_fusion.6
  370.0 1.7 convolution_convert_fusion.7
  371.7 1.2 select_convert_fusion
  372.9 51.9 %reduce-scatter.2.cloned.1.call-done = bf16[256,2048]{1,0:T(8,128)(2,1)} async-done(((bf16[256,8192]{1,0:T(8,128)(2,1)}), bf16[256,2048]{1,0:T(8,128)(2,1)}) %reduce-scatter.2.cloned.1.call-update) | async-done | bytes 1048592 | tf_op jit(solution)/shard_map/reduce_scatter | solution.py:165
  424.8 1.5 collective-permute-start.8
  426.3 3.5 fusion.13
  430.0 1.3 copy.87
  431.3 1.3 copy.88
  432.6 17.5 %collective-permute-done.8 = bf16[256,2048]{1,0:T(8,128)(2,1)} collective-permute-done((bf16[256,2048]{1,0:T(8,128)(2,1)}, bf16[256,2048]{1,0:T(8,128)(2,1)}, u32[]{:S(2)}, u32[]{:S(2)}) %collective-permute-start.8) | collective-permute-done | bytes 1048608 | tf_op jit(solution)/shard_map/ppermute | solution.py:13
  450.1 2.3 select_bitcast_fusion
  (98 shorter events, 11.6 us)
Async XLA Ops:
  7.2 224.7 %all-gather.6.cloned.1.call-start = ((), (), s32[]{:S(2)}) async-start(), calls=%async_computation.3 | async-start | bytes 5242880 | tf_op jit(solution)/shard_map/all_gather | solution.py:130
  7.2 26.4 %collective-permute-start = (bf16[1,1,256,2048]{3,2,1,0:T(8,128)(2,1)}, bf16[1,1,256,2048]{3,2,1,0:T(8,128)(2,1)S(1)}, u32[]{:S(2)}, u32[]{:S(2)}) collective-permute-start(bf16[1,1,256,2048]{3,2,1,0:T(8,128)(2,1)} %param.14), channel_id=1, source_target_pairs={{0,16},{16,0},{1,17},{17,1},{2,18},{18,2},{3,19},{19,3},{4,20},{20... | collective-permute-start | bytes 3145736 | tf_op jit(solution)/shard_map/ppermute | solution.py:13
  34.7 50.1 %copy-start.7 = (bf16[1,2048,256]{2,1,0:T(8,128)(2,1)S(1)}, bf16[1,2048,256]{2,1,0:T(8,128)(2,1)}, u32[]{:S(2)}) copy-start(bf16[1,2048,256]{2,1,0:T(8,128)(2,1)} %param.20) | copy-start | bytes 3145732
  34.7 233.4 %all-gather.4.cloned.1.call-start = ((), (), s32[]{:S(2)}) async-start(), calls=%async_computation.1 | async-start | bytes 10485760 | tf_op jit(solution)/shard_map/all_gather | solution.py:107
  34.7 47.2 %collective-permute-start.5 = (bf16[1,1,512,2048]{3,2,1,0:T(8,128)(2,1)}, bf16[1,1,512,2048]{3,2,1,0:T(8,128)(2,1)}, u32[]{:S(2)}, u32[]{:S(2)}) collective-permute-start(bf16[1,1,512,2048]{3,2,1,0:T(8,128)(2,1)} %param.13), channel_id=1, source_target_pairs={{0,16},{16,0},{1,17},{17,1},{2,18},{18,2},{3,19},{19,3},{4,20},{20... | collective-permute-start | bytes 6291464 | tf_op jit(solution)/shard_map/ppermute | solution.py:13
  82.0 115.8 %copy-start.8 = (bf16[1,2048,256]{2,1,0:T(8,128)(2,1)S(1)}, bf16[1,2048,256]{2,1,0:T(8,128)(2,1)}, u32[]{:S(2)}) copy-start(bf16[1,2048,256]{2,1,0:T(8,128)(2,1)} %param.21) | copy-start | bytes 3145732
  82.0 342.9 %reduce-scatter.2.cloned.1.call-start = ((), (), s32[]{:S(2)}) async-start(), calls=%async_computation.2 | async-start | bytes 5242880 | tf_op jit(solution)/shard_map/reduce_scatter | solution.py:165
  82.0 117.5 %collective-permute-start.6 = (bf16[1,2048,1024]{2,1,0:T(8,128)(2,1)}, bf16[1,2048,1024]{2,1,0:T(8,128)(2,1)}, u32[]{:S(2)}, u32[]{:S(2)}) collective-permute-start(bf16[1,2048,1024]{2,1,0:T(8,128)(2,1)} %param.19), channel_id=1, source_target_pairs={{0,2},{1,3},{2,0},{3,1},{4,6},{5,7},{6,4},{7,5},{8,10},{9,11},{10,... | collective-permute-start | bytes 12582920 | tf_op jit(solution)/shard_map/ppermute | solution.py:19
  84.8 111.5 %collective-permute-start.3 = (bf16[1,2048,256]{2,1,0:T(8,128)(2,1)S(1)}, bf16[1,2048,256]{2,1,0:T(8,128)(2,1)S(1)}, u32[]{:S(2)}, u32[]{:S(2)}) collective-permute-start(bf16[1,2048,256]{2,1,0:T(8,128)(2,1)S(1)} %copy-done.7), channel_id=1, source_target_pairs={{0,2},{1,3},{2,0},{3,1},{4,6},{5,7},{6,4},{7,5},{8,10},{9,11},{10,... | collective-permute-start | bytes 3145736 | tf_op jit(solution)/shard_map/ppermute | solution.py:19
  197.8 36.0 %collective-permute-start.4 = (bf16[2,2048,256]{2,1,0:T(8,128)(2,1)}, bf16[2,2048,256]{2,1,0:T(8,128)(2,1)}, u32[]{:S(2)}, u32[]{:S(2)}) collective-permute-start(bf16[2,2048,256]{2,1,0:T(8,128)(2,1)} %pad_maximum_fusion.3), channel_id=1, source_target_pairs={{0,1},{1,0},{2,3},{3,2},{4,5},{5,4},{6,7},{7,6},{8,9},{9,8},{10,11... | collective-permute-start | bytes 6291464 | tf_op jit(solution)/shard_map/ppermute | solution.py:19
  197.8 25.6 %collective-permute-start.1 = (bf16[1,2048,256]{2,1,0:T(8,128)(2,1)S(1)}, bf16[1,2048,256]{2,1,0:T(8,128)(2,1)S(1)}, u32[]{:S(2)}, u32[]{:S(2)}) collective-permute-start(bf16[1,2048,256]{2,1,0:T(8,128)(2,1)S(1)} %copy-done.8), channel_id=1, source_target_pairs={{0,2},{1,3},{2,0},{3,1},{4,6},{5,7},{6,4},{7,5},{8,10},{9,11},{10,... | collective-permute-start | bytes 3145736 | tf_op jit(solution)/shard_map/ppermute | solution.py:19
  207.0 86.3 %collective-permute-start.7 = (bf16[2,2048,1024]{2,1,0:T(8,128)(2,1)}, bf16[2,2048,1024]{2,1,0:T(8,128)(2,1)}, u32[]{:S(2)}, u32[]{:S(2)}) collective-permute-start(bf16[2,2048,1024]{2,1,0:T(8,128)(2,1)} %pad_maximum_fusion), channel_id=1, source_target_pairs={{0,1},{1,0},{2,3},{3,2},{4,5},{5,4},{6,7},{7,6},{8,9},{9,8},{10,11... | collective-permute-start | bytes 25165832 | tf_op jit(solution)/shard_map/ppermute | solution.py:19
  223.3 1.7 copy-start.5
  225.0 5.0 %copy-start.26 = (s32[1,2]{1,0:T(1,128)S(1)}, s32[1,2]{1,0:T(1,128)}, u32[]{:S(2)}) copy-start(s32[1,2]{1,0:T(1,128)} %param.15) | copy-start | bytes 28
  225.0 19.8 %collective-permute-start.2 = (bf16[2,2048,256]{2,1,0:T(8,128)(2,1)}, bf16[2,2048,256]{2,1,0:T(8,128)(2,1)}, u32[]{:S(2)}, u32[]{:S(2)}) collective-permute-start(bf16[2,2048,256]{2,1,0:T(8,128)(2,1)} %pad_maximum_fusion.2), channel_id=1, source_target_pairs={{0,1},{1,0},{2,3},{3,2},{4,5},{5,4},{6,7},{7,6},{8,9},{9,8},{10,11... | collective-permute-start | bytes 6291464 | tf_op jit(solution)/shard_map/ppermute | solution.py:19
  231.8 18.7 %copy-start.22 = (pred[512]{0:T(512)(128)(4,1)}, pred[512]{0:T(512)(128)(4,1)S(1)}, u32[]{:S(2)}) copy-start(pred[512]{0:T(512)(128)(4,1)S(1)} %iota_compare_fusion) | copy-start | bytes 1540
  231.8 4.0 copy-start
  237.7 4.2 copy-start.24
  240.1 6.8 %copy-start.19 = (f32[256,2]{0,1:T(2,128)}, f32[256,2]{0,1:T(2,128)S(1)}, u32[]{:S(2)}) copy-start(f32[256,2]{0,1:T(2,128)S(1)} %get-tuple-element.30) | copy-start | bytes 6148
  241.2 0.6 copy-start.17
  242.6 4.3 copy-start.1
  268.1 5.1 %copy-start.16 = (f32[1,8192]{1,0:T(1,128)S(1)}, f32[1,8192]{1,0:T(1,128)}, u32[]{:S(2)}) copy-start(f32[1,8192]{1,0:T(1,128)} %param.18) | copy-start | bytes 98308
  283.1 5.3 %copy-start.10 = (bf16[512,8192]{1,0:T(8,128)(2,1)S(1)}, bf16[512,8192]{1,0:T(8,128)(2,1)}, u32[]{:S(2)}) copy-start(bf16[512,8192]{1,0:T(8,128)(2,1)} %fusion.3) | copy-start | bytes 25165828
  322.2 5.3 %copy-start.11 = (bf16[2,4,512,256]{2,3,1,0:T(8,128)(2,1)S(1)}, bf16[2,4,512,256]{2,3,1,0:T(8,128)(2,1)}, u32[]{:S(2)}) copy-start(bf16[2,4,512,256]{2,3,1,0:T(8,128)(2,1)} %fusion.52) | copy-start | bytes 6291460
  322.2 5.3 %copy-start.13 = (f32[2,4,512,256]{2,3,1,0:T(8,128)S(1)}, f32[2,4,512,256]{2,3,1,0:T(8,128)}, u32[]{:S(2)}) copy-start(f32[2,4,512,256]{2,3,1,0:T(8,128)} %get-tuple-element.33) | copy-start | bytes 12582916
  322.3 6.0 %copy-start.14 = (f32[512,2,4,128]{3,2,1,0:T(4,128)S(1)}, f32[512,2,4,128]{3,2,1,0:T(4,128)}, u32[]{:S(2)}) copy-start(f32[512,2,4,128]{3,2,1,0:T(4,128)} %reshape.185) | copy-start | bytes 6291460
  322.3 6.0 %copy-start.21 = (f32[512,2,4]{0,2,1:T(4,128)S(1)}, f32[512,2,4]{0,2,1:T(4,128)}, u32[]{:S(2)}) copy-start(f32[512,2,4]{0,2,1:T(4,128)} %rsqrt.32) | copy-start | bytes 49156
  322.3 6.0 %copy-start.27 = (f32[1,128]{1,0:T(1,128)S(1)}, f32[1,128]{1,0:T(1,128)}, u32[]{:S(2)}) copy-start(f32[1,128]{1,0:T(1,128)} %param.22) | copy-start | bytes 1540
  322.3 6.0 %copy-start.28 = (pred[256]{0:T(512)(128)(4,1)S(1)}, pred[256]{0:T(512)(128)(4,1)}, u32[]{:S(2)}) copy-start(pred[256]{0:T(512)(128)(4,1)} %iota_compare_fusion.1) | copy-start | bytes 772
  328.3 1.7 copy-start.25
  328.3 1.9 copy-start.20
  328.3 1.9 copy-start.18
  330.2 3.8 copy-start.23
  332.1 1.9 copy-start.3
  334.9 2.5 copy-start.9
  337.4 1.5 copy-start.6
  349.7 3.5 copy-start.2
  355.4 7.2 %collective-permute-start.9 = (bf16[2,2048,512]{1,2,0:T(8,128)(2,1)S(1)}, bf16[2,2048,512]{1,2,0:T(8,128)(2,1)S(1)}, u32[]{:S(2)}, u32[]{:S(2)}) collective-permute-start(bf16[2,2048,512]{1,2,0:T(8,128)(2,1)S(1)} %pad_maximum_fusion.1), channel_id=1, source_target_pairs={{0,1},{1,0},{2,3},{3,2},{4,5},{5,4},{6,7},{7,6},{8,9},{9,8},{10,11... | collective-permute-start | bytes 12582920 | tf_op jit(solution)/shard_map/ppermute | solution.py:19
  356.4 10.9 %copy-start.4 = (bf16[2,4,512,256]{2,3,1,0:T(8,128)(2,1)S(1)}, bf16[2,4,512,256]{2,3,1,0:T(8,128)(2,1)}, u32[]{:S(2)}) copy-start(bf16[2,4,512,256]{2,3,1,0:T(8,128)(2,1)} %get-tuple-element.25) | copy-start | bytes 6291460
  362.6 2.6 copy-start.12
  365.2 61.1 %collective-permute-start.10 = (bf16[1,2048,512]{1,2,0:T(8,128)(2,1)}, bf16[1,2048,512]{1,2,0:T(8,128)(2,1)}, u32[]{:S(2)}, u32[]{:S(2)}) collective-permute-start(bf16[1,2048,512]{1,2,0:T(8,128)(2,1)} %add_convert_fusion), channel_id=1, source_target_pairs={{0,2},{1,3},{2,0},{3,1},{4,6},{5,7},{6,4},{7,5},{8,10},{9,11},{10,... | collective-permute-start | bytes 6291464 | tf_op jit(solution)/shard_map/ppermute | solution.py:19
  424.8 25.3 %collective-permute-start.8 = (bf16[256,2048]{1,0:T(8,128)(2,1)}, bf16[256,2048]{1,0:T(8,128)(2,1)}, u32[]{:S(2)}, u32[]{:S(2)}) collective-permute-start(bf16[256,2048]{1,0:T(8,128)(2,1)} %reduce-scatter.2.cloned.1.call-done), channel_id=1, source_target_pairs={{0,16},{16,0},{1,17},{17,1},{2,18},{18,2},{3,19},{19,3},{4,20},{20... | collective-permute-start | bytes 3145736 | tf_op jit(solution)/shard_map/ppermute | solution.py:13
  430.0 20.2 %copy-start.15 = (bf16[256,2048]{1,0:T(8,128)(2,1)S(1)}, bf16[256,2048]{1,0:T(8,128)(2,1)}, u32[]{:S(2)}) copy-start(bf16[256,2048]{1,0:T(8,128)(2,1)} %reduce-scatter.2.cloned.1.call-done) | copy-start | bytes 3145732
Sparse Core Ops, SparseCore 0:
  34.8 83.4 all-gather.5
  119.9 148.1 all-gather.3
  349.9 74.9 reduce-scatter.1

commit v2 on v1

--- a/solution.py
+++ b/solution.py
@@ -75,8 +75,13 @@
     return jnp.where(present[:, None], jnp.tanh(gate_value) * context, 0.0)
 
 
-def columns_of(values, start, width):
-    return lax.dynamic_slice_in_dim(values, start, width, axis=1)
+def code_columns(values, index, count, width):
+    pieces = [lax.dynamic_slice_in_dim(values, (index ^ code) * width, width, axis=1) for code in range(count)]
+    return jnp.concatenate(pieces, axis=1)
+
+
+def stacked(held):
+    return jnp.concatenate([held[code] for code in range(len(held))], axis=0)
 
 
 def per_device(
@@ -96,29 +101,13 @@
 ):
     sections = lax.axis_size("section")
     section = lax.axis_index("section")
+    dp_count = lax.axis_size("dp")
     dp_index = lax.axis_index("dp")
     block_rows = query_weight.shape[1]
 
-    query_blocks = gather_blocks(query_weight[0], "dp")
-    key_blocks = gather_blocks(key_weight[0], "dp")
-    value_blocks = gather_blocks(value_weight[0], "dp")
-
-    arrived = shifted(text_in, "section", 1)
-    full_text = lax.all_gather(arrived, "mp", axis=3, tiled=True)[0, 0]
-    text_rows = full_text.shape[0]
-    normed = norm_rows(full_text, norm_gain[0]).astype(jnp.bfloat16)
-    width_q = query_weight.shape[2]
-    query_raw = None
-    for code, block in query_blocks.items():
-        part = jnp.dot(
-            columns_of(normed, (dp_index ^ code) * block_rows, block_rows),
-            block,
-            preferred_element_type=jnp.float32,
-        )
-        query_raw = part if query_raw is None else query_raw + part
-    queries = norm_rows(query_raw.reshape(text_rows, width_q // HD, HD), query_gain[0]).astype(
-        jnp.bfloat16
-    )
+    query_full = stacked(gather_blocks(query_weight[0], "dp"))
+    key_full = stacked(gather_blocks(key_weight[0], "dp"))
+    value_full = stacked(gather_blocks(value_weight[0], "dp"))
 
     slot_rows = vision.shape[2]
     part_width = vision.shape[3]
@@ -128,40 +117,68 @@
         moved = shifted(vision, "section", steps)[0, 0]
         image_part = jnp.where((section - steps) % sections == wanted, moved, image_part)
     image = lax.all_gather(image_part, "mp", axis=1, tiled=True)
+    image_code = code_columns(image, dp_index, dp_count, block_rows)
 
     width_k = key_weight.shape[2]
-    keys_raw = None
-    values_raw = None
-    for code in key_blocks:
-        piece = columns_of(image, (dp_index ^ code) * block_rows, block_rows)
-        key_part = jnp.dot(piece, key_blocks[code], preferred_element_type=jnp.float32)
-        value_part = jnp.dot(piece, value_blocks[code], preferred_element_type=jnp.float32)
-        keys_raw = key_part if keys_raw is None else keys_raw + key_part
-        values_raw = value_part if values_raw is None else values_raw + value_part
-    keys_raw = keys_raw.reshape(slot_rows, width_k // HD, HD)
-    values_raw = values_raw.reshape(slot_rows, width_k // HD, HD)
+    keys_raw = jnp.dot(image_code, key_full, preferred_element_type=jnp.float32).reshape(
+        slot_rows, width_k // HD, HD
+    )
+    values_raw = jnp.dot(image_code, value_full, preferred_element_type=jnp.float32).reshape(
+        slot_rows, width_k // HD, HD
+    )
     usable = jnp.arange(slot_rows) < tile_counts[0, wanted] * TILE_ROWS
-    present = jnp.arange(text_rows) < lengths[0, 0]
-
-    def forward(keys_in, values_in):
-        return attend(queries, keys_in, values_in, key_gain[0], usable, present, cross_gate[0])
-
-    context, pullback = jax.vjp(forward, keys_raw, values_raw)
-    gated_context = context.astype(jnp.bfloat16).reshape(1, 1, text_rows, width_q)
-    key_back, value_back = pullback(context_grad[0, 0].astype(jnp.float32))
+
+    text_rows = text_in.shape[2]
+    width_q = query_weight.shape[2]
+    chunks = 4 if text_rows % 32 == 0 else 1
+    rows = text_rows // chunks
+    contexts = []
+    key_back = None
+    value_back = None
+    pieces = [
+        shifted(text_in[:, :, chunk * rows : (chunk + 1) * rows, :], "section", 1)
+        for chunk in range(chunks)
+    ]
+    first, image_code = lax.optimization_barrier((pieces[0], image_code))
+    gathered = lax.all_gather(first, "mp", axis=3, tiled=True)
+    for chunk in range(chunks):
+        full_text = gathered[0, 0]
+        if chunk + 1 < chunks:
+            following, full_text = lax.optimization_barrier((pieces[chunk + 1], full_text))
+            gathered = lax.all_gather(following, "mp", axis=3, tiled=True)
+        normed = norm_rows(full_text, norm_gain[0]).astype(jnp.bfloat16)
+        query_raw = jnp.dot(
+            code_columns(normed, dp_index, dp_count, block_rows),
+            query_full,
+            preferred_element_type=jnp.float32,
+        )
+        queries = norm_rows(query_raw.reshape(rows, width_q // HD, HD), query_gain[0]).astype(
+            jnp.bfloat16
+        )
+        present = chunk * rows + jnp.arange(rows) < lengths[0, 0]
+
+        def forward(keys_in, values_in):
+            return attend(queries, keys_in, values_in, key_gain[0], usable, present, cross_gate[0])
+
+        context, pullback = jax.vjp(forward, keys_raw, values_raw)
+        contexts.append(context.astype(jnp.bfloat16))
+        key_part, value_part = pullback(
+            context_grad[0, 0, chunk * rows : (chunk + 1) * rows].astype(jnp.float32)
+        )
+        key_back = key_part if key_back is None else key_back + key_part
+        value_back = value_part if value_back is None else value_back + value_part
+        if chunk + 1 < chunks:
+            gathered, key_back, value_back = lax.optimization_barrier((gathered, key_back, value_back))
+    gated_context = jnp.concatenate(contexts, axis=0).reshape(1, 1, text_rows, width_q)
     key_flat = key_back.reshape(slot_rows, width_k).astype(jnp.bfloat16)
     value_flat = value_back.reshape(slot_rows, width_k).astype(jnp.bfloat16)
 
     contract = (((1,), (1,)), ((), ()))
-    partial_sum = jnp.zeros((slot_rows, image.shape[1]), jnp.bfloat16)
-    for code in key_blocks:
-        term = lax.dot_general(key_flat, key_blocks[code], contract, preferred_element_type=jnp.float32)
-        term = term + lax.dot_general(
-            value_flat, value_blocks[code], contract, preferred_element_type=jnp.float32
-        )
-        partial_sum = lax.dynamic_update_slice_in_dim(
-            partial_sum, term.astype(jnp.bfloat16), (dp_index ^ code) * block_rows, axis=1
-        )
+    partial_sum = lax.dot_general(key_flat, key_full, contract, preferred_element_type=jnp.float32)
+    partial_sum = partial_sum + lax.dot_general(
+        value_flat, value_full, contract, preferred_element_type=jnp.float32
+    )
+    partial_sum = code_columns(partial_sum.astype(jnp.bfloat16), dp_index, dp_count, block_rows)
     summed = lax.psum_scatter(partial_sum, "mp", scatter_dimension=1, tiled=True)
 
     routed = summed
@@ -172,14 +189,10 @@
     vision_grad = routed.reshape(1, 1, slot_rows, part_width)
 
     inner = (((0,), (0,)), ((), ()))
-    grad_blocks = {}
-    for code in key_blocks:
-        piece = columns_of(image, (dp_index ^ code) * block_rows, block_rows)
-        key_part = lax.dot_general(piece, key_flat, inner, preferred_element_type=jnp.float32)
-        value_part = lax.dot_general(piece, value_flat, inner, preferred_element_type=jnp.float32)
-        grad_blocks[code] = jnp.concatenate(
-            [key_part.astype(jnp.bfloat16), value_part.astype(jnp.bfloat16)], axis=1
-        )
+    key_grad = lax.dot_general(image_code, key_flat, inner, preferred_element_type=jnp.float32)
+    value_grad = lax.dot_general(image_code, value_flat, inner, preferred_element_type=jnp.float32)
+    both = jnp.concatenate([key_grad.astype(jnp.bfloat16), value_grad.astype(jnp.bfloat16)], axis=1)
+    grad_blocks = {code: both[code * block_rows : (code + 1) * block_rows] for code in range(dp_count)}
     both_grads = scatter_blocks(grad_blocks, "dp").astype(jnp.bfloat16)
     key_weight_grad = both_grads[:, :width_k][None]
     value_weight_grad = both_grads[:, width_k:][None]

time: 468 us -> 577 us (1.23)
  other arithmetic: 51.5 us -> 115 us
  local copies, waits for them, and re-layouts: 19.7 us -> 39.5 us
  starting transfers between devices: 12.8 us -> 29.4 us
  matrix products: 70.6 us -> 83 us
    concatenate x0 -> x3, other arithmetic: none -> 52.3 us  [the longest x1 47.9 us: stacked(): return jnp.concatenate([held[code] for code in range(len(held))], axis=0)]
    ppermute x3 -> x6, waiting for transfers between devices: 84.3 us -> 42.4 us  [shifted(): return lax.ppermute(value, axis, pairs)]
    all_gather x1 -> x4, waiting for transfers between devices: 15.4 us -> 54.3 us  [the longest x3 29.4 us: per_device(): gathered = lax.all_gather(following, 'mp', axis=3, tiled=True)]
    all_gather x1 -> x4, starting transfers between devices: 0.04 us -> 12.7 us  [the longest x3 12.6 us: per_device(): gathered = lax.all_gather(following, 'mp', axis=3, tiled=True)]
    squeeze x0 -> x3, local copies, waits for them, and re-layouts: none -> 12.2 us  [gather_blocks(): held[code ^ mask] = arrived[position]]
    reduce_sum x2 -> x8, other arithmetic: 8.03 us -> 11.7 us  [norm_rows(): jnp.mean(values * values, axis=-1, keepdims=True) + 1e-05]
    dot_general x28 -> x10, matrix products: 59.9 us -> 58.9 us  [the longest x4 27.2 us: per_device(): jnp.dot(code_columns(normed, dp_index, dp_count, block_rows), query_full,...]
  transfers between devices with their start and end apart: 14 -> 20, of which waited for: 8 -> 10; matrix products, arithmetic and copies ran while one was open for 18% -> 33% of each run, Pallas kernels for 0% -> 0%
where the time goes in v2:
time: 577 us; the launch traced here: 567 us
  waiting for transfers between devices  280 us (49%)
  other arithmetic  115 us (20%)
  matrix products  83 us (14%)
  local copies, waits for them, and re-layouts  39.5 us (7%)
  starting transfers between devices  29.4 us (5%)
  between operations  20.2 us (4%)
    ppermute x8, waiting for transfers between devices, swapped(): return lax.ppermute(value, axis, pairs)  129 us
    reduce_scatter x1, waiting for transfers between devices, per_device(): lax.psum_scatter(partial_sum, 'mp', scatter_dimension=1, tiled=True)  54.5 us
    concatenate x1, other arithmetic, stacked(): return jnp.concatenate([held[code] for code in range(len(held))], axis=0)  47.9 us
    ppermute x6, waiting for transfers between devices, shifted(): return lax.ppermute(value, axis, pairs)  42.4 us
    all_gather x3, waiting for transfers between devices, per_device(): gathered = lax.all_gather(following, 'mp', axis=3, tiled=True)  29.4 us
    dot_general x4, matrix products, per_device(): jnp.dot(code_columns(normed, dp_index, dp_count, block_rows), query_full,...  27.2 us
    all_gather x1, waiting for transfers between devices, per_device(): gathered = lax.all_gather(first, 'mp', axis=3, tiled=True)  25 us
    all_gather x3, starting transfers between devices, per_device(): gathered = lax.all_gather(following, 'mp', axis=3, tiled=True)  12.6 us
  transfers between devices with their start and end apart: 20, of which 10 were waited for; matrix products, arithmetic and copies ran while one was open for 33% of the time, Pallas kernels for 0%

profile of v2, /device:TPU:0, one launch (start us, length us, event | category | flops | bytes accessed | tf_op | source)
XLA Modules:
  0.0 567.4 jit_solution(8521746681068985001)
XLA Ops:
  7.2 3.0 collective-permute-start
  10.2 1.3 constant_dynamic-slice_fusion.4
  12.2 21.4 %collective-permute-done = bf16[1,1,256,2048]{3,2,1,0:T(8,128)(2,1)S(1)} collective-permute-done((bf16[1,1,256,2048]{3,2,1,0:T(8,128)(2,1)}, bf16[1,1,256,2048]{3,2,1,0:T(8,128)(2,1)S(1)}, u32[]{:S(2)}, u32[]{:S(2)}) %collective-permute-start) | collective-permute-done | bytes 1048608 | tf_op jit(solution)/shard_map/ppermute | solution.py:13
  34.8 3.1 collective-permute-start.7
  37.9 1.9 collective-permute-start.1
  39.8 112.1 %collective-permute-done.3 = bf16[1,2048,256]{2,1,0:T(8,128)(2,1)S(1)} collective-permute-done((bf16[1,2048,256]{2,1,0:T(8,128)(2,1)}, bf16[1,2048,256]{2,1,0:T(8,128)(2,1)S(1)}, u32[]{:S(2)}, u32[]{:S(2)}) %collective-permute-start.3) | collective-permute-done | bytes 1048608 | tf_op jit(solution)/shard_map/ppermute | solution.py:19
  152.0 3.1 pad_maximum_fusion.9
  155.1 1.4 fusion.252
  156.5 1.5 collective-permute-start.10
  161.0 2.5 slice_convert_fusion
  163.6 9.2 %collective-permute-done.1 = bf16[1,2048,256]{2,1,0:T(8,128)(2,1)} collective-permute-done((bf16[1,2048,256]{2,1,0:T(8,128)(2,1)}, bf16[1,2048,256]{2,1,0:T(8,128)(2,1)}, u32[]{:S(2)}, u32[]{:S(2)}) %collective-permute-start.1) | collective-permute-done | bytes 1048608 | tf_op jit(solution)/shard_map/ppermute | solution.py:19
  172.8 3.1 pad_maximum_fusion.8
  175.9 6.2 %pad_maximum_fusion.1 = bf16[2,2048,1024]{2,1,0:T(8,128)(2,1)} fusion(bf16[1,2048,1024]{2,1,0:T(8,128)(2,1)} %collective-permute-done.7, bf16[1,2048,1024]{2,1,0:T(8,128)(2,1)S(1)} %copy-done.4), kind=kLoop, calls=%fused_computation.15 | loop fusion | flops 4194304 | bytes 16777216 | tf_op jit(solution)/shard_map/stack | solution.py:36
  187.0 1.6 collective-permute-start.6
  188.6 3.0 slice_bitcast_fusion.7
  191.6 2.8 dynamic-slice_bitcast_fusion.3
  194.4 2.3 pad_maximum_fusion.2
  197.6 3.5 collective-permute-done.6
  201.1 1.5 collective-permute-start.5
  202.8 3.2 slice_bitcast_fusion.9
  205.9 8.6 %multiply_reduce_fusion.4 = (f32[256,2]{0,1:T(2,128)S(1)}, f32[256,256]{0,1:T(8,128)S(1)}) fusion(bf16[2048,256]{1,0:T(8,128)(2,1)} %get-tuple-element.93, bf16[2048,256]{1,0:T(8,128)(2,1)} %bitcast.356, bf16[2048,256]{1,0:T(8,128)(2,1)} %get-tuple-element.92, bf16[2048,256]{1,0:T(8,128)(2,1)} %bitcast.354, bf16[256,2048]{1,0:T(8,128)(2,1)S(1)} %copy-done.14, ...), kind=kOutput, calls=%fused_computation.291 | convolution fusion | flops 1107426816 | bytes 8652800 | tf_op jit(solution)/shard_map/dot_general | solution.py:123
  214.7 5.2 convolution_convert_fusion.6
  224.6 25.0 %all-gather.7.cloned.1.call-done = bf16[1,1,128,8192]{3,2,1,0:T(8,128)(2,1)} async-done(((bf16[1,1,128,2048]{3,2,1,0:T(8,128)(2,1)}), bf16[1,1,128,8192]{3,2,1,0:T(8,128)(2,1)}) %all-gather.7.cloned.1.call-update) | async-done | bytes 2097168 | tf_op jit(solution)/shard_map/all_gather | solution.py:143
  249.6 2.1 fusion.5
  251.7 2.2 fusion.7
  254.0 6.0 %slice_bitcast_fusion.1 = (bf16[2048,1024]{1,0:T(8,128)(2,1)S(1)}, bf16[2048,1024]{1,0:T(8,128)(2,1)}) fusion(bf16[2,2048,1024]{2,1,0:T(8,128)(2,1)} %collective-permute-done.8), kind=kLoop, calls=%fused_computation.37 | loop fusion | bytes 16777216 | tf_op jit(solution)/shard_map/squeeze | solution.py:38
  260.1 47.9 %pad_maximum_fusion = bf16[8192,1024]{1,0:T(8,128)(2,1)S(1)} fusion(bf16[2048,1024]{1,0:T(8,128)(2,1)} %get-tuple-element.63, bf16[2048,1024]{1,0:T(8,128)(2,1)} %bitcast.27, bf16[2048,1024]{1,0:T(8,128)(2,1)S(1)} %get-tuple-element.62, bf16[2048,1024]{1,0:T(8,128)(2,1)S(1)} %bitcast.321), kind=kLoop, calls=%fused_computation.4 | loop fusion | flops 67108864 | bytes 33554432 | tf_op jit(solution)/shard_map/concatenate | solution.py:84
  308.0 5.7 %copy-done.3 = bf16[8192,1024]{1,0:T(8,128)(2,1)} copy-done((bf16[8192,1024]{1,0:T(8,128)(2,1)}, bf16[8192,1024]{1,0:T(8,128)(2,1)S(1)}, u32[]{:S(2)}) %copy-start.3) | copy-done | bytes 16777240
  313.7 2.3 fusion.25
  319.0 2.6 fusion.254
  321.6 1.6 divide_convert_fusion.3
  323.2 2.1 fusion.88
  327.5 12.5 %all-gather.13.cloned.1.call-start = ((), (), s32[]{:S(2)}) async-start(), calls=%async_computation.4 | async-start | bytes 2621440 | tf_op jit(solution)/shard_map/all_gather | solution.py:148
  340.0 2.1 fusion.8
  342.1 2.2 fusion.10
  344.5 8.2 %fusion.33 = f32[128,1024]{1,0:T(8,128)S(1)} fusion(bf16[8192,1024]{1,0:T(8,128)(2,1)} %copy-done.3, bf16[128,2048]{1,0:T(8,128)(2,1)S(1)} %get-tuple-element.83, bf16[128,2048]{1,0:T(8,128)(2,1)S(1)} %get-tuple-element.84, bf16[128,2048]{1,0:T(8,128)(2,1)S(1)} %get-tuple-element.85, bf16[128,2048]{1,0:T(8,128)(2,1)S(1)} %get-tuple-element.82), kind=kOutput, calls=%fused_computation.67 | convolution fusion | flops 2155872256 | bytes 19398656 | tf_op jit(solution)/shard_map/dot_general | solution.py:150
  355.6 2.6 fusion.257
  358.3 1.6 divide_convert_fusion.2
  359.9 2.1 fusion.87
  364.2 7.9 %all-gather.11.cloned.1.call-done = bf16[1,1,128,8192]{3,2,1,0:T(8,128)(2,1)} async-done(((bf16[1,1,128,2048]{3,2,1,0:T(8,128)(2,1)}), bf16[1,1,128,8192]{3,2,1,0:T(8,128)(2,1)}) %all-gather.11.cloned.1.call-update) | async-done | bytes 2097168 | tf_op jit(solution)/shard_map/all_gather | solution.py:148
  372.2 2.1 fusion.11
  374.3 2.2 fusion.13
  376.6 8.6 %fusion.41 = f32[128,1024]{1,0:T(8,128)S(1)} fusion(bf16[8192,1024]{1,0:T(8,128)(2,1)} %copy-done.3, bf16[128,2048]{1,0:T(8,128)(2,1)S(1)} %get-tuple-element.79, bf16[128,2048]{1,0:T(8,128)(2,1)S(1)} %get-tuple-element.80, bf16[128,2048]{1,0:T(8,128)(2,1)S(1)} %get-tuple-element.81, bf16[128,2048]{1,0:T(8,128)(2,1)S(1)} %get-tuple-element.78), kind=kOutput, calls=%fused_computation.75 | convolution fusion | flops 2155872256 | bytes 19398656 | tf_op jit(solution)/shard_map/dot_general | solution.py:150
  388.2 2.6 fusion.260
  390.9 1.6 divide_convert_fusion.1
  392.5 2.1 fusion.86
  396.8 21.4 %all-gather.13.cloned.1.call-done = bf16[1,1,128,8192]{3,2,1,0:T(8,128)(2,1)} async-done(((bf16[1,1,128,2048]{3,2,1,0:T(8,128)(2,1)}), bf16[1,1,128,8192]{3,2,1,0:T(8,128)(2,1)}) %all-gather.13.cloned.1.call-update) | async-done | bytes 2097168 | tf_op jit(solution)/shard_map/all_gather | solution.py:148
  418.2 2.1 fusion.14
  420.3 2.2 fusion.16
  422.7 8.1 %fusion.49 = f32[128,1024]{1,0:T(8,128)S(1)} fusion(bf16[8192,1024]{1,0:T(8,128)(2,1)} %copy-done.3, bf16[128,2048]{1,0:T(8,128)(2,1)S(1)} %get-tuple-element.75, bf16[128,2048]{1,0:T(8,128)(2,1)S(1)} %get-tuple-element.76, bf16[128,2048]{1,0:T(8,128)(2,1)S(1)} %get-tuple-element.77, bf16[128,2048]{1,0:T(8,128)(2,1)S(1)} %get-tuple-element.74), kind=kOutput, calls=%fused_computation.83 | convolution fusion | flops 2155872256 | bytes 19398656 | tf_op jit(solution)/shard_map/dot_general | solution.py:150
  433.8 2.6 fusion.263
  436.4 1.4 fusion.116
  439.9 7.1 %fusion.122 = f32[256,8192]{1,0:T(8,128)} fusion(bf16[256,256]{0,1:T(8,128)(2,1)S(1)} %bitcast.364, bf16[2048,256]{1,0:T(8,128)(2,1)} %get-tuple-element.87, bf16[2048,256]{1,0:T(8,128)(2,1)} %bitcast.9, bf16[2048,256]{1,0:T(8,128)(2,1)} %get-tuple-element.86, bf16[2048,256]{1,0:T(8,128)(2,1)} %bitcast.353), kind=kOutput, calls=%fused_computation.198 | convolution fusion | flops 1090519040 | bytes 12713984 | tf_op jit(solution)/shard_map/dot_general | solution.py:178
  448.3 6.0 %fusion.4 = bf16[256,8192]{1,0:T(8,128)(2,1)S(1)} fusion(f32[256,8192]{1,0:T(8,128)} %fusion.122, bf16[256,256]{0,1:T(8,128)(2,1)S(1)} %bitcast.362, bf16[2048,256]{1,0:T(8,128)(2,1)} %get-tuple-element.93, bf16[2048,256]{1,0:T(8,128)(2,1)} %bitcast.357, bf16[2048,256]{1,0:T(8,128)(2,1)} %get-tuple-element.92, bf16[2048,256]{1,0:T(8,128)(2,1)} %bitcast.355), kind=kOutput, calls=%fused_computation.14 | convolution fusion | flops 1094713344 | bytes 16908288 | tf_op jit(solution)/shard_map/dot_general | solution.py:177
  454.8 2.1 pad_maximum_fusion.5
  457.0 3.6 convolution_convert_fusion.1
  463.1 7.1 %collective-permute-done.12 = bf16[2,2048,512]{1,2,0:T(8,128)(2,1)S(1)} collective-permute-done((bf16[2,2048,512]{1,2,0:T(8,128)(2,1)S(1)}, bf16[2,2048,512]{1,2,0:T(8,128)(2,1)S(1)}, u32[]{:S(2)}, u32[]{:S(2)}) %collective-permute-start.12) | collective-permute-done | bytes 4194336 | tf_op jit(solution)/shard_map/ppermute | solution.py:19
  470.2 2.5 fusion.19
  472.9 1.5 collective-permute-start.13
  478.1 54.5 %reduce-scatter.2.cloned.1.call-done = bf16[256,2048]{1,0:T(8,128)(2,1)} async-done(((bf16[256,8192]{1,0:T(8,128)(2,1)}), bf16[256,2048]{1,0:T(8,128)(2,1)}) %reduce-scatter.2.cloned.1.call-update) | async-done | bytes 1048592 | tf_op jit(solution)/shard_map/reduce_scatter | solution.py:182
  532.6 1.5 collective-permute-start.11
  534.1 3.5 fusion.17
  540.4 17.5 %collective-permute-done.11 = bf16[256,2048]{1,0:T(8,128)(2,1)} collective-permute-done((bf16[256,2048]{1,0:T(8,128)(2,1)}, bf16[256,2048]{1,0:T(8,128)(2,1)}, u32[]{:S(2)}, u32[]{:S(2)}) %collective-permute-start.11) | collective-permute-done | bytes 1048608 | tf_op jit(solution)/shard_map/ppermute | solution.py:13
  557.9 2.3 select_bitcast_fusion
  (218 shorter events, 42.8 us)
Async XLA Ops:
  7.2 184.4 %all-gather.15.cloned.1.call-start = ((), (), s32[]{:S(2)}) async-start(), calls=%async_computation.6 | async-start | bytes 5242880 | tf_op jit(solution)/shard_map/all_gather | solution.py:119
  7.2 26.4 %collective-permute-start = (bf16[1,1,256,2048]{3,2,1,0:T(8,128)(2,1)}, bf16[1,1,256,2048]{3,2,1,0:T(8,128)(2,1)S(1)}, u32[]{:S(2)}, u32[]{:S(2)}) collective-permute-start(bf16[1,1,256,2048]{3,2,1,0:T(8,128)(2,1)} %param.14), channel_id=1, source_target_pairs={{0,16},{16,0},{1,17},{17,1},{2,18},{18,2},{3,19},{19,3},{4,20},{20... | collective-permute-start | bytes 3145736 | tf_op jit(solution)/shard_map/ppermute | solution.py:13
  12.2 142.9 %copy-start.15 = (bf16[1,1,512,2048]{3,2,1,0:T(8,128)(2,1)S(1)}, bf16[1,1,512,2048]{3,2,1,0:T(8,128)(2,1)}, u32[]{:S(2)}) copy-start(bf16[1,1,512,2048]{3,2,1,0:T(8,128)(2,1)} %param.13) | copy-start | bytes 6291460
  34.7 125.7 %copy-start.44 = (s32[1,2]{1,0:T(1,128)S(1)}, s32[1,2]{1,0:T(1,128)}, u32[]{:S(2)}) copy-start(s32[1,2]{1,0:T(1,128)} %param.15) | copy-start | bytes 28
  34.7 214.8 %all-gather.7.cloned.1.call-start = ((), (), s32[]{:S(2)}) async-start(), calls=%async_computation.1 | async-start | bytes 2621440 | tf_op jit(solution)/shard_map/all_gather | solution.py:143
  34.8 141.1 %collective-permute-start.7 = (bf16[1,2048,1024]{2,1,0:T(8,128)(2,1)}, bf16[1,2048,1024]{2,1,0:T(8,128)(2,1)}, u32[]{:S(2)}, u32[]{:S(2)}) collective-permute-start(bf16[1,2048,1024]{2,1,0:T(8,128)(2,1)} %param.19), channel_id=1, source_target_pairs={{0,2},{1,3},{2,0},{3,1},{4,6},{5,7},{6,4},{7,5},{8,10},{9,11},{10,... | collective-permute-start | bytes 12582920 | tf_op jit(solution)/shard_map/ppermute | solution.py:19
  37.8 114.2 %collective-permute-start.3 = (bf16[1,2048,256]{2,1,0:T(8,128)(2,1)}, bf16[1,2048,256]{2,1,0:T(8,128)(2,1)S(1)}, u32[]{:S(2)}, u32[]{:S(2)}) collective-permute-start(bf16[1,2048,256]{2,1,0:T(8,128)(2,1)} %param.20), channel_id=1, source_target_pairs={{0,2},{1,3},{2,0},{3,1},{4,6},{5,7},{6,4},{7,5},{8,10},{9,11},{10,... | collective-permute-start | bytes 3145736 | tf_op jit(solution)/shard_map/ppermute | solution.py:19
  37.9 134.9 %collective-permute-start.1 = (bf16[1,2048,256]{2,1,0:T(8,128)(2,1)}, bf16[1,2048,256]{2,1,0:T(8,128)(2,1)}, u32[]{:S(2)}, u32[]{:S(2)}) collective-permute-start(bf16[1,2048,256]{2,1,0:T(8,128)(2,1)} %param.21), channel_id=1, source_target_pairs={{0,2},{1,3},{2,0},{3,1},{4,6},{5,7},{6,4},{7,5},{8,10},{9,11},{10,... | collective-permute-start | bytes 3145736 | tf_op jit(solution)/shard_map/ppermute | solution.py:19
  152.0 4.5 copy-start.23
  155.1 31.9 %collective-permute-start.4 = (bf16[2,2048,256]{2,1,0:T(8,128)(2,1)}, bf16[2,2048,256]{2,1,0:T(8,128)(2,1)}, u32[]{:S(2)}, u32[]{:S(2)}) collective-permute-start(bf16[2,2048,256]{2,1,0:T(8,128)(2,1)} %pad_maximum_fusion.9), channel_id=1, source_target_pairs={{0,1},{1,0},{2,3},{3,2},{4,5},{5,4},{6,7},{7,6},{8,9},{9,8},{10,11... | collective-permute-start | bytes 6291464 | tf_op jit(solution)/shard_map/ppermute | solution.py:19
  156.5 215.7 %collective-permute-start.10 = (bf16[1,1,128,2048]{3,2,1,0:T(8,128)(2,1)}, bf16[1,1,128,2048]{3,2,1,0:T(8,128)(2,1)}, u32[]{:S(2)}, u32[]{:S(2)}) collective-permute-start(bf16[1,1,128,2048]{3,2,1,0:T(8,128)(2,1)} %get-tuple-element.96), channel_id=1, source_target_pairs={{0,16},{16,0},{1,17},{17,1},{2,18},{18,2},{3,19},{19,3},{4,20},{20... | collective-permute-start | bytes 1572872 | tf_op jit(solution)/shard_map/ppermute | solution.py:13
  158.0 169.5 %collective-permute-start.9 = (bf16[1,1,128,2048]{3,2,1,0:T(8,128)(2,1)}, bf16[1,1,128,2048]{3,2,1,0:T(8,128)(2,1)}, u32[]{:S(2)}, u32[]{:S(2)}) collective-permute-start(bf16[1,1,128,2048]{3,2,1,0:T(8,128)(2,1)} %get-tuple-element.97), channel_id=1, source_target_pairs={{0,16},{16,0},{1,17},{17,1},{2,18},{18,2},{3,19},{19,3},{4,20},{20... | collective-permute-start | bytes 1572872 | tf_op jit(solution)/shard_map/ppermute | solution.py:13
  160.4 15.4 %copy-start.4 = (bf16[1,2048,1024]{2,1,0:T(8,128)(2,1)S(1)}, bf16[1,2048,1024]{2,1,0:T(8,128)(2,1)}, u32[]{:S(2)}) copy-start(bf16[1,2048,1024]{2,1,0:T(8,128)(2,1)} %param.19) | copy-start | bytes 12582916
  175.8 26.9 %collective-permute-start.2 = (bf16[2,2048,256]{2,1,0:T(8,128)(2,1)}, bf16[2,2048,256]{2,1,0:T(8,128)(2,1)}, u32[]{:S(2)}, u32[]{:S(2)}) collective-permute-start(bf16[2,2048,256]{2,1,0:T(8,128)(2,1)} %pad_maximum_fusion.8), channel_id=1, source_target_pairs={{0,1},{1,0},{2,3},{3,2},{4,5},{5,4},{6,7},{7,6},{8,9},{9,8},{10,11... | collective-permute-start | bytes 6291464 | tf_op jit(solution)/shard_map/ppermute | solution.py:19
  182.0 72.0 %collective-permute-start.8 = (bf16[2,2048,1024]{2,1,0:T(8,128)(2,1)}, bf16[2,2048,1024]{2,1,0:T(8,128)(2,1)}, u32[]{:S(2)}, u32[]{:S(2)}) collective-permute-start(bf16[2,2048,1024]{2,1,0:T(8,128)(2,1)} %pad_maximum_fusion.1), channel_id=1, source_target_pairs={{0,1},{1,0},{2,3},{3,2},{4,5},{5,4},{6,7},{7,6},{8,9},{9,8},{10,11... | collective-permute-start | bytes 25165832 | tf_op jit(solution)/shard_map/ppermute | solution.py:19
  187.0 32.9 %copy-start.36 = (pred[128]{0:T(512)(128)(4,1)}, pred[128]{0:T(512)(128)(4,1)S(1)}, u32[]{:S(2)}) copy-start(pred[128]{0:T(512)(128)(4,1)S(1)} %get-tuple-element.125) | copy-start | bytes 388
  187.0 34.1 %copy-start.33 = (pred[128]{0:T(512)(128)(4,1)}, pred[128]{0:T(512)(128)(4,1)S(1)}, u32[]{:S(2)}) copy-start(pred[128]{0:T(512)(128)(4,1)S(1)} %get-tuple-element.124) | copy-start | bytes 388
  187.0 36.0 %copy-start.30 = (pred[128]{0:T(512)(128)(4,1)}, pred[128]{0:T(512)(128)(4,1)S(1)}, u32[]{:S(2)}) copy-start(pred[128]{0:T(512)(128)(4,1)S(1)} %get-tuple-element.123) | copy-start | bytes 388
  187.0 37.2 %copy-start.28 = (pred[128]{0:T(512)(128)(4,1)}, pred[128]{0:T(512)(128)(4,1)S(1)}, u32[]{:S(2)}) copy-start(pred[128]{0:T(512)(128)(4,1)S(1)} %get-tuple-element.122) | copy-start | bytes 388
  187.0 14.1 %collective-permute-start.6 = (bf16[1,1,128,2048]{3,2,1,0:T(8,128)(2,1)}, bf16[1,1,128,2048]{3,2,1,0:T(8,128)(2,1)S(1)}, u32[]{:S(2)}, u32[]{:S(2)}) collective-permute-start(bf16[1,1,128,2048]{3,2,1,0:T(8,128)(2,1)} %get-tuple-element.94), channel_id=1, source_target_pairs={{0,16},{16,0},{1,17},{17,1},{2,18},{18,2},{3,19},{19,3},{4,20},{20... | collective-permute-start | bytes 1572872 | tf_op jit(solution)/shard_map/ppermute | solution.py:13
  194.4 2.6 copy-start.9
  194.4 2.9 copy-start.11
  194.4 3.2 copy-start.13
  201.1 23.4 %collective-permute-start.5 = (bf16[1,1,128,2048]{3,2,1,0:T(8,128)(2,1)}, bf16[1,1,128,2048]{3,2,1,0:T(8,128)(2,1)}, u32[]{:S(2)}, u32[]{:S(2)}) collective-permute-start(bf16[1,1,128,2048]{3,2,1,0:T(8,128)(2,1)} %get-tuple-element.95), channel_id=1, source_target_pairs={{0,16},{16,0},{1,17},{17,1},{2,18},{18,2},{3,19},{19,3},{4,20},{20... | collective-permute-start | bytes 1572872 | tf_op jit(solution)/shard_map/ppermute | solution.py:13
  202.7 124.8 %all-gather.9.cloned.1.call-start = ((), (), s32[]{:S(2)}) async-start(), calls=%async_computation.2 | async-start | bytes 2621440 | tf_op jit(solution)/shard_map/all_gather | solution.py:148
  202.7 3.2 copy-start.8
  202.7 3.2 copy-start.10
  202.7 3.2 copy-start.12
  202.7 3.2 copy-start.14
  214.7 7.5 %copy-start.27 = (f32[1,128]{1,0:T(1,128)S(1)}, f32[1,128]{1,0:T(1,128)}, u32[]{:S(2)}) copy-start(f32[1,128]{1,0:T(1,128)} %param.23) | copy-start | bytes 1540
  219.9 31.8 %copy-start.24 = (f32[1,8192]{1,0:T(1,128)S(1)}, f32[1,8192]{1,0:T(1,128)}, u32[]{:S(2)}) copy-start(f32[1,8192]{1,0:T(1,128)} %param.18) | copy-start | bytes 98308
  249.5 122.6 %all-gather.11.cloned.1.call-start = ((), (), s32[]{:S(2)}) async-start(), calls=%async_computation.3 | async-start | bytes 2621440 | tf_op jit(solution)/shard_map/all_gather | solution.py:148
  254.0 6.1 %copy-start.5 = (bf16[1,2048,1024]{2,1,0:T(8,128)(2,1)S(1)}, bf16[1,2048,1024]{2,1,0:T(8,128)(2,1)}, u32[]{:S(2)}) copy-start(bf16[1,2048,1024]{2,1,0:T(8,128)(2,1)} %param.19) | copy-start | bytes 12582916
  308.0 5.7 %copy-start.3 = (bf16[8192,1024]{1,0:T(8,128)(2,1)}, bf16[8192,1024]{1,0:T(8,128)(2,1)S(1)}, u32[]{:S(2)}) copy-start(bf16[8192,1024]{1,0:T(8,128)(2,1)S(1)} %pad_maximum_fusion) | copy-start | bytes 50331652
  319.0 2.7 copy-start.41
  321.6 3.7 copy-start.37
  327.5 90.8 %all-gather.13.cloned.1.call-start = ((), (), s32[]{:S(2)}) async-start(), calls=%async_computation.4 | async-start | bytes 2621440 | tf_op jit(solution)/shard_map/all_gather | solution.py:148
  355.6 2.7 copy-start.42
  358.2 3.9 copy-start.34
  359.8 2.7 copy-start.20
  359.9 3.4 copy-start.17
  372.2 160.5 %reduce-scatter.2.cloned.1.call-start = ((), (), s32[]{:S(2)}) async-start(), calls=%async_computation.5 | async-start | bytes 5242880 | tf_op jit(solution)/shard_map/reduce_scatter | solution.py:182
  388.2 2.7 copy-start.43
  390.9 3.8 copy-start.31
  392.5 2.7 copy-start.21
  392.5 3.4 copy-start.16
  433.7 2.7 copy-start.39
  439.8 7.2 %copy-start.19 = (f32[2,4,128,256]{2,3,1,0:T(8,128)S(1)}, f32[2,4,128,256]{2,3,1,0:T(8,128)}, u32[]{:S(2)}) copy-start(f32[2,4,128,256]{2,3,1,0:T(8,128)} %get-tuple-element.121) | copy-start | bytes 3145732
  439.8 7.2 %copy-start.26 = (f32[128,2,4,128]{3,2,1,0:T(4,128)S(1)}, f32[128,2,4,128]{3,2,1,0:T(4,128)}, u32[]{:S(2)}) copy-start(f32[128,2,4,128]{3,2,1,0:T(4,128)} %reshape.315) | copy-start | bytes 1572868
  439.8 7.2 %copy-start.40 = (f32[128,8]{0,1:T(8,128)S(1)}, f32[128,8]{0,1:T(8,128)}, u32[]{:S(2)}) copy-start(f32[128,8]{0,1:T(8,128)} %copy-done.39) | copy-start | bytes 12292
  439.8 7.2 %copy-start.45 = (f32[1,128]{1,0:T(1,128)S(1)}, f32[1,128]{1,0:T(1,128)}, u32[]{:S(2)}) copy-start(f32[1,128]{1,0:T(1,128)} %param.22) | copy-start | bytes 1540
  439.9 7.2 %copy-start.46 = (pred[256]{0:T(512)(128)(4,1)S(1)}, pred[256]{0:T(512)(128)(4,1)}, u32[]{:S(2)}) copy-start(pred[256]{0:T(512)(128)(4,1)} %iota_compare_fusion) | copy-start | bytes 772
  457.0 3.6 copy-start.2
  460.6 9.6 %copy-start = (bf16[8192,256]{0,1:T(8,128)(2,1)}, bf16[8192,256]{0,1:T(8,128)(2,1)S(1)}, u32[]{:S(2)}) copy-start(bf16[8192,256]{0,1:T(8,128)(2,1)S(1)} %convolution_convert_fusion.1) | copy-start | bytes 12582916
  461.9 8.3 %copy-start.1 = (bf16[8192,256]{0,1:T(8,128)(2,1)}, bf16[8192,256]{0,1:T(8,128)(2,1)S(1)}, u32[]{:S(2)}) copy-start(bf16[8192,256]{0,1:T(8,128)(2,1)S(1)} %convolution_convert_fusion) | copy-start | bytes 12582916
  463.0 12.4 %copy-start.38 = (pred[128]{0:T(512)(128)(4,1)S(1)}, pred[128]{0:T(512)(128)(4,1)}, u32[]{:S(2)}) copy-start(pred[128]{0:T(512)(128)(4,1)} %copy-done.36) | copy-start | bytes 388
  463.0 12.9 %copy-start.35 = (pred[128]{0:T(512)(128)(4,1)S(1)}, pred[128]{0:T(512)(128)(4,1)}, u32[]{:S(2)}) copy-start(pred[128]{0:T(512)(128)(4,1)} %copy-done.33) | copy-start | bytes 388
  463.0 7.2 %collective-permute-start.12 = (bf16[2,2048,512]{1,2,0:T(8,128)(2,1)S(1)}, bf16[2,2048,512]{1,2,0:T(8,128)(2,1)S(1)}, u32[]{:S(2)}, u32[]{:S(2)}) collective-permute-start(bf16[2,2048,512]{1,2,0:T(8,128)(2,1)S(1)} %pad_maximum_fusion.6), channel_id=1, source_target_pairs={{0,1},{1,0},{2,3},{3,2},{4,5},{5,4},{6,7},{7,6},{8,9},{9,8},{10,11... | collective-permute-start | bytes 12582920 | tf_op jit(solution)/shard_map/ppermute | solution.py:19
  470.2 2.6 copy-start.6
  472.9 3.5 copy-start.32
  472.9 4.1 copy-start.29
  472.9 61.2 %collective-permute-start.13 = (bf16[1,2048,512]{1,2,0:T(8,128)(2,1)}, bf16[1,2048,512]{1,2,0:T(8,128)(2,1)}, u32[]{:S(2)}, u32[]{:S(2)}) collective-permute-start(bf16[1,2048,512]{1,2,0:T(8,128)(2,1)} %fusion.19), channel_id=1, source_target_pairs={{0,2},{1,3},{2,0},{3,1},{4,6},{5,7},{6,4},{7,5},{8,10},{9,11},{10,... | collective-permute-start | bytes 6291464 | tf_op jit(solution)/shard_map/ppermute | solution.py:19
  532.6 25.2 %collective-permute-start.11 = (bf16[256,2048]{1,0:T(8,128)(2,1)}, bf16[256,2048]{1,0:T(8,128)(2,1)}, u32[]{:S(2)}, u32[]{:S(2)}) collective-permute-start(bf16[256,2048]{1,0:T(8,128)(2,1)} %reduce-scatter.2.cloned.1.call-done), channel_id=1, source_target_pairs={{0,16},{16,0},{1,17},{17,1},{2,18},{18,2},{3,19},{19,3},{4,20},{20... | collective-permute-start | bytes 3145736 | tf_op jit(solution)/shard_map/ppermute | solution.py:13
  537.6 20.3 %copy-start.18 = (bf16[256,2048]{1,0:T(8,128)(2,1)S(1)}, bf16[256,2048]{1,0:T(8,128)(2,1)}, u32[]{:S(2)}) copy-start(bf16[256,2048]{1,0:T(8,128)(2,1)} %reduce-scatter.2.cloned.1.call-done) | copy-start | bytes 3145732
  (3 other events, 4.8 us)
Sparse Core Ops, SparseCore 0:
  34.8 83.4 all-gather.14
  202.8 46.6 all-gather.6
  251.1 44.6 all-gather.8
  327.6 44.4 all-gather.10
  373.5 44.6 all-gather.12
  457.1 75.4 reduce-scatter.1

commit v3 on v1

--- a/solution.py
+++ b/solution.py
@@ -103,23 +103,6 @@
     key_blocks = gather_blocks(key_weight[0], "dp")
     value_blocks = gather_blocks(value_weight[0], "dp")
 
-    arrived = shifted(text_in, "section", 1)
-    full_text = lax.all_gather(arrived, "mp", axis=3, tiled=True)[0, 0]
-    text_rows = full_text.shape[0]
-    normed = norm_rows(full_text, norm_gain[0]).astype(jnp.bfloat16)
-    width_q = query_weight.shape[2]
-    query_raw = None
-    for code, block in query_blocks.items():
-        part = jnp.dot(
-            columns_of(normed, (dp_index ^ code) * block_rows, block_rows),
-            block,
-            preferred_element_type=jnp.float32,
-        )
-        query_raw = part if query_raw is None else query_raw + part
-    queries = norm_rows(query_raw.reshape(text_rows, width_q // HD, HD), query_gain[0]).astype(
-        jnp.bfloat16
-    )
-
     slot_rows = vision.shape[2]
     part_width = vision.shape[3]
     wanted = image_of[0, section]
@@ -141,14 +124,49 @@
     keys_raw = keys_raw.reshape(slot_rows, width_k // HD, HD)
     values_raw = values_raw.reshape(slot_rows, width_k // HD, HD)
     usable = jnp.arange(slot_rows) < tile_counts[0, wanted] * TILE_ROWS
-    present = jnp.arange(text_rows) < lengths[0, 0]
-
-    def forward(keys_in, values_in):
-        return attend(queries, keys_in, values_in, key_gain[0], usable, present, cross_gate[0])
-
-    context, pullback = jax.vjp(forward, keys_raw, values_raw)
-    gated_context = context.astype(jnp.bfloat16).reshape(1, 1, text_rows, width_q)
-    key_back, value_back = pullback(context_grad[0, 0].astype(jnp.float32))
+
+    arrived = shifted(text_in, "section", 1)
+    text_rows = text_in.shape[2]
+    width_q = query_weight.shape[2]
+    chunks = 2 if text_rows % 16 == 0 else 1
+    rows = text_rows // chunks
+    contexts = []
+    key_back = None
+    value_back = None
+    gathered = [
+        lax.all_gather(arrived[:, :, chunk * rows : (chunk + 1) * rows], "mp", axis=3, tiled=True)
+        for chunk in range(chunks)
+    ]
+    for chunk in range(chunks):
+        lower = chunk * rows
+        full_text = gathered[chunk][0, 0]
+        normed = norm_rows(full_text, norm_gain[0]).astype(jnp.bfloat16)
+        query_raw = None
+        for code, block in query_blocks.items():
+            part = jnp.dot(
+                columns_of(normed, (dp_index ^ code) * block_rows, block_rows),
+                block,
+                preferred_element_type=jnp.float32,
+            )
+            query_raw = part if query_raw is None else query_raw + part
+        queries = norm_rows(query_raw.reshape(rows, width_q // HD, HD), query_gain[0]).astype(
+            jnp.bfloat16
+        )
+        present = lower + jnp.arange(rows) < lengths[0, 0]
+
+        def forward(keys_in, values_in):
+            return attend(queries, keys_in, values_in, key_gain[0], usable, present, cross_gate[0])
+
+        context, pullback = jax.vjp(forward, keys_raw, values_raw)
+        contexts.append(context.astype(jnp.bfloat16))
+        key_part, value_part = pullback(context_grad[0, 0, lower : lower + rows].astype(jnp.float32))
+        key_back = key_part if key_back is None else key_back + key_part
+        value_back = value_part if value_back is None else value_back + value_part
+        if chunk + 1 < chunks:
+            gathered[chunk + 1], key_back, value_back = lax.optimization_barrier(
+                (gathered[chunk + 1], key_back, value_back)
+            )
+    gated_context = jnp.concatenate(contexts, axis=0).reshape(1, 1, text_rows, width_q)
     key_flat = key_back.reshape(slot_rows, width_k).astype(jnp.bfloat16)
     value_flat = value_back.reshape(slot_rows, width_k).astype(jnp.bfloat16)
 

time: 468 us -> 442 us (0.944)
  waiting for transfers between devices: 285 us -> 263 us
  local copies, waits for them, and re-layouts: 19.7 us -> 26.4 us
  other arithmetic: 51.5 us -> 46.4 us
    ppermute x8, waiting for transfers between devices: 134 us -> 84.5 us  [swapped(): return lax.ppermute(value, axis, pairs)]
    all_gather x1 -> x2, waiting for transfers between devices: 15.4 us -> 42.9 us  [per_device(): lax.all_gather(arrived[:, :, chunk * rows:(chunk + 1) * rows], 'mp', axis...]
    convert_element_type x1 -> x2, other arithmetic: 9.86 us -> 2.37 us  [per_device(): normed = norm_rows(full_text, norm_gain[0]).astype(jnp.bfloat16)]
    unnamed x61 -> x110, local copies, waits for them, and re-layouts: 5.88 us -> 10.3 us
    dot_general x4 -> x8, matrix products: 20.8 us -> 23.5 us  [per_device(): jnp.dot(columns_of(normed, (dp_index ^ code) * block_rows, block_rows), b...]
  transfers between devices with their start and end apart: 14 -> 15, of which waited for: 8 -> 9; matrix products, arithmetic and copies ran while one was open for 18% -> 20% of each run, Pallas kernels for 0% -> 0%
where the time goes in v3:
time: 442 us; the launch traced here: 438 us
  waiting for transfers between devices  263 us (60%)
  matrix products  70.8 us (16%)
  other arithmetic  46.4 us (10%)
  local copies, waits for them, and re-layouts  26.4 us (6%)
  between operations  20.1 us (5%)
  starting transfers between devices  10.6 us (2%)
    ppermute x8, waiting for transfers between devices, swapped(): return lax.ppermute(value, axis, pairs)  84.5 us
    ppermute x3, waiting for transfers between devices, shifted(): return lax.ppermute(value, axis, pairs)  83.8 us
    reduce_scatter x1, waiting for transfers between devices, per_device(): lax.psum_scatter(partial_sum, 'mp', scatter_dimension=1, tiled=True)  52.1 us
    all_gather x2, waiting for transfers between devices, per_device(): lax.all_gather(arrived[:, :, chunk * rows:(chunk + 1) * rows], 'mp', axis...  42.9 us
    dot_general x8, matrix products, per_device(): jnp.dot(columns_of(normed, (dp_index ^ code) * block_rows, block_rows), b...  23.5 us
    another operation x3, other arithmetic, gather_blocks(): arrived = swapped(jnp.stack([held[c] for c in codes]), axis, mask)  10.6 us
    unnamed x110, local copies, waits for them, and re-layouts  10.3 us
  transfers between devices with their start and end apart: 15, of which 9 were waited for; matrix products, arithmetic and copies ran while one was open for 20% of the time, Pallas kernels for 0%

profile of v3, /device:TPU:0, one launch (start us, length us, event | category | flops | bytes accessed | tf_op | source)
XLA Modules:
  0.0 437.7 jit_solution(3981258700873169620)
XLA Ops:
  7.2 3.0 collective-permute-start
  10.2 1.4 constant_dynamic-slice_fusion
  12.3 21.3 %collective-permute-done = bf16[1,1,256,2048]{3,2,1,0:T(8,128)(2,1)S(1)} collective-permute-done((bf16[1,1,256,2048]{3,2,1,0:T(8,128)(2,1)}, bf16[1,1,256,2048]{3,2,1,0:T(8,128)(2,1)S(1)}, u32[]{:S(2)}, u32[]{:S(2)}) %collective-permute-start) | collective-permute-done | bytes 1048608 | tf_op jit(solution)/shard_map/ppermute | solution.py:13
  33.6 2.3 broadcast_select_fusion
  36.0 1.8 collective-permute-start.5
  38.1 45.0 %collective-permute-done.5 = bf16[1,1,512,2048]{3,2,1,0:T(8,128)(2,1)S(1)} collective-permute-done((bf16[1,1,512,2048]{3,2,1,0:T(8,128)(2,1)}, bf16[1,1,512,2048]{3,2,1,0:T(8,128)(2,1)S(1)}, u32[]{:S(2)}, u32[]{:S(2)}) %collective-permute-start.5) | collective-permute-done | bytes 2097184 | tf_op jit(solution)/shard_map/ppermute | solution.py:13
  83.1 1.5 fusion.242
  84.6 1.5 collective-permute-start.3
  86.7 44.9 %collective-permute-done.6 = bf16[1,2048,1024]{2,1,0:T(8,128)(2,1)} collective-permute-done((bf16[1,2048,1024]{2,1,0:T(8,128)(2,1)}, bf16[1,2048,1024]{2,1,0:T(8,128)(2,1)}, u32[]{:S(2)}, u32[]{:S(2)}) %collective-permute-start.6) | collective-permute-done | bytes 4194336 | tf_op jit(solution)/shard_map/ppermute | solution.py:19
  131.6 7.5 %pad_maximum_fusion = bf16[2,2048,1024]{2,1,0:T(8,128)(2,1)} fusion(bf16[1,2048,1024]{2,1,0:T(8,128)(2,1)} %collective-permute-done.6, bf16[1,2048,1024]{2,1,0:T(8,128)(2,1)} %param.19), kind=kLoop, calls=%fused_computation.12 | loop fusion | flops 4194304 | bytes 16777216 | tf_op jit(solution)/shard_map/stack | solution.py:36
  139.1 14.8 %collective-permute-done.3 = bf16[1,2048,256]{2,1,0:T(8,128)(2,1)S(1)} collective-permute-done((bf16[1,2048,256]{2,1,0:T(8,128)(2,1)S(1)}, bf16[1,2048,256]{2,1,0:T(8,128)(2,1)S(1)}, u32[]{:S(2)}, u32[]{:S(2)}) %collective-permute-start.3) | collective-permute-done | bytes 1048608 | tf_op jit(solution)/shard_map/ppermute | solution.py:19
  154.0 1.5 pad_maximum_fusion.3
  155.5 18.6 %collective-permute-done.1 = bf16[1,2048,256]{2,1,0:T(8,128)(2,1)S(1)} collective-permute-done((bf16[1,2048,256]{2,1,0:T(8,128)(2,1)}, bf16[1,2048,256]{2,1,0:T(8,128)(2,1)S(1)}, u32[]{:S(2)}, u32[]{:S(2)}) %collective-permute-start.1) | collective-permute-done | bytes 1048608 | tf_op jit(solution)/shard_map/ppermute | solution.py:19
  174.1 1.6 pad_maximum_fusion.2
  175.6 1.6 slice_convert_fusion
  180.0 2.5 copy.158
  182.5 2.6 copy.161
  186.3 1.2 iota_compare_fusion
  187.9 1.9 fusion.94
  189.8 2.1 fusion.101
  192.5 2.6 multiply_reduce_fusion.2
  196.9 2.2 fusion.111
  199.2 2.2 fusion.103
  201.9 1.8 fusion.72
  203.7 1.5 convolution_convert_fusion.9
  205.2 1.5 convolution_convert_fusion.8
  206.7 3.6 fusion.2
  210.8 1.2 fusion.4
  213.0 1.3 fusion.15
  214.2 3.5 fusion.11
  217.8 3.5 fusion.20
  221.3 3.5 fusion.63
  224.8 1.4 reshape.219
  227.4 3.6 fusion.244
  231.1 2.5 divide_convert_fusion.1
  237.4 42.9 %all-gather.7.cloned.1.call-done = bf16[1,1,256,8192]{3,2,1,0:T(8,128)(2,1)} async-done(((bf16[1,1,256,2048]{3,2,1,0:T(8,128)(2,1)}), bf16[1,1,256,8192]{3,2,1,0:T(8,128)(2,1)}) %all-gather.7.cloned.1.call-update) | async-done | bytes 4194320 | tf_op jit(solution)/shard_map/all_gather | solution.py:137
  280.3 3.3 fusion.5
  286.0 1.3 fusion.13
  287.2 3.5 fusion.19
  290.7 3.5 fusion.59
  294.2 3.5 fusion.62
  298.7 1.4 reshape.220
  300.2 1.4 copy.165
  302.1 3.7 fusion.249
  305.8 2.4 fusion.44
  314.3 2.5 broadcast_in_dim.96
  316.8 1.5 fusion.22
  318.7 1.7 fusion.151
  320.4 1.7 fusion.152
  322.2 1.5 fusion.24
  323.6 2.7 fusion.26
  326.4 2.8 fusion.28
  329.1 1.8 convolution_convert_fusion.4
  331.0 1.7 convolution_convert_fusion.5
  335.3 6.2 %collective-permute-done.9 = bf16[2,2048,512]{1,2,0:T(8,128)(2,1)S(1)} collective-permute-done((bf16[2,2048,512]{1,2,0:T(8,128)(2,1)S(1)}, bf16[2,2048,512]{1,2,0:T(8,128)(2,1)S(1)}, u32[]{:S(2)}, u32[]{:S(2)}) %collective-permute-start.9) | collective-permute-done | bytes 4194336 | tf_op jit(solution)/shard_map/ppermute | solution.py:19
  341.5 2.0 copy-done.19
  343.5 2.3 add_convert_fusion
  345.8 1.5 collective-permute-start.10
  352.5 52.1 %reduce-scatter.2.cloned.1.call-done = bf16[256,2048]{1,0:T(8,128)(2,1)} async-done(((bf16[256,8192]{1,0:T(8,128)(2,1)}), bf16[256,2048]{1,0:T(8,128)(2,1)}) %reduce-scatter.2.cloned.1.call-update) | async-done | bytes 1048592 | tf_op jit(solution)/shard_map/reduce_scatter | solution.py:183
  404.6 1.5 collective-permute-start.8
  406.1 3.5 fusion.8
  409.7 1.3 copy.140
  411.1 1.3 copy.141
  412.4 17.5 %collective-permute-done.8 = bf16[256,2048]{1,0:T(8,128)(2,1)} collective-permute-done((bf16[256,2048]{1,0:T(8,128)(2,1)}, bf16[256,2048]{1,0:T(8,128)(2,1)}, u32[]{:S(2)}, u32[]{:S(2)}) %collective-permute-start.8) | collective-permute-done | bytes 1048608 | tf_op jit(solution)/shard_map/ppermute | solution.py:13
  (183 shorter events, 29.4 us)
Async XLA Ops:
  7.2 180.7 %all-gather.9.cloned.1.call-start = ((), (), s32[]{:S(2)}) async-start(), calls=%async_computation.4 | async-start | bytes 5242880 | tf_op jit(solution)/shard_map/all_gather | solution.py:113
  7.2 26.4 %collective-permute-start = (bf16[1,1,256,2048]{3,2,1,0:T(8,128)(2,1)}, bf16[1,1,256,2048]{3,2,1,0:T(8,128)(2,1)S(1)}, u32[]{:S(2)}, u32[]{:S(2)}) collective-permute-start(bf16[1,1,256,2048]{3,2,1,0:T(8,128)(2,1)} %param.14), channel_id=1, source_target_pairs={{0,16},{16,0},{1,17},{17,1},{2,18},{18,2},{3,19},{19,3},{4,20},{20... | collective-permute-start | bytes 3145736 | tf_op jit(solution)/shard_map/ppermute | solution.py:13
  12.3 72.3 %copy-start.6 = (bf16[1,2048,256]{2,1,0:T(8,128)(2,1)S(1)}, bf16[1,2048,256]{2,1,0:T(8,128)(2,1)}, u32[]{:S(2)}) copy-start(bf16[1,2048,256]{2,1,0:T(8,128)(2,1)} %param.20) | copy-start | bytes 3145732
  35.9 170.8 %all-gather.5.cloned.1.call-start = ((), (), s32[]{:S(2)}) async-start(), calls=%async_computation.1 | async-start | bytes 5242880 | tf_op jit(solution)/shard_map/all_gather | solution.py:137
  36.0 47.1 %collective-permute-start.5 = (bf16[1,1,512,2048]{3,2,1,0:T(8,128)(2,1)}, bf16[1,1,512,2048]{3,2,1,0:T(8,128)(2,1)S(1)}, u32[]{:S(2)}, u32[]{:S(2)}) collective-permute-start(bf16[1,1,512,2048]{3,2,1,0:T(8,128)(2,1)} %param.13), channel_id=1, source_target_pairs={{0,16},{16,0},{1,17},{17,1},{2,18},{18,2},{3,19},{19,3},{4,20},{20... | collective-permute-start | bytes 6291464 | tf_op jit(solution)/shard_map/ppermute | solution.py:13
  37.8 93.8 %collective-permute-start.6 = (bf16[1,2048,1024]{2,1,0:T(8,128)(2,1)}, bf16[1,2048,1024]{2,1,0:T(8,128)(2,1)}, u32[]{:S(2)}, u32[]{:S(2)}) collective-permute-start(bf16[1,2048,1024]{2,1,0:T(8,128)(2,1)} %param.19), channel_id=1, source_target_pairs={{0,2},{1,3},{2,0},{3,1},{4,6},{5,7},{6,4},{7,5},{8,10},{9,11},{10,... | collective-permute-start | bytes 12582920 | tf_op jit(solution)/shard_map/ppermute | solution.py:19
  84.5 195.8 %all-gather.7.cloned.1.call-start = ((), (), s32[]{:S(2)}) async-start(), calls=%async_computation.2 | async-start | bytes 5242880 | tf_op jit(solution)/shard_map/all_gather | solution.py:137
  84.6 69.4 %collective-permute-start.3 = (bf16[1,2048,256]{2,1,0:T(8,128)(2,1)S(1)}, bf16[1,2048,256]{2,1,0:T(8,128)(2,1)S(1)}, u32[]{:S(2)}, u32[]{:S(2)}) collective-permute-start(bf16[1,2048,256]{2,1,0:T(8,128)(2,1)S(1)} %copy-done.6), channel_id=1, source_target_pairs={{0,2},{1,3},{2,0},{3,1},{4,6},{5,7},{6,4},{7,5},{8,10},{9,11},{10,... | collective-permute-start | bytes 3145736 | tf_op jit(solution)/shard_map/ppermute | solution.py:19
  86.1 88.0 %collective-permute-start.1 = (bf16[1,2048,256]{2,1,0:T(8,128)(2,1)}, bf16[1,2048,256]{2,1,0:T(8,128)(2,1)S(1)}, u32[]{:S(2)}, u32[]{:S(2)}) collective-permute-start(bf16[1,2048,256]{2,1,0:T(8,128)(2,1)} %param.21), channel_id=1, source_target_pairs={{0,2},{1,3},{2,0},{3,1},{4,6},{5,7},{6,4},{7,5},{8,10},{9,11},{10,... | collective-permute-start | bytes 3145736 | tf_op jit(solution)/shard_map/ppermute | solution.py:19
  139.1 35.0 %copy-start.8 = (bf16[1,2048,256]{2,1,0:T(8,128)(2,1)S(1)}, bf16[1,2048,256]{2,1,0:T(8,128)(2,1)}, u32[]{:S(2)}) copy-start(bf16[1,2048,256]{2,1,0:T(8,128)(2,1)} %param.21) | copy-start | bytes 3145732
  139.1 36.5 %copy-start.28 = (bf16[1,1,512,1024]{3,2,1,0:T(8,128)(2,1)S(1)}, bf16[1,1,512,1024]{3,2,1,0:T(8,128)(2,1)}, u32[]{:S(2)}) copy-start(bf16[1,1,512,1024]{3,2,1,0:T(8,128)(2,1)} %param.25) | copy-start | bytes 3145732
  139.1 78.6 %collective-permute-start.7 = (bf16[2,2048,1024]{2,1,0:T(8,128)(2,1)}, bf16[2,2048,1024]{2,1,0:T(8,128)(2,1)}, u32[]{:S(2)}, u32[]{:S(2)}) collective-permute-start(bf16[2,2048,1024]{2,1,0:T(8,128)(2,1)} %pad_maximum_fusion), channel_id=1, source_target_pairs={{0,1},{1,0},{2,3},{3,2},{4,5},{5,4},{6,7},{7,6},{8,9},{9,8},{10,11... | collective-permute-start | bytes 25165832 | tf_op jit(solution)/shard_map/ppermute | solution.py:19
  155.5 34.3 %collective-permute-start.4 = (bf16[2,2048,256]{2,1,0:T(8,128)(2,1)}, bf16[2,2048,256]{2,1,0:T(8,128)(2,1)}, u32[]{:S(2)}, u32[]{:S(2)}) collective-permute-start(bf16[2,2048,256]{2,1,0:T(8,128)(2,1)} %pad_maximum_fusion.3), channel_id=1, source_target_pairs={{0,1},{1,0},{2,3},{3,2},{4,5},{5,4},{6,7},{7,6},{8,9},{9,8},{10,11... | collective-permute-start | bytes 6291464 | tf_op jit(solution)/shard_map/ppermute | solution.py:19
  175.6 10.1 %copy-start.48 = (s32[1,2]{1,0:T(1,128)S(1)}, s32[1,2]{1,0:T(1,128)}, u32[]{:S(2)}) copy-start(s32[1,2]{1,0:T(1,128)} %param.15) | copy-start | bytes 28
  175.6 23.5 %collective-permute-start.2 = (bf16[2,2048,256]{2,1,0:T(8,128)(2,1)}, bf16[2,2048,256]{2,1,0:T(8,128)(2,1)}, u32[]{:S(2)}, u32[]{:S(2)}) collective-permute-start(bf16[2,2048,256]{2,1,0:T(8,128)(2,1)} %pad_maximum_fusion.2), channel_id=1, source_target_pairs={{0,1},{1,0},{2,3},{3,2},{4,5},{5,4},{6,7},{7,6},{8,9},{9,8},{10,11... | collective-permute-start | bytes 6291464 | tf_op jit(solution)/shard_map/ppermute | solution.py:19
  187.6 16.1 %copy-start.45 = (pred[256]{0:T(512)(128)(4,1)}, pred[256]{0:T(512)(128)(4,1)S(1)}, u32[]{:S(2)}) copy-start(pred[256]{0:T(512)(128)(4,1)S(1)} %get-tuple-element.51) | copy-start | bytes 772
  187.6 17.6 %copy-start.43 = (pred[256]{0:T(512)(128)(4,1)}, pred[256]{0:T(512)(128)(4,1)S(1)}, u32[]{:S(2)}) copy-start(pred[256]{0:T(512)(128)(4,1)S(1)} %get-tuple-element.50) | copy-start | bytes 772
  187.6 217.0 %reduce-scatter.2.cloned.1.call-start = ((), (), s32[]{:S(2)}) async-start(), calls=%async_computation.3 | async-start | bytes 5242880 | tf_op jit(solution)/shard_map/reduce_scatter | solution.py:183
  187.9 4.0 copy-start
  189.8 6.3 %copy-start.35 = (f32[1,128]{1,0:T(1,128)S(1)}, f32[1,128]{1,0:T(1,128)}, u32[]{:S(2)}) copy-start(f32[1,128]{1,0:T(1,128)} %param.23) | copy-start | bytes 1540
  192.5 8.9 %copy-start.9 = (bf16[1,2048,256]{2,1,0:T(8,128)(2,1)S(1)}, bf16[1,2048,256]{2,1,0:T(8,128)(2,1)}, u32[]{:S(2)}) copy-start(bf16[1,2048,256]{2,1,0:T(8,128)(2,1)} %param.21) | copy-start | bytes 3145732
  196.1 5.2 %copy-start.1 = (bf16[1,1,256,8192]{3,2,1,0:T(8,128)(2,1)S(1)}, bf16[1,1,256,8192]{3,2,1,0:T(8,128)(2,1)}, u32[]{:S(2)}) copy-start(bf16[1,1,256,8192]{3,2,1,0:T(8,128)(2,1)} %all-gather.9.cloned.1.call-done) | copy-start | bytes 12582916
  199.1 4.6 %copy-start.13 = (f32[1,1,256,1024]{2,3,1,0:T(8,128)S(1)}, f32[1,1,256,1024]{2,3,1,0:T(8,128)}, u32[]{:S(2)}) copy-start(f32[1,1,256,1024]{2,3,1,0:T(8,128)} %copy.158) | copy-start | bytes 3145732
  201.3 3.9 copy-start.11
  203.7 6.5 %copy-start.24 = (bf16[256,256]{0,1:T(8,128)(2,1)}, bf16[256,256]{0,1:T(8,128)(2,1)S(1)}, u32[]{:S(2)}) copy-start(bf16[256,256]{0,1:T(8,128)(2,1)S(1)} %fusion.72) | copy-start | bytes 393220
  203.7 6.5 %copy-start.33 = (f32[1,8192]{1,0:T(1,128)S(1)}, f32[1,8192]{1,0:T(1,128)}, u32[]{:S(2)}) copy-start(f32[1,8192]{1,0:T(1,128)} %param.18) | copy-start | bytes 98308
  206.7 4.1 copy-start.4
  210.8 2.2 copy-start.22
  227.4 3.7 copy-start.38
  227.4 6.2 %copy-start.14 = (f32[1,1,256,1024]{2,3,1,0:T(8,128)S(1)}, f32[1,1,256,1024]{2,3,1,0:T(8,128)}, u32[]{:S(2)}) copy-start(f32[1,1,256,1024]{2,3,1,0:T(8,128)} %copy.158) | copy-start | bytes 3145732
  231.0 2.6 copy-start.46
  231.0 3.8 copy-start.21
  231.0 3.8 copy-start.26
  231.0 3.8 copy-start.30
  231.1 3.8 copy-start.49
  231.1 3.8 copy-start.51
  231.1 3.8 copy-start.39
  233.6 2.2 copy-start.15
  235.8 47.8 %copy-start.34 = (f32[1,8192]{1,0:T(1,128)S(1)}, f32[1,8192]{1,0:T(1,128)}, u32[]{:S(2)}) copy-start(f32[1,8192]{1,0:T(1,128)} %param.18) | copy-start | bytes 98308
  280.3 3.4 copy-start.5
  283.8 2.2 copy-start.23
  302.0 3.8 copy-start.40
  302.1 6.2 %copy-start.12 = (f32[1,1,256,1024]{2,3,1,0:T(8,128)S(1)}, f32[1,1,256,1024]{2,3,1,0:T(8,128)}, u32[]{:S(2)}) copy-start(f32[1,1,256,1024]{2,3,1,0:T(8,128)} %copy.161) | copy-start | bytes 3145732
  302.1 6.2 %copy-start.44 = (pred[256]{0:T(512)(128)(4,1)S(1)}, pred[256]{0:T(512)(128)(4,1)}, u32[]{:S(2)}) copy-start(pred[256]{0:T(512)(128)(4,1)} %copy-done.43) | copy-start | bytes 772
  305.8 3.7 copy-start.20
  305.8 3.7 copy-start.27
  305.8 3.7 copy-start.31
  305.8 3.7 copy-start.50
  305.8 3.7 copy-start.52
  305.8 3.7 copy-start.41
  308.3 2.4 copy-start.17
  309.5 3.2 copy-start.7
  312.7 4.0 copy-start.10
  329.1 3.5 copy-start.2
  334.3 7.2 %collective-permute-start.9 = (bf16[2,2048,512]{1,2,0:T(8,128)(2,1)S(1)}, bf16[2,2048,512]{1,2,0:T(8,128)(2,1)S(1)}, u32[]{:S(2)}, u32[]{:S(2)}) collective-permute-start(bf16[2,2048,512]{1,2,0:T(8,128)(2,1)S(1)} %pad_maximum_fusion.1), channel_id=1, source_target_pairs={{0,1},{1,0},{2,3},{3,2},{4,5},{5,4},{6,7},{7,6},{8,9},{9,8},{10,11... | collective-permute-start | bytes 12582920 | tf_op jit(solution)/shard_map/ppermute | solution.py:19
  334.8 13.0 %copy-start.16 = (bf16[2,4,256,256]{2,3,1,0:T(8,128)(2,1)S(1)}, bf16[2,4,256,256]{2,3,1,0:T(8,128)(2,1)}, u32[]{:S(2)}) copy-start(bf16[2,4,256,256]{2,3,1,0:T(8,128)(2,1)} %copy-done.15) | copy-start | bytes 3145732
  334.8 13.0 %copy-start.25 = (bf16[256,256]{0,1:T(8,128)(2,1)S(1)}, bf16[256,256]{0,1:T(8,128)(2,1)}, u32[]{:S(2)}) copy-start(bf16[256,256]{0,1:T(8,128)(2,1)} %copy-done.24) | copy-start | bytes 393220
  335.3 13.1 %copy-start.18 = (bf16[2,4,256,256]{2,3,1,0:T(8,128)(2,1)S(1)}, bf16[2,4,256,256]{2,3,1,0:T(8,128)(2,1)}, u32[]{:S(2)}) copy-start(bf16[2,4,256,256]{2,3,1,0:T(8,128)(2,1)} %copy-done.17) | copy-start | bytes 3145732
  341.5 2.0 copy-start.19
  345.8 3.2 copy-start.47
  345.8 60.3 %collective-permute-start.10 = (bf16[1,2048,512]{1,2,0:T(8,128)(2,1)}, bf16[1,2048,512]{1,2,0:T(8,128)(2,1)}, u32[]{:S(2)}, u32[]{:S(2)}) collective-permute-start(bf16[1,2048,512]{1,2,0:T(8,128)(2,1)} %add_convert_fusion), channel_id=1, source_target_pairs={{0,2},{1,3},{2,0},{3,1},{4,6},{5,7},{6,4},{7,5},{8,10},{9,11},{10,... | collective-permute-start | bytes 6291464 | tf_op jit(solution)/shard_map/ppermute | solution.py:19
  349.0 2.6 copy-start.3
  404.6 25.3 %collective-permute-start.8 = (bf16[256,2048]{1,0:T(8,128)(2,1)}, bf16[256,2048]{1,0:T(8,128)(2,1)}, u32[]{:S(2)}, u32[]{:S(2)}) collective-permute-start(bf16[256,2048]{1,0:T(8,128)(2,1)} %reduce-scatter.2.cloned.1.call-done), channel_id=1, source_target_pairs={{0,16},{16,0},{1,17},{17,1},{2,18},{18,2},{3,19},{19,3},{4,20},{20... | collective-permute-start | bytes 3145736 | tf_op jit(solution)/shard_map/ppermute | solution.py:13
  409.6 20.3 %copy-start.29 = (bf16[256,2048]{1,0:T(8,128)(2,1)S(1)}, bf16[256,2048]{1,0:T(8,128)(2,1)}, u32[]{:S(2)}) copy-start(bf16[256,2048]{1,0:T(8,128)(2,1)} %reduce-scatter.2.cloned.1.call-done) | copy-start | bytes 3145732
  (4 other events, 4.7 us)
Sparse Core Ops, SparseCore 0:
  36.0 81.2 all-gather.8
  119.5 79.2 all-gather.4
  201.0 79.2 all-gather.6
  329.3 75.2 reduce-scatter.1

commit v4 on v3

--- a/solution.py
+++ b/solution.py
@@ -106,11 +106,11 @@
     slot_rows = vision.shape[2]
     part_width = vision.shape[3]
     wanted = image_of[0, section]
-    image_part = vision[0, 0]
+    owned = lax.all_gather(vision[0, 0], "mp", axis=1, tiled=True)
+    image = owned
     for steps in range(1, sections):
-        moved = shifted(vision, "section", steps)[0, 0]
-        image_part = jnp.where((section - steps) % sections == wanted, moved, image_part)
-    image = lax.all_gather(image_part, "mp", axis=1, tiled=True)
+        moved = shifted(owned, "section", steps)
+        image = jnp.where((section - steps) % sections == wanted, moved, image)
 
     width_k = key_weight.shape[2]
     keys_raw = None

time: 442 us -> 450 us (1.018)
  waiting for transfers between devices: 263 us -> 250 us
  other arithmetic: 46.4 us -> 54 us
  matrix products: 70.8 us -> 77.9 us
  local copies, waits for them, and re-layouts: 26.4 us -> 32.9 us
    all_gather x2, waiting for transfers between devices: 42.9 us -> 14.3 us  [per_device(): lax.all_gather(arrived[:, :, chunk * rows:(chunk + 1) * rows], 'mp', axis...]
    ppermute x3, waiting for transfers between devices: 83.8 us -> 60.7 us  [shifted(): return lax.ppermute(value, axis, pairs)]
    ppermute x8, waiting for transfers between devices: 84.5 us -> 106 us  [swapped(): return lax.ppermute(value, axis, pairs)]
    all_gather x1, waiting for transfers between devices: 0.02 us -> 17 us  [per_device(): owned = lax.all_gather(vision[0, 0], 'mp', axis=1, tiled=True)]
    unnamed x110 -> x116, local copies, waits for them, and re-layouts: 10.3 us -> 14.1 us
  transfers between devices with their start and end apart: 15 -> 15, of which waited for: 9 -> 8; matrix products, arithmetic and copies ran while one was open for 20% -> 23% of each run, Pallas kernels for 0% -> 0%
where the time goes in v4:
time: 450 us; the launch traced here: 446 us
  waiting for transfers between devices  250 us (56%)
  matrix products  77.9 us (17%)
  other arithmetic  54 us (12%)
  local copies, waits for them, and re-layouts  32.9 us (7%)
  between operations  19.3 us (4%)
  starting transfers between devices  12.2 us (3%)
    ppermute x8, waiting for transfers between devices, swapped(): return lax.ppermute(value, axis, pairs)  106 us
    ppermute x3, waiting for transfers between devices, shifted(): return lax.ppermute(value, axis, pairs)  60.7 us
    reduce_scatter x1, waiting for transfers between devices, per_device(): lax.psum_scatter(partial_sum, 'mp', scatter_dimension=1, tiled=True)  51.4 us
    dot_general x8, matrix products, per_device(): jnp.dot(columns_of(normed, (dp_index ^ code) * block_rows, block_rows), b...  27.1 us
    all_gather x1, waiting for transfers between devices, per_device(): owned = lax.all_gather(vision[0, 0], 'mp', axis=1, tiled=True)  17 us
    all_gather x2, waiting for transfers between devices, per_device(): lax.all_gather(arrived[:, :, chunk * rows:(chunk + 1) * rows], 'mp', axis...  14.3 us
    unnamed x116, local copies, waits for them, and re-layouts  14.1 us
    another operation x3, other arithmetic, gather_blocks(): arrived = swapped(jnp.stack([held[c] for c in codes]), axis, mask)  11.8 us
  transfers between devices with their start and end apart: 15, of which 8 were waited for; matrix products, arithmetic and copies ran while one was open for 23% of the time, Pallas kernels for 0%

profile of v4, /device:TPU:0, one launch (start us, length us, event | category | flops | bytes accessed | tf_op | source)
XLA Modules:
  0.0 446.1 jit_solution(8309002358217120080)
XLA Ops:
  8.0 3.0 collective-permute-start.5
  11.0 45.8 %collective-permute-done.5 = bf16[1,1,512,2048]{3,2,1,0:T(8,128)(2,1)S(1)} collective-permute-done((bf16[1,1,512,2048]{3,2,1,0:T(8,128)(2,1)}, bf16[1,1,512,2048]{3,2,1,0:T(8,128)(2,1)S(1)}, u32[]{:S(2)}, u32[]{:S(2)}) %collective-permute-start.5) | collective-permute-done | bytes 2097184 | tf_op jit(solution)/shard_map/ppermute | solution.py:13
  56.8 1.5 fusion.230
  58.3 1.8 collective-permute-start.6
  60.4 1.8 collective-permute-start.1
  65.9 2.8 slice_convert_fusion
  68.7 2.5 copy.158
  71.2 2.5 copy.161
  76.1 17.0 %all-gather.9.cloned.1.call-done = bf16[1,1,256,8192]{3,2,1,0:T(8,128)(2,1)} async-done(((bf16[1,1,256,2048]{3,2,1,0:T(8,128)(2,1)}), bf16[1,1,256,8192]{3,2,1,0:T(8,128)(2,1)}) %all-gather.9.cloned.1.call-update) | async-done | bytes 4194320 | tf_op jit(solution)/shard_map/all_gather | solution.py:109
  93.1 1.5 collective-permute-start
  94.6 80.0 %collective-permute-done.3 = bf16[1,2048,256]{2,1,0:T(8,128)(2,1)S(1)} collective-permute-done((bf16[1,2048,256]{2,1,0:T(8,128)(2,1)S(1)}, bf16[1,2048,256]{2,1,0:T(8,128)(2,1)S(1)}, u32[]{:S(2)}, u32[]{:S(2)}) %collective-permute-start.3) | collective-permute-done | bytes 1048608 | tf_op jit(solution)/shard_map/ppermute | solution.py:19
  174.6 1.5 pad_maximum_fusion.3
  176.2 19.4 %collective-permute-done.1 = bf16[1,2048,256]{2,1,0:T(8,128)(2,1)} collective-permute-done((bf16[1,2048,256]{2,1,0:T(8,128)(2,1)S(1)}, bf16[1,2048,256]{2,1,0:T(8,128)(2,1)}, u32[]{:S(2)}, u32[]{:S(2)}) %collective-permute-start.1) | collective-permute-done | bytes 1048608 | tf_op jit(solution)/shard_map/ppermute | solution.py:19
  195.5 2.8 pad_maximum_fusion.2
  198.6 7.5 %pad_maximum_fusion = bf16[2,2048,1024]{2,1,0:T(8,128)(2,1)} fusion(bf16[1,2048,1024]{2,1,0:T(8,128)(2,1)} %collective-permute-done.6, bf16[1,2048,1024]{2,1,0:T(8,128)(2,1)} %param.19), kind=kLoop, calls=%fused_computation.12 | loop fusion | flops 4194304 | bytes 16777216 | tf_op jit(solution)/shard_map/stack | solution.py:36
  206.6 3.6 fusion.2
  212.9 2.3 fusion.15
  215.3 4.6 %fusion.11 = f32[256,1024]{1,0:T(8,128)} fusion(bf16[1,2048,1024]{2,1,0:T(8,128)(2,1)} %collective-permute-done.6, bf16[256,8192]{1,0:T(8,128)(2,1)S(1)} %fusion.4, s32[]{:T(128)S(6)} %select_n.103), kind=kOutput, calls=%fused_computation.21 | convolution fusion | flops 1073741824 | bytes 6291460 | tf_op jit(solution)/shard_map/dot_general | solution.py:146
  219.9 2.8 broadcast_select_fusion
  223.3 2.6 fusion.139
  225.9 1.8 fusion.140
  230.9 2.6 fusion.136
  233.5 2.2 fusion.138
  235.6 1.9 fusion.103
  238.1 1.4 convolution_convert_fusion.9
  239.6 1.5 convolution_convert_fusion.8
  241.1 3.6 fusion.20
  244.7 4.7 %fusion.63 = f32[256,1024]{1,0:T(8,128)} fusion(f32[256,1024]{1,0:T(8,128)S(1)} %fusion.20, bf16[2,2048,1024]{2,1,0:T(8,128)(2,1)} %collective-permute-done.7, bf16[256,8192]{1,0:T(8,128)(2,1)S(1)} %copy-done.17, s32[]{:T(128)S(6)} %select_n.104, f32[256,1024]{1,0:T(8,128)S(1)} %copy-done.30, f32[256,1024]{1,0:T(8,128)S(1)} %copy-done.31), kind=kOutput, calls=%fused_computation.100 | convolution fusion | flops 1074528256 | bytes 9437188 | tf_op jit(solution)/shard_map/dot_general | solution.py:146
  249.5 2.7 reshape.217
  254.6 1.6 reduce_sum.99
  256.3 3.5 fusion.232
  259.9 2.4 divide_convert_fusion.1
  266.3 14.3 %all-gather.7.cloned.1.call-done = bf16[1,1,256,8192]{3,2,1,0:T(8,128)(2,1)} async-done(((bf16[1,1,256,2048]{3,2,1,0:T(8,128)(2,1)}), bf16[1,1,256,8192]{3,2,1,0:T(8,128)(2,1)}) %all-gather.7.cloned.1.call-update) | async-done | bytes 4194320 | tf_op jit(solution)/shard_map/all_gather | solution.py:137
  280.6 3.3 fusion.5
  287.5 3.5 fusion.19
  291.0 3.5 fusion.59
  294.5 3.5 fusion.62
  300.0 2.7 reshape.218
  302.7 2.4 copy.165
  305.1 1.6 reduce_sum.107
  306.8 3.9 fusion.237
  310.8 2.4 fusion.44
  313.8 2.6 convolution_convert_fusion.4
  320.0 2.5 broadcast_in_dim.96
  322.5 1.5 fusion.22
  324.1 1.7 fusion.101
  325.8 1.7 fusion.135
  327.5 1.7 fusion.137
  329.2 1.6 fusion.24
  330.8 2.8 fusion.26
  333.6 2.8 fusion.28
  336.4 1.8 convolution_convert_fusion.5
  338.2 1.7 convolution_convert_fusion.2
  342.2 6.2 %collective-permute-done.9 = bf16[2,2048,512]{1,2,0:T(8,128)(2,1)S(1)} collective-permute-done((bf16[2,2048,512]{1,2,0:T(8,128)(2,1)S(1)}, bf16[2,2048,512]{1,2,0:T(8,128)(2,1)S(1)}, u32[]{:S(2)}, u32[]{:S(2)}) %collective-permute-start.9) | collective-permute-done | bytes 4194336 | tf_op jit(solution)/shard_map/ppermute | solution.py:19
  348.4 2.0 copy-done.19
  350.4 2.3 add_convert_fusion
  352.7 1.5 collective-permute-start.10
  359.0 1.4 convolution_convert_fusion.7
  360.4 51.4 %reduce-scatter.2.cloned.1.call-done = bf16[256,2048]{1,0:T(8,128)(2,1)} async-done(((bf16[256,8192]{1,0:T(8,128)(2,1)}), bf16[256,2048]{1,0:T(8,128)(2,1)}) %reduce-scatter.2.cloned.1.call-update) | async-done | bytes 1048592 | tf_op jit(solution)/shard_map/reduce_scatter | solution.py:183
  411.8 1.5 collective-permute-start.8
  413.3 4.0 fusion.8
  418.5 2.3 copy.140
  422.2 14.9 %collective-permute-done.8 = bf16[256,2048]{1,0:T(8,128)(2,1)} collective-permute-done((bf16[256,2048]{1,0:T(8,128)(2,1)}, bf16[256,2048]{1,0:T(8,128)(2,1)}, u32[]{:S(2)}, u32[]{:S(2)}) %collective-permute-start.8) | collective-permute-done | bytes 1048608 | tf_op jit(solution)/shard_map/ppermute | solution.py:13
  437.0 2.3 select_bitcast_fusion
  (189 shorter events, 36.2 us)
Async XLA Ops:
  7.2 53.0 %copy-start.6 = (bf16[1,2048,256]{2,1,0:T(8,128)(2,1)S(1)}, bf16[1,2048,256]{2,1,0:T(8,128)(2,1)}, u32[]{:S(2)}) copy-start(bf16[1,2048,256]{2,1,0:T(8,128)(2,1)} %param.20) | copy-start | bytes 3145732
  7.2 53.3 %copy-start.7 = (bf16[1,2048,256]{2,1,0:T(8,128)(2,1)S(1)}, bf16[1,2048,256]{2,1,0:T(8,128)(2,1)}, u32[]{:S(2)}) copy-start(bf16[1,2048,256]{2,1,0:T(8,128)(2,1)} %param.21) | copy-start | bytes 3145732
  7.2 55.0 %copy-start.50 = (s32[1,2]{1,0:T(1,128)S(1)}, s32[1,2]{1,0:T(1,128)}, u32[]{:S(2)}) copy-start(s32[1,2]{1,0:T(1,128)} %param.17) | copy-start | bytes 28
  7.2 85.9 %all-gather.9.cloned.1.call-start = ((), (), s32[]{:S(2)}) async-start(), calls=%async_computation.4 | async-start | bytes 5242880 | tf_op jit(solution)/shard_map/all_gather | solution.py:109
  7.9 198.7 %all-gather.5.cloned.1.call-start = ((), (), s32[]{:S(2)}) async-start(), calls=%async_computation.1 | async-start | bytes 5242880 | tf_op jit(solution)/shard_map/all_gather | solution.py:137
  8.0 48.8 %collective-permute-start.5 = (bf16[1,1,512,2048]{3,2,1,0:T(8,128)(2,1)}, bf16[1,1,512,2048]{3,2,1,0:T(8,128)(2,1)S(1)}, u32[]{:S(2)}, u32[]{:S(2)}) collective-permute-start(bf16[1,1,512,2048]{3,2,1,0:T(8,128)(2,1)} %param.13), channel_id=1, source_target_pairs={{0,16},{16,0},{1,17},{17,1},{2,18},{18,2},{3,19},{19,3},{4,20},{20... | collective-permute-start | bytes 6291464 | tf_op jit(solution)/shard_map/ppermute | solution.py:13
  58.3 16.1 %copy-start.51 = (s32[1,2]{1,0:T(1,128)S(1)}, s32[1,2]{1,0:T(1,128)}, u32[]{:S(2)}) copy-start(s32[1,2]{1,0:T(1,128)} %param.15) | copy-start | bytes 28
  58.3 222.3 %all-gather.7.cloned.1.call-start = ((), (), s32[]{:S(2)}) async-start(), calls=%async_computation.2 | async-start | bytes 5242880 | tf_op jit(solution)/shard_map/all_gather | solution.py:137
  58.3 140.2 %collective-permute-start.6 = (bf16[1,2048,1024]{2,1,0:T(8,128)(2,1)}, bf16[1,2048,1024]{2,1,0:T(8,128)(2,1)}, u32[]{:S(2)}, u32[]{:S(2)}) collective-permute-start(bf16[1,2048,1024]{2,1,0:T(8,128)(2,1)} %param.19), channel_id=1, source_target_pairs={{0,2},{1,3},{2,0},{3,1},{4,6},{5,7},{6,4},{7,5},{8,10},{9,11},{10,... | collective-permute-start | bytes 12582920 | tf_op jit(solution)/shard_map/ppermute | solution.py:19
  60.2 114.4 %collective-permute-start.3 = (bf16[1,2048,256]{2,1,0:T(8,128)(2,1)S(1)}, bf16[1,2048,256]{2,1,0:T(8,128)(2,1)S(1)}, u32[]{:S(2)}, u32[]{:S(2)}) collective-permute-start(bf16[1,2048,256]{2,1,0:T(8,128)(2,1)S(1)} %copy-done.6), channel_id=1, source_target_pairs={{0,2},{1,3},{2,0},{3,1},{4,6},{5,7},{6,4},{7,5},{8,10},{9,11},{10,... | collective-permute-start | bytes 3145736 | tf_op jit(solution)/shard_map/ppermute | solution.py:19
  60.4 135.1 %collective-permute-start.1 = (bf16[1,2048,256]{2,1,0:T(8,128)(2,1)S(1)}, bf16[1,2048,256]{2,1,0:T(8,128)(2,1)}, u32[]{:S(2)}, u32[]{:S(2)}) collective-permute-start(bf16[1,2048,256]{2,1,0:T(8,128)(2,1)S(1)} %copy-done.7), channel_id=1, source_target_pairs={{0,2},{1,3},{2,0},{3,1},{4,6},{5,7},{6,4},{7,5},{8,10},{9,11},{10,... | collective-permute-start | bytes 3145736 | tf_op jit(solution)/shard_map/ppermute | solution.py:19
  76.1 162.0 %copy-start.47 = (pred[256]{0:T(512)(128)(4,1)}, pred[256]{0:T(512)(128)(4,1)S(1)}, u32[]{:S(2)}) copy-start(pred[256]{0:T(512)(128)(4,1)S(1)} %get-tuple-element.51) | copy-start | bytes 772
  76.1 163.4 %copy-start.45 = (pred[256]{0:T(512)(128)(4,1)}, pred[256]{0:T(512)(128)(4,1)S(1)}, u32[]{:S(2)}) copy-start(pred[256]{0:T(512)(128)(4,1)S(1)} %get-tuple-element.50) | copy-start | bytes 772
  93.1 126.8 %collective-permute-start = (bf16[256,8192]{1,0:T(8,128)(2,1)}, bf16[256,8192]{1,0:T(8,128)(2,1)}, u32[]{:S(2)}, u32[]{:S(2)}) collective-permute-start(bf16[256,8192]{1,0:T(8,128)(2,1)} %bitcast.300), channel_id=1, source_target_pairs={{0,16},{16,0},{1,17},{17,1},{2,18},{18,2},{3,19},{19,3},{4,20},{20... | collective-permute-start | bytes 12582920 | tf_op jit(solution)/shard_map/ppermute | solution.py:13
  176.2 47.1 %collective-permute-start.4 = (bf16[2,2048,256]{2,1,0:T(8,128)(2,1)}, bf16[2,2048,256]{2,1,0:T(8,128)(2,1)}, u32[]{:S(2)}, u32[]{:S(2)}) collective-permute-start(bf16[2,2048,256]{2,1,0:T(8,128)(2,1)} %pad_maximum_fusion.3), channel_id=1, source_target_pairs={{0,1},{1,0},{2,3},{3,2},{4,5},{5,4},{6,7},{7,6},{8,9},{9,8},{10,11... | collective-permute-start | bytes 6291464 | tf_op jit(solution)/shard_map/ppermute | solution.py:19
  198.3 32.5 %collective-permute-start.2 = (bf16[2,2048,256]{2,1,0:T(8,128)(2,1)}, bf16[2,2048,256]{2,1,0:T(8,128)(2,1)}, u32[]{:S(2)}, u32[]{:S(2)}) collective-permute-start(bf16[2,2048,256]{2,1,0:T(8,128)(2,1)} %pad_maximum_fusion.2), channel_id=1, source_target_pairs={{0,1},{1,0},{2,3},{3,2},{4,5},{5,4},{6,7},{7,6},{8,9},{9,8},{10,11... | collective-permute-start | bytes 6291464 | tf_op jit(solution)/shard_map/ppermute | solution.py:19
  198.3 213.4 %reduce-scatter.2.cloned.1.call-start = ((), (), s32[]{:S(2)}) async-start(), calls=%async_computation.3 | async-start | bytes 5242880 | tf_op jit(solution)/shard_map/reduce_scatter | solution.py:183
  198.6 11.7 %copy-start.37 = (f32[1,8192]{1,0:T(1,128)S(1)}, f32[1,8192]{1,0:T(1,128)}, u32[]{:S(2)}) copy-start(f32[1,8192]{1,0:T(1,128)} %param.18) | copy-start | bytes 98308
  206.1 35.0 %collective-permute-start.7 = (bf16[2,2048,1024]{2,1,0:T(8,128)(2,1)}, bf16[2,2048,1024]{2,1,0:T(8,128)(2,1)}, u32[]{:S(2)}, u32[]{:S(2)}) collective-permute-start(bf16[2,2048,1024]{2,1,0:T(8,128)(2,1)} %pad_maximum_fusion), channel_id=1, source_target_pairs={{0,1},{1,0},{2,3},{3,2},{4,5},{5,4},{6,7},{7,6},{8,9},{9,8},{10,11... | collective-permute-start | bytes 25165832 | tf_op jit(solution)/shard_map/ppermute | solution.py:19
  206.6 4.2 copy-start.4
  210.7 2.2 copy-start.24
  212.9 7.0 %copy-start.16 = (bf16[256,8192]{1,0:T(8,128)(2,1)}, bf16[256,8192]{1,0:T(8,128)(2,1)S(1)}, u32[]{:S(2)}) copy-start(bf16[256,8192]{1,0:T(8,128)(2,1)S(1)} %fusion.4) | copy-start | bytes 12582916
  215.3 4.6 %copy-start.18 = (bf16[1,1,256,8192]{3,2,1,0:T(8,128)(2,1)S(1)}, bf16[1,1,256,8192]{3,2,1,0:T(8,128)(2,1)}, u32[]{:S(2)}) copy-start(bf16[1,1,256,8192]{3,2,1,0:T(8,128)(2,1)} %all-gather.9.cloned.1.call-done) | copy-start | bytes 12582916
  222.7 6.3 %copy-start = (bf16[256,8192]{1,0:T(8,128)(2,1)}, bf16[256,8192]{1,0:T(8,128)(2,1)S(1)}, u32[]{:S(2)}) copy-start(bf16[256,8192]{1,0:T(8,128)(2,1)S(1)} %broadcast_select_fusion) | copy-start | bytes 12582916
  223.2 6.8 %copy-start.39 = (f32[1,128]{1,0:T(1,128)S(1)}, f32[1,128]{1,0:T(1,128)}, u32[]{:S(2)}) copy-start(f32[1,128]{1,0:T(1,128)} %param.23) | copy-start | bytes 1540
  230.0 5.6 %copy-start.1 = (bf16[256,8192]{1,0:T(8,128)(2,1)S(1)}, bf16[256,8192]{1,0:T(8,128)(2,1)}, u32[]{:S(2)}) copy-start(bf16[256,8192]{1,0:T(8,128)(2,1)} %copy-done) | copy-start | bytes 12582916
  233.4 4.7 %copy-start.10 = (f32[1,1,256,1024]{2,3,1,0:T(8,128)S(1)}, f32[1,1,256,1024]{2,3,1,0:T(8,128)}, u32[]{:S(2)}) copy-start(f32[1,1,256,1024]{2,3,1,0:T(8,128)} %copy.158) | copy-start | bytes 3145732
  235.6 3.9 copy-start.8
  237.5 3.5 copy-start.17
  238.1 2.9 copy-start.26
  241.0 3.7 copy-start.30
  241.0 3.7 copy-start.31
  256.3 6.0 %copy-start.48 = (pred[256]{0:T(512)(128)(4,1)S(1)}, pred[256]{0:T(512)(128)(4,1)}, u32[]{:S(2)}) copy-start(pred[256]{0:T(512)(128)(4,1)} %copy-done.47) | copy-start | bytes 772
  259.9 2.5 copy-start.11
  259.9 3.7 copy-start.23
  259.9 3.7 copy-start.29
  259.9 3.7 copy-start.34
  259.9 3.7 copy-start.52
  259.9 3.7 copy-start.54
  262.3 2.2 copy-start.12
  264.6 19.3 %copy-start.38 = (f32[1,8192]{1,0:T(1,128)S(1)}, f32[1,8192]{1,0:T(1,128)}, u32[]{:S(2)}) copy-start(f32[1,8192]{1,0:T(1,128)} %param.18) | copy-start | bytes 98308
  280.6 3.4 copy-start.5
  306.7 6.5 %copy-start.42 = (f32[256,2,4]{0,2,1:T(4,128)}, f32[256,2,4]{0,2,1:T(4,128)S(1)}, u32[]{:S(2)}) copy-start(f32[256,2,4]{0,2,1:T(4,128)S(1)} %rsqrt.57) | copy-start | bytes 24580
  306.8 6.5 %copy-start.46 = (pred[256]{0:T(512)(128)(4,1)S(1)}, pred[256]{0:T(512)(128)(4,1)}, u32[]{:S(2)}) copy-start(pred[256]{0:T(512)(128)(4,1)} %copy-done.45) | copy-start | bytes 772
  310.7 2.5 copy-start.9
  310.7 3.0 copy-start.35
  310.7 5.7 %copy-start.22 = (bf16[2,4,256,256]{2,3,1,0:T(8,128)(2,1)S(1)}, bf16[2,4,256,256]{2,3,1,0:T(8,128)(2,1)}, u32[]{:S(2)}) copy-start(bf16[2,4,256,256]{2,3,1,0:T(8,128)(2,1)} %convolution_convert_fusion.8) | copy-start | bytes 3145732
  310.7 5.7 %copy-start.28 = (f32[2,4,256,256]{2,3,1,0:T(8,128)S(1)}, f32[2,4,256,256]{2,3,1,0:T(8,128)}, u32[]{:S(2)}) copy-start(f32[2,4,256,256]{2,3,1,0:T(8,128)} %get-tuple-element.49) | copy-start | bytes 6291460
  310.7 5.7 %copy-start.33 = (f32[256,2,4,128]{3,2,1,0:T(4,128)S(1)}, f32[256,2,4,128]{3,2,1,0:T(4,128)}, u32[]{:S(2)}) copy-start(f32[256,2,4,128]{3,2,1,0:T(4,128)} %reshape.218) | copy-start | bytes 3145732
  310.8 5.7 %copy-start.53 = (f32[1,128]{1,0:T(1,128)S(1)}, f32[1,128]{1,0:T(1,128)}, u32[]{:S(2)}) copy-start(f32[1,128]{1,0:T(1,128)} %param.22) | copy-start | bytes 1540
  310.8 5.7 %copy-start.55 = (pred[256]{0:T(512)(128)(4,1)S(1)}, pred[256]{0:T(512)(128)(4,1)}, u32[]{:S(2)}) copy-start(pred[256]{0:T(512)(128)(4,1)} %iota_compare_fusion) | copy-start | bytes 772
  313.2 4.2 copy-start.14
  313.3 3.2 copy-start.43
  336.4 3.6 copy-start.2
  336.4 4.0 copy-start.21
  341.2 7.2 %collective-permute-start.9 = (bf16[2,2048,512]{1,2,0:T(8,128)(2,1)S(1)}, bf16[2,2048,512]{1,2,0:T(8,128)(2,1)S(1)}, u32[]{:S(2)}, u32[]{:S(2)}) collective-permute-start(bf16[2,2048,512]{1,2,0:T(8,128)(2,1)S(1)} %pad_maximum_fusion.1), channel_id=1, source_target_pairs={{0,1},{1,0},{2,3},{3,2},{4,5},{5,4},{6,7},{7,6},{8,9},{9,8},{10,11... | collective-permute-start | bytes 12582920 | tf_op jit(solution)/shard_map/ppermute | solution.py:19
  341.7 13.2 %copy-start.13 = (bf16[2,4,256,256]{2,3,1,0:T(8,128)(2,1)S(1)}, bf16[2,4,256,256]{2,3,1,0:T(8,128)(2,1)}, u32[]{:S(2)}) copy-start(bf16[2,4,256,256]{2,3,1,0:T(8,128)(2,1)} %copy-done.12) | copy-start | bytes 3145732
  341.7 13.2 %copy-start.27 = (bf16[256,256]{0,1:T(8,128)(2,1)S(1)}, bf16[256,256]{0,1:T(8,128)(2,1)}, u32[]{:S(2)}) copy-start(bf16[256,256]{0,1:T(8,128)(2,1)} %copy-done.26) | copy-start | bytes 393220
  342.2 13.2 %copy-start.15 = (bf16[2,4,256,256]{2,3,1,0:T(8,128)(2,1)S(1)}, bf16[2,4,256,256]{2,3,1,0:T(8,128)(2,1)}, u32[]{:S(2)}) copy-start(bf16[2,4,256,256]{2,3,1,0:T(8,128)(2,1)} %copy-done.14) | copy-start | bytes 3145732
  352.7 3.3 copy-start.49
  352.7 60.6 %collective-permute-start.10 = (bf16[1,2048,512]{1,2,0:T(8,128)(2,1)}, bf16[1,2048,512]{1,2,0:T(8,128)(2,1)}, u32[]{:S(2)}, u32[]{:S(2)}) collective-permute-start(bf16[1,2048,512]{1,2,0:T(8,128)(2,1)} %add_convert_fusion), channel_id=1, source_target_pairs={{0,2},{1,3},{2,0},{3,1},{4,6},{5,7},{6,4},{7,5},{8,10},{9,11},{10,... | collective-permute-start | bytes 6291464 | tf_op jit(solution)/shard_map/ppermute | solution.py:19
  356.0 2.6 copy-start.3
  411.8 25.3 %collective-permute-start.8 = (bf16[256,2048]{1,0:T(8,128)(2,1)}, bf16[256,2048]{1,0:T(8,128)(2,1)}, u32[]{:S(2)}, u32[]{:S(2)}) collective-permute-start(bf16[256,2048]{1,0:T(8,128)(2,1)} %reduce-scatter.2.cloned.1.call-done), channel_id=1, source_target_pairs={{0,16},{16,0},{1,17},{17,1},{2,18},{18,2},{3,19},{19,3},{4,20},{20... | collective-permute-start | bytes 3145736 | tf_op jit(solution)/shard_map/ppermute | solution.py:13
  418.5 18.5 %copy-start.32 = (bf16[256,2048]{1,0:T(8,128)(2,1)S(1)}, bf16[256,2048]{1,0:T(8,128)(2,1)}, u32[]{:S(2)}) copy-start(bf16[256,2048]{1,0:T(8,128)(2,1)} %reduce-scatter.2.cloned.1.call-done) | copy-start | bytes 3145732
  (7 other events, 9.2 us)
Sparse Core Ops, SparseCore 0:
  9.6 83.4 all-gather.8
  95.2 79.2 all-gather.4
  198.5 82.0 all-gather.6
  336.5 75.2 reduce-scatter.1

commit v5 on v3

--- a/solution.py
+++ b/solution.py
@@ -128,17 +128,21 @@
     arrived = shifted(text_in, "section", 1)
     text_rows = text_in.shape[2]
     width_q = query_weight.shape[2]
-    chunks = 2 if text_rows % 16 == 0 else 1
-    rows = text_rows // chunks
+    if text_rows % 64 == 0:
+        bounds = [0, text_rows // 2, text_rows * 3 // 4, text_rows]
+    else:
+        bounds = [0, text_rows]
+    chunks = len(bounds) - 1
     contexts = []
     key_back = None
     value_back = None
     gathered = [
-        lax.all_gather(arrived[:, :, chunk * rows : (chunk + 1) * rows], "mp", axis=3, tiled=True)
+        lax.all_gather(arrived[:, :, bounds[chunk] : bounds[chunk + 1]], "mp", axis=3, tiled=True)
         for chunk in range(chunks)
     ]
     for chunk in range(chunks):
-        lower = chunk * rows
+        lower = bounds[chunk]
+        rows = bounds[chunk + 1] - lower
         full_text = gathered[chunk][0, 0]
         normed = norm_rows(full_text, norm_gain[0]).astype(jnp.bfloat16)
         query_raw = None

time: 442 us -> 480 us (1.086)
  matrix products: 70.8 us -> 93.2 us
  other arithmetic: 46.4 us -> 66.4 us
  waiting for transfers between devices: 263 us -> 247 us
  local copies, waits for them, and re-layouts: 26.4 us -> 35.9 us
    all_gather x2 -> x3, waiting for transfers between devices: 42.9 us -> 0.01 us  [per_device(): lax.all_gather(arrived[:, :, bounds[chunk]:bounds[chunk + 1]], 'mp', axis...]
    ppermute x8, waiting for transfers between devices: 84.5 us -> 113 us  [swapped(): return lax.ppermute(value, axis, pairs)]
    dot_general x8 -> x12, matrix products: 23.5 us -> 33 us  [per_device(): jnp.dot(columns_of(normed, (dp_index ^ code) * block_rows, block_rows), b...]
    reduce_sum x4 -> x6, other arithmetic: 7.49 us -> 12.5 us  [norm_rows(): jnp.mean(values * values, axis=-1, keepdims=True) + 1e-05]
    unnamed x110 -> x95, local copies, waits for them, and re-layouts: 10.3 us -> 9.9 us
  transfers between devices with their start and end apart: 15 -> 16, of which waited for: 9 -> 6; matrix products, arithmetic and copies ran while one was open for 20% -> 29% of each run, Pallas kernels for 0% -> 0%
where the time goes in v5:
time: 480 us; the launch traced here: 476 us
  waiting for transfers between devices  247 us (51%)
  matrix products  93.2 us (19%)
  other arithmetic  66.4 us (14%)
  local copies, waits for them, and re-layouts  35.9 us (7%)
  between operations  19.6 us (4%)
  starting transfers between devices  14.7 us (3%)
    ppermute x8, waiting for transfers between devices, swapped(): return lax.ppermute(value, axis, pairs)  113 us
    ppermute x3, waiting for transfers between devices, shifted(): return lax.ppermute(value, axis, pairs)  81.8 us
    reduce_scatter x1, waiting for transfers between devices, per_device(): lax.psum_scatter(partial_sum, 'mp', scatter_dimension=1, tiled=True)  52.2 us
    dot_general x12, matrix products, per_device(): jnp.dot(columns_of(normed, (dp_index ^ code) * block_rows, block_rows), b...  33 us
    reduce_sum x6, other arithmetic, norm_rows(): jnp.mean(values * values, axis=-1, keepdims=True) + 1e-05  12.5 us
    another operation x3, other arithmetic, gather_blocks(): arrived = swapped(jnp.stack([held[c] for c in codes]), axis, mask)  10.5 us
    unnamed x95, local copies, waits for them, and re-layouts  9.9 us
  transfers between devices with their start and end apart: 16, of which 6 were waited for; matrix products, arithmetic and copies ran while one was open for 29% of the time, Pallas kernels for 0%

profile of v5, /device:TPU:0, one launch (start us, length us, event | category | flops | bytes accessed | tf_op | source)
XLA Modules:
  0.0 476.4 jit_solution(6359668729089075005)
XLA Ops:
  7.2 3.0 collective-permute-start
  12.2 21.4 %collective-permute-done = bf16[1,1,256,2048]{3,2,1,0:T(8,128)(2,1)S(1)} collective-permute-done((bf16[1,1,256,2048]{3,2,1,0:T(8,128)(2,1)}, bf16[1,1,256,2048]{3,2,1,0:T(8,128)(2,1)S(1)}, u32[]{:S(2)}, u32[]{:S(2)}) %collective-permute-start) | collective-permute-done | bytes 1048608 | tf_op jit(solution)/shard_map/ppermute | solution.py:13
  34.7 1.8 collective-permute-start.5
  36.5 45.3 %collective-permute-done.5 = bf16[1,1,512,2048]{3,2,1,0:T(8,128)(2,1)S(1)} collective-permute-done((bf16[1,1,512,2048]{3,2,1,0:T(8,128)(2,1)}, bf16[1,1,512,2048]{3,2,1,0:T(8,128)(2,1)S(1)}, u32[]{:S(2)}, u32[]{:S(2)}) %collective-permute-start.5) | collective-permute-done | bytes 2097184 | tf_op jit(solution)/shard_map/ppermute | solution.py:13
  83.5 2.7 collective-permute-start.6
  86.2 2.3 fusion.305
  88.6 2.1 collective-permute-start.1
  90.6 109.7 %collective-permute-done.3 = bf16[1,2048,256]{2,1,0:T(8,128)(2,1)S(1)} collective-permute-done((bf16[1,2048,256]{2,1,0:T(8,128)(2,1)}, bf16[1,2048,256]{2,1,0:T(8,128)(2,1)S(1)}, u32[]{:S(2)}, u32[]{:S(2)}) %collective-permute-start.3) | collective-permute-done | bytes 1048608 | tf_op jit(solution)/shard_map/ppermute | solution.py:19
  200.3 2.7 pad_maximum_fusion.3
  203.0 6.2 %pad_maximum_fusion = bf16[2,2048,1024]{2,1,0:T(8,128)(2,1)} fusion(bf16[1,2048,1024]{2,1,0:T(8,128)(2,1)} %collective-permute-done.6, bf16[1,2048,1024]{2,1,0:T(8,128)(2,1)S(1)} %copy-done.4), kind=kLoop, calls=%fused_computation.8 | loop fusion | flops 4194304 | bytes 16777216 | tf_op jit(solution)/shard_map/stack | solution.py:36
  211.1 2.1 slice_convert_fusion
  213.2 2.5 copy.218
  217.1 2.1 slice_convert_fusion.1
  219.2 2.0 copy.221
  221.3 2.0 copy.224
  228.8 1.9 fusion.121
  230.7 2.1 fusion.128
  232.8 1.8 convolution_add_fusion.5
  234.6 2.5 multiply_reduce_fusion.3
  239.0 2.2 fusion.138
  241.2 2.2 fusion.130
  244.0 1.8 fusion.87
  249.6 3.4 fusion.3
  256.9 3.5 fusion.17
  260.3 3.5 fusion.30
  263.9 3.5 fusion.63
  271.3 3.6 fusion.307
  275.0 2.4 divide_convert_fusion
  281.4 2.1 fusion.6
  283.5 2.2 fusion.8
  285.6 2.9 fusion.29
  288.6 3.1 fusion.26
  292.8 3.8 fusion.79
  296.5 2.1 reshape.287
  300.6 1.9 reduce_sum.153
  304.0 2.6 fusion.312
  308.3 2.3 fusion.99
  312.7 2.2 fusion.9
  315.0 2.2 fusion.11
  317.9 2.9 fusion.28
  320.8 3.3 fusion.25
  324.2 3.8 fusion.73
  328.0 2.1 reshape.288
  332.0 1.9 reduce_sum.161
  335.4 2.6 fusion.315
  338.0 2.4 fusion.117
  340.4 2.1 fusion.98
  344.6 1.8 fusion.123
  348.0 2.5 broadcast_in_dim.159
  354.2 1.7 fusion.167
  357.5 2.8 fusion.36
  360.2 2.8 fusion.38
  363.0 1.8 convolution_convert_fusion.2
  367.8 2.4 pad_maximum_fusion.1
  371.1 1.9 fusion.40
  373.1 1.7 fusion.39
  374.8 2.9 collective-permute-done.9
  377.7 3.9 add_convert_fusion
  381.6 2.2 collective-permute-start.10
  389.9 52.2 %reduce-scatter.2.cloned.1.call-done = bf16[256,2048]{1,0:T(8,128)(2,1)} async-done(((bf16[256,8192]{1,0:T(8,128)(2,1)}), bf16[256,2048]{1,0:T(8,128)(2,1)}) %reduce-scatter.2.cloned.1.call-update) | async-done | bytes 1048592 | tf_op jit(solution)/shard_map/reduce_scatter | solution.py:187
  443.5 3.9 fusion.12
  448.6 2.3 copy.193
  452.2 15.1 %collective-permute-done.8 = bf16[256,2048]{1,0:T(8,128)(2,1)} collective-permute-done((bf16[256,2048]{1,0:T(8,128)(2,1)}, bf16[256,2048]{1,0:T(8,128)(2,1)}, u32[]{:S(2)}, u32[]{:S(2)}) %collective-permute-start.8) | collective-permute-done | bytes 1048608 | tf_op jit(solution)/shard_map/ppermute | solution.py:13
  467.3 2.3 select_bitcast_fusion
  (200 shorter events, 61.8 us)
Async XLA Ops:
  7.2 221.6 %all-gather.12.cloned.1.call-start = ((), (), s32[]{:S(2)}) async-start(), calls=%async_computation.5 | async-start | bytes 5242880 | tf_op jit(solution)/shard_map/all_gather | solution.py:113
  7.2 26.4 %collective-permute-start = (bf16[1,1,256,2048]{3,2,1,0:T(8,128)(2,1)}, bf16[1,1,256,2048]{3,2,1,0:T(8,128)(2,1)S(1)}, u32[]{:S(2)}, u32[]{:S(2)}) collective-permute-start(bf16[1,1,256,2048]{3,2,1,0:T(8,128)(2,1)} %param.14), channel_id=1, source_target_pairs={{0,16},{16,0},{1,17},{17,1},{2,18},{18,2},{3,19},{19,3},{4,20},{20... | collective-permute-start | bytes 3145736 | tf_op jit(solution)/shard_map/ppermute | solution.py:13
  34.7 214.9 %all-gather.6.cloned.1.call-start = ((), (), s32[]{:S(2)}) async-start(), calls=%async_computation.1 | async-start | bytes 5242880 | tf_op jit(solution)/shard_map/all_gather | solution.py:140
  34.7 47.1 %collective-permute-start.5 = (bf16[1,1,512,2048]{3,2,1,0:T(8,128)(2,1)}, bf16[1,1,512,2048]{3,2,1,0:T(8,128)(2,1)S(1)}, u32[]{:S(2)}, u32[]{:S(2)}) collective-permute-start(bf16[1,1,512,2048]{3,2,1,0:T(8,128)(2,1)} %param.13), channel_id=1, source_target_pairs={{0,16},{16,0},{1,17},{17,1},{2,18},{18,2},{3,19},{19,3},{4,20},{20... | collective-permute-start | bytes 6291464 | tf_op jit(solution)/shard_map/ppermute | solution.py:13
  81.8 1.7 copy-start.20
  83.1 198.3 %all-gather.8.cloned.1.call-start = ((), (), s32[]{:S(2)}) async-start(), calls=%async_computation.2 | async-start | bytes 2621440 | tf_op jit(solution)/shard_map/all_gather | solution.py:140
  83.5 119.5 %collective-permute-start.6 = (bf16[1,2048,1024]{2,1,0:T(8,128)(2,1)}, bf16[1,2048,1024]{2,1,0:T(8,128)(2,1)}, u32[]{:S(2)}, u32[]{:S(2)}) collective-permute-start(bf16[1,2048,1024]{2,1,0:T(8,128)(2,1)} %param.19), channel_id=1, source_target_pairs={{0,2},{1,3},{2,0},{3,1},{4,6},{5,7},{6,4},{7,5},{8,10},{9,11},{10,... | collective-permute-start | bytes 12582920 | tf_op jit(solution)/shard_map/ppermute | solution.py:19
  86.2 114.1 %collective-permute-start.3 = (bf16[1,2048,256]{2,1,0:T(8,128)(2,1)}, bf16[1,2048,256]{2,1,0:T(8,128)(2,1)S(1)}, u32[]{:S(2)}, u32[]{:S(2)}) collective-permute-start(bf16[1,2048,256]{2,1,0:T(8,128)(2,1)} %param.20), channel_id=1, source_target_pairs={{0,2},{1,3},{2,0},{3,1},{4,6},{5,7},{6,4},{7,5},{8,10},{9,11},{10,... | collective-permute-start | bytes 3145736 | tf_op jit(solution)/shard_map/ppermute | solution.py:19
  88.5 224.2 %all-gather.10.cloned.1.call-start = ((), (), s32[]{:S(2)}) async-start(), calls=%async_computation.3 | async-start | bytes 2621440 | tf_op jit(solution)/shard_map/all_gather | solution.py:140
  88.6 114.5 %copy-start.4 = (bf16[1,2048,1024]{2,1,0:T(8,128)(2,1)S(1)}, bf16[1,2048,1024]{2,1,0:T(8,128)(2,1)}, u32[]{:S(2)}) copy-start(bf16[1,2048,1024]{2,1,0:T(8,128)(2,1)} %param.19) | copy-start | bytes 12582916
  88.6 135.9 %collective-permute-start.1 = (bf16[1,2048,256]{2,1,0:T(8,128)(2,1)}, bf16[1,2048,256]{2,1,0:T(8,128)(2,1)S(1)}, u32[]{:S(2)}, u32[]{:S(2)}) collective-permute-start(bf16[1,2048,256]{2,1,0:T(8,128)(2,1)} %param.21), channel_id=1, source_target_pairs={{0,2},{1,3},{2,0},{3,1},{4,6},{5,7},{6,4},{7,5},{8,10},{9,11},{10,... | collective-permute-start | bytes 3145736 | tf_op jit(solution)/shard_map/ppermute | solution.py:19
  203.0 27.7 %collective-permute-start.4 = (bf16[2,2048,256]{2,1,0:T(8,128)(2,1)}, bf16[2,2048,256]{2,1,0:T(8,128)(2,1)}, u32[]{:S(2)}, u32[]{:S(2)}) collective-permute-start(bf16[2,2048,256]{2,1,0:T(8,128)(2,1)} %pad_maximum_fusion.3), channel_id=1, source_target_pairs={{0,1},{1,0},{2,3},{3,2},{4,5},{5,4},{6,7},{7,6},{8,9},{9,8},{10,11... | collective-permute-start | bytes 6291464 | tf_op jit(solution)/shard_map/ppermute | solution.py:19
  209.3 14.7 %copy-start.42 = (s32[1,2]{1,0:T(1,128)S(1)}, s32[1,2]{1,0:T(1,128)}, u32[]{:S(2)}) copy-start(s32[1,2]{1,0:T(1,128)} %param.15) | copy-start | bytes 28
  209.3 15.3 %copy-start.9 = (bf16[1,2048,256]{2,1,0:T(8,128)(2,1)S(1)}, bf16[1,2048,256]{2,1,0:T(8,128)(2,1)}, u32[]{:S(2)}) copy-start(bf16[1,2048,256]{2,1,0:T(8,128)(2,1)} %param.21) | copy-start | bytes 3145732
  209.3 51.1 %collective-permute-start.7 = (bf16[2,2048,1024]{2,1,0:T(8,128)(2,1)}, bf16[2,2048,1024]{2,1,0:T(8,128)(2,1)}, u32[]{:S(2)}, u32[]{:S(2)}) collective-permute-start(bf16[2,2048,1024]{2,1,0:T(8,128)(2,1)} %pad_maximum_fusion), channel_id=1, source_target_pairs={{0,1},{1,0},{2,3},{3,2},{4,5},{5,4},{6,7},{7,6},{8,9},{9,8},{10,11... | collective-permute-start | bytes 25165832 | tf_op jit(solution)/shard_map/ppermute | solution.py:19
  226.1 15.1 %collective-permute-start.2 = (bf16[2,2048,256]{2,1,0:T(8,128)(2,1)}, bf16[2,2048,256]{2,1,0:T(8,128)(2,1)}, u32[]{:S(2)}, u32[]{:S(2)}) collective-permute-start(bf16[2,2048,256]{2,1,0:T(8,128)(2,1)} %pad_maximum_fusion.2), channel_id=1, source_target_pairs={{0,1},{1,0},{2,3},{3,2},{4,5},{5,4},{6,7},{7,6},{8,9},{9,8},{10,11... | collective-permute-start | bytes 6291464 | tf_op jit(solution)/shard_map/ppermute | solution.py:19
  228.5 18.8 %copy-start.34 = (pred[128]{0:T(512)(128)(4,1)}, pred[128]{0:T(512)(128)(4,1)S(1)}, u32[]{:S(2)}) copy-start(pred[128]{0:T(512)(128)(4,1)S(1)} %get-tuple-element.61) | copy-start | bytes 388
  228.5 213.5 %reduce-scatter.2.cloned.1.call-start = ((), (), s32[]{:S(2)}) async-start(), calls=%async_computation.4 | async-start | bytes 5242880 | tf_op jit(solution)/shard_map/reduce_scatter | solution.py:187
  228.8 4.1 copy-start
  230.7 7.5 %copy-start.29 = (f32[1,128]{1,0:T(1,128)S(1)}, f32[1,128]{1,0:T(1,128)}, u32[]{:S(2)}) copy-start(f32[1,128]{1,0:T(1,128)} %param.23) | copy-start | bytes 1540
  237.1 8.7 %copy-start.30 = (f32[256,2]{0,1:T(2,128)}, f32[256,2]{0,1:T(2,128)S(1)}, u32[]{:S(2)}) copy-start(f32[256,2]{0,1:T(2,128)S(1)} %get-tuple-element.52) | copy-start | bytes 6148
  238.2 5.2 %copy-start.1 = (bf16[1,1,256,8192]{3,2,1,0:T(8,128)(2,1)S(1)}, bf16[1,1,256,8192]{3,2,1,0:T(8,128)(2,1)}, u32[]{:S(2)}) copy-start(bf16[1,1,256,8192]{3,2,1,0:T(8,128)(2,1)} %all-gather.12.cloned.1.call-done) | copy-start | bytes 12582916
  241.2 4.6 copy-start.11
  241.2 4.6 copy-start.39
  243.4 3.9 copy-start.14
  243.4 5.0 %copy-start.13 = (f32[1,1,128,1024]{2,3,1,0:T(8,128)S(1)}, f32[1,1,128,1024]{2,3,1,0:T(8,128)}, u32[]{:S(2)}) copy-start(f32[1,1,128,1024]{2,3,1,0:T(8,128)} %copy.224) | copy-start | bytes 1572868
  243.4 5.0 %copy-start.37 = (pred[128]{0:T(512)(128)(4,1)S(1)}, pred[128]{0:T(512)(128)(4,1)}, u32[]{:S(2)}) copy-start(pred[128]{0:T(512)(128)(4,1)} %get-tuple-element.60) | copy-start | bytes 388
  245.8 7.2 %copy-start.28 = (f32[1,8192]{1,0:T(1,128)S(1)}, f32[1,8192]{1,0:T(1,128)}, u32[]{:S(2)}) copy-start(f32[1,8192]{1,0:T(1,128)} %param.18) | copy-start | bytes 98308
  249.6 3.8 copy-start.8
  253.4 2.2 copy-start.5
  271.3 3.7 copy-start.32
  275.0 2.5 copy-start.19
  275.0 2.9 copy-start.21
  275.0 3.1 copy-start.24
  275.0 3.1 copy-start.43
  275.0 3.1 copy-start.44
  275.0 3.1 copy-start.33
  278.1 1.1 copy-start.31
  278.1 2.0 copy-start.12
  278.1 2.0 copy-start.40
  288.6 3.5 copy-start.6
  306.6 4.0 copy-start.15
  306.6 4.0 copy-start.35
  308.3 2.7 copy-start.16
  308.3 2.8 copy-start.27
  308.3 3.5 copy-start.22
  312.7 4.4 copy-start.7
  338.0 4.7 copy-start.26
  344.6 3.4 copy-start.25
  344.6 5.9 %copy-start.10 = (bf16[1,2048,256]{2,1,0:T(8,128)(2,1)S(1)}, bf16[1,2048,256]{2,1,0:T(8,128)(2,1)}, u32[]{:S(2)}) copy-start(bf16[1,2048,256]{2,1,0:T(8,128)(2,1)} %param.21) | copy-start | bytes 3145732
  363.0 3.5 copy-start.2
  370.2 7.5 %collective-permute-start.9 = (bf16[2,2048,512]{1,2,0:T(8,128)(2,1)}, bf16[2,2048,512]{1,2,0:T(8,128)(2,1)}, u32[]{:S(2)}, u32[]{:S(2)}) collective-permute-start(bf16[2,2048,512]{1,2,0:T(8,128)(2,1)} %pad_maximum_fusion.1), channel_id=1, source_target_pairs={{0,1},{1,0},{2,3},{3,2},{4,5},{5,4},{6,7},{7,6},{8,9},{9,8},{10,11... | collective-permute-start | bytes 12582920 | tf_op jit(solution)/shard_map/ppermute | solution.py:19
  373.1 10.8 %copy-start.18 = (bf16[2,4,128,256]{2,3,1,0:T(8,128)(2,1)S(1)}, bf16[2,4,128,256]{2,3,1,0:T(8,128)(2,1)}, u32[]{:S(2)}) copy-start(bf16[2,4,128,256]{2,3,1,0:T(8,128)(2,1)} %get-tuple-element.45) | copy-start | bytes 1572868
  374.8 9.4 %copy-start.17 = (bf16[2,4,128,256]{2,3,1,0:T(8,128)(2,1)S(1)}, bf16[2,4,128,256]{2,3,1,0:T(8,128)(2,1)}, u32[]{:S(2)}) copy-start(bf16[2,4,128,256]{2,3,1,0:T(8,128)(2,1)} %copy-done.16) | copy-start | bytes 1572868
  381.6 3.8 copy-start.38
  381.6 3.9 copy-start.36
  381.6 4.0 copy-start.41
  381.6 61.9 %collective-permute-start.10 = (bf16[1,2048,512]{1,2,0:T(8,128)(2,1)}, bf16[1,2048,512]{1,2,0:T(8,128)(2,1)}, u32[]{:S(2)}, u32[]{:S(2)}) collective-permute-start(bf16[1,2048,512]{1,2,0:T(8,128)(2,1)} %add_convert_fusion), channel_id=1, source_target_pairs={{0,2},{1,3},{2,0},{3,1},{4,6},{5,7},{6,4},{7,5},{8,10},{9,11},{10,... | collective-permute-start | bytes 6291464 | tf_op jit(solution)/shard_map/ppermute | solution.py:19
  385.4 2.6 copy-start.3
  442.1 25.3 %collective-permute-start.8 = (bf16[256,2048]{1,0:T(8,128)(2,1)}, bf16[256,2048]{1,0:T(8,128)(2,1)}, u32[]{:S(2)}, u32[]{:S(2)}) collective-permute-start(bf16[256,2048]{1,0:T(8,128)(2,1)} %reduce-scatter.2.cloned.1.call-done), channel_id=1, source_target_pairs={{0,16},{16,0},{1,17},{17,1},{2,18},{18,2},{3,19},{19,3},{4,20},{20... | collective-permute-start | bytes 3145736 | tf_op jit(solution)/shard_map/ppermute | solution.py:13
  448.6 18.7 %copy-start.23 = (bf16[256,2048]{1,0:T(8,128)(2,1)S(1)}, bf16[256,2048]{1,0:T(8,128)(2,1)}, u32[]{:S(2)}) copy-start(bf16[256,2048]{1,0:T(8,128)(2,1)} %reduce-scatter.2.cloned.1.call-done) | copy-start | bytes 3145732
Sparse Core Ops, SparseCore 0:
  34.8 82.2 all-gather.11
  119.3 79.2 all-gather.5
  200.2 44.4 all-gather.7
  246.1 44.6 all-gather.9
  363.1 78.8 reduce-scatter.1

commit v6 on v5

--- a/solution.py
+++ b/solution.py
@@ -129,7 +129,7 @@
     text_rows = text_in.shape[2]
     width_q = query_weight.shape[2]
     if text_rows % 64 == 0:
-        bounds = [0, text_rows // 2, text_rows * 3 // 4, text_rows]
+        bounds = [0, text_rows * 5 // 8, text_rows]
     else:
         bounds = [0, text_rows]
     chunks = len(bounds) - 1

time: 480 us -> 465 us (0.969)
  waiting for transfers between devices: 247 us -> 263 us
  matrix products: 93.2 us -> 78.9 us
  other arithmetic: 66.4 us -> 53.7 us
  local copies, waits for them, and re-layouts: 35.9 us -> 29.3 us
    all_gather x3 -> x2, waiting for transfers between devices: 0.01 us -> 10.5 us  [per_device(): lax.all_gather(arrived[:, :, bounds[chunk]:bounds[chunk + 1]], 'mp', axis...]
    dot_general x12 -> x8, matrix products: 33 us -> 25.1 us  [per_device(): jnp.dot(columns_of(normed, (dp_index ^ code) * block_rows, block_rows), b...]
    ppermute x8, waiting for transfers between devices: 113 us -> 118 us  [swapped(): return lax.ppermute(value, axis, pairs)]
    reduce_sum x6 -> x4, other arithmetic: 12.5 us -> 8.34 us  [norm_rows(): jnp.mean(values * values, axis=-1, keepdims=True) + 1e-05]
    unnamed x95 -> x78, local copies, waits for them, and re-layouts: 9.9 us -> 9.12 us
  transfers between devices with their start and end apart: 16 -> 15, of which waited for: 6 -> 7; matrix products, arithmetic and copies ran while one was open for 29% -> 22% of each run, Pallas kernels for 0% -> 0%
where the time goes in v6:
time: 465 us; the launch traced here: 458 us
  waiting for transfers between devices  263 us (57%)
  matrix products  78.9 us (17%)
  other arithmetic  53.7 us (12%)
  local copies, waits for them, and re-layouts  29.3 us (6%)
  between operations  19.4 us (4%)
  starting transfers between devices  13.4 us (3%)
    ppermute x8, waiting for transfers between devices, swapped(): return lax.ppermute(value, axis, pairs)  118 us
    ppermute x3, waiting for transfers between devices, shifted(): return lax.ppermute(value, axis, pairs)  82.7 us
    reduce_scatter x1, waiting for transfers between devices, per_device(): lax.psum_scatter(partial_sum, 'mp', scatter_dimension=1, tiled=True)  51.4 us
    dot_general x8, matrix products, per_device(): jnp.dot(columns_of(normed, (dp_index ^ code) * block_rows, block_rows), b...  25.1 us
    another operation x3, other arithmetic, gather_blocks(): arrived = swapped(jnp.stack([held[c] for c in codes]), axis, mask)  12.5 us
    all_gather x2, waiting for transfers between devices, per_device(): lax.all_gather(arrived[:, :, bounds[chunk]:bounds[chunk + 1]], 'mp', axis...  10.5 us
  transfers between devices with their start and end apart: 15, of which 7 were waited for; matrix products, arithmetic and copies ran while one was open for 22% of the time, Pallas kernels for 0%

profile of v6, /device:TPU:0, one launch (start us, length us, event | category | flops | bytes accessed | tf_op | source)
XLA Modules:
  0.0 457.8 jit_solution(11686172392094442887)
XLA Ops:
  7.2 3.0 collective-permute-start
  10.2 1.4 constant_dynamic-slice_fusion
  12.3 21.3 %collective-permute-done = bf16[1,1,256,2048]{3,2,1,0:T(8,128)(2,1)S(1)} collective-permute-done((bf16[1,1,256,2048]{3,2,1,0:T(8,128)(2,1)}, bf16[1,1,256,2048]{3,2,1,0:T(8,128)(2,1)S(1)}, u32[]{:S(2)}, u32[]{:S(2)}) %collective-permute-start) | collective-permute-done | bytes 1048608 | tf_op jit(solution)/shard_map/ppermute | solution.py:13
  33.6 2.3 broadcast_select_fusion
  36.0 1.8 collective-permute-start.5
  37.8 43.9 %collective-permute-done.5 = bf16[1,1,512,2048]{3,2,1,0:T(8,128)(2,1)S(1)} collective-permute-done((bf16[1,1,512,2048]{3,2,1,0:T(8,128)(2,1)S(1)}, bf16[1,1,512,2048]{3,2,1,0:T(8,128)(2,1)S(1)}, u32[]{:S(2)}, u32[]{:S(2)}) %collective-permute-start.5) | collective-permute-done | bytes 2097184 | tf_op jit(solution)/shard_map/ppermute | solution.py:13
  84.3 2.7 collective-permute-start.6
  87.1 1.9 collective-permute-start.1
  89.0 112.1 %collective-permute-done.3 = bf16[1,2048,256]{2,1,0:T(8,128)(2,1)S(1)} collective-permute-done((bf16[1,2048,256]{2,1,0:T(8,128)(2,1)}, bf16[1,2048,256]{2,1,0:T(8,128)(2,1)S(1)}, u32[]{:S(2)}, u32[]{:S(2)}) %collective-permute-start.3) | collective-permute-done | bytes 1048608 | tf_op jit(solution)/shard_map/ppermute | solution.py:19
  201.2 3.2 pad_maximum_fusion.3
  204.3 6.2 %pad_maximum_fusion = bf16[2,2048,1024]{2,1,0:T(8,128)(2,1)} fusion(bf16[1,2048,1024]{2,1,0:T(8,128)(2,1)} %collective-permute-done.6, bf16[1,2048,1024]{2,1,0:T(8,128)(2,1)S(1)} %copy-done.5), kind=kLoop, calls=%fused_computation.7 | loop fusion | flops 4194304 | bytes 16777216 | tf_op jit(solution)/shard_map/stack | solution.py:36
  212.4 2.3 slice_convert_fusion
  214.7 1.9 reshape.224
  217.9 2.0 slice_convert_fusion.1
  219.8 2.4 reshape.226
  223.5 3.2 pad_maximum_fusion.2
  228.3 2.1 slice.63
  230.7 1.9 fusion.123
  232.6 2.1 fusion.130
  234.7 1.8 convolution_add_fusion.5
  236.5 2.5 multiply_reduce_fusion.2
  239.0 1.9 copy.90
  240.9 1.7 multiply_convert_fusion
  242.7 1.9 fusion.140
  244.6 2.1 fusion.132
  247.3 1.9 fusion.99
  249.1 1.7 convolution_convert_fusion.8
  252.1 3.8 fusion.2
  256.2 1.6 fusion.4
  257.8 3.9 fusion.11
  261.8 1.6 fusion.61
  263.3 3.8 fusion.20
  267.1 4.2 fusion.60
  271.4 1.7 reshape.219
  274.1 4.0 fusion.270
  278.2 3.2 divide_convert_fusion
  281.9 2.2 fusion.116
  285.4 10.5 %all-gather.7.cloned.1.call-done = bf16[1,1,192,8192]{3,2,1,0:T(8,128)(2,1)} async-done(((bf16[1,1,192,2048]{3,2,1,0:T(8,128)(2,1)}), bf16[1,1,192,8192]{3,2,1,0:T(8,128)(2,1)}) %all-gather.7.cloned.1.call-update) | async-done | bytes 3145744 | tf_op jit(solution)/shard_map/all_gather | solution.py:140
  296.0 2.8 fusion.5
  302.0 3.2 fusion.19
  305.2 3.2 fusion.85
  308.5 4.2 fusion.84
  312.6 1.5 reshape.220
  316.3 1.4 reduce_sum.107
  318.9 2.9 fusion.275
  321.7 3.0 fusion.51
  324.8 4.5 fusion.113
  331.4 1.7 fusion.125
  333.6 2.5 broadcast_in_dim.128
  336.1 1.5 fusion.33
  338.4 1.7 fusion.152
  340.1 1.8 fusion.153
  341.9 1.6 fusion.35
  343.5 2.8 fusion.37
  346.3 2.8 fusion.39
  349.1 1.8 convolution_convert_fusion.4
  351.0 1.7 convolution_convert_fusion.5
  355.5 6.2 %collective-permute-done.9 = bf16[2,2048,512]{1,2,0:T(8,128)(2,1)S(1)} collective-permute-done((bf16[2,2048,512]{1,2,0:T(8,128)(2,1)S(1)}, bf16[2,2048,512]{1,2,0:T(8,128)(2,1)S(1)}, u32[]{:S(2)}, u32[]{:S(2)}) %collective-permute-start.9) | collective-permute-done | bytes 4194336 | tf_op jit(solution)/shard_map/ppermute | solution.py:19
  361.7 2.8 add_convert_fusion
  364.5 1.5 collective-permute-start.10
  373.4 51.4 %reduce-scatter.2.cloned.1.call-done = bf16[256,2048]{1,0:T(8,128)(2,1)} async-done(((bf16[256,8192]{1,0:T(8,128)(2,1)}), bf16[256,2048]{1,0:T(8,128)(2,1)}) %reduce-scatter.2.cloned.1.call-update) | async-done | bytes 1048592 | tf_op jit(solution)/shard_map/reduce_scatter | solution.py:187
  424.7 1.5 collective-permute-start.8
  426.2 3.5 fusion.8
  432.5 17.5 %collective-permute-done.8 = bf16[256,2048]{1,0:T(8,128)(2,1)} collective-permute-done((bf16[256,2048]{1,0:T(8,128)(2,1)}, bf16[256,2048]{1,0:T(8,128)(2,1)}, u32[]{:S(2)}, u32[]{:S(2)}) %collective-permute-start.8) | collective-permute-done | bytes 1048608 | tf_op jit(solution)/shard_map/ppermute | solution.py:13
  (156 shorter events, 34.0 us)
Async XLA Ops:
  7.2 223.5 %all-gather.9.cloned.1.call-start = ((), (), s32[]{:S(2)}) async-start(), calls=%async_computation.4 | async-start | bytes 5242880 | tf_op jit(solution)/shard_map/all_gather | solution.py:113
  7.2 26.4 %collective-permute-start = (bf16[1,1,256,2048]{3,2,1,0:T(8,128)(2,1)}, bf16[1,1,256,2048]{3,2,1,0:T(8,128)(2,1)S(1)}, u32[]{:S(2)}, u32[]{:S(2)}) collective-permute-start(bf16[1,1,256,2048]{3,2,1,0:T(8,128)(2,1)} %param.14), channel_id=1, source_target_pairs={{0,16},{16,0},{1,17},{17,1},{2,18},{18,2},{3,19},{19,3},{4,20},{20... | collective-permute-start | bytes 3145736 | tf_op jit(solution)/shard_map/ppermute | solution.py:13
  12.2 23.7 %copy-start.34 = (bf16[1,1,512,2048]{3,2,1,0:T(8,128)(2,1)S(1)}, bf16[1,1,512,2048]{3,2,1,0:T(8,128)(2,1)}, u32[]{:S(2)}) copy-start(bf16[1,1,512,2048]{3,2,1,0:T(8,128)(2,1)} %param.13) | copy-start | bytes 6291460
  35.9 216.2 %all-gather.5.cloned.1.call-start = ((), (), s32[]{:S(2)}) async-start(), calls=%async_computation.1 | async-start | bytes 6553600 | tf_op jit(solution)/shard_map/all_gather | solution.py:140
  36.0 45.7 %collective-permute-start.5 = (bf16[1,1,512,2048]{3,2,1,0:T(8,128)(2,1)S(1)}, bf16[1,1,512,2048]{3,2,1,0:T(8,128)(2,1)S(1)}, u32[]{:S(2)}, u32[]{:S(2)}) collective-permute-start(bf16[1,1,512,2048]{3,2,1,0:T(8,128)(2,1)S(1)} %copy-done.34), channel_id=1, source_target_pairs={{0,16},{16,0},{1,17},{17,1},{2,18},{18,2},{3,19},{19,3},{4,20},{20... | collective-permute-start | bytes 6291464 | tf_op jit(solution)/shard_map/ppermute | solution.py:13
  81.6 1.3 copy-start.23
  84.2 211.8 %all-gather.7.cloned.1.call-start = ((), (), s32[]{:S(2)}) async-start(), calls=%async_computation.2 | async-start | bytes 3932160 | tf_op jit(solution)/shard_map/all_gather | solution.py:140
  84.2 120.1 %copy-start.5 = (bf16[1,2048,1024]{2,1,0:T(8,128)(2,1)S(1)}, bf16[1,2048,1024]{2,1,0:T(8,128)(2,1)}, u32[]{:S(2)}) copy-start(bf16[1,2048,1024]{2,1,0:T(8,128)(2,1)} %param.19) | copy-start | bytes 12582916
  84.3 120.1 %collective-permute-start.6 = (bf16[1,2048,1024]{2,1,0:T(8,128)(2,1)}, bf16[1,2048,1024]{2,1,0:T(8,128)(2,1)}, u32[]{:S(2)}, u32[]{:S(2)}) collective-permute-start(bf16[1,2048,1024]{2,1,0:T(8,128)(2,1)} %param.19), channel_id=1, source_target_pairs={{0,2},{1,3},{2,0},{3,1},{4,6},{5,7},{6,4},{7,5},{8,10},{9,11},{10,... | collective-permute-start | bytes 12582920 | tf_op jit(solution)/shard_map/ppermute | solution.py:19
  87.0 114.2 %collective-permute-start.3 = (bf16[1,2048,256]{2,1,0:T(8,128)(2,1)}, bf16[1,2048,256]{2,1,0:T(8,128)(2,1)S(1)}, u32[]{:S(2)}, u32[]{:S(2)}) collective-permute-start(bf16[1,2048,256]{2,1,0:T(8,128)(2,1)} %param.20), channel_id=1, source_target_pairs={{0,2},{1,3},{2,0},{3,1},{4,6},{5,7},{6,4},{7,5},{8,10},{9,11},{10,... | collective-permute-start | bytes 3145736 | tf_op jit(solution)/shard_map/ppermute | solution.py:19
  87.1 136.4 %collective-permute-start.1 = (bf16[1,2048,256]{2,1,0:T(8,128)(2,1)}, bf16[1,2048,256]{2,1,0:T(8,128)(2,1)S(1)}, u32[]{:S(2)}, u32[]{:S(2)}) collective-permute-start(bf16[1,2048,256]{2,1,0:T(8,128)(2,1)} %param.21), channel_id=1, source_target_pairs={{0,2},{1,3},{2,0},{3,1},{4,6},{5,7},{6,4},{7,5},{8,10},{9,11},{10,... | collective-permute-start | bytes 3145736 | tf_op jit(solution)/shard_map/ppermute | solution.py:19
  201.2 29.5 %copy-start.9 = (bf16[1,2048,256]{2,1,0:T(8,128)(2,1)}, bf16[1,2048,256]{2,1,0:T(8,128)(2,1)S(1)}, u32[]{:S(2)}) copy-start(bf16[1,2048,256]{2,1,0:T(8,128)(2,1)S(1)} %collective-permute-done.3) | copy-start | bytes 3145732
  204.3 28.3 %collective-permute-start.4 = (bf16[2,2048,256]{2,1,0:T(8,128)(2,1)}, bf16[2,2048,256]{2,1,0:T(8,128)(2,1)}, u32[]{:S(2)}, u32[]{:S(2)}) collective-permute-start(bf16[2,2048,256]{2,1,0:T(8,128)(2,1)} %pad_maximum_fusion.3), channel_id=1, source_target_pairs={{0,1},{1,0},{2,3},{3,2},{4,5},{5,4},{6,7},{7,6},{8,9},{9,8},{10,11... | collective-permute-start | bytes 6291464 | tf_op jit(solution)/shard_map/ppermute | solution.py:19
  210.6 52.8 %collective-permute-start.7 = (bf16[2,2048,1024]{2,1,0:T(8,128)(2,1)}, bf16[2,2048,1024]{2,1,0:T(8,128)(2,1)}, u32[]{:S(2)}, u32[]{:S(2)}) collective-permute-start(bf16[2,2048,1024]{2,1,0:T(8,128)(2,1)} %pad_maximum_fusion), channel_id=1, source_target_pairs={{0,1},{1,0},{2,3},{3,2},{4,5},{5,4},{6,7},{7,6},{8,9},{9,8},{10,11... | collective-permute-start | bytes 25165832 | tf_op jit(solution)/shard_map/ppermute | solution.py:19
  214.7 8.2 %copy-start.35 = (s32[1,2]{1,0:T(1,128)S(1)}, s32[1,2]{1,0:T(1,128)}, u32[]{:S(2)}) copy-start(s32[1,2]{1,0:T(1,128)} %param.15) | copy-start | bytes 28
  223.5 19.2 %copy-start.11 = (bf16[1,2048,256]{2,1,0:T(8,128)(2,1)}, bf16[1,2048,256]{2,1,0:T(8,128)(2,1)S(1)}, u32[]{:S(2)}) copy-start(bf16[1,2048,256]{2,1,0:T(8,128)(2,1)S(1)} %collective-permute-done.1) | copy-start | bytes 3145732
  226.6 17.9 %collective-permute-start.2 = (bf16[2,2048,256]{2,1,0:T(8,128)(2,1)}, bf16[2,2048,256]{2,1,0:T(8,128)(2,1)}, u32[]{:S(2)}, u32[]{:S(2)}) collective-permute-start(bf16[2,2048,256]{2,1,0:T(8,128)(2,1)} %pad_maximum_fusion.2), channel_id=1, source_target_pairs={{0,1},{1,0},{2,3},{3,2},{4,5},{5,4},{6,7},{7,6},{8,9},{9,8},{10,11... | collective-permute-start | bytes 6291464 | tf_op jit(solution)/shard_map/ppermute | solution.py:19
  230.4 194.3 %reduce-scatter.2.cloned.1.call-start = ((), (), s32[]{:S(2)}) async-start(), calls=%async_computation.3 | async-start | bytes 5242880 | tf_op jit(solution)/shard_map/reduce_scatter | solution.py:187
  230.7 4.0 copy-start
  236.5 4.4 copy-start.30
  239.0 7.7 %copy-start.13 = (bf16[1,2048,256]{2,1,0:T(8,128)(2,1)S(1)}, bf16[1,2048,256]{2,1,0:T(8,128)(2,1)}, u32[]{:S(2)}) copy-start(bf16[1,2048,256]{2,1,0:T(8,128)(2,1)} %param.21) | copy-start | bytes 3145732
  242.7 4.0 copy-start.1
  247.2 3.5 copy-start.16
  247.2 3.5 copy-start.31
  250.8 5.1 %copy-start.27 = (f32[1,8192]{1,0:T(1,128)S(1)}, f32[1,8192]{1,0:T(1,128)}, u32[]{:S(2)}) copy-start(f32[1,8192]{1,0:T(1,128)} %param.18) | copy-start | bytes 98308
  252.1 4.1 copy-start.4
  257.8 4.0 copy-start.6
  273.2 0.9 copy-start.28
  273.2 0.9 copy-start.33
  273.2 0.9 copy-start.36
  278.2 3.2 copy-start.19
  278.2 3.4 copy-start.22
  278.2 3.7 copy-start.25
  284.1 1.0 copy-start.15
  296.0 2.8 copy-start.8
  298.8 2.2 copy-start.7
  315.3 3.6 copy-start.29
  321.7 3.1 copy-start.21
  329.4 3.7 copy-start.17
  330.3 2.8 copy-start.18
  330.3 2.8 copy-start.32
  333.6 2.6 copy-start.14
  336.1 1.5 copy-start.12
  340.1 1.8 copy-start.10
  349.1 3.5 copy-start.2
  354.5 7.2 %collective-permute-start.9 = (bf16[2,2048,512]{1,2,0:T(8,128)(2,1)S(1)}, bf16[2,2048,512]{1,2,0:T(8,128)(2,1)S(1)}, u32[]{:S(2)}, u32[]{:S(2)}) collective-permute-start(bf16[2,2048,512]{1,2,0:T(8,128)(2,1)S(1)} %pad_maximum_fusion.1), channel_id=1, source_target_pairs={{0,1},{1,0},{2,3},{3,2},{4,5},{5,4},{6,7},{7,6},{8,9},{9,8},{10,11... | collective-permute-start | bytes 12582920 | tf_op jit(solution)/shard_map/ppermute | solution.py:19
  361.7 2.8 copy-start.20
  364.5 61.6 %collective-permute-start.10 = (bf16[1,2048,512]{1,2,0:T(8,128)(2,1)}, bf16[1,2048,512]{1,2,0:T(8,128)(2,1)}, u32[]{:S(2)}, u32[]{:S(2)}) collective-permute-start(bf16[1,2048,512]{1,2,0:T(8,128)(2,1)} %add_convert_fusion), channel_id=1, source_target_pairs={{0,2},{1,3},{2,0},{3,1},{4,6},{5,7},{6,4},{7,5},{8,10},{9,11},{10,... | collective-permute-start | bytes 6291464 | tf_op jit(solution)/shard_map/ppermute | solution.py:19
  368.9 1.0 copy-start.24
  369.9 2.6 copy-start.3
  424.7 25.2 %collective-permute-start.8 = (bf16[256,2048]{1,0:T(8,128)(2,1)}, bf16[256,2048]{1,0:T(8,128)(2,1)}, u32[]{:S(2)}, u32[]{:S(2)}) collective-permute-start(bf16[256,2048]{1,0:T(8,128)(2,1)} %reduce-scatter.2.cloned.1.call-done), channel_id=1, source_target_pairs={{0,16},{16,0},{1,17},{17,1},{2,18},{18,2},{3,19},{19,3},{4,20},{20... | collective-permute-start | bytes 3145736 | tf_op jit(solution)/shard_map/ppermute | solution.py:13
  429.8 20.1 %copy-start.26 = (bf16[256,2048]{1,0:T(8,128)(2,1)S(1)}, bf16[256,2048]{1,0:T(8,128)(2,1)}, u32[]{:S(2)}) copy-start(bf16[256,2048]{1,0:T(8,128)(2,1)} %reduce-scatter.2.cloned.1.call-done) | copy-start | bytes 3145732
Sparse Core Ops, SparseCore 0:
  36.0 82.2 all-gather.8
  119.9 96.5 all-gather.4
  230.6 65.3 all-gather.6
  349.2 75.4 reduce-scatter.1

commit v7 on v3

--- a/solution.py
+++ b/solution.py
@@ -37,6 +37,29 @@
         for position, code in enumerate(codes):
             held[code ^ mask] = arrived[position]
     return held
+
+
+def gather_groups(block, axis):
+    count = lax.axis_size(axis)
+    codes = [0]
+    stack = block[None]
+    groups = [(codes, stack)]
+    for mask in bit_order(count, True):
+        arrived = swapped(stack, axis, mask)
+        moved = [code ^ mask for code in codes]
+        groups = [(codes, stack), (moved, arrived)]
+        stack = jnp.concatenate([stack, arrived], axis=0)
+        codes = codes + moved
+    return groups
+
+
+def code_slices(values, index, codes, width):
+    pieces = [lax.dynamic_slice_in_dim(values, (index ^ code) * width, width, axis=1) for code in codes]
+    return pieces[0] if len(pieces) == 1 else jnp.concatenate(pieces, axis=1)
+
+
+def flat(stack):
+    return stack.reshape(stack.shape[0] * stack.shape[1], stack.shape[2])
 
 
 def scatter_blocks(by_code, axis):
@@ -99,9 +122,10 @@
     dp_index = lax.axis_index("dp")
     block_rows = query_weight.shape[1]
 
-    query_blocks = gather_blocks(query_weight[0], "dp")
-    key_blocks = gather_blocks(key_weight[0], "dp")
-    value_blocks = gather_blocks(value_weight[0], "dp")
+    dp_count = lax.axis_size("dp")
+    query_groups = gather_groups(query_weight[0], "dp")
+    key_groups = gather_groups(key_weight[0], "dp")
+    value_groups = gather_groups(value_weight[0], "dp")
 
     slot_rows = vision.shape[2]
     part_width = vision.shape[3]
@@ -115,10 +139,10 @@
     width_k = key_weight.shape[2]
     keys_raw = None
     values_raw = None
-    for code in key_blocks:
-        piece = columns_of(image, (dp_index ^ code) * block_rows, block_rows)
-        key_part = jnp.dot(piece, key_blocks[code], preferred_element_type=jnp.float32)
-        value_part = jnp.dot(piece, value_blocks[code], preferred_element_type=jnp.float32)
+    for (codes, key_stack), (_, value_stack) in zip(key_groups, value_groups):
+        piece = code_slices(image, dp_index, codes, block_rows)
+        key_part = jnp.dot(piece, flat(key_stack), preferred_element_type=jnp.float32)
+        value_part = jnp.dot(piece, flat(value_stack), preferred_element_type=jnp.float32)
         keys_raw = key_part if keys_raw is None else keys_raw + key_part
         values_raw = value_part if values_raw is None else values_raw + value_part
     keys_raw = keys_raw.reshape(slot_rows, width_k // HD, HD)
@@ -142,10 +166,10 @@
         full_text = gathered[chunk][0, 0]
         normed = norm_rows(full_text, norm_gain[0]).astype(jnp.bfloat16)
         query_raw = None
-        for code, block in query_blocks.items():
+        for codes, stack in query_groups:
             part = jnp.dot(
-                columns_of(normed, (dp_index ^ code) * block_rows, block_rows),
-                block,
+                code_slices(normed, dp_index, codes, block_rows),
+                flat(stack),
                 preferred_element_type=jnp.float32,
             )
             query_raw = part if query_raw is None else query_raw + part
@@ -171,15 +195,17 @@
     value_flat = value_back.reshape(slot_rows, width_k).astype(jnp.bfloat16)
 
     contract = (((1,), (1,)), ((), ()))
-    partial_sum = jnp.zeros((slot_rows, image.shape[1]), jnp.bfloat16)
-    for code in key_blocks:
-        term = lax.dot_general(key_flat, key_blocks[code], contract, preferred_element_type=jnp.float32)
+    by_code = {}
+    for (codes, key_stack), (_, value_stack) in zip(key_groups, value_groups):
+        term = lax.dot_general(key_flat, flat(key_stack), contract, preferred_element_type=jnp.float32)
         term = term + lax.dot_general(
-            value_flat, value_blocks[code], contract, preferred_element_type=jnp.float32
+            value_flat, flat(value_stack), contract, preferred_element_type=jnp.float32
         )
-        partial_sum = lax.dynamic_update_slice_in_dim(
-            partial_sum, term.astype(jnp.bfloat16), (dp_index ^ code) * block_rows, axis=1
-        )
+        term = term.astype(jnp.bfloat16)
+        for position, code in enumerate(codes):
+            by_code[code] = term[:, position * block_rows : (position + 1) * block_rows]
+    in_code_order = jnp.concatenate([by_code[code] for code in range(dp_count)], axis=1)
+    partial_sum = code_slices(in_code_order, dp_index, list(range(dp_count)), block_rows)
     summed = lax.psum_scatter(partial_sum, "mp", scatter_dimension=1, tiled=True)
 
     routed = summed
@@ -191,13 +217,13 @@
 
     inner = (((0,), (0,)), ((), ()))
     grad_blocks = {}
-    for code in key_blocks:
-        piece = columns_of(image, (dp_index ^ code) * block_rows, block_rows)
+    for codes, _ in key_groups:
+        piece = code_slices(image, dp_index, codes, block_rows)
         key_part = lax.dot_general(piece, key_flat, inner, preferred_element_type=jnp.float32)
         value_part = lax.dot_general(piece, value_flat, inner, preferred_element_type=jnp.float32)
-        grad_blocks[code] = jnp.concatenate(
-            [key_part.astype(jnp.bfloat16), value_part.astype(jnp.bfloat16)], axis=1
-        )
+        both = jnp.concatenate([key_part.astype(jnp.bfloat16), value_part.astype(jnp.bfloat16)], axis=1)
+        for position, code in enumerate(codes):
+            grad_blocks[code] = both[position * block_rows : (position + 1) * block_rows]
     both_grads = scatter_blocks(grad_blocks, "dp").astype(jnp.bfloat16)
     key_weight_grad = both_grads[:, :width_k][None]
     value_weight_grad = both_grads[:, width_k:][None]

time: 442 us -> 445 us (level)
  local copies, waits for them, and re-layouts: 26.4 us -> 39.3 us
  other arithmetic: 46.4 us -> 37.9 us
    another operation x3 -> x0, other arithmetic: 10.6 us -> none  [gather_blocks(): arrived = swapped(jnp.stack([held[c] for c in codes]), axis, mask)]
    unnamed x110 -> x107, local copies, waits for them, and re-layouts: 10.3 us -> 17.1 us
    concatenate x0 -> x3, local copies, waits for them, and re-layouts: none -> 6.62 us  [gather_groups(): stack = jnp.concatenate([stack, arrived], axis=0)]
    ppermute x8, waiting for transfers between devices: 84.5 us -> 78.5 us  [swapped(): return lax.ppermute(value, axis, pairs)]
    dot_general x24 -> x12, matrix products: 50.1 us -> 51.2 us  [the longest x4 23.2 us: per_device(): jnp.dot(code_slices(normed, dp_index, codes, block_rows), flat(stack), pr...]
where the time goes in v7:
time: 445 us; the launch traced here: 441 us
  waiting for transfers between devices  263 us (59%)
  matrix products  69.2 us (16%)
  local copies, waits for them, and re-layouts  39.3 us (9%)
  other arithmetic  37.9 us (9%)
  between operations  19.4 us (4%)
  starting transfers between devices  12.7 us (3%)
    ppermute x3, waiting for transfers between devices, shifted(): return lax.ppermute(value, axis, pairs)  84 us
    ppermute x8, waiting for transfers between devices, swapped(): return lax.ppermute(value, axis, pairs)  78.5 us
    reduce_scatter x1, waiting for transfers between devices, per_device(): lax.psum_scatter(partial_sum, 'mp', scatter_dimension=1, tiled=True)  54.2 us
    all_gather x2, waiting for transfers between devices, per_device(): lax.all_gather(arrived[:, :, chunk * rows:(chunk + 1) * rows], 'mp', axis...  45.9 us
    dot_general x4, matrix products, per_device(): jnp.dot(code_slices(normed, dp_index, codes, block_rows), flat(stack), pr...  23.2 us
    unnamed x107, local copies, waits for them, and re-layouts  17.1 us
    dot_general x2, matrix products, per_device(): lax.dot_general(value_flat, flat(value_stack), contract, preferred_elemen...  9.03 us
  transfers between devices with their start and end apart: 15, of which 9 were waited for; matrix products, arithmetic and copies ran while one was open for 20% of the time, Pallas kernels for 0%

profile of v7, /device:TPU:0, one launch (start us, length us, event | category | flops | bytes accessed | tf_op | source)
XLA Modules:
  0.0 441.2 jit_solution(8414879762329955062)
XLA Ops:
  7.2 3.0 collective-permute-start
  10.2 1.3 constant_dynamic-slice_fusion.4
  12.2 21.4 %collective-permute-done = bf16[1,1,256,2048]{3,2,1,0:T(8,128)(2,1)S(1)} collective-permute-done((bf16[1,1,256,2048]{3,2,1,0:T(8,128)(2,1)}, bf16[1,1,256,2048]{3,2,1,0:T(8,128)(2,1)S(1)}, u32[]{:S(2)}, u32[]{:S(2)}) %collective-permute-start) | collective-permute-done | bytes 1048608 | tf_op jit(solution)/shard_map/ppermute | solution.py:13
  33.6 1.1 broadcast_select_fusion
  34.8 1.8 collective-permute-start.5
  36.6 1.5 collective-permute-start.6
  38.1 44.8 %collective-permute-done.5 = bf16[1,1,512,2048]{3,2,1,0:T(8,128)(2,1)S(1)} collective-permute-done((bf16[1,1,512,2048]{3,2,1,0:T(8,128)(2,1)S(1)}, bf16[1,1,512,2048]{3,2,1,0:T(8,128)(2,1)S(1)}, u32[]{:S(2)}, u32[]{:S(2)}) %collective-permute-start.5) | collective-permute-done | bytes 2097184 | tf_op jit(solution)/shard_map/ppermute | solution.py:13
  82.9 1.5 fusion.169
  84.4 1.5 collective-permute-start.3
  85.9 4.7 %constant_dynamic-update-slice_fusion.5 = bf16[2,2048,1024]{2,1,0:T(8,128)(2,1)} fusion(bf16[1,2048,1024]{2,1,0:T(8,128)(2,1)} %param.19), kind=kLoop, calls=%fused_computation.195 | loop fusion | bytes 8388608
  90.6 39.7 %collective-permute-done.6 = bf16[1,2048,1024]{2,1,0:T(8,128)(2,1)} collective-permute-done((bf16[1,2048,1024]{2,1,0:T(8,128)(2,1)}, bf16[1,2048,1024]{2,1,0:T(8,128)(2,1)}, u32[]{:S(2)}, u32[]{:S(2)}) %collective-permute-start.6) | collective-permute-done | bytes 4194336 | tf_op jit(solution)/shard_map/ppermute | solution.py:19
  130.3 4.6 %constant_dynamic-update-slice_fusion.4 = bf16[2,2048,1024]{2,1,0:T(8,128)(2,1)} fusion(bf16[2,2048,1024]{2,1,0:T(8,128)(2,1)} %constant_dynamic-update-slice_fusion.5, bf16[1,2048,1024]{2,1,0:T(8,128)(2,1)} %collective-permute-done.6), kind=kLoop, calls=%fused_computation.194 | loop fusion | bytes 8388608 | tf_op jit(solution)/shard_map/concatenate | solution.py:51
  134.9 1.5 collective-permute-start.1
  136.4 1.0 constant_dynamic-update-slice_fusion.3
  137.5 15.2 %collective-permute-done.3 = bf16[1,2048,256]{2,1,0:T(8,128)(2,1)S(1)} collective-permute-done((bf16[1,2048,256]{2,1,0:T(8,128)(2,1)S(1)}, bf16[1,2048,256]{2,1,0:T(8,128)(2,1)S(1)}, u32[]{:S(2)}, u32[]{:S(2)}) %collective-permute-start.3) | collective-permute-done | bytes 1048608 | tf_op jit(solution)/shard_map/ppermute | solution.py:19
  153.7 1.1 constant_dynamic-update-slice_fusion.1
  154.8 19.3 %collective-permute-done.1 = bf16[1,2048,256]{2,1,0:T(8,128)(2,1)S(1)} collective-permute-done((bf16[1,2048,256]{2,1,0:T(8,128)(2,1)S(1)}, bf16[1,2048,256]{2,1,0:T(8,128)(2,1)S(1)}, u32[]{:S(2)}, u32[]{:S(2)}) %collective-permute-start.1) | collective-permute-done | bytes 1048608 | tf_op jit(solution)/shard_map/ppermute | solution.py:19
  174.1 1.0 constant_dynamic-update-slice_fusion
  180.0 1.2 iota_compare_fusion
  181.9 2.7 dynamic-slice_bitcast_fusion.3
  184.7 4.0 fusion.165
  188.7 3.2 multiply_reduce_fusion.2
  192.0 1.1 copy.116
  193.9 3.2 fusion.166
  197.2 2.6 fusion.71
  199.7 1.5 convolution_convert_fusion.5
  201.2 1.5 convolution_convert_fusion.4
  202.7 3.3 fusion.2
  206.3 1.2 fusion.4
  208.0 6.0 %fusion.35 = f32[256,1024]{1,0:T(8,128)S(1)} fusion(bf16[4096,1024]{1,0:T(8,128)(2,1)} %bitcast.23, bf16[256,2048]{1,0:T(8,128)(2,1)S(1)} %get-tuple-element.43, bf16[256,2048]{1,0:T(8,128)(2,1)S(1)} %get-tuple-element.44), kind=kOutput, calls=%fused_computation.65 | convolution fusion | flops 2151677952 | bytes 11534336 | tf_op jit(solution)/shard_map/dot_general | solution.py:170
  214.1 5.8 %fusion.62 = f32[256,1024]{1,0:T(8,128)S(1)} fusion(f32[256,1024]{1,0:T(8,128)S(1)} %fusion.35, bf16[4096,1024]{1,0:T(8,128)(2,1)} %bitcast.22, bf16[256,2048]{1,0:T(8,128)(2,1)S(1)} %get-tuple-element.45, bf16[256,2048]{1,0:T(8,128)(2,1)S(1)} %get-tuple-element.42), kind=kOutput, calls=%fused_computation.96 | convolution fusion | flops 2151940096 | bytes 12582912 | tf_op jit(solution)/shard_map/dot_general | solution.py:170
  219.8 1.4 reshape.218
  223.5 3.9 fusion.171
  227.5 2.4 divide_convert_fusion.1
  234.2 45.9 %all-gather.7.cloned.1.call-done = bf16[1,1,256,8192]{3,2,1,0:T(8,128)(2,1)} async-done(((bf16[1,1,256,2048]{3,2,1,0:T(8,128)(2,1)}), bf16[1,1,256,8192]{3,2,1,0:T(8,128)(2,1)}) %all-gather.7.cloned.1.call-update) | async-done | bytes 4194320 | tf_op jit(solution)/shard_map/all_gather | solution.py:161
  280.1 3.3 fusion.5
  283.5 1.2 fusion.7
  285.2 5.7 %fusion.43 = f32[256,1024]{1,0:T(8,128)S(1)} fusion(bf16[4096,1024]{1,0:T(8,128)(2,1)} %bitcast.23, bf16[256,2048]{1,0:T(8,128)(2,1)S(1)} %get-tuple-element.39, bf16[256,2048]{1,0:T(8,128)(2,1)S(1)} %get-tuple-element.40), kind=kOutput, calls=%fused_computation.73 | convolution fusion | flops 2151677952 | bytes 11534336 | tf_op jit(solution)/shard_map/dot_general | solution.py:170
  290.9 5.7 %fusion.59 = f32[256,1024]{1,0:T(8,128)S(1)} fusion(f32[256,1024]{1,0:T(8,128)S(1)} %fusion.43, bf16[4096,1024]{1,0:T(8,128)(2,1)} %bitcast.22, bf16[256,2048]{1,0:T(8,128)(2,1)S(1)} %get-tuple-element.41, bf16[256,2048]{1,0:T(8,128)(2,1)S(1)} %get-tuple-element.38), kind=kOutput, calls=%fused_computation.95 | convolution fusion | flops 2151940096 | bytes 12582912 | tf_op jit(solution)/shard_map/dot_general | solution.py:170
  296.6 1.0 multiply_bitcast_fusion
  297.7 1.4 reshape.219
  299.1 1.4 copy.165
  302.5 3.5 fusion.176
  306.1 2.3 fusion.25
  309.4 4.5 %fusion.189 = f32[256,4096]{1,0:T(8,128)} fusion(bf16[256,256]{0,1:T(8,128)(2,1)S(1)} %bitcast.249, bf16[4096,256]{1,0:T(8,128)(2,1)} %bitcast.5), kind=kOutput, calls=%fused_computation.249 | convolution fusion | flops 536870912 | bytes 6422528 | tf_op jit(solution)/shard_map/dot_general | solution.py:201
  313.9 4.5 %fusion.190 = f32[256,4096]{1,0:T(8,128)} fusion(bf16[256,256]{0,1:T(8,128)(2,1)S(1)} %bitcast.250, bf16[4096,256]{1,0:T(8,128)(2,1)} %bitcast.8), kind=kOutput, calls=%fused_computation.250 | convolution fusion | flops 536870912 | bytes 6422528 | tf_op jit(solution)/shard_map/dot_general | solution.py:201
  319.9 3.6 fusion.8
  323.8 1.9 copy-done.2
  325.7 2.3 fusion.9
  329.3 2.2 pad_maximum_fusion.1
  331.5 1.2 copy-done.18
  332.7 2.0 convolution_convert_fusion.1
  339.3 4.2 collective-permute-done.9
  343.5 2.7 fusion.26
  346.2 1.5 collective-permute-start.10
  350.1 1.4 select_convert_fusion.1
  351.7 1.0 maximum_bitcast_fusion
  352.7 54.2 %reduce-scatter.2.cloned.1.call-done = bf16[256,2048]{1,0:T(8,128)(2,1)} async-done(((bf16[256,8192]{1,0:T(8,128)(2,1)}), bf16[256,2048]{1,0:T(8,128)(2,1)}) %reduce-scatter.2.cloned.1.call-update) | async-done | bytes 1048592 | tf_op jit(solution)/shard_map/reduce_scatter | solution.py:209
  406.9 1.5 collective-permute-start.8
  408.4 3.2 fusion.10
  411.7 1.3 copy.140
  413.0 1.3 copy.141
  414.3 17.8 %collective-permute-done.8 = bf16[256,2048]{1,0:T(8,128)(2,1)} collective-permute-done((bf16[256,2048]{1,0:T(8,128)(2,1)}, bf16[256,2048]{1,0:T(8,128)(2,1)}, u32[]{:S(2)}, u32[]{:S(2)}) %collective-permute-start.8) | collective-permute-done | bytes 1048608 | tf_op jit(solution)/shard_map/ppermute | solution.py:13
  432.2 2.3 select_bitcast_fusion
  (170 shorter events, 24.6 us)
Async XLA Ops:
  7.2 174.8 %all-gather.9.cloned.1.call-start = ((), (), s32[]{:S(2)}) async-start(), calls=%async_computation.4 | async-start | bytes 5242880 | tf_op jit(solution)/shard_map/all_gather | solution.py:137
  7.2 26.4 %collective-permute-start = (bf16[1,1,256,2048]{3,2,1,0:T(8,128)(2,1)}, bf16[1,1,256,2048]{3,2,1,0:T(8,128)(2,1)S(1)}, u32[]{:S(2)}, u32[]{:S(2)}) collective-permute-start(bf16[1,1,256,2048]{3,2,1,0:T(8,128)(2,1)} %param.14), channel_id=1, source_target_pairs={{0,16},{16,0},{1,17},{17,1},{2,18},{18,2},{3,19},{19,3},{4,20},{20... | collective-permute-start | bytes 3145736 | tf_op jit(solution)/shard_map/ppermute | solution.py:13
  12.2 22.6 %copy-start.44 = (bf16[1,1,512,2048]{3,2,1,0:T(8,128)(2,1)S(1)}, bf16[1,1,512,2048]{3,2,1,0:T(8,128)(2,1)}, u32[]{:S(2)}) copy-start(bf16[1,1,512,2048]{3,2,1,0:T(8,128)(2,1)} %param.13) | copy-start | bytes 6291460
  34.7 49.7 %copy-start.21 = (bf16[1,2048,256]{2,1,0:T(8,128)(2,1)S(1)}, bf16[1,2048,256]{2,1,0:T(8,128)(2,1)}, u32[]{:S(2)}) copy-start(bf16[1,2048,256]{2,1,0:T(8,128)(2,1)} %param.20) | copy-start | bytes 3145732
  34.7 168.0 %all-gather.5.cloned.1.call-start = ((), (), s32[]{:S(2)}) async-start(), calls=%async_computation.1 | async-start | bytes 5242880 | tf_op jit(solution)/shard_map/all_gather | solution.py:161
  34.8 48.1 %collective-permute-start.5 = (bf16[1,1,512,2048]{3,2,1,0:T(8,128)(2,1)S(1)}, bf16[1,1,512,2048]{3,2,1,0:T(8,128)(2,1)S(1)}, u32[]{:S(2)}, u32[]{:S(2)}) collective-permute-start(bf16[1,1,512,2048]{3,2,1,0:T(8,128)(2,1)S(1)} %copy-done.44), channel_id=1, source_target_pairs={{0,16},{16,0},{1,17},{17,1},{2,18},{18,2},{3,19},{19,3},{4,20},{20... | collective-permute-start | bytes 6291464 | tf_op jit(solution)/shard_map/ppermute | solution.py:13
  36.6 93.8 %collective-permute-start.6 = (bf16[1,2048,1024]{2,1,0:T(8,128)(2,1)}, bf16[1,2048,1024]{2,1,0:T(8,128)(2,1)}, u32[]{:S(2)}, u32[]{:S(2)}) collective-permute-start(bf16[1,2048,1024]{2,1,0:T(8,128)(2,1)} %param.19), channel_id=1, source_target_pairs={{0,2},{1,3},{2,0},{3,1},{4,6},{5,7},{6,4},{7,5},{8,10},{9,11},{10,... | collective-permute-start | bytes 12582920 | tf_op jit(solution)/shard_map/ppermute | solution.py:19
  84.3 195.7 %all-gather.7.cloned.1.call-start = ((), (), s32[]{:S(2)}) async-start(), calls=%async_computation.2 | async-start | bytes 5242880 | tf_op jit(solution)/shard_map/all_gather | solution.py:161
  84.4 68.3 %collective-permute-start.3 = (bf16[1,2048,256]{2,1,0:T(8,128)(2,1)S(1)}, bf16[1,2048,256]{2,1,0:T(8,128)(2,1)S(1)}, u32[]{:S(2)}, u32[]{:S(2)}) collective-permute-start(bf16[1,2048,256]{2,1,0:T(8,128)(2,1)S(1)} %copy-done.21), channel_id=1, source_target_pairs={{0,2},{1,3},{2,0},{3,1},{4,6},{5,7},{6,4},{7,5},{8,10},{9,11},{10,... | collective-permute-start | bytes 3145736 | tf_op jit(solution)/shard_map/ppermute | solution.py:19
  90.6 44.3 %copy-start.22 = (bf16[1,2048,256]{2,1,0:T(8,128)(2,1)S(1)}, bf16[1,2048,256]{2,1,0:T(8,128)(2,1)}, u32[]{:S(2)}) copy-start(bf16[1,2048,256]{2,1,0:T(8,128)(2,1)} %param.21) | copy-start | bytes 3145732
  134.9 73.1 %collective-permute-start.7 = (bf16[2,2048,1024]{2,1,0:T(8,128)(2,1)}, bf16[2,2048,1024]{2,1,0:T(8,128)(2,1)}, u32[]{:S(2)}, u32[]{:S(2)}) collective-permute-start(bf16[2,2048,1024]{2,1,0:T(8,128)(2,1)} %constant_dynamic-update-slice_fusion.4), channel_id=1, source_target_pairs={{0,1},{1,0},{2,3},{3,2},{4,5},{5,4},{6,7},{7,6},{8,9},{9,8},{10,11... | collective-permute-start | bytes 25165832 | tf_op jit(solution)/shard_map/ppermute | solution.py:19
  134.9 39.2 %collective-permute-start.1 = (bf16[1,2048,256]{2,1,0:T(8,128)(2,1)S(1)}, bf16[1,2048,256]{2,1,0:T(8,128)(2,1)S(1)}, u32[]{:S(2)}, u32[]{:S(2)}) collective-permute-start(bf16[1,2048,256]{2,1,0:T(8,128)(2,1)S(1)} %copy-done.22), channel_id=1, source_target_pairs={{0,2},{1,3},{2,0},{3,1},{4,6},{5,7},{6,4},{7,5},{8,10},{9,11},{10,... | collective-permute-start | bytes 3145736 | tf_op jit(solution)/shard_map/ppermute | solution.py:19
  153.7 24.1 %copy-start.11 = (bf16[1,1,512,1024]{3,2,1,0:T(8,128)(2,1)S(1)}, bf16[1,1,512,1024]{3,2,1,0:T(8,128)(2,1)}, u32[]{:S(2)}) copy-start(bf16[1,1,512,1024]{3,2,1,0:T(8,128)(2,1)} %param.25) | copy-start | bytes 3145732
  153.7 31.0 %collective-permute-start.4 = (bf16[2,2048,256]{2,1,0:T(8,128)(2,1)}, bf16[2,2048,256]{2,1,0:T(8,128)(2,1)}, u32[]{:S(2)}, u32[]{:S(2)}) collective-permute-start(bf16[2,2048,256]{2,1,0:T(8,128)(2,1)} %constant_dynamic-update-slice_fusion.2), channel_id=1, source_target_pairs={{0,1},{1,0},{2,3},{3,2},{4,5},{5,4},{6,7},{7,6},{8,9},{9,8},{10,11... | collective-permute-start | bytes 6291464 | tf_op jit(solution)/shard_map/ppermute | solution.py:19
  175.1 18.7 %collective-permute-start.2 = (bf16[2,2048,256]{2,1,0:T(8,128)(2,1)}, bf16[2,2048,256]{2,1,0:T(8,128)(2,1)}, u32[]{:S(2)}, u32[]{:S(2)}) collective-permute-start(bf16[2,2048,256]{2,1,0:T(8,128)(2,1)} %constant_dynamic-update-slice_fusion), channel_id=1, source_target_pairs={{0,1},{1,0},{2,3},{3,2},{4,5},{5,4},{6,7},{7,6},{8,9},{9,8},{10,11... | collective-permute-start | bytes 6291464 | tf_op jit(solution)/shard_map/ppermute | solution.py:19
  178.0 1.4 copy-start.45
  181.7 19.5 %copy-start.38 = (pred[256]{0:T(512)(128)(4,1)}, pred[256]{0:T(512)(128)(4,1)S(1)}, u32[]{:S(2)}) copy-start(pred[256]{0:T(512)(128)(4,1)S(1)} %get-tuple-element.72) | copy-start | bytes 772
  181.7 225.2 %reduce-scatter.2.cloned.1.call-start = ((), (), s32[]{:S(2)}) async-start(), calls=%async_computation.3 | async-start | bytes 5242880 | tf_op jit(solution)/shard_map/reduce_scatter | solution.py:209
  184.6 4.1 copy-start.17
  184.7 4.1 copy-start.19
  184.7 4.1 copy-start.14
  184.7 12.5 %copy-start.12 = (bf16[256,2048]{1,0:T(8,128)(2,1)}, bf16[256,2048]{1,0:T(8,128)(2,1)S(1)}, u32[]{:S(2)}) copy-start(bf16[256,2048]{1,0:T(8,128)(2,1)S(1)} %get-tuple-element.46) | copy-start | bytes 3145732
  188.7 4.3 copy-start.30
  192.0 5.1 %copy-start.36 = (f32[256,2]{0,1:T(2,128)}, f32[256,2]{0,1:T(2,128)S(1)}, u32[]{:S(2)}) copy-start(f32[256,2]{0,1:T(2,128)S(1)} %get-tuple-element.66) | copy-start | bytes 6148
  193.9 3.3 copy-start.15
  197.2 2.6 copy-start.41
  201.2 4.8 %copy-start.28 = (f32[1,8192]{1,0:T(1,128)S(1)}, f32[1,8192]{1,0:T(1,128)}, u32[]{:S(2)}) copy-start(f32[1,8192]{1,0:T(1,128)} %param.18) | copy-start | bytes 98308
  202.7 3.6 copy-start
  223.5 4.0 copy-start.33
  227.5 2.5 copy-start.42
  227.5 3.8 copy-start.10
  230.0 1.3 copy-start.8
  230.0 1.7 copy-start.25
  230.0 1.7 copy-start.34
  230.0 1.6 copy-start.46
  230.0 1.6 copy-start.48
  231.6 1.1 copy-start.37
  233.3 50.1 %copy-start.29 = (f32[1,8192]{1,0:T(1,128)S(1)}, f32[1,8192]{1,0:T(1,128)}, u32[]{:S(2)}) copy-start(f32[1,8192]{1,0:T(1,128)} %param.18) | copy-start | bytes 98308
  280.1 3.4 copy-start.1
  302.5 3.6 copy-start.31
  306.1 2.3 copy-start.39
  313.9 4.6 %copy-start.7 = (bf16[2,4,256,256]{2,3,1,0:T(8,128)(2,1)S(1)}, bf16[2,4,256,256]{2,3,1,0:T(8,128)(2,1)}, u32[]{:S(2)}) copy-start(bf16[2,4,256,256]{2,3,1,0:T(8,128)(2,1)} %convolution_convert_fusion.4) | copy-start | bytes 3145732
  313.9 4.6 %copy-start.9 = (f32[2,4,256,256]{2,3,1,0:T(8,128)S(1)}, f32[2,4,256,256]{2,3,1,0:T(8,128)}, u32[]{:S(2)}) copy-start(f32[2,4,256,256]{2,3,1,0:T(8,128)} %get-tuple-element.71) | copy-start | bytes 6291460
  313.9 4.6 %copy-start.24 = (f32[256,2,4,128]{3,2,1,0:T(4,128)S(1)}, f32[256,2,4,128]{3,2,1,0:T(4,128)}, u32[]{:S(2)}) copy-start(f32[256,2,4,128]{3,2,1,0:T(4,128)} %reshape.219) | copy-start | bytes 3145732
  313.9 4.6 %copy-start.32 = (f32[256,2,4]{0,2,1:T(4,128)S(1)}, f32[256,2,4]{0,2,1:T(4,128)}, u32[]{:S(2)}) copy-start(f32[256,2,4]{0,2,1:T(4,128)} %copy-done.31) | copy-start | bytes 24580
  313.9 4.6 %copy-start.47 = (f32[1,128]{1,0:T(1,128)S(1)}, f32[1,128]{1,0:T(1,128)}, u32[]{:S(2)}) copy-start(f32[1,128]{1,0:T(1,128)} %param.22) | copy-start | bytes 1540
  313.9 4.6 %copy-start.49 = (pred[256]{0:T(512)(128)(4,1)S(1)}, pred[256]{0:T(512)(128)(4,1)}, u32[]{:S(2)}) copy-start(pred[256]{0:T(512)(128)(4,1)} %iota_compare_fusion) | copy-start | bytes 772
  318.5 1.1 copy-start.35
  318.5 1.1 copy-start.27
  323.5 2.2 copy-start.2
  331.4 1.2 copy-start.18
  332.7 2.0 copy-start.20
  335.8 1.5 copy-start.13
  335.8 1.9 copy-start.16
  336.2 7.2 %collective-permute-start.9 = (bf16[2,2048,512]{1,2,0:T(8,128)(2,1)S(1)}, bf16[2,2048,512]{1,2,0:T(8,128)(2,1)S(1)}, u32[]{:S(2)}, u32[]{:S(2)}) collective-permute-start(bf16[2,2048,512]{1,2,0:T(8,128)(2,1)S(1)} %pad_maximum_fusion.2), channel_id=1, source_target_pairs={{0,1},{1,0},{2,3},{3,2},{4,5},{5,4},{6,7},{7,6},{8,9},{9,8},{10,11... | collective-permute-start | bytes 12582920 | tf_op jit(solution)/shard_map/ppermute | solution.py:19
  338.5 5.0 %copy-start.3 = (bf16[4096,256]{0,1:T(8,128)(2,1)}, bf16[4096,256]{0,1:T(8,128)(2,1)S(1)}, u32[]{:S(2)}) copy-start(bf16[4096,256]{0,1:T(8,128)(2,1)S(1)} %convolution_convert_fusion.3) | copy-start | bytes 6291460
  339.2 6.9 %copy-start.5 = (bf16[4096,256]{0,1:T(8,128)(2,1)}, bf16[4096,256]{0,1:T(8,128)(2,1)S(1)}, u32[]{:S(2)}) copy-start(bf16[4096,256]{0,1:T(8,128)(2,1)S(1)} %convolution_convert_fusion.2) | copy-start | bytes 6291460
  343.5 2.7 copy-start.6
  346.2 62.2 %collective-permute-start.10 = (bf16[1,2048,512]{1,2,0:T(8,128)(2,1)}, bf16[1,2048,512]{1,2,0:T(8,128)(2,1)}, u32[]{:S(2)}, u32[]{:S(2)}) collective-permute-start(bf16[1,2048,512]{1,2,0:T(8,128)(2,1)} %fusion.26), channel_id=1, source_target_pairs={{0,2},{1,3},{2,0},{3,1},{4,6},{5,7},{6,4},{7,5},{8,10},{9,11},{10,... | collective-permute-start | bytes 6291464 | tf_op jit(solution)/shard_map/ppermute | solution.py:19
  348.6 1.6 copy-start.43
  349.6 1.9 copy-start.40
  350.1 58.2 %copy-start.4 = (bf16[4096,256]{0,1:T(8,128)(2,1)S(1)}, bf16[4096,256]{0,1:T(8,128)(2,1)}, u32[]{:S(2)}) copy-start(bf16[4096,256]{0,1:T(8,128)(2,1)} %copy-done.3) | copy-start | bytes 6291460
  406.9 25.3 %collective-permute-start.8 = (bf16[256,2048]{1,0:T(8,128)(2,1)}, bf16[256,2048]{1,0:T(8,128)(2,1)}, u32[]{:S(2)}, u32[]{:S(2)}) collective-permute-start(bf16[256,2048]{1,0:T(8,128)(2,1)} %reduce-scatter.2.cloned.1.call-done), channel_id=1, source_target_pairs={{0,16},{16,0},{1,17},{17,1},{2,18},{18,2},{3,19},{19,3},{4,20},{20... | collective-permute-start | bytes 3145736 | tf_op jit(solution)/shard_map/ppermute | solution.py:13
  411.7 20.5 %copy-start.23 = (bf16[256,2048]{1,0:T(8,128)(2,1)S(1)}, bf16[256,2048]{1,0:T(8,128)(2,1)}, u32[]{:S(2)}) copy-start(bf16[256,2048]{1,0:T(8,128)(2,1)} %reduce-scatter.2.cloned.1.call-done) | copy-start | bytes 3145732
  (1 other events, 1.0 us)
Sparse Core Ops, SparseCore 0:
  34.8 82.2 all-gather.8
  119.3 79.2 all-gather.4
  200.7 79.2 all-gather.6
  331.6 75.2 reduce-scatter.1

commit v8 on v4

--- a/solution.py
+++ b/solution.py
@@ -106,11 +106,17 @@
     slot_rows = vision.shape[2]
     part_width = vision.shape[3]
     wanted = image_of[0, section]
-    owned = lax.all_gather(vision[0, 0], "mp", axis=1, tiled=True)
-    image = owned
-    for steps in range(1, sections):
-        moved = shifted(owned, "section", steps)
-        image = jnp.where((section - steps) % sections == wanted, moved, image)
+    halves = 2 if slot_rows % 16 == 0 else 1
+    half_rows = slot_rows // halves
+    image_halves = []
+    for half in range(halves):
+        local = vision[:, :, half * half_rows : (half + 1) * half_rows]
+        image_part = local[0, 0]
+        for steps in range(1, sections):
+            moved = shifted(local, "section", steps)[0, 0]
+            image_part = jnp.where((section - steps) % sections == wanted, moved, image_part)
+        image_halves.append(lax.all_gather(image_part, "mp", axis=1, tiled=True))
+    image = image_halves[0] if halves == 1 else jnp.concatenate(image_halves, axis=0)
 
     width_k = key_weight.shape[2]
     keys_raw = None

time: 450 us -> 477 us (1.060)
  waiting for transfers between devices: 250 us -> 281 us
  matrix products: 77.9 us -> 69.9 us
    ppermute x3 -> x4, waiting for transfers between devices: 60.7 us -> 83.6 us  [shifted(): return lax.ppermute(value, axis, pairs)]
    all_gather x1 -> x2, waiting for transfers between devices: 17 us -> 0.04 us  [per_device(): image_halves.append(lax.all_gather(image_part, 'mp', axis=1, tiled=True))]
    ppermute x8, waiting for transfers between devices: 106 us -> 119 us  [swapped(): return lax.ppermute(value, axis, pairs)]
    all_gather x2, waiting for transfers between devices: 14.3 us -> 25.8 us  [per_device(): lax.all_gather(arrived[:, :, chunk * rows:(chunk + 1) * rows], 'mp', axis...]
    unnamed x116 -> x122, local copies, waits for them, and re-layouts: 14.1 us -> 11.3 us
  transfers between devices with their start and end apart: 15 -> 17, of which waited for: 8 -> 8; matrix products, arithmetic and copies ran while one was open for 23% -> 20% of each run, Pallas kernels for 0% -> 0%
where the time goes in v8:
time: 477 us; the launch traced here: 473 us
  waiting for transfers between devices  281 us (59%)
  matrix products  69.9 us (15%)
  other arithmetic  56.9 us (12%)
  local copies, waits for them, and re-layouts  32.2 us (7%)
  between operations  19.2 us (4%)
  starting transfers between devices  13.4 us (3%)
    ppermute x8, waiting for transfers between devices, swapped(): return lax.ppermute(value, axis, pairs)  119 us
    ppermute x4, waiting for transfers between devices, shifted(): return lax.ppermute(value, axis, pairs)  83.6 us
    reduce_scatter x1, waiting for transfers between devices, per_device(): lax.psum_scatter(partial_sum, 'mp', scatter_dimension=1, tiled=True)  52.6 us
    all_gather x2, waiting for transfers between devices, per_device(): lax.all_gather(arrived[:, :, chunk * rows:(chunk + 1) * rows], 'mp', axis...  25.8 us
    dot_general x8, matrix products, per_device(): jnp.dot(columns_of(normed, (dp_index ^ code) * block_rows, block_rows), b...  24.5 us
    unnamed x122, local copies, waits for them, and re-layouts  11.3 us
    another operation x3, other arithmetic, gather_blocks(): arrived = swapped(jnp.stack([held[c] for c in codes]), axis, mask)  10.8 us
    reduce_sum x4, other arithmetic, norm_rows(): jnp.mean(values * values, axis=-1, keepdims=True) + 1e-05  9.68 us
  transfers between devices with their start and end apart: 17, of which 8 were waited for; matrix products, arithmetic and copies ran while one was open for 20% of the time, Pallas kernels for 0%

profile of v8, /device:TPU:0, one launch (start us, length us, event | category | flops | bytes accessed | tf_op | source)
XLA Modules:
  0.0 473.0 jit_solution(11582725057521671457)
XLA Ops:
  8.4 3.0 collective-permute-start.1
  11.4 1.3 constant_dynamic-slice_fusion
  13.3 10.0 %collective-permute-done.1 = bf16[1,1,128,2048]{3,2,1,0:T(8,128)(2,1)S(1)} collective-permute-done((bf16[1,1,128,2048]{3,2,1,0:T(8,128)(2,1)S(1)}, bf16[1,1,128,2048]{3,2,1,0:T(8,128)(2,1)S(1)}, u32[]{:S(2)}, u32[]{:S(2)}) %collective-permute-start.1) | collective-permute-done | bytes 524320 | tf_op jit(solution)/shard_map/ppermute | solution.py:13
  23.3 2.1 broadcast_select_fusion
  25.5 1.8 collective-permute-start
  27.3 11.4 %collective-permute-done = bf16[1,1,128,2048]{3,2,1,0:T(8,128)(2,1)S(1)} collective-permute-done((bf16[1,1,128,2048]{3,2,1,0:T(8,128)(2,1)S(1)}, bf16[1,1,128,2048]{3,2,1,0:T(8,128)(2,1)S(1)}, u32[]{:S(2)}, u32[]{:S(2)}) %collective-permute-start) | collective-permute-done | bytes 524320 | tf_op jit(solution)/shard_map/ppermute | solution.py:13
  39.6 1.5 collective-permute-start.6
  41.1 44.7 %collective-permute-done.6 = bf16[1,1,512,2048]{3,2,1,0:T(8,128)(2,1)S(1)} collective-permute-done((bf16[1,1,512,2048]{3,2,1,0:T(8,128)(2,1)}, bf16[1,1,512,2048]{3,2,1,0:T(8,128)(2,1)S(1)}, u32[]{:S(2)}, u32[]{:S(2)}) %collective-permute-start.6) | collective-permute-done | bytes 2097184 | tf_op jit(solution)/shard_map/ppermute | solution.py:13
  85.8 1.5 fusion.198
  90.5 113.0 %collective-permute-done.4 = bf16[1,2048,256]{2,1,0:T(8,128)(2,1)S(1)} collective-permute-done((bf16[1,2048,256]{2,1,0:T(8,128)(2,1)S(1)}, bf16[1,2048,256]{2,1,0:T(8,128)(2,1)S(1)}, u32[]{:S(2)}, u32[]{:S(2)}) %collective-permute-start.4) | collective-permute-done | bytes 1048608 | tf_op jit(solution)/shard_map/ppermute | solution.py:19
  203.6 1.6 pad_maximum_fusion.3
  205.2 7.5 %pad_maximum_fusion = bf16[2,2048,1024]{2,1,0:T(8,128)(2,1)} fusion(bf16[1,2048,1024]{2,1,0:T(8,128)(2,1)} %collective-permute-done.7, bf16[1,2048,1024]{2,1,0:T(8,128)(2,1)} %param.19), kind=kLoop, calls=%fused_computation.12 | loop fusion | flops 4194304 | bytes 16777216 | tf_op jit(solution)/shard_map/stack | solution.py:36
  215.7 2.4 slice_convert_fusion
  218.1 2.6 copy.158
  220.7 1.3 copy.161
  224.9 1.7 pad_maximum_fusion.2
  226.9 2.6 fusion.92
  230.0 1.9 fusion.140
  232.5 2.5 multiply_reduce_fusion.2
  236.9 1.9 fusion.107
  238.9 1.8 fusion.139
  241.2 1.8 fusion.72
  243.1 1.5 convolution_convert_fusion.9
  244.6 1.5 convolution_convert_fusion.8
  246.1 3.3 fusion.2
  249.6 2.1 fusion.4
  253.1 3.5 fusion.11
  256.6 3.5 fusion.20
  260.1 4.5 fusion.63
  264.6 3.1 reshape.221
  267.7 1.3 multiply_bitcast_fusion.1
  270.2 1.6 reduce_sum.99
  271.9 3.6 fusion.200
  275.5 2.5 divide_convert_fusion.1
  282.7 25.8 %all-gather.9.cloned.1.call-done = bf16[1,1,256,8192]{3,2,1,0:T(8,128)(2,1)} async-done(((bf16[1,1,256,2048]{3,2,1,0:T(8,128)(2,1)}), bf16[1,1,256,8192]{3,2,1,0:T(8,128)(2,1)}) %all-gather.9.cloned.1.call-update) | async-done | bytes 4194320 | tf_op jit(solution)/shard_map/all_gather | solution.py:143
  308.5 3.3 fusion.5
  312.0 2.1 fusion.7
  315.4 3.5 fusion.19
  318.9 3.5 fusion.59
  322.4 3.5 fusion.62
  327.9 2.7 reshape.222
  330.6 2.4 copy.165
  333.0 1.6 reduce_sum.107
  334.7 3.6 fusion.205
  338.3 2.4 fusion.44
  341.8 1.4 convolution_convert_fusion.4
  346.5 1.7 fusion.99
  348.3 2.5 broadcast_in_dim.96
  350.7 1.5 fusion.22
  352.7 1.7 fusion.137
  354.4 1.8 fusion.138
  356.2 1.5 fusion.24
  357.8 2.7 fusion.26
  360.5 2.7 fusion.28
  368.1 6.2 %collective-permute-done.10 = bf16[2,2048,512]{1,2,0:T(8,128)(2,1)S(1)} collective-permute-done((bf16[2,2048,512]{1,2,0:T(8,128)(2,1)S(1)}, bf16[2,2048,512]{1,2,0:T(8,128)(2,1)S(1)}, u32[]{:S(2)}, u32[]{:S(2)}) %collective-permute-start.10) | collective-permute-done | bytes 4194336 | tf_op jit(solution)/shard_map/ppermute | solution.py:19
  374.3 2.7 add_convert_fusion
  377.0 1.5 collective-permute-start.11
  386.1 52.6 %reduce-scatter.2.cloned.1.call-done = bf16[256,2048]{1,0:T(8,128)(2,1)} async-done(((bf16[256,8192]{1,0:T(8,128)(2,1)}), bf16[256,2048]{1,0:T(8,128)(2,1)}) %reduce-scatter.2.cloned.1.call-update) | async-done | bytes 1048592 | tf_op jit(solution)/shard_map/reduce_scatter | solution.py:189
  438.7 1.5 collective-permute-start.9
  440.1 3.5 fusion.8
  443.8 1.3 copy.140
  445.1 1.3 copy.141
  446.4 17.5 %collective-permute-done.9 = bf16[256,2048]{1,0:T(8,128)(2,1)} collective-permute-done((bf16[256,2048]{1,0:T(8,128)(2,1)}, bf16[256,2048]{1,0:T(8,128)(2,1)}, u32[]{:S(2)}, u32[]{:S(2)}) %collective-permute-start.9) | collective-permute-done | bytes 1048608 | tf_op jit(solution)/shard_map/ppermute | solution.py:13
  464.0 2.3 select_bitcast_fusion
  (203 shorter events, 40.2 us)
Async XLA Ops:
  7.2 31.5 %copy-start.24 = (bf16[1,1,256,2048]{3,2,1,0:T(8,128)(2,1)S(1)}, bf16[1,1,256,2048]{3,2,1,0:T(8,128)(2,1)}, u32[]{:S(2)}) copy-start(bf16[1,1,256,2048]{3,2,1,0:T(8,128)(2,1)} %param.14) | copy-start | bytes 3145732
  7.2 219.6 %all-gather.13.cloned.1.call-start = ((), (), s32[]{:S(2)}) async-start(), calls=%async_computation.5 | async-start | bytes 2621440 | tf_op jit(solution)/shard_map/all_gather | solution.py:118
  8.4 14.9 %collective-permute-start.1 = (bf16[1,1,128,2048]{3,2,1,0:T(8,128)(2,1)S(1)}, bf16[1,1,128,2048]{3,2,1,0:T(8,128)(2,1)S(1)}, u32[]{:S(2)}, u32[]{:S(2)}) collective-permute-start(bf16[1,1,128,2048]{3,2,1,0:T(8,128)(2,1)S(1)} %slice.49), channel_id=1, source_target_pairs={{0,16},{16,0},{1,17},{17,1},{2,18},{18,2},{3,19},{19,3},{4,20},{20... | collective-permute-start | bytes 1572872 | tf_op jit(solution)/shard_map/ppermute | solution.py:13
  25.4 201.4 %all-gather.11.cloned.1.call-start = ((), (), s32[]{:S(2)}) async-start(), calls=%async_computation.4 | async-start | bytes 2621440 | tf_op jit(solution)/shard_map/all_gather | solution.py:118
  25.5 13.2 %collective-permute-start = (bf16[1,1,128,2048]{3,2,1,0:T(8,128)(2,1)S(1)}, bf16[1,1,128,2048]{3,2,1,0:T(8,128)(2,1)S(1)}, u32[]{:S(2)}, u32[]{:S(2)}) collective-permute-start(bf16[1,1,128,2048]{3,2,1,0:T(8,128)(2,1)S(1)} %get-tuple-element.47), channel_id=1, source_target_pairs={{0,16},{16,0},{1,17},{17,1},{2,18},{18,2},{3,19},{19,3},{4,20},{20... | collective-permute-start | bytes 1572872 | tf_op jit(solution)/shard_map/ppermute | solution.py:13
  39.5 49.0 %copy-start.5 = (bf16[1,2048,256]{2,1,0:T(8,128)(2,1)S(1)}, bf16[1,2048,256]{2,1,0:T(8,128)(2,1)}, u32[]{:S(2)}) copy-start(bf16[1,2048,256]{2,1,0:T(8,128)(2,1)} %param.20) | copy-start | bytes 3145732
  39.5 49.9 %copy-start.7 = (bf16[1,2048,256]{2,1,0:T(8,128)(2,1)S(1)}, bf16[1,2048,256]{2,1,0:T(8,128)(2,1)}, u32[]{:S(2)}) copy-start(bf16[1,2048,256]{2,1,0:T(8,128)(2,1)} %param.21) | copy-start | bytes 3145732
  39.5 206.5 %all-gather.7.cloned.1.call-start = ((), (), s32[]{:S(2)}) async-start(), calls=%async_computation.1 | async-start | bytes 5242880 | tf_op jit(solution)/shard_map/all_gather | solution.py:143
  39.6 46.2 %collective-permute-start.6 = (bf16[1,1,512,2048]{3,2,1,0:T(8,128)(2,1)}, bf16[1,1,512,2048]{3,2,1,0:T(8,128)(2,1)S(1)}, u32[]{:S(2)}, u32[]{:S(2)}) collective-permute-start(bf16[1,1,512,2048]{3,2,1,0:T(8,128)(2,1)} %param.13), channel_id=1, source_target_pairs={{0,16},{16,0},{1,17},{17,1},{2,18},{18,2},{3,19},{19,3},{4,20},{20... | collective-permute-start | bytes 6291464 | tf_op jit(solution)/shard_map/ppermute | solution.py:13
  87.2 221.3 %all-gather.9.cloned.1.call-start = ((), (), s32[]{:S(2)}) async-start(), calls=%async_computation.2 | async-start | bytes 5242880 | tf_op jit(solution)/shard_map/all_gather | solution.py:143
  87.3 117.9 %collective-permute-start.7 = (bf16[1,2048,1024]{2,1,0:T(8,128)(2,1)}, bf16[1,2048,1024]{2,1,0:T(8,128)(2,1)}, u32[]{:S(2)}, u32[]{:S(2)}) collective-permute-start(bf16[1,2048,1024]{2,1,0:T(8,128)(2,1)} %param.19), channel_id=1, source_target_pairs={{0,2},{1,3},{2,0},{3,1},{4,6},{5,7},{6,4},{7,5},{8,10},{9,11},{10,... | collective-permute-start | bytes 12582920 | tf_op jit(solution)/shard_map/ppermute | solution.py:19
  88.5 115.1 %collective-permute-start.4 = (bf16[1,2048,256]{2,1,0:T(8,128)(2,1)S(1)}, bf16[1,2048,256]{2,1,0:T(8,128)(2,1)S(1)}, u32[]{:S(2)}, u32[]{:S(2)}) collective-permute-start(bf16[1,2048,256]{2,1,0:T(8,128)(2,1)S(1)} %copy-done.5), channel_id=1, source_target_pairs={{0,2},{1,3},{2,0},{3,1},{4,6},{5,7},{6,4},{7,5},{8,10},{9,11},{10,... | collective-permute-start | bytes 3145736 | tf_op jit(solution)/shard_map/ppermute | solution.py:19
  89.4 135.5 %collective-permute-start.2 = (bf16[1,2048,256]{2,1,0:T(8,128)(2,1)S(1)}, bf16[1,2048,256]{2,1,0:T(8,128)(2,1)S(1)}, u32[]{:S(2)}, u32[]{:S(2)}) collective-permute-start(bf16[1,2048,256]{2,1,0:T(8,128)(2,1)S(1)} %copy-done.7), channel_id=1, source_target_pairs={{0,2},{1,3},{2,0},{3,1},{4,6},{5,7},{6,4},{7,5},{8,10},{9,11},{10,... | collective-permute-start | bytes 3145736 | tf_op jit(solution)/shard_map/ppermute | solution.py:19
  205.2 24.8 %collective-permute-start.5 = (bf16[2,2048,256]{2,1,0:T(8,128)(2,1)}, bf16[2,2048,256]{2,1,0:T(8,128)(2,1)}, u32[]{:S(2)}, u32[]{:S(2)}) collective-permute-start(bf16[2,2048,256]{2,1,0:T(8,128)(2,1)} %pad_maximum_fusion.3), channel_id=1, source_target_pairs={{0,1},{1,0},{2,3},{3,2},{4,5},{5,4},{6,7},{7,6},{8,9},{9,8},{10,11... | collective-permute-start | bytes 6291464 | tf_op jit(solution)/shard_map/ppermute | solution.py:19
  212.7 43.8 %collective-permute-start.8 = (bf16[2,2048,1024]{2,1,0:T(8,128)(2,1)}, bf16[2,2048,1024]{2,1,0:T(8,128)(2,1)}, u32[]{:S(2)}, u32[]{:S(2)}) collective-permute-start(bf16[2,2048,1024]{2,1,0:T(8,128)(2,1)} %pad_maximum_fusion), channel_id=1, source_target_pairs={{0,1},{1,0},{2,3},{3,2},{4,5},{5,4},{6,7},{7,6},{8,9},{9,8},{10,11... | collective-permute-start | bytes 25165832 | tf_op jit(solution)/shard_map/ppermute | solution.py:19
  218.1 4.4 copy-start.53
  224.9 19.8 %copy-start.48 = (pred[256]{0:T(512)(128)(4,1)}, pred[256]{0:T(512)(128)(4,1)S(1)}, u32[]{:S(2)}) copy-start(pred[256]{0:T(512)(128)(4,1)S(1)} %get-tuple-element.56) | copy-start | bytes 772
  226.5 12.3 %collective-permute-start.3 = (bf16[2,2048,256]{2,1,0:T(8,128)(2,1)}, bf16[2,2048,256]{2,1,0:T(8,128)(2,1)}, u32[]{:S(2)}, u32[]{:S(2)}) collective-permute-start(bf16[2,2048,256]{2,1,0:T(8,128)(2,1)} %pad_maximum_fusion.2), channel_id=1, source_target_pairs={{0,1},{1,0},{2,3},{3,2},{4,5},{5,4},{6,7},{7,6},{8,9},{9,8},{10,11... | collective-permute-start | bytes 6291464 | tf_op jit(solution)/shard_map/ppermute | solution.py:19
  226.6 212.1 %reduce-scatter.2.cloned.1.call-start = ((), (), s32[]{:S(2)}) async-start(), calls=%async_computation.3 | async-start | bytes 5242880 | tf_op jit(solution)/shard_map/reduce_scatter | solution.py:189
  226.8 2.6 copy-start.6
  229.4 2.5 copy-start.2
  229.4 2.5 copy-start.10
  232.5 3.6 copy-start.40
  236.1 2.8 copy-start.3
  236.9 3.7 copy-start.13
  240.7 2.4 copy-start.17
  240.7 2.4 copy-start.50
  241.2 3.4 copy-start.15
  243.1 3.0 copy-start.31
  246.1 3.5 copy-start
  249.6 2.2 copy-start.29
  271.9 3.6 copy-start.45
  275.5 2.6 copy-start.18
  275.5 2.6 copy-start.51
  275.5 3.8 copy-start.34
  278.0 3.0 copy-start.19
  278.0 2.1 copy-start.37
  278.0 2.1 copy-start.46
  278.0 2.1 copy-start.54
  278.0 2.1 copy-start.57
  308.5 3.4 copy-start.1
  311.9 2.2 copy-start.30
  330.6 4.1 copy-start.55
  334.7 3.6 copy-start.43
  338.3 2.4 copy-start.16
  338.3 2.4 copy-start.49
  340.6 2.6 copy-start.21
  340.7 2.6 copy-start.26
  340.7 2.6 copy-start.33
  340.7 2.8 copy-start.36
  340.7 2.8 copy-start.44
  340.7 2.8 copy-start.56
  340.7 2.8 copy-start.58
  348.2 2.5 copy-start.8
  354.4 1.8 copy-start.11
  367.1 7.2 %collective-permute-start.10 = (bf16[2,2048,512]{1,2,0:T(8,128)(2,1)S(1)}, bf16[2,2048,512]{1,2,0:T(8,128)(2,1)S(1)}, u32[]{:S(2)}, u32[]{:S(2)}) collective-permute-start(bf16[2,2048,512]{1,2,0:T(8,128)(2,1)S(1)} %pad_maximum_fusion.1), channel_id=1, source_target_pairs={{0,1},{1,0},{2,3},{3,2},{4,5},{5,4},{6,7},{7,6},{8,9},{9,8},{10,11... | collective-permute-start | bytes 12582920 | tf_op jit(solution)/shard_map/ppermute | solution.py:19
  368.1 11.0 %copy-start.20 = (bf16[2,4,256,256]{2,3,1,0:T(8,128)(2,1)S(1)}, bf16[2,4,256,256]{2,3,1,0:T(8,128)(2,1)}, u32[]{:S(2)}) copy-start(bf16[2,4,256,256]{2,3,1,0:T(8,128)(2,1)} %copy-done.19) | copy-start | bytes 3145732
  368.1 11.0 %copy-start.32 = (bf16[256,256]{0,1:T(8,128)(2,1)S(1)}, bf16[256,256]{0,1:T(8,128)(2,1)}, u32[]{:S(2)}) copy-start(bf16[256,256]{0,1:T(8,128)(2,1)} %copy-done.31) | copy-start | bytes 393220
  374.3 2.7 copy-start.23
  377.0 4.4 copy-start.22
  377.0 63.1 %collective-permute-start.11 = (bf16[1,2048,512]{1,2,0:T(8,128)(2,1)}, bf16[1,2048,512]{1,2,0:T(8,128)(2,1)}, u32[]{:S(2)}, u32[]{:S(2)}) collective-permute-start(bf16[1,2048,512]{1,2,0:T(8,128)(2,1)} %add_convert_fusion), channel_id=1, source_target_pairs={{0,2},{1,3},{2,0},{3,1},{4,6},{5,7},{6,4},{7,5},{8,10},{9,11},{10,... | collective-permute-start | bytes 6291464 | tf_op jit(solution)/shard_map/ppermute | solution.py:19
  380.2 3.6 copy-start.52
  438.7 25.3 %collective-permute-start.9 = (bf16[256,2048]{1,0:T(8,128)(2,1)}, bf16[256,2048]{1,0:T(8,128)(2,1)}, u32[]{:S(2)}, u32[]{:S(2)}) collective-permute-start(bf16[256,2048]{1,0:T(8,128)(2,1)} %reduce-scatter.2.cloned.1.call-done), channel_id=1, source_target_pairs={{0,16},{16,0},{1,17},{17,1},{2,18},{18,2},{3,19},{19,3},{4,20},{20... | collective-permute-start | bytes 3145736 | tf_op jit(solution)/shard_map/ppermute | solution.py:13
  443.8 20.2 %copy-start.35 = (bf16[256,2048]{1,0:T(8,128)(2,1)S(1)}, bf16[256,2048]{1,0:T(8,128)(2,1)}, u32[]{:S(2)}) copy-start(bf16[256,2048]{1,0:T(8,128)(2,1)} %reduce-scatter.2.cloned.1.call-done) | copy-start | bytes 3145732
  (12 other events, 15.3 us)
Sparse Core Ops, SparseCore 0:
  25.5 47.4 all-gather.12
  74.6 44.6 all-gather.10
  121.4 79.4 all-gather.6
  226.7 81.7 all-gather.8
  363.3 75.2 reduce-scatter.1

commit v9 on v7

--- a/solution.py
+++ b/solution.py
@@ -58,8 +58,8 @@
     return pieces[0] if len(pieces) == 1 else jnp.concatenate(pieces, axis=1)
 
 
-def flat(stack):
-    return stack.reshape(stack.shape[0] * stack.shape[1], stack.shape[2])
+def flat(stack, start, width):
+    return stack[:, :, start : start + width].reshape(stack.shape[0] * stack.shape[1], width)
 
 
 def scatter_blocks(by_code, axis):
@@ -123,9 +123,11 @@
     block_rows = query_weight.shape[1]
 
     dp_count = lax.axis_size("dp")
-    query_groups = gather_groups(query_weight[0], "dp")
-    key_groups = gather_groups(key_weight[0], "dp")
-    value_groups = gather_groups(value_weight[0], "dp")
+    width_q = query_weight.shape[2]
+    width_k = key_weight.shape[2]
+    weight_groups = gather_groups(
+        jnp.concatenate([query_weight[0], key_weight[0], value_weight[0]], axis=1), "dp"
+    )
 
     slot_rows = vision.shape[2]
     part_width = vision.shape[3]
@@ -137,21 +139,19 @@
     image = lax.all_gather(image_part, "mp", axis=1, tiled=True)
 
     width_k = key_weight.shape[2]
-    keys_raw = None
-    values_raw = None
-    for (codes, key_stack), (_, value_stack) in zip(key_groups, value_groups):
+    pair_raw = None
+    for codes, stack in weight_groups:
         piece = code_slices(image, dp_index, codes, block_rows)
-        key_part = jnp.dot(piece, flat(key_stack), preferred_element_type=jnp.float32)
-        value_part = jnp.dot(piece, flat(value_stack), preferred_element_type=jnp.float32)
-        keys_raw = key_part if keys_raw is None else keys_raw + key_part
-        values_raw = value_part if values_raw is None else values_raw + value_part
+        part = jnp.dot(piece, flat(stack, width_q, 2 * width_k), preferred_element_type=jnp.float32)
+        pair_raw = part if pair_raw is None else pair_raw + part
+    keys_raw = pair_raw[:, :width_k]
+    values_raw = pair_raw[:, width_k:]
     keys_raw = keys_raw.reshape(slot_rows, width_k // HD, HD)
     values_raw = values_raw.reshape(slot_rows, width_k // HD, HD)
     usable = jnp.arange(slot_rows) < tile_counts[0, wanted] * TILE_ROWS
 
     arrived = shifted(text_in, "section", 1)
     text_rows = text_in.shape[2]
-    width_q = query_weight.shape[2]
     chunks = 2 if text_rows % 16 == 0 else 1
     rows = text_rows // chunks
     contexts = []
@@ -166,10 +166,10 @@
         full_text = gathered[chunk][0, 0]
         normed = norm_rows(full_text, norm_gain[0]).astype(jnp.bfloat16)
         query_raw = None
-        for codes, stack in query_groups:
+        for codes, stack in weight_groups:
             part = jnp.dot(
                 code_slices(normed, dp_index, codes, block_rows),
-                flat(stack),
+                flat(stack, 0, width_q),
                 preferred_element_type=jnp.float32,
             )
             query_raw = part if query_raw is None else query_raw + part
@@ -195,13 +195,12 @@
     value_flat = value_back.reshape(slot_rows, width_k).astype(jnp.bfloat16)
 
     contract = (((1,), (1,)), ((), ()))
+    pair_flat = jnp.concatenate([key_flat, value_flat], axis=1)
     by_code = {}
-    for (codes, key_stack), (_, value_stack) in zip(key_groups, value_groups):
-        term = lax.dot_general(key_flat, flat(key_stack), contract, preferred_element_type=jnp.float32)
-        term = term + lax.dot_general(
-            value_flat, flat(value_stack), contract, preferred_element_type=jnp.float32
-        )
-        term = term.astype(jnp.bfloat16)
+    for codes, stack in weight_groups:
+        term = lax.dot_general(
+            pair_flat, flat(stack, width_q, 2 * width_k), contract, preferred_element_type=jnp.float32
+        ).astype(jnp.bfloat16)
         for position, code in enumerate(codes):
             by_code[code] = term[:, position * block_rows : (position + 1) * block_rows]
     in_code_order = jnp.concatenate([by_code[code] for code in range(dp_count)], axis=1)
@@ -217,7 +216,7 @@
 
     inner = (((0,), (0,)), ((), ()))
     grad_blocks = {}
-    for codes, _ in key_groups:
+    for codes, _ in weight_groups:
         piece = code_slices(image, dp_index, codes, block_rows)
         key_part = lax.dot_general(piece, key_flat, inner, preferred_element_type=jnp.float32)
         value_part = lax.dot_general(piece, value_flat, inner, preferred_element_type=jnp.float32)

time: 445 us -> 476 us (1.070)
  waiting for transfers between devices: 263 us -> 295 us
  other arithmetic: 37.9 us -> 66.6 us
  matrix products: 69.2 us -> 42.5 us
    ppermute x3, waiting for transfers between devices: 84 us -> 39.4 us  [shifted(): return lax.ppermute(value, axis, pairs)]
    all_gather x2, waiting for transfers between devices: 45.9 us -> 86.9 us  [per_device(): lax.all_gather(arrived[:, :, chunk * rows:(chunk + 1) * rows], 'mp', axis...]
    ppermute x8 -> x4, waiting for transfers between devices: 78.5 us -> 113 us  [swapped(): return lax.ppermute(value, axis, pairs)]
    dot_general x12 -> x8, matrix products: 51.2 us -> 23.8 us  [the longest x4 16.4 us: per_device(): jnp.dot(code_slices(normed, dp_index, codes, block_rows), flat(stack, 0,...]
    concatenate x0 -> x3, other arithmetic: none -> 22.1 us  [gather_groups(): stack = jnp.concatenate([stack, arrived], axis=0)]
    slice x0 -> x4, local copies, waits for them, and re-layouts: none -> 11.8 us  [the longest x2 10.8 us: flat(): stack[:, :, start:start + width]]
    broadcast_in_dim x0 -> x1, other arithmetic: none -> 8 us  [gather_groups(): stack = block[None]]
    concatenate x3 -> x0, local copies, waits for them, and re-layouts: 6.62 us -> none  [gather_groups(): stack = jnp.concatenate([stack, arrived], axis=0)]
  transfers between devices with their start and end apart: 15 -> 11, of which waited for: 9 -> 7; matrix products, arithmetic and copies ran while one was open for 20% -> 21% of each run, Pallas kernels for 0% -> 0%
where the time goes in v9:
time: 476 us; the launch traced here: 473 us
  waiting for transfers between devices  295 us (62%)
  other arithmetic  66.6 us (14%)
  matrix products  42.5 us (9%)
  local copies, waits for them, and re-layouts  39.5 us (8%)
  between operations  19.7 us (4%)
  starting transfers between devices  9.24 us (2%)
    ppermute x4, waiting for transfers between devices, swapped(): return lax.ppermute(value, axis, pairs)  113 us
    all_gather x2, waiting for transfers between devices, per_device(): lax.all_gather(arrived[:, :, chunk * rows:(chunk + 1) * rows], 'mp', axis...  86.9 us
    reduce_scatter x1, waiting for transfers between devices, per_device(): lax.psum_scatter(partial_sum, 'mp', scatter_dimension=1, tiled=True)  56 us
    ppermute x3, waiting for transfers between devices, shifted(): return lax.ppermute(value, axis, pairs)  39.4 us
    concatenate x3, other arithmetic, gather_groups(): stack = jnp.concatenate([stack, arrived], axis=0)  22.1 us
    dot_general x4, matrix products, per_device(): jnp.dot(code_slices(normed, dp_index, codes, block_rows), flat(stack, 0,...  16.4 us
    unnamed x116, local copies, waits for them, and re-layouts  11.4 us
    slice x2, local copies, waits for them, and re-layouts, flat(): stack[:, :, start:start + width]  10.8 us
  transfers between devices with their start and end apart: 11, of which 7 were waited for; matrix products, arithmetic and copies ran while one was open for 21% of the time, Pallas kernels for 0%

profile of v9, /device:TPU:0, one launch (start us, length us, event | category | flops | bytes accessed | tf_op | source)
XLA Modules:
  0.0 472.6 jit_solution(16655274354026086795)
XLA Ops:
  7.2 8.0 %maximum_bitcast_fusion = bf16[1,2048,1536]{2,1,0:T(8,128)(2,1)} fusion(bf16[2048,256]{1,0:T(8,128)(2,1)} %bitcast.268, bf16[2048,256]{1,0:T(8,128)(2,1)} %bitcast.269, bf16[2048,1024]{1,0:T(8,128)(2,1)} %bitcast.252), kind=kLoop, calls=%fused_computation.18 | loop fusion | flops 18874368 | bytes 12582912 | tf_op jit(solution)/shard_map/broadcast_in_dim | solution.py:45
  15.2 3.0 collective-permute-start.1
  18.2 1.5 collective-permute-start
  21.0 21.8 %collective-permute-done = bf16[1,1,256,2048]{3,2,1,0:T(8,128)(2,1)S(1)} collective-permute-done((bf16[1,1,256,2048]{3,2,1,0:T(8,128)(2,1)S(1)}, bf16[1,1,256,2048]{3,2,1,0:T(8,128)(2,1)S(1)}, u32[]{:S(2)}, u32[]{:S(2)}) %collective-permute-start) | collective-permute-done | bytes 1048608 | tf_op jit(solution)/shard_map/ppermute | solution.py:13
  42.8 1.1 broadcast_select_fusion
  44.0 1.6 collective-permute-start.3
  45.5 108.5 %collective-permute-done.1 = bf16[1,2048,1536]{2,1,0:T(8,128)(2,1)} collective-permute-done((bf16[1,2048,1536]{2,1,0:T(8,128)(2,1)}, bf16[1,2048,1536]{2,1,0:T(8,128)(2,1)}, u32[]{:S(2)}, u32[]{:S(2)}) %collective-permute-start.1) | collective-permute-done | bytes 6291488 | tf_op jit(solution)/shard_map/ppermute | solution.py:19
  154.0 10.5 %pad_maximum_fusion = bf16[2,2048,1536]{2,1,0:T(8,128)(2,1)} fusion(bf16[1,2048,1536]{2,1,0:T(8,128)(2,1)} %collective-permute-done.1, bf16[1,2048,1536]{2,1,0:T(8,128)(2,1)} %maximum_bitcast_fusion), kind=kLoop, calls=%fused_computation.4 | loop fusion | flops 6291456 | bytes 25165824 | tf_op jit(solution)/shard_map/concatenate | solution.py:51
  164.6 1.5 fusion.177
  171.0 1.2 iota_compare_fusion
  172.8 4.0 fusion.9
  176.8 7.5 %fusion.8 = bf16[2,2048,1024]{2,1,0:T(8,128)(2,1)} fusion(bf16[1,2048,1536]{2,1,0:T(8,128)(2,1)} %maximum_bitcast_fusion, bf16[1,2048,1536]{2,1,0:T(8,128)(2,1)} %collective-permute-done.1), kind=kLoop, calls=%fused_computation.17 | loop fusion | flops 4194304 | bytes 20971520 | tf_op jit(solution)/shard_map/concatenate | solution.py:51
  184.4 4.0 dynamic-slice_bitcast_fusion.3
  188.4 60.3 %all-gather.5.cloned.1.call-done = bf16[1,1,256,8192]{3,2,1,0:T(8,128)(2,1)} async-done(((bf16[1,1,256,2048]{3,2,1,0:T(8,128)(2,1)}), bf16[1,1,256,8192]{3,2,1,0:T(8,128)(2,1)}) %all-gather.5.cloned.1.call-update) | async-done | bytes 4194320 | tf_op jit(solution)/shard_map/all_gather | solution.py:161
  248.6 3.3 fusion.2
  252.1 1.2 fusion.4
  253.3 2.2 constant_dynamic-slice_fusion.12
  255.5 3.0 slice.95
  258.5 2.0 copy-done
  260.5 1.2 fusion.111
  261.7 0.9 copy-done.3
  263.0 1.2 convolution_add_fusion
  265.1 1.0 fusion.178
  267.5 7.8 %slice.101 = bf16[2,2048,1024]{2,1,0:T(8,128)(2,1)} slice(bf16[2,2048,1536]{2,1,0:T(8,128)(2,1)} %collective-permute-done.2), slice={[0:2], [0:2048], [0:1024]} | slice | bytes 16777216 | tf_op jit(solution)/shard_map/slice | solution.py:62
  275.3 5.9 %fusion.35 = f32[256,1024]{1,0:T(8,128)S(1)} fusion(bf16[4096,1024]{1,0:T(8,128)(2,1)} %bitcast.248, bf16[256,2048]{1,0:T(8,128)(2,1)S(1)} %copy-done.23, bf16[256,2048]{1,0:T(8,128)(2,1)S(1)} %copy-done.24), kind=kOutput, calls=%fused_computation.71 | convolution fusion | flops 2151677952 | bytes 11534336 | tf_op jit(solution)/shard_map/dot_general | solution.py:170
  281.2 5.7 %fusion.62 = f32[256,1024]{1,0:T(8,128)S(1)} fusion(f32[256,1024]{1,0:T(8,128)S(1)} %fusion.35, bf16[4096,1024]{1,0:T(8,128)(2,1)} %bitcast.244, bf16[256,2048]{1,0:T(8,128)(2,1)S(1)} %copy-done.22, bf16[256,2048]{1,0:T(8,128)(2,1)S(1)} %copy-done.21), kind=kOutput, calls=%fused_computation.102 | convolution fusion | flops 2151940096 | bytes 12582912 | tf_op jit(solution)/shard_map/dot_general | solution.py:170
  287.0 1.4 reshape.204
  288.7 1.0 reduce_sum.99
  289.7 1.0 copy.165
  290.7 1.5 convolution_convert_fusion.7
  292.2 3.8 fusion.180
  296.0 2.5 divide_convert_fusion.1
  299.2 0.9 fusion.79
  302.0 0.9 add_add_fusion.1
  302.9 26.6 %all-gather.7.cloned.1.call-done = bf16[1,1,256,8192]{3,2,1,0:T(8,128)(2,1)} async-done(((bf16[1,1,256,2048]{3,2,1,0:T(8,128)(2,1)}), bf16[1,1,256,8192]{3,2,1,0:T(8,128)(2,1)}) %all-gather.7.cloned.1.call-update) | async-done | bytes 4194320 | tf_op jit(solution)/shard_map/all_gather | solution.py:161
  329.5 3.3 fusion.5
  333.0 2.2 fusion.7
  335.7 2.4 fusion.43
  338.7 2.3 fusion.59
  341.0 1.4 reshape.205
  342.8 1.0 reduce_sum.107
  343.8 1.0 copy.177
  344.8 1.4 convolution_convert_fusion.6
  346.2 3.5 fusion.185
  349.8 2.4 fusion.25
  352.2 1.1 fusion.85
  353.5 1.1 fusion.82
  355.2 3.6 convolution_convert_fusion.4
  358.9 1.3 convolution_convert_fusion.5
  361.6 2.2 pad_maximum_fusion.2
  363.8 1.2 copy-done.18
  365.0 2.0 convolution_convert_fusion.1
  368.7 1.0 copy-done.14
  371.6 4.2 collective-permute-done.5
  375.9 2.7 fusion.26
  378.6 1.5 collective-permute-start.6
  382.3 1.0 maximum_bitcast_fusion.1
  383.3 56.0 %reduce-scatter.2.cloned.1.call-done = bf16[256,2048]{1,0:T(8,128)(2,1)} async-done(((bf16[256,8192]{1,0:T(8,128)(2,1)}), bf16[256,2048]{1,0:T(8,128)(2,1)}) %reduce-scatter.2.cloned.1.call-update) | async-done | bytes 1048592 | tf_op jit(solution)/shard_map/reduce_scatter | solution.py:208
  439.3 1.4 collective-permute-start.4
  440.8 3.5 fusion.10
  444.4 1.3 copy.190
  445.7 1.3 copy.191
  447.0 17.5 %collective-permute-done.4 = bf16[256,2048]{1,0:T(8,128)(2,1)} collective-permute-done((bf16[256,2048]{1,0:T(8,128)(2,1)}, bf16[256,2048]{1,0:T(8,128)(2,1)}, u32[]{:S(2)}, u32[]{:S(2)}) %collective-permute-start.4) | collective-permute-done | bytes 1048608 | tf_op jit(solution)/shard_map/ppermute | solution.py:13
  464.5 1.1 select_bitcast_fusion
  (178 shorter events, 17.1 us)
Async XLA Ops:
  7.2 177.2 %all-gather.9.cloned.1.call-start = ((), (), s32[]{:S(2)}) async-start(), calls=%async_computation.4 | async-start | bytes 5242880 | tf_op jit(solution)/shard_map/all_gather | solution.py:139
  7.2 11.0 %copy-start.25 = (bf16[1,1,256,2048]{3,2,1,0:T(8,128)(2,1)S(1)}, bf16[1,1,256,2048]{3,2,1,0:T(8,128)(2,1)}, u32[]{:S(2)}) copy-start(bf16[1,1,256,2048]{3,2,1,0:T(8,128)(2,1)} %param.14) | copy-start | bytes 3145732
  7.2 12.5 %copy-start.46 = (s32[1,2]{1,0:T(1,128)S(1)}, s32[1,2]{1,0:T(1,128)}, u32[]{:S(2)}) copy-start(s32[1,2]{1,0:T(1,128)} %param.17) | copy-start | bytes 28
  15.2 138.8 %collective-permute-start.1 = (bf16[1,2048,1536]{2,1,0:T(8,128)(2,1)}, bf16[1,2048,1536]{2,1,0:T(8,128)(2,1)}, u32[]{:S(2)}, u32[]{:S(2)}) collective-permute-start(bf16[1,2048,1536]{2,1,0:T(8,128)(2,1)} %maximum_bitcast_fusion), channel_id=1, source_target_pairs={{0,2},{1,3},{2,0},{3,1},{4,6},{5,7},{6,4},{7,5},{8,10},{9,11},{10,... | collective-permute-start | bytes 18874376 | tf_op jit(solution)/shard_map/ppermute | solution.py:19
  18.2 24.6 %collective-permute-start = (bf16[1,1,256,2048]{3,2,1,0:T(8,128)(2,1)S(1)}, bf16[1,1,256,2048]{3,2,1,0:T(8,128)(2,1)S(1)}, u32[]{:S(2)}, u32[]{:S(2)}) collective-permute-start(bf16[1,1,256,2048]{3,2,1,0:T(8,128)(2,1)S(1)} %copy-done.25), channel_id=1, source_target_pairs={{0,16},{16,0},{1,17},{17,1},{2,18},{18,2},{3,19},{19,3},{4,20},{20... | collective-permute-start | bytes 3145736 | tf_op jit(solution)/shard_map/ppermute | solution.py:13
  43.9 204.7 %all-gather.5.cloned.1.call-start = ((), (), s32[]{:S(2)}) async-start(), calls=%async_computation.1 | async-start | bytes 5242880 | tf_op jit(solution)/shard_map/all_gather | solution.py:161
  44.0 120.6 %collective-permute-start.3 = (bf16[1,1,512,2048]{3,2,1,0:T(8,128)(2,1)}, bf16[1,1,512,2048]{3,2,1,0:T(8,128)(2,1)S(1)}, u32[]{:S(2)}, u32[]{:S(2)}) collective-permute-start(bf16[1,1,512,2048]{3,2,1,0:T(8,128)(2,1)} %param.13), channel_id=1, source_target_pairs={{0,16},{16,0},{1,17},{17,1},{2,18},{18,2},{3,19},{19,3},{4,20},{20... | collective-permute-start | bytes 6291464 | tf_op jit(solution)/shard_map/ppermute | solution.py:13
  164.6 2.9 copy-start.12
  164.6 90.9 %collective-permute-start.2 = (bf16[2,2048,1536]{2,1,0:T(8,128)(2,1)}, bf16[2,2048,1536]{2,1,0:T(8,128)(2,1)}, u32[]{:S(2)}, u32[]{:S(2)}) collective-permute-start(bf16[2,2048,1536]{2,1,0:T(8,128)(2,1)} %pad_maximum_fusion), channel_id=1, source_target_pairs={{0,1},{1,0},{2,3},{3,2},{4,5},{5,4},{6,7},{7,6},{8,9},{9,8},{10,11... | collective-permute-start | bytes 37748744 | tf_op jit(solution)/shard_map/ppermute | solution.py:19
  166.1 4.3 copy-start.47
  166.1 163.4 %all-gather.7.cloned.1.call-start = ((), (), s32[]{:S(2)}) async-start(), calls=%async_computation.2 | async-start | bytes 5242880 | tf_op jit(solution)/shard_map/all_gather | solution.py:161
  172.8 117.9 %copy-start.42 = (pred[256]{0:T(512)(128)(4,1)}, pred[256]{0:T(512)(128)(4,1)S(1)}, u32[]{:S(2)}) copy-start(pred[256]{0:T(512)(128)(4,1)S(1)} %get-tuple-element.77) | copy-start | bytes 772
  172.8 266.5 %reduce-scatter.2.cloned.1.call-start = ((), (), s32[]{:S(2)}) async-start(), calls=%async_computation.3 | async-start | bytes 5242880 | tf_op jit(solution)/shard_map/reduce_scatter | solution.py:208
  184.4 67.5 %copy-start.33 = (f32[1,8192]{1,0:T(1,128)S(1)}, f32[1,8192]{1,0:T(1,128)}, u32[]{:S(2)}) copy-start(f32[1,8192]{1,0:T(1,128)} %param.18) | copy-start | bytes 98308
  188.4 73.4 %copy-start.13 = (bf16[256,2048]{1,0:T(8,128)(2,1)}, bf16[256,2048]{1,0:T(8,128)(2,1)S(1)}, u32[]{:S(2)}) copy-start(bf16[256,2048]{1,0:T(8,128)(2,1)S(1)} %get-tuple-element.50) | copy-start | bytes 3145732
  248.6 3.4 copy-start.2
  255.5 5.0 %copy-start.17 = (bf16[256,2048]{1,0:T(8,128)(2,1)S(1)}, bf16[256,2048]{1,0:T(8,128)(2,1)}, u32[]{:S(2)}) copy-start(bf16[256,2048]{1,0:T(8,128)(2,1)} %get-tuple-element.51) | copy-start | bytes 3145732
  255.5 5.0 %copy-start.19 = (bf16[256,2048]{1,0:T(8,128)(2,1)S(1)}, bf16[256,2048]{1,0:T(8,128)(2,1)}, u32[]{:S(2)}) copy-start(bf16[256,2048]{1,0:T(8,128)(2,1)} %get-tuple-element.53) | copy-start | bytes 3145732
  258.5 2.0 copy-start
  260.5 2.2 copy-start.3
  260.5 2.5 copy-start.15
  263.0 3.7 copy-start.34
  267.5 7.8 %copy-start.23 = (bf16[256,2048]{1,0:T(8,128)(2,1)S(1)}, bf16[256,2048]{1,0:T(8,128)(2,1)}, u32[]{:S(2)}) copy-start(bf16[256,2048]{1,0:T(8,128)(2,1)} %get-tuple-element.47) | copy-start | bytes 3145732
  267.5 7.8 %copy-start.24 = (bf16[256,2048]{1,0:T(8,128)(2,1)S(1)}, bf16[256,2048]{1,0:T(8,128)(2,1)}, u32[]{:S(2)}) copy-start(bf16[256,2048]{1,0:T(8,128)(2,1)} %get-tuple-element.48) | copy-start | bytes 3145732
  275.3 5.9 %copy-start.21 = (bf16[256,2048]{1,0:T(8,128)(2,1)S(1)}, bf16[256,2048]{1,0:T(8,128)(2,1)}, u32[]{:S(2)}) copy-start(bf16[256,2048]{1,0:T(8,128)(2,1)} %get-tuple-element.46) | copy-start | bytes 3145732
  275.3 5.9 %copy-start.22 = (bf16[256,2048]{1,0:T(8,128)(2,1)S(1)}, bf16[256,2048]{1,0:T(8,128)(2,1)}, u32[]{:S(2)}) copy-start(bf16[256,2048]{1,0:T(8,128)(2,1)} %get-tuple-element.49) | copy-start | bytes 3145732
  290.7 5.3 %copy-start.39 = (f32[256,2,4]{0,2,1:T(4,128)}, f32[256,2,4]{0,2,1:T(4,128)S(1)}, u32[]{:S(2)}) copy-start(f32[256,2,4]{0,2,1:T(4,128)S(1)} %rsqrt.54) | copy-start | bytes 24580
  295.9 2.6 copy-start.9
  295.9 2.9 copy-start.11
  295.9 3.2 copy-start.28
  296.0 3.2 copy-start.48
  296.0 3.2 copy-start.50
  296.0 3.1 copy-start.40
  299.1 2.1 copy-start.35
  329.5 3.4 copy-start.1
  329.5 6.1 %slice-start.2 = ((s8[8388608]{0:T(1024)(128)(4,1)}), s8[4194304]{0:T(1024)(128)(4,1)S(1)}, s32[]{:S(2)}) async-start(s8[8388608]{0:T(1024)(128)(4,1)} %bitcast.249), calls=%async_computation.7 | async-start | bytes 8388608
  333.0 2.7 slice-start.3
  335.2 3.0 slice-start
  335.7 3.0 slice-start.1
  341.0 3.7 copy-start.45
  344.7 5.0 %copy-start.37 = (f32[256,2,4]{0,2,1:T(4,128)}, f32[256,2,4]{0,2,1:T(4,128)S(1)}, u32[]{:S(2)}) copy-start(f32[256,2,4]{0,2,1:T(4,128)S(1)} %rsqrt.57) | copy-start | bytes 24580
  349.7 3.6 copy-start.8
  349.7 3.6 copy-start.10
  349.7 3.7 copy-start.27
  349.7 3.7 copy-start.49
  349.7 3.7 copy-start.51
  349.8 3.6 copy-start.38
  353.4 1.4 copy-start.41
  353.4 1.4 copy-start.30
  353.4 1.7 copy-start.29
  353.5 1.7 copy-start.31
  355.2 3.7 copy-start.4
  363.8 1.2 copy-start.18
  365.0 2.0 copy-start.20
  368.2 1.5 copy-start.14
  368.2 1.9 copy-start.16
  368.6 7.2 %collective-permute-start.5 = (bf16[2,2048,512]{1,2,0:T(8,128)(2,1)S(1)}, bf16[2,2048,512]{1,2,0:T(8,128)(2,1)S(1)}, u32[]{:S(2)}, u32[]{:S(2)}) collective-permute-start(bf16[2,2048,512]{1,2,0:T(8,128)(2,1)S(1)} %pad_maximum_fusion.3), channel_id=1, source_target_pairs={{0,1},{1,0},{2,3},{3,2},{4,5},{5,4},{6,7},{7,6},{8,9},{9,8},{10,11... | collective-permute-start | bytes 12582920 | tf_op jit(solution)/shard_map/ppermute | solution.py:19
  370.9 7.7 %copy-start.5 = (bf16[4096,256]{0,1:T(8,128)(2,1)}, bf16[4096,256]{0,1:T(8,128)(2,1)S(1)}, u32[]{:S(2)}) copy-start(bf16[4096,256]{0,1:T(8,128)(2,1)S(1)} %convolution_convert_fusion.3) | copy-start | bytes 6291460
  371.6 6.9 %copy-start.6 = (bf16[4096,256]{0,1:T(8,128)(2,1)}, bf16[4096,256]{0,1:T(8,128)(2,1)S(1)}, u32[]{:S(2)}) copy-start(bf16[4096,256]{0,1:T(8,128)(2,1)S(1)} %convolution_convert_fusion.2) | copy-start | bytes 6291460
  375.9 2.7 copy-start.7
  378.6 3.5 copy-start.44
  378.6 62.2 %collective-permute-start.6 = (bf16[1,2048,512]{1,2,0:T(8,128)(2,1)}, bf16[1,2048,512]{1,2,0:T(8,128)(2,1)}, u32[]{:S(2)}, u32[]{:S(2)}) collective-permute-start(bf16[1,2048,512]{1,2,0:T(8,128)(2,1)} %fusion.26), channel_id=1, source_target_pairs={{0,2},{1,3},{2,0},{3,1},{4,6},{5,7},{6,4},{7,5},{8,10},{9,11},{10,... | collective-permute-start | bytes 6291464 | tf_op jit(solution)/shard_map/ppermute | solution.py:19
  439.3 25.2 %collective-permute-start.4 = (bf16[256,2048]{1,0:T(8,128)(2,1)}, bf16[256,2048]{1,0:T(8,128)(2,1)}, u32[]{:S(2)}, u32[]{:S(2)}) collective-permute-start(bf16[256,2048]{1,0:T(8,128)(2,1)} %reduce-scatter.2.cloned.1.call-done), channel_id=1, source_target_pairs={{0,16},{16,0},{1,17},{17,1},{2,18},{18,2},{3,19},{19,3},{4,20},{20... | collective-permute-start | bytes 3145736 | tf_op jit(solution)/shard_map/ppermute | solution.py:13
  444.3 20.3 %copy-start.26 = (bf16[256,2048]{1,0:T(8,128)(2,1)S(1)}, bf16[256,2048]{1,0:T(8,128)(2,1)}, u32[]{:S(2)}) copy-start(bf16[256,2048]{1,0:T(8,128)(2,1)} %reduce-scatter.2.cloned.1.call-done) | copy-start | bytes 3145732
  (3 other events, 2.9 us)
Sparse Core Ops, SparseCore 0:
  44.1 81.0 all-gather.8
  166.2 82.3 all-gather.4
  250.2 79.2 all-gather.6
  364.0 75.2 reduce-scatter.1

commit v10 on v3

--- a/solution.py
+++ b/solution.py
@@ -183,8 +183,13 @@
     summed = lax.psum_scatter(partial_sum, "mp", scatter_dimension=1, tiled=True)
 
     routed = summed
+    split = slot_rows // 2 if slot_rows % 16 == 0 else slot_rows
     for steps in range(1, sections):
-        moved = shifted(summed, "section", steps)
+        moved = [
+            shifted(summed[lower : lower + split], "section", steps)
+            for lower in range(0, slot_rows, split)
+        ]
+        moved = moved[0] if len(moved) == 1 else jnp.concatenate(moved, axis=0)
         source = (section - steps) % sections
         routed = jnp.where(image_of[0, source] == section, moved, routed)
     vision_grad = routed.reshape(1, 1, slot_rows, part_width)

time: 442 us -> 446 us (level)
  local copies, waits for them, and re-layouts: 26.4 us -> 32.1 us
    reduce_scatter x1, waiting for transfers between devices: 52.1 us -> 7.89 us  [per_device(): lax.psum_scatter(partial_sum, 'mp', scatter_dimension=1, tiled=True)]
    ppermute x8, waiting for transfers between devices: 84.5 us -> 126 us  [swapped(): return lax.ppermute(value, axis, pairs)]
    unnamed x110 -> x112, local copies, waits for them, and re-layouts: 10.3 us -> 12.1 us
    ppermute x3 -> x4, waiting for transfers between devices: 83.8 us -> 82.2 us  [shifted(): return lax.ppermute(value, axis, pairs)]
  transfers between devices with their start and end apart: 15 -> 16, of which waited for: 9 -> 11; matrix products, arithmetic and copies ran while one was open for 20% -> 20% of each run, Pallas kernels for 0% -> 0%
where the time goes in v10:
time: 446 us; the launch traced here: 443 us
  waiting for transfers between devices  260 us (58%)
  matrix products  71 us (16%)
  other arithmetic  46.2 us (10%)
  local copies, waits for them, and re-layouts  32.1 us (7%)
  between operations  20.2 us (5%)
  starting transfers between devices  13.6 us (3%)
    ppermute x8, waiting for transfers between devices, swapped(): return lax.ppermute(value, axis, pairs)  126 us
    ppermute x4, waiting for transfers between devices, shifted(): return lax.ppermute(value, axis, pairs)  82.2 us
    all_gather x2, waiting for transfers between devices, per_device(): lax.all_gather(arrived[:, :, chunk * rows:(chunk + 1) * rows], 'mp', axis...  43.8 us
    dot_general x8, matrix products, per_device(): jnp.dot(columns_of(normed, (dp_index ^ code) * block_rows, block_rows), b...  23.5 us
    unnamed x112, local copies, waits for them, and re-layouts  12.1 us
    another operation x3, other arithmetic, gather_blocks(): arrived = swapped(jnp.stack([held[c] for c in codes]), axis, mask)  10.6 us
  transfers between devices with their start and end apart: 16, of which 11 were waited for; matrix products, arithmetic and copies ran while one was open for 20% of the time, Pallas kernels for 0%

profile of v10, /device:TPU:0, one launch (start us, length us, event | category | flops | bytes accessed | tf_op | source)
XLA Modules:
  0.0 442.7 jit_solution(17340284541530590545)
XLA Ops:
  7.2 3.0 collective-permute-start
  12.3 21.3 %collective-permute-done = bf16[1,1,256,2048]{3,2,1,0:T(8,128)(2,1)S(1)} collective-permute-done((bf16[1,1,256,2048]{3,2,1,0:T(8,128)(2,1)}, bf16[1,1,256,2048]{3,2,1,0:T(8,128)(2,1)S(1)}, u32[]{:S(2)}, u32[]{:S(2)}) %collective-permute-start) | collective-permute-done | bytes 1048608 | tf_op jit(solution)/shard_map/ppermute | solution.py:13
  34.7 1.8 collective-permute-start.5
  36.5 2.7 collective-permute-start.6
  39.3 43.8 %collective-permute-done.5 = bf16[1,1,512,2048]{3,2,1,0:T(8,128)(2,1)S(1)} collective-permute-done((bf16[1,1,512,2048]{3,2,1,0:T(8,128)(2,1)}, bf16[1,1,512,2048]{3,2,1,0:T(8,128)(2,1)S(1)}, u32[]{:S(2)}, u32[]{:S(2)}) %collective-permute-start.5) | collective-permute-done | bytes 2097184 | tf_op jit(solution)/shard_map/ppermute | solution.py:13
  83.1 1.6 fusion.243
  84.7 1.5 collective-permute-start.3
  86.8 44.3 %collective-permute-done.6 = bf16[1,2048,1024]{2,1,0:T(8,128)(2,1)} collective-permute-done((bf16[1,2048,1024]{2,1,0:T(8,128)(2,1)}, bf16[1,2048,1024]{2,1,0:T(8,128)(2,1)}, u32[]{:S(2)}, u32[]{:S(2)}) %collective-permute-start.6) | collective-permute-done | bytes 4194336 | tf_op jit(solution)/shard_map/ppermute | solution.py:19
  131.1 7.5 %pad_maximum_fusion = bf16[2,2048,1024]{2,1,0:T(8,128)(2,1)} fusion(bf16[1,2048,1024]{2,1,0:T(8,128)(2,1)} %collective-permute-done.6, bf16[1,2048,1024]{2,1,0:T(8,128)(2,1)} %param.19), kind=kLoop, calls=%fused_computation.12 | loop fusion | flops 4194304 | bytes 16777216 | tf_op jit(solution)/shard_map/stack | solution.py:36
  138.6 14.9 %collective-permute-done.3 = bf16[1,2048,256]{2,1,0:T(8,128)(2,1)S(1)} collective-permute-done((bf16[1,2048,256]{2,1,0:T(8,128)(2,1)S(1)}, bf16[1,2048,256]{2,1,0:T(8,128)(2,1)S(1)}, u32[]{:S(2)}, u32[]{:S(2)}) %collective-permute-start.3) | collective-permute-done | bytes 1048608 | tf_op jit(solution)/shard_map/ppermute | solution.py:19
  153.5 1.5 pad_maximum_fusion.3
  155.0 19.1 %collective-permute-done.1 = bf16[1,2048,256]{2,1,0:T(8,128)(2,1)S(1)} collective-permute-done((bf16[1,2048,256]{2,1,0:T(8,128)(2,1)}, bf16[1,2048,256]{2,1,0:T(8,128)(2,1)S(1)}, u32[]{:S(2)}, u32[]{:S(2)}) %collective-permute-start.1) | collective-permute-done | bytes 1048608 | tf_op jit(solution)/shard_map/ppermute | solution.py:19
  174.1 1.6 pad_maximum_fusion.2
  175.6 1.6 slice_convert_fusion
  179.9 2.5 copy.158
  182.5 2.6 copy.161
  187.8 1.9 fusion.95
  189.8 2.1 fusion.102
  192.4 2.6 multiply_reduce_fusion.2
  196.9 2.2 fusion.112
  199.1 2.2 fusion.104
  201.8 1.8 fusion.72
  203.7 1.5 convolution_convert_fusion.9
  205.2 1.5 convolution_convert_fusion.8
  206.6 3.7 fusion.2
  214.2 3.5 fusion.11
  217.7 3.5 fusion.20
  221.2 3.6 fusion.63
  224.8 1.4 reshape.219
  227.4 3.6 fusion.246
  231.1 2.5 divide_convert_fusion.1
  237.5 43.8 %all-gather.7.cloned.1.call-done = bf16[1,1,256,8192]{3,2,1,0:T(8,128)(2,1)} async-done(((bf16[1,1,256,2048]{3,2,1,0:T(8,128)(2,1)}), bf16[1,1,256,8192]{3,2,1,0:T(8,128)(2,1)}) %all-gather.7.cloned.1.call-update) | async-done | bytes 4194320 | tf_op jit(solution)/shard_map/all_gather | solution.py:137
  281.3 3.3 fusion.5
  288.2 3.5 fusion.19
  291.7 3.5 fusion.59
  295.2 3.5 fusion.62
  299.7 1.4 reshape.220
  301.2 1.4 copy.165
  303.1 3.7 fusion.251
  306.8 2.4 fusion.44
  315.2 2.5 broadcast_in_dim.96
  317.7 1.6 fusion.22
  319.8 1.7 fusion.152
  321.5 1.7 fusion.153
  323.2 1.6 fusion.24
  324.8 2.8 fusion.26
  327.5 2.8 fusion.28
  330.4 1.8 convolution_convert_fusion.4
  332.2 1.7 convolution_convert_fusion.5
  336.6 6.2 %collective-permute-done.10 = bf16[2,2048,512]{1,2,0:T(8,128)(2,1)S(1)} collective-permute-done((bf16[2,2048,512]{1,2,0:T(8,128)(2,1)S(1)}, bf16[2,2048,512]{1,2,0:T(8,128)(2,1)S(1)}, u32[]{:S(2)}, u32[]{:S(2)}) %collective-permute-start.10) | collective-permute-done | bytes 4194336 | tf_op jit(solution)/shard_map/ppermute | solution.py:19
  342.8 2.0 copy-done.19
  344.8 2.2 add_convert_fusion
  347.0 1.5 collective-permute-start.11
  353.8 41.2 %collective-permute-done.11 = bf16[1,2048,512]{1,2,0:T(8,128)(2,1)} collective-permute-done((bf16[1,2048,512]{1,2,0:T(8,128)(2,1)}, bf16[1,2048,512]{1,2,0:T(8,128)(2,1)}, u32[]{:S(2)}, u32[]{:S(2)}) %collective-permute-start.11) | collective-permute-done | bytes 2097184 | tf_op jit(solution)/shard_map/ppermute | solution.py:19
  395.0 2.9 fusion.8
  397.9 7.9 %reduce-scatter.2.cloned.1.call-done = bf16[256,2048]{1,0:T(8,128)(2,1)} async-done(((bf16[256,8192]{1,0:T(8,128)(2,1)}), bf16[256,2048]{1,0:T(8,128)(2,1)}) %reduce-scatter.2.cloned.1.call-update) | async-done | bytes 1048592 | tf_op jit(solution)/shard_map/reduce_scatter | solution.py:183
  405.8 2.3 fusion.244
  408.1 1.4 collective-permute-start.8
  410.2 1.6 slice_bitcast_fusion.15
  411.7 2.3 copy.140
  414.0 2.3 copy.141
  416.2 7.0 %collective-permute-done.8 = bf16[128,2048]{1,0:T(8,128)(2,1)} collective-permute-done((bf16[128,2048]{1,0:T(8,128)(2,1)}, bf16[128,2048]{1,0:T(8,128)(2,1)}, u32[]{:S(2)}, u32[]{:S(2)}) %collective-permute-start.8) | collective-permute-done | bytes 524320 | tf_op jit(solution)/shard_map/ppermute | solution.py:13
  423.3 10.1 %collective-permute-done.9 = bf16[128,2048]{1,0:T(8,128)(2,1)} collective-permute-done((bf16[128,2048]{1,0:T(8,128)(2,1)}, bf16[128,2048]{1,0:T(8,128)(2,1)}, u32[]{:S(2)}, u32[]{:S(2)}) %collective-permute-start.9) | collective-permute-done | bytes 524320 | tf_op jit(solution)/shard_map/ppermute | solution.py:13
  433.4 2.6 fusion.89
  (188 shorter events, 36.0 us)
Async XLA Ops:
  7.2 180.6 %all-gather.9.cloned.1.call-start = ((), (), s32[]{:S(2)}) async-start(), calls=%async_computation.4 | async-start | bytes 5242880 | tf_op jit(solution)/shard_map/all_gather | solution.py:113
  7.2 26.4 %collective-permute-start = (bf16[1,1,256,2048]{3,2,1,0:T(8,128)(2,1)}, bf16[1,1,256,2048]{3,2,1,0:T(8,128)(2,1)S(1)}, u32[]{:S(2)}, u32[]{:S(2)}) collective-permute-start(bf16[1,1,256,2048]{3,2,1,0:T(8,128)(2,1)} %param.14), channel_id=1, source_target_pairs={{0,16},{16,0},{1,17},{17,1},{2,18},{18,2},{3,19},{19,3},{4,20},{20... | collective-permute-start | bytes 3145736 | tf_op jit(solution)/shard_map/ppermute | solution.py:13
  12.3 72.4 %copy-start.6 = (bf16[1,2048,256]{2,1,0:T(8,128)(2,1)S(1)}, bf16[1,2048,256]{2,1,0:T(8,128)(2,1)}, u32[]{:S(2)}) copy-start(bf16[1,2048,256]{2,1,0:T(8,128)(2,1)} %param.20) | copy-start | bytes 3145732
  34.7 171.9 %all-gather.5.cloned.1.call-start = ((), (), s32[]{:S(2)}) async-start(), calls=%async_computation.1 | async-start | bytes 5242880 | tf_op jit(solution)/shard_map/all_gather | solution.py:137
  34.7 48.3 %collective-permute-start.5 = (bf16[1,1,512,2048]{3,2,1,0:T(8,128)(2,1)}, bf16[1,1,512,2048]{3,2,1,0:T(8,128)(2,1)S(1)}, u32[]{:S(2)}, u32[]{:S(2)}) collective-permute-start(bf16[1,1,512,2048]{3,2,1,0:T(8,128)(2,1)} %param.13), channel_id=1, source_target_pairs={{0,16},{16,0},{1,17},{17,1},{2,18},{18,2},{3,19},{19,3},{4,20},{20... | collective-permute-start | bytes 6291464 | tf_op jit(solution)/shard_map/ppermute | solution.py:13
  36.5 94.5 %collective-permute-start.6 = (bf16[1,2048,1024]{2,1,0:T(8,128)(2,1)}, bf16[1,2048,1024]{2,1,0:T(8,128)(2,1)}, u32[]{:S(2)}, u32[]{:S(2)}) collective-permute-start(bf16[1,2048,1024]{2,1,0:T(8,128)(2,1)} %param.19), channel_id=1, source_target_pairs={{0,2},{1,3},{2,0},{3,1},{4,6},{5,7},{6,4},{7,5},{8,10},{9,11},{10,... | collective-permute-start | bytes 12582920 | tf_op jit(solution)/shard_map/ppermute | solution.py:19
  84.6 196.6 %all-gather.7.cloned.1.call-start = ((), (), s32[]{:S(2)}) async-start(), calls=%async_computation.2 | async-start | bytes 5242880 | tf_op jit(solution)/shard_map/all_gather | solution.py:137
  84.7 68.8 %collective-permute-start.3 = (bf16[1,2048,256]{2,1,0:T(8,128)(2,1)S(1)}, bf16[1,2048,256]{2,1,0:T(8,128)(2,1)S(1)}, u32[]{:S(2)}, u32[]{:S(2)}) collective-permute-start(bf16[1,2048,256]{2,1,0:T(8,128)(2,1)S(1)} %copy-done.6), channel_id=1, source_target_pairs={{0,2},{1,3},{2,0},{3,1},{4,6},{5,7},{6,4},{7,5},{8,10},{9,11},{10,... | collective-permute-start | bytes 3145736 | tf_op jit(solution)/shard_map/ppermute | solution.py:19
  86.2 87.9 %collective-permute-start.1 = (bf16[1,2048,256]{2,1,0:T(8,128)(2,1)}, bf16[1,2048,256]{2,1,0:T(8,128)(2,1)S(1)}, u32[]{:S(2)}, u32[]{:S(2)}) collective-permute-start(bf16[1,2048,256]{2,1,0:T(8,128)(2,1)} %param.21), channel_id=1, source_target_pairs={{0,2},{1,3},{2,0},{3,1},{4,6},{5,7},{6,4},{7,5},{8,10},{9,11},{10,... | collective-permute-start | bytes 3145736 | tf_op jit(solution)/shard_map/ppermute | solution.py:19
  138.6 35.5 %copy-start.8 = (bf16[1,2048,256]{2,1,0:T(8,128)(2,1)S(1)}, bf16[1,2048,256]{2,1,0:T(8,128)(2,1)}, u32[]{:S(2)}) copy-start(bf16[1,2048,256]{2,1,0:T(8,128)(2,1)} %param.21) | copy-start | bytes 3145732
  138.6 37.1 %copy-start.30 = (bf16[1,1,512,1024]{3,2,1,0:T(8,128)(2,1)S(1)}, bf16[1,1,512,1024]{3,2,1,0:T(8,128)(2,1)}, u32[]{:S(2)}) copy-start(bf16[1,1,512,1024]{3,2,1,0:T(8,128)(2,1)} %param.25) | copy-start | bytes 3145732
  138.6 79.1 %collective-permute-start.7 = (bf16[2,2048,1024]{2,1,0:T(8,128)(2,1)}, bf16[2,2048,1024]{2,1,0:T(8,128)(2,1)}, u32[]{:S(2)}, u32[]{:S(2)}) collective-permute-start(bf16[2,2048,1024]{2,1,0:T(8,128)(2,1)} %pad_maximum_fusion), channel_id=1, source_target_pairs={{0,1},{1,0},{2,3},{3,2},{4,5},{5,4},{6,7},{7,6},{8,9},{9,8},{10,11... | collective-permute-start | bytes 25165832 | tf_op jit(solution)/shard_map/ppermute | solution.py:19
  155.0 34.8 %collective-permute-start.4 = (bf16[2,2048,256]{2,1,0:T(8,128)(2,1)}, bf16[2,2048,256]{2,1,0:T(8,128)(2,1)}, u32[]{:S(2)}, u32[]{:S(2)}) collective-permute-start(bf16[2,2048,256]{2,1,0:T(8,128)(2,1)} %pad_maximum_fusion.3), channel_id=1, source_target_pairs={{0,1},{1,0},{2,3},{3,2},{4,5},{5,4},{6,7},{7,6},{8,9},{9,8},{10,11... | collective-permute-start | bytes 6291464 | tf_op jit(solution)/shard_map/ppermute | solution.py:19
  175.6 10.1 %copy-start.49 = (s32[1,2]{1,0:T(1,128)S(1)}, s32[1,2]{1,0:T(1,128)}, u32[]{:S(2)}) copy-start(s32[1,2]{1,0:T(1,128)} %param.15) | copy-start | bytes 28
  175.6 23.5 %collective-permute-start.2 = (bf16[2,2048,256]{2,1,0:T(8,128)(2,1)}, bf16[2,2048,256]{2,1,0:T(8,128)(2,1)}, u32[]{:S(2)}, u32[]{:S(2)}) collective-permute-start(bf16[2,2048,256]{2,1,0:T(8,128)(2,1)} %pad_maximum_fusion.2), channel_id=1, source_target_pairs={{0,1},{1,0},{2,3},{3,2},{4,5},{5,4},{6,7},{7,6},{8,9},{9,8},{10,11... | collective-permute-start | bytes 6291464 | tf_op jit(solution)/shard_map/ppermute | solution.py:19
  187.5 16.1 %copy-start.46 = (pred[256]{0:T(512)(128)(4,1)}, pred[256]{0:T(512)(128)(4,1)S(1)}, u32[]{:S(2)}) copy-start(pred[256]{0:T(512)(128)(4,1)S(1)} %get-tuple-element.53) | copy-start | bytes 772
  187.5 17.6 %copy-start.44 = (pred[256]{0:T(512)(128)(4,1)}, pred[256]{0:T(512)(128)(4,1)S(1)}, u32[]{:S(2)}) copy-start(pred[256]{0:T(512)(128)(4,1)S(1)} %get-tuple-element.52) | copy-start | bytes 772
  187.6 218.3 %reduce-scatter.2.cloned.1.call-start = ((), (), s32[]{:S(2)}) async-start(), calls=%async_computation.3 | async-start | bytes 5242880 | tf_op jit(solution)/shard_map/reduce_scatter | solution.py:183
  187.8 4.0 copy-start
  189.7 6.3 %copy-start.36 = (f32[1,128]{1,0:T(1,128)S(1)}, f32[1,128]{1,0:T(1,128)}, u32[]{:S(2)}) copy-start(f32[1,128]{1,0:T(1,128)} %param.23) | copy-start | bytes 1540
  192.4 8.9 %copy-start.9 = (bf16[1,2048,256]{2,1,0:T(8,128)(2,1)S(1)}, bf16[1,2048,256]{2,1,0:T(8,128)(2,1)}, u32[]{:S(2)}) copy-start(bf16[1,2048,256]{2,1,0:T(8,128)(2,1)} %param.21) | copy-start | bytes 3145732
  196.1 5.2 %copy-start.1 = (bf16[1,1,256,8192]{3,2,1,0:T(8,128)(2,1)S(1)}, bf16[1,1,256,8192]{3,2,1,0:T(8,128)(2,1)}, u32[]{:S(2)}) copy-start(bf16[1,1,256,8192]{3,2,1,0:T(8,128)(2,1)} %all-gather.9.cloned.1.call-done) | copy-start | bytes 12582916
  199.1 4.6 %copy-start.13 = (f32[1,1,256,1024]{2,3,1,0:T(8,128)S(1)}, f32[1,1,256,1024]{2,3,1,0:T(8,128)}, u32[]{:S(2)}) copy-start(f32[1,1,256,1024]{2,3,1,0:T(8,128)} %copy.158) | copy-start | bytes 3145732
  201.3 3.9 copy-start.11
  203.7 6.6 %copy-start.34 = (f32[1,8192]{1,0:T(1,128)S(1)}, f32[1,8192]{1,0:T(1,128)}, u32[]{:S(2)}) copy-start(f32[1,8192]{1,0:T(1,128)} %param.18) | copy-start | bytes 98308
  206.6 4.2 copy-start.4
  210.8 2.2 copy-start.24
  227.3 3.7 copy-start.39
  227.4 6.2 %copy-start.14 = (f32[1,1,256,1024]{2,3,1,0:T(8,128)S(1)}, f32[1,1,256,1024]{2,3,1,0:T(8,128)}, u32[]{:S(2)}) copy-start(f32[1,1,256,1024]{2,3,1,0:T(8,128)} %copy.158) | copy-start | bytes 3145732
  231.0 2.6 copy-start.47
  231.0 3.8 copy-start.23
  231.0 3.8 copy-start.28
  231.0 3.8 copy-start.31
  231.0 3.8 copy-start.50
  231.0 3.8 copy-start.52
  231.0 3.8 copy-start.40
  233.5 2.2 copy-start.15
  235.8 48.8 %copy-start.35 = (f32[1,8192]{1,0:T(1,128)S(1)}, f32[1,8192]{1,0:T(1,128)}, u32[]{:S(2)}) copy-start(f32[1,8192]{1,0:T(1,128)} %param.18) | copy-start | bytes 98308
  281.3 3.4 copy-start.5
  284.7 2.2 copy-start.25
  303.0 3.7 copy-start.41
  303.0 6.2 %copy-start.12 = (f32[1,1,256,1024]{2,3,1,0:T(8,128)S(1)}, f32[1,1,256,1024]{2,3,1,0:T(8,128)}, u32[]{:S(2)}) copy-start(f32[1,1,256,1024]{2,3,1,0:T(8,128)} %copy.161) | copy-start | bytes 3145732
  303.0 6.2 %copy-start.45 = (pred[256]{0:T(512)(128)(4,1)S(1)}, pred[256]{0:T(512)(128)(4,1)}, u32[]{:S(2)}) copy-start(pred[256]{0:T(512)(128)(4,1)} %copy-done.44) | copy-start | bytes 772
  306.7 3.7 copy-start.22
  306.7 3.7 copy-start.29
  306.7 3.7 copy-start.32
  306.7 3.7 copy-start.51
  306.7 3.7 copy-start.53
  306.8 3.7 copy-start.42
  309.2 2.4 copy-start.17
  310.5 3.2 copy-start.7
  313.7 4.0 copy-start.10
  330.4 3.5 copy-start.2
  335.6 7.2 %collective-permute-start.10 = (bf16[2,2048,512]{1,2,0:T(8,128)(2,1)S(1)}, bf16[2,2048,512]{1,2,0:T(8,128)(2,1)S(1)}, u32[]{:S(2)}, u32[]{:S(2)}) collective-permute-start(bf16[2,2048,512]{1,2,0:T(8,128)(2,1)S(1)} %pad_maximum_fusion.1), channel_id=1, source_target_pairs={{0,1},{1,0},{2,3},{3,2},{4,5},{5,4},{6,7},{7,6},{8,9},{9,8},{10,11... | collective-permute-start | bytes 12582920 | tf_op jit(solution)/shard_map/ppermute | solution.py:19
  336.1 13.1 %copy-start.16 = (bf16[2,4,256,256]{2,3,1,0:T(8,128)(2,1)S(1)}, bf16[2,4,256,256]{2,3,1,0:T(8,128)(2,1)}, u32[]{:S(2)}) copy-start(bf16[2,4,256,256]{2,3,1,0:T(8,128)(2,1)} %copy-done.15) | copy-start | bytes 3145732
  336.1 13.1 %copy-start.27 = (bf16[256,256]{0,1:T(8,128)(2,1)S(1)}, bf16[256,256]{0,1:T(8,128)(2,1)}, u32[]{:S(2)}) copy-start(bf16[256,256]{0,1:T(8,128)(2,1)} %copy-done.26) | copy-start | bytes 393220
  336.6 13.1 %copy-start.18 = (bf16[2,4,256,256]{2,3,1,0:T(8,128)(2,1)S(1)}, bf16[2,4,256,256]{2,3,1,0:T(8,128)(2,1)}, u32[]{:S(2)}) copy-start(bf16[2,4,256,256]{2,3,1,0:T(8,128)(2,1)} %copy-done.17) | copy-start | bytes 3145732
  347.0 3.3 copy-start.48
  347.0 48.0 %collective-permute-start.11 = (bf16[1,2048,512]{1,2,0:T(8,128)(2,1)}, bf16[1,2048,512]{1,2,0:T(8,128)(2,1)}, u32[]{:S(2)}, u32[]{:S(2)}) collective-permute-start(bf16[1,2048,512]{1,2,0:T(8,128)(2,1)} %add_convert_fusion), channel_id=1, source_target_pairs={{0,2},{1,3},{2,0},{3,1},{4,6},{5,7},{6,4},{7,5},{8,10},{9,11},{10,... | collective-permute-start | bytes 6291464 | tf_op jit(solution)/shard_map/ppermute | solution.py:19
  350.3 2.6 copy-start.3
  350.3 44.7 %copy-start.20 = (bf16[2,2048,512]{1,2,0:T(8,128)(2,1)S(1)}, bf16[2,2048,512]{1,2,0:T(8,128)(2,1)}, u32[]{:S(2)}) copy-start(bf16[2,2048,512]{1,2,0:T(8,128)(2,1)} %copy-done.19) | copy-start | bytes 12582916
  408.1 15.1 %collective-permute-start.8 = (bf16[128,2048]{1,0:T(8,128)(2,1)}, bf16[128,2048]{1,0:T(8,128)(2,1)}, u32[]{:S(2)}, u32[]{:S(2)}) collective-permute-start(bf16[128,2048]{1,0:T(8,128)(2,1)} %get-tuple-element.40), channel_id=1, source_target_pairs={{0,16},{16,0},{1,17},{17,1},{2,18},{18,2},{3,19},{19,3},{4,20},{20... | collective-permute-start | bytes 1572872 | tf_op jit(solution)/shard_map/ppermute | solution.py:13
  409.6 23.8 %copy-start.21 = (bf16[256,2048]{1,0:T(8,128)(2,1)S(1)}, bf16[256,2048]{1,0:T(8,128)(2,1)}, u32[]{:S(2)}) copy-start(bf16[256,2048]{1,0:T(8,128)(2,1)} %reduce-scatter.2.cloned.1.call-done) | copy-start | bytes 3145732
  409.6 23.8 %collective-permute-start.9 = (bf16[128,2048]{1,0:T(8,128)(2,1)}, bf16[128,2048]{1,0:T(8,128)(2,1)}, u32[]{:S(2)}, u32[]{:S(2)}) collective-permute-start(bf16[128,2048]{1,0:T(8,128)(2,1)} %get-tuple-element.41), channel_id=1, source_target_pairs={{0,16},{16,0},{1,17},{17,1},{2,18},{18,2},{3,19},{19,3},{4,20},{20... | collective-permute-start | bytes 1572872 | tf_op jit(solution)/shard_map/ppermute | solution.py:13
  (6 other events, 8.2 us)
Sparse Core Ops, SparseCore 0:
  34.8 83.4 all-gather.8
  120.5 79.2 all-gather.4
  201.9 79.2 all-gather.6
  330.5 75.2 reduce-scatter.1

commit v11 on v3

--- a/solution.py
+++ b/solution.py
@@ -171,15 +171,19 @@
     value_flat = value_back.reshape(slot_rows, width_k).astype(jnp.bfloat16)
 
     contract = (((1,), (1,)), ((), ()))
-    partial_sum = jnp.zeros((slot_rows, image.shape[1]), jnp.bfloat16)
-    for code in key_blocks:
+    dp_count = lax.axis_size("dp")
+    terms = []
+    for code in range(dp_count):
         term = lax.dot_general(key_flat, key_blocks[code], contract, preferred_element_type=jnp.float32)
         term = term + lax.dot_general(
             value_flat, value_blocks[code], contract, preferred_element_type=jnp.float32
         )
-        partial_sum = lax.dynamic_update_slice_in_dim(
-            partial_sum, term.astype(jnp.bfloat16), (dp_index ^ code) * block_rows, axis=1
-        )
+        terms.append(term.astype(jnp.bfloat16))
+    in_code_order = jnp.concatenate(terms, axis=1)
+    partial_sum = jnp.concatenate(
+        [columns_of(in_code_order, (dp_index ^ block) * block_rows, block_rows) for block in range(dp_count)],
+        axis=1,
+    )
     summed = lax.psum_scatter(partial_sum, "mp", scatter_dimension=1, tiled=True)
 
     routed = summed

time: 442 us -> 443 us (level)
  other arithmetic: 46.4 us -> 52.3 us
    unnamed x110 -> x104, local copies, waits for them, and re-layouts: 10.3 us -> 9.34 us
where the time goes in v11:
time: 443 us; the launch traced here: 439 us
  waiting for transfers between devices  261 us (59%)
  matrix products  69 us (16%)
  other arithmetic  52.3 us (12%)
  local copies, waits for them, and re-layouts  25 us (6%)
  between operations  19.2 us (4%)
  starting transfers between devices  12.5 us (3%)
    ppermute x8, waiting for transfers between devices, swapped(): return lax.ppermute(value, axis, pairs)  84.7 us
    ppermute x3, waiting for transfers between devices, shifted(): return lax.ppermute(value, axis, pairs)  82.7 us
    reduce_scatter x1, waiting for transfers between devices, per_device(): lax.psum_scatter(partial_sum, 'mp', scatter_dimension=1, tiled=True)  52.1 us
    all_gather x2, waiting for transfers between devices, per_device(): lax.all_gather(arrived[:, :, chunk * rows:(chunk + 1) * rows], 'mp', axis...  41.7 us
    dot_general x8, matrix products, per_device(): jnp.dot(columns_of(normed, (dp_index ^ code) * block_rows, block_rows), b...  23.5 us
    another operation x3, other arithmetic, gather_blocks(): arrived = swapped(jnp.stack([held[c] for c in codes]), axis, mask)  10.7 us
    unnamed x104, local copies, waits for them, and re-layouts  9.34 us
    reduce_sum x4, other arithmetic, norm_rows(): jnp.mean(values * values, axis=-1, keepdims=True) + 1e-05  9.33 us
  transfers between devices with their start and end apart: 15, of which 9 were waited for; matrix products, arithmetic and copies ran while one was open for 20% of the time, Pallas kernels for 0%

profile of v11, /device:TPU:0, one launch (start us, length us, event | category | flops | bytes accessed | tf_op | source)
XLA Modules:
  0.0 439.3 jit_solution(8494541676896940097)
XLA Ops:
  7.2 3.0 collective-permute-start
  10.2 1.4 constant_dynamic-slice_fusion.4
  12.2 21.4 %collective-permute-done = bf16[1,1,256,2048]{3,2,1,0:T(8,128)(2,1)S(1)} collective-permute-done((bf16[1,1,256,2048]{3,2,1,0:T(8,128)(2,1)}, bf16[1,1,256,2048]{3,2,1,0:T(8,128)(2,1)S(1)}, u32[]{:S(2)}, u32[]{:S(2)}) %collective-permute-start) | collective-permute-done | bytes 1048608 | tf_op jit(solution)/shard_map/ppermute | solution.py:13
  34.7 1.8 collective-permute-start.5
  36.5 1.5 collective-permute-start.6
  38.1 43.8 %collective-permute-done.5 = bf16[1,1,512,2048]{3,2,1,0:T(8,128)(2,1)S(1)} collective-permute-done((bf16[1,1,512,2048]{3,2,1,0:T(8,128)(2,1)}, bf16[1,1,512,2048]{3,2,1,0:T(8,128)(2,1)S(1)}, u32[]{:S(2)}, u32[]{:S(2)}) %collective-permute-start.5) | collective-permute-done | bytes 2097184 | tf_op jit(solution)/shard_map/ppermute | solution.py:13
  81.8 1.5 fusion.238
  83.4 2.7 collective-permute-start.3
  86.2 44.1 %collective-permute-done.6 = bf16[1,2048,1024]{2,1,0:T(8,128)(2,1)} collective-permute-done((bf16[1,2048,1024]{2,1,0:T(8,128)(2,1)}, bf16[1,2048,1024]{2,1,0:T(8,128)(2,1)}, u32[]{:S(2)}, u32[]{:S(2)}) %collective-permute-start.6) | collective-permute-done | bytes 4194336 | tf_op jit(solution)/shard_map/ppermute | solution.py:19
  130.3 7.5 %pad_maximum_fusion = bf16[2,2048,1024]{2,1,0:T(8,128)(2,1)} fusion(bf16[1,2048,1024]{2,1,0:T(8,128)(2,1)} %collective-permute-done.6, bf16[1,2048,1024]{2,1,0:T(8,128)(2,1)} %param.19), kind=kLoop, calls=%fused_computation.12 | loop fusion | flops 4194304 | bytes 16777216 | tf_op jit(solution)/shard_map/stack | solution.py:36
  137.8 14.9 %collective-permute-done.3 = bf16[1,2048,256]{2,1,0:T(8,128)(2,1)S(1)} collective-permute-done((bf16[1,2048,256]{2,1,0:T(8,128)(2,1)S(1)}, bf16[1,2048,256]{2,1,0:T(8,128)(2,1)S(1)}, u32[]{:S(2)}, u32[]{:S(2)}) %collective-permute-start.3) | collective-permute-done | bytes 1048608 | tf_op jit(solution)/shard_map/ppermute | solution.py:19
  152.7 1.7 pad_maximum_fusion.5
  154.4 19.5 %collective-permute-done.1 = bf16[1,2048,256]{2,1,0:T(8,128)(2,1)S(1)} collective-permute-done((bf16[1,2048,256]{2,1,0:T(8,128)(2,1)S(1)}, bf16[1,2048,256]{2,1,0:T(8,128)(2,1)S(1)}, u32[]{:S(2)}, u32[]{:S(2)}) %collective-permute-start.1) | collective-permute-done | bytes 1048608 | tf_op jit(solution)/shard_map/ppermute | solution.py:19
  173.9 1.6 pad_maximum_fusion.4
  179.1 1.3 copy.158
  180.4 1.6 copy.161
  185.1 2.2 fusion.90
  187.3 2.1 fusion.97
  190.0 2.5 multiply_reduce_fusion.2
  194.4 2.2 fusion.107
  196.6 2.2 fusion.99
  198.8 1.8 convolution_add_fusion.7
  200.6 1.8 fusion.68
  202.4 1.5 convolution_convert_fusion.9
  203.9 1.5 convolution_convert_fusion.8
  205.3 3.7 fusion.2
  209.5 2.1 fusion.4
  211.7 1.3 fusion.15
  213.0 3.5 fusion.11
  216.5 3.5 fusion.20
  219.9 3.6 fusion.59
  223.5 1.4 reshape.219
  225.2 1.4 reduce_sum.99
  228.2 3.7 fusion.240
  232.0 2.4 divide_convert_fusion.1
  238.3 41.7 %all-gather.7.cloned.1.call-done = bf16[1,1,256,8192]{3,2,1,0:T(8,128)(2,1)} async-done(((bf16[1,1,256,2048]{3,2,1,0:T(8,128)(2,1)}), bf16[1,1,256,8192]{3,2,1,0:T(8,128)(2,1)}) %all-gather.7.cloned.1.call-update) | async-done | bytes 4194320 | tf_op jit(solution)/shard_map/all_gather | solution.py:137
  280.1 3.3 fusion.5
  287.0 3.5 fusion.19
  290.4 3.5 fusion.55
  293.9 3.5 fusion.58
  298.5 1.4 reshape.220
  299.9 1.4 copy.165
  304.0 1.3 rsqrt.57
  305.3 3.6 fusion.245
  309.0 3.1 fusion.40
  315.5 1.8 fusion.83
  318.3 1.7 fusion.147
  320.6 1.8 fusion.148
  322.4 1.7 fusion.22
  324.6 1.7 fusion.24
  327.3 2.2 pad_maximum_fusion.2
  329.6 1.8 convolution_convert_fusion.5
  331.4 1.7 convolution_convert_fusion.4
  335.7 6.2 %collective-permute-done.9 = bf16[2,2048,512]{1,2,0:T(8,128)(2,1)S(1)} collective-permute-done((bf16[2,2048,512]{1,2,0:T(8,128)(2,1)S(1)}, bf16[2,2048,512]{1,2,0:T(8,128)(2,1)S(1)}, u32[]{:S(2)}, u32[]{:S(2)}) %collective-permute-start.9) | collective-permute-done | bytes 4194336 | tf_op jit(solution)/shard_map/ppermute | solution.py:19
  341.9 2.0 copy-done.18
  343.9 2.3 add_convert_fusion
  346.2 1.5 collective-permute-start.10
  352.9 52.1 %reduce-scatter.2.cloned.1.call-done = bf16[256,2048]{1,0:T(8,128)(2,1)} async-done(((bf16[256,8192]{1,0:T(8,128)(2,1)}), bf16[256,2048]{1,0:T(8,128)(2,1)}) %reduce-scatter.2.cloned.1.call-update) | async-done | bytes 1048592 | tf_op jit(solution)/shard_map/reduce_scatter | solution.py:187
  405.0 1.5 collective-permute-start.8
  406.5 3.5 fusion.8
  410.1 1.3 copy.140
  411.5 1.3 copy.141
  412.8 17.5 %collective-permute-done.8 = bf16[256,2048]{1,0:T(8,128)(2,1)} collective-permute-done((bf16[256,2048]{1,0:T(8,128)(2,1)}, bf16[256,2048]{1,0:T(8,128)(2,1)}, u32[]{:S(2)}, u32[]{:S(2)}) %collective-permute-start.8) | collective-permute-done | bytes 1048608 | tf_op jit(solution)/shard_map/ppermute | solution.py:13
  430.3 2.3 select_bitcast_fusion
  (179 shorter events, 34.5 us)
Async XLA Ops:
  7.2 177.9 %all-gather.9.cloned.1.call-start = ((), (), s32[]{:S(2)}) async-start(), calls=%async_computation.4 | async-start | bytes 5242880 | tf_op jit(solution)/shard_map/all_gather | solution.py:113
  7.2 26.4 %collective-permute-start = (bf16[1,1,256,2048]{3,2,1,0:T(8,128)(2,1)}, bf16[1,1,256,2048]{3,2,1,0:T(8,128)(2,1)S(1)}, u32[]{:S(2)}, u32[]{:S(2)}) collective-permute-start(bf16[1,1,256,2048]{3,2,1,0:T(8,128)(2,1)} %param.14), channel_id=1, source_target_pairs={{0,16},{16,0},{1,17},{17,1},{2,18},{18,2},{3,19},{19,3},{4,20},{20... | collective-permute-start | bytes 3145736 | tf_op jit(solution)/shard_map/ppermute | solution.py:13
  12.1 71.2 %copy-start.6 = (bf16[1,2048,256]{2,1,0:T(8,128)(2,1)S(1)}, bf16[1,2048,256]{2,1,0:T(8,128)(2,1)}, u32[]{:S(2)}) copy-start(bf16[1,2048,256]{2,1,0:T(8,128)(2,1)} %param.20) | copy-start | bytes 3145732
  12.2 74.0 %copy-start.16 = (bf16[1,2048,256]{2,1,0:T(8,128)(2,1)S(1)}, bf16[1,2048,256]{2,1,0:T(8,128)(2,1)}, u32[]{:S(2)}) copy-start(bf16[1,2048,256]{2,1,0:T(8,128)(2,1)} %param.21) | copy-start | bytes 3145732
  34.7 170.6 %all-gather.5.cloned.1.call-start = ((), (), s32[]{:S(2)}) async-start(), calls=%async_computation.1 | async-start | bytes 5242880 | tf_op jit(solution)/shard_map/all_gather | solution.py:137
  34.7 47.1 %collective-permute-start.5 = (bf16[1,1,512,2048]{3,2,1,0:T(8,128)(2,1)}, bf16[1,1,512,2048]{3,2,1,0:T(8,128)(2,1)S(1)}, u32[]{:S(2)}, u32[]{:S(2)}) collective-permute-start(bf16[1,1,512,2048]{3,2,1,0:T(8,128)(2,1)} %param.13), channel_id=1, source_target_pairs={{0,16},{16,0},{1,17},{17,1},{2,18},{18,2},{3,19},{19,3},{4,20},{20... | collective-permute-start | bytes 6291464 | tf_op jit(solution)/shard_map/ppermute | solution.py:13
  36.5 93.8 %collective-permute-start.6 = (bf16[1,2048,1024]{2,1,0:T(8,128)(2,1)}, bf16[1,2048,1024]{2,1,0:T(8,128)(2,1)}, u32[]{:S(2)}, u32[]{:S(2)}) collective-permute-start(bf16[1,2048,1024]{2,1,0:T(8,128)(2,1)} %param.19), channel_id=1, source_target_pairs={{0,2},{1,3},{2,0},{3,1},{4,6},{5,7},{6,4},{7,5},{8,10},{9,11},{10,... | collective-permute-start | bytes 12582920 | tf_op jit(solution)/shard_map/ppermute | solution.py:19
  83.3 196.7 %all-gather.7.cloned.1.call-start = ((), (), s32[]{:S(2)}) async-start(), calls=%async_computation.2 | async-start | bytes 5242880 | tf_op jit(solution)/shard_map/all_gather | solution.py:137
  83.4 69.3 %collective-permute-start.3 = (bf16[1,2048,256]{2,1,0:T(8,128)(2,1)S(1)}, bf16[1,2048,256]{2,1,0:T(8,128)(2,1)S(1)}, u32[]{:S(2)}, u32[]{:S(2)}) collective-permute-start(bf16[1,2048,256]{2,1,0:T(8,128)(2,1)S(1)} %copy-done.6), channel_id=1, source_target_pairs={{0,2},{1,3},{2,0},{3,1},{4,6},{5,7},{6,4},{7,5},{8,10},{9,11},{10,... | collective-permute-start | bytes 3145736 | tf_op jit(solution)/shard_map/ppermute | solution.py:19
  86.1 87.7 %collective-permute-start.1 = (bf16[1,2048,256]{2,1,0:T(8,128)(2,1)S(1)}, bf16[1,2048,256]{2,1,0:T(8,128)(2,1)S(1)}, u32[]{:S(2)}, u32[]{:S(2)}) collective-permute-start(bf16[1,2048,256]{2,1,0:T(8,128)(2,1)S(1)} %copy-done.16), channel_id=1, source_target_pairs={{0,2},{1,3},{2,0},{3,1},{4,6},{5,7},{6,4},{7,5},{8,10},{9,11},{10,... | collective-permute-start | bytes 3145736 | tf_op jit(solution)/shard_map/ppermute | solution.py:19
  137.8 37.6 %copy-start.26 = (bf16[1,1,512,1024]{3,2,1,0:T(8,128)(2,1)S(1)}, bf16[1,1,512,1024]{3,2,1,0:T(8,128)(2,1)}, u32[]{:S(2)}) copy-start(bf16[1,1,512,1024]{3,2,1,0:T(8,128)(2,1)} %param.25) | copy-start | bytes 3145732
  137.8 78.6 %collective-permute-start.7 = (bf16[2,2048,1024]{2,1,0:T(8,128)(2,1)}, bf16[2,2048,1024]{2,1,0:T(8,128)(2,1)}, u32[]{:S(2)}, u32[]{:S(2)}) collective-permute-start(bf16[2,2048,1024]{2,1,0:T(8,128)(2,1)} %pad_maximum_fusion), channel_id=1, source_target_pairs={{0,1},{1,0},{2,3},{3,2},{4,5},{5,4},{6,7},{7,6},{8,9},{9,8},{10,11... | collective-permute-start | bytes 25165832 | tf_op jit(solution)/shard_map/ppermute | solution.py:19
  152.7 22.7 %copy-start.11 = (bf16[1,2048,256]{2,1,0:T(8,128)(2,1)}, bf16[1,2048,256]{2,1,0:T(8,128)(2,1)S(1)}, u32[]{:S(2)}) copy-start(bf16[1,2048,256]{2,1,0:T(8,128)(2,1)S(1)} %collective-permute-done.3) | copy-start | bytes 3145732
  154.4 32.9 %collective-permute-start.4 = (bf16[2,2048,256]{2,1,0:T(8,128)(2,1)}, bf16[2,2048,256]{2,1,0:T(8,128)(2,1)}, u32[]{:S(2)}, u32[]{:S(2)}) collective-permute-start(bf16[2,2048,256]{2,1,0:T(8,128)(2,1)} %pad_maximum_fusion.5), channel_id=1, source_target_pairs={{0,1},{1,0},{2,3},{3,2},{4,5},{5,4},{6,7},{7,6},{8,9},{9,8},{10,11... | collective-permute-start | bytes 6291464 | tf_op jit(solution)/shard_map/ppermute | solution.py:19
  175.4 7.2 %copy-start.44 = (s32[1,2]{1,0:T(1,128)S(1)}, s32[1,2]{1,0:T(1,128)}, u32[]{:S(2)}) copy-start(s32[1,2]{1,0:T(1,128)} %param.15) | copy-start | bytes 28
  175.4 21.2 %collective-permute-start.2 = (bf16[2,2048,256]{2,1,0:T(8,128)(2,1)}, bf16[2,2048,256]{2,1,0:T(8,128)(2,1)}, u32[]{:S(2)}, u32[]{:S(2)}) collective-permute-start(bf16[2,2048,256]{2,1,0:T(8,128)(2,1)} %pad_maximum_fusion.4), channel_id=1, source_target_pairs={{0,1},{1,0},{2,3},{3,2},{4,5},{5,4},{6,7},{7,6},{8,9},{9,8},{10,11... | collective-permute-start | bytes 6291464 | tf_op jit(solution)/shard_map/ppermute | solution.py:19
  182.0 21.9 %copy-start.7 = (f32[1,1,256,1024]{2,3,1,0:T(8,128)}, f32[1,1,256,1024]{2,3,1,0:T(8,128)S(1)}, u32[]{:S(2)}) copy-start(f32[1,1,256,1024]{2,3,1,0:T(8,128)S(1)} %copy.161) | copy-start | bytes 3145732
  184.8 19.1 %copy-start.39 = (pred[256]{0:T(512)(128)(4,1)}, pred[256]{0:T(512)(128)(4,1)S(1)}, u32[]{:S(2)}) copy-start(pred[256]{0:T(512)(128)(4,1)S(1)} %get-tuple-element.54) | copy-start | bytes 772
  184.8 220.2 %reduce-scatter.2.cloned.1.call-start = ((), (), s32[]{:S(2)}) async-start(), calls=%async_computation.3 | async-start | bytes 5242880 | tf_op jit(solution)/shard_map/reduce_scatter | solution.py:187
  185.1 4.3 copy-start
  187.3 6.2 %copy-start.33 = (f32[1,128]{1,0:T(1,128)S(1)}, f32[1,128]{1,0:T(1,128)}, u32[]{:S(2)}) copy-start(f32[1,128]{1,0:T(1,128)} %param.23) | copy-start | bytes 1540
  193.5 5.3 %copy-start.1 = (bf16[1,1,256,8192]{3,2,1,0:T(8,128)(2,1)S(1)}, bf16[1,1,256,8192]{3,2,1,0:T(8,128)(2,1)}, u32[]{:S(2)}) copy-start(bf16[1,1,256,8192]{3,2,1,0:T(8,128)(2,1)} %all-gather.9.cloned.1.call-done) | copy-start | bytes 12582916
  196.6 5.8 %copy-start.9 = (f32[1,1,256,1024]{2,3,1,0:T(8,128)S(1)}, f32[1,1,256,1024]{2,3,1,0:T(8,128)}, u32[]{:S(2)}) copy-start(f32[1,1,256,1024]{2,3,1,0:T(8,128)} %copy.158) | copy-start | bytes 3145732
  196.6 5.8 %copy-start.41 = (pred[256]{0:T(512)(128)(4,1)S(1)}, pred[256]{0:T(512)(128)(4,1)}, u32[]{:S(2)}) copy-start(pred[256]{0:T(512)(128)(4,1)} %get-tuple-element.55) | copy-start | bytes 772
  205.3 4.2 copy-start.4
  209.5 2.2 copy-start.22
  228.2 6.2 %copy-start.10 = (f32[1,1,256,1024]{2,3,1,0:T(8,128)S(1)}, f32[1,1,256,1024]{2,3,1,0:T(8,128)}, u32[]{:S(2)}) copy-start(f32[1,1,256,1024]{2,3,1,0:T(8,128)} %copy.158) | copy-start | bytes 3145732
  231.9 2.5 copy-start.42
  231.9 3.8 copy-start.21
  231.9 3.8 copy-start.24
  231.9 3.8 copy-start.28
  231.9 3.8 copy-start.36
  231.9 3.8 copy-start.45
  231.9 3.8 copy-start.48
  234.4 2.2 copy-start.13
  236.6 46.7 %copy-start.32 = (f32[1,8192]{1,0:T(1,128)S(1)}, f32[1,8192]{1,0:T(1,128)}, u32[]{:S(2)}) copy-start(f32[1,8192]{1,0:T(1,128)} %param.18) | copy-start | bytes 98308
  280.1 3.4 copy-start.5
  283.5 2.2 copy-start.23
  297.4 7.9 %copy-start.46 = (f32[1,128]{1,0:T(1,128)S(1)}, f32[1,128]{1,0:T(1,128)}, u32[]{:S(2)}) copy-start(f32[1,128]{1,0:T(1,128)} %param.22) | copy-start | bytes 1540
  302.4 6.6 %copy-start.19 = (bf16[2,4,256,256]{2,3,1,0:T(8,128)(2,1)S(1)}, bf16[2,4,256,256]{2,3,1,0:T(8,128)(2,1)}, u32[]{:S(2)}) copy-start(bf16[2,4,256,256]{2,3,1,0:T(8,128)(2,1)} %convolution_convert_fusion.8) | copy-start | bytes 3145732
  308.9 3.2 copy-start.20
  308.9 3.2 copy-start.25
  308.9 3.2 copy-start.29
  309.0 3.2 copy-start.37
  309.0 3.2 copy-start.47
  309.0 3.2 copy-start.49
  312.2 1.1 copy-start.35
  312.2 1.3 copy-start.38
  312.2 1.3 copy-start.31
  312.2 3.2 copy-start.8
  312.2 3.2 copy-start.40
  315.4 2.3 copy-start.30
  315.4 2.4 copy-start.17
  320.5 3.5 copy-start.12
  329.5 3.5 copy-start.2
  334.7 7.2 %collective-permute-start.9 = (bf16[2,2048,512]{1,2,0:T(8,128)(2,1)S(1)}, bf16[2,2048,512]{1,2,0:T(8,128)(2,1)S(1)}, u32[]{:S(2)}, u32[]{:S(2)}) collective-permute-start(bf16[2,2048,512]{1,2,0:T(8,128)(2,1)S(1)} %pad_maximum_fusion.3), channel_id=1, source_target_pairs={{0,1},{1,0},{2,3},{3,2},{4,5},{5,4},{6,7},{7,6},{8,9},{9,8},{10,11... | collective-permute-start | bytes 12582920 | tf_op jit(solution)/shard_map/ppermute | solution.py:19
  335.2 13.1 %copy-start.14 = (bf16[2,4,256,256]{2,3,1,0:T(8,128)(2,1)S(1)}, bf16[2,4,256,256]{2,3,1,0:T(8,128)(2,1)}, u32[]{:S(2)}) copy-start(bf16[2,4,256,256]{2,3,1,0:T(8,128)(2,1)} %copy-done.13) | copy-start | bytes 3145732
  335.7 13.2 %copy-start.15 = (bf16[2,4,256,256]{2,3,1,0:T(8,128)(2,1)S(1)}, bf16[2,4,256,256]{2,3,1,0:T(8,128)(2,1)}, u32[]{:S(2)}) copy-start(bf16[2,4,256,256]{2,3,1,0:T(8,128)(2,1)} %get-tuple-element.39) | copy-start | bytes 3145732
  341.9 2.0 copy-start.18
  346.2 3.2 copy-start.43
  346.2 60.3 %collective-permute-start.10 = (bf16[1,2048,512]{1,2,0:T(8,128)(2,1)}, bf16[1,2048,512]{1,2,0:T(8,128)(2,1)}, u32[]{:S(2)}, u32[]{:S(2)}) collective-permute-start(bf16[1,2048,512]{1,2,0:T(8,128)(2,1)} %add_convert_fusion), channel_id=1, source_target_pairs={{0,2},{1,3},{2,0},{3,1},{4,6},{5,7},{6,4},{7,5},{8,10},{9,11},{10,... | collective-permute-start | bytes 6291464 | tf_op jit(solution)/shard_map/ppermute | solution.py:19
  349.4 2.6 copy-start.3
  405.0 25.3 %collective-permute-start.8 = (bf16[256,2048]{1,0:T(8,128)(2,1)}, bf16[256,2048]{1,0:T(8,128)(2,1)}, u32[]{:S(2)}, u32[]{:S(2)}) collective-permute-start(bf16[256,2048]{1,0:T(8,128)(2,1)} %reduce-scatter.2.cloned.1.call-done), channel_id=1, source_target_pairs={{0,16},{16,0},{1,17},{17,1},{2,18},{18,2},{3,19},{19,3},{4,20},{20... | collective-permute-start | bytes 3145736 | tf_op jit(solution)/shard_map/ppermute | solution.py:13
  410.0 20.3 %copy-start.27 = (bf16[256,2048]{1,0:T(8,128)(2,1)S(1)}, bf16[256,2048]{1,0:T(8,128)(2,1)}, u32[]{:S(2)}) copy-start(bf16[256,2048]{1,0:T(8,128)(2,1)} %reduce-scatter.2.cloned.1.call-done) | copy-start | bytes 3145732
  (1 other events, 0.9 us)
Sparse Core Ops, SparseCore 0:
  34.8 82.2 all-gather.8
  119.3 79.2 all-gather.4
  200.7 79.2 all-gather.6
  329.7 75.2 reduce-scatter.1

commit v12 on v3

--- a/solution.py
+++ b/solution.py
@@ -37,6 +37,25 @@
         for position, code in enumerate(codes):
             held[code ^ mask] = arrived[position]
     return held
+
+
+def gather_groups(block, axis):
+    count = lax.axis_size(axis)
+    codes = [0]
+    stack = block[None]
+    groups = [(codes, stack)]
+    for mask in bit_order(count, True):
+        arrived = swapped(stack, axis, mask)
+        moved = [code ^ mask for code in codes]
+        groups = [(codes, stack), (moved, arrived)]
+        stack = jnp.concatenate([stack, arrived], axis=0)
+        codes = codes + moved
+    return groups
+
+
+def code_slices(values, index, codes, width):
+    pieces = [lax.dynamic_slice_in_dim(values, (index ^ code) * width, width, axis=1) for code in codes]
+    return pieces[0] if len(pieces) == 1 else jnp.concatenate(pieces, axis=1)
 
 
 def scatter_blocks(by_code, axis):
@@ -99,7 +118,7 @@
     dp_index = lax.axis_index("dp")
     block_rows = query_weight.shape[1]
 
-    query_blocks = gather_blocks(query_weight[0], "dp")
+    query_groups = gather_groups(query_weight[0], "dp")
     key_blocks = gather_blocks(key_weight[0], "dp")
     value_blocks = gather_blocks(value_weight[0], "dp")
 
@@ -142,10 +161,10 @@
         full_text = gathered[chunk][0, 0]
         normed = norm_rows(full_text, norm_gain[0]).astype(jnp.bfloat16)
         query_raw = None
-        for code, block in query_blocks.items():
+        for codes, stack in query_groups:
             part = jnp.dot(
-                columns_of(normed, (dp_index ^ code) * block_rows, block_rows),
-                block,
+                code_slices(normed, dp_index, codes, block_rows),
+                stack.reshape(stack.shape[0] * stack.shape[1], stack.shape[2]),
                 preferred_element_type=jnp.float32,
             )
             query_raw = part if query_raw is None else query_raw + part

time: 442 us -> 452 us (1.023)
  local copies, waits for them, and re-layouts: 26.4 us -> 45.7 us
  waiting for transfers between devices: 263 us -> 251 us
    all_gather x2, waiting for transfers between devices: 42.9 us -> 32.9 us  [per_device(): lax.all_gather(arrived[:, :, chunk * rows:(chunk + 1) * rows], 'mp', axis...]
    another operation x3 -> x2, other arithmetic: 10.6 us -> 3.03 us  [gather_blocks(): arrived = swapped(jnp.stack([held[c] for c in codes]), axis, mask)]
    unnamed x110 -> x101, local copies, waits for them, and re-layouts: 10.3 us -> 16.1 us
    concatenate x0 -> x1, local copies, waits for them, and re-layouts: none -> 4.56 us  [gather_groups(): stack = jnp.concatenate([stack, arrived], axis=0)]
    dot_general x8 -> x4, matrix products: 23.5 us -> 23.9 us  [per_device(): jnp.dot(code_slices(normed, dp_index, codes, block_rows), stack.reshape(s...]
  transfers between devices with their start and end apart: 15 -> 15, of which waited for: 9 -> 9; matrix products, arithmetic and copies ran while one was open for 20% -> 23% of each run, Pallas kernels for 0% -> 0%
where the time goes in v12:
time: 452 us; the launch traced here: 446 us
  waiting for transfers between devices  251 us (56%)
  matrix products  73 us (16%)
  other arithmetic  46.8 us (10%)
  local copies, waits for them, and re-layouts  45.7 us (10%)
  between operations  19.5 us (4%)
  starting transfers between devices  10.3 us (2%)
    ppermute x8, waiting for transfers between devices, swapped(): return lax.ppermute(value, axis, pairs)  83.3 us
    ppermute x3, waiting for transfers between devices, shifted(): return lax.ppermute(value, axis, pairs)  82.3 us
    reduce_scatter x1, waiting for transfers between devices, per_device(): lax.psum_scatter(partial_sum, 'mp', scatter_dimension=1, tiled=True)  52 us
    all_gather x2, waiting for transfers between devices, per_device(): lax.all_gather(arrived[:, :, chunk * rows:(chunk + 1) * rows], 'mp', axis...  32.9 us
    dot_general x4, matrix products, per_device(): jnp.dot(code_slices(normed, dp_index, codes, block_rows), stack.reshape(s...  23.9 us
    unnamed x101, local copies, waits for them, and re-layouts  16.1 us
    reduce_sum x4, other arithmetic, norm_rows(): jnp.mean(values * values, axis=-1, keepdims=True) + 1e-05  11.7 us
  transfers between devices with their start and end apart: 15, of which 9 were waited for; matrix products, arithmetic and copies ran while one was open for 23% of the time, Pallas kernels for 0%

profile of v12, /device:TPU:0, one launch (start us, length us, event | category | flops | bytes accessed | tf_op | source)
XLA Modules:
  0.0 445.9 jit_solution(15120146229728908013)
XLA Ops:
  7.2 3.0 collective-permute-start
  10.2 1.4 constant_dynamic-slice_fusion
  12.3 21.3 %collective-permute-done = bf16[1,1,256,2048]{3,2,1,0:T(8,128)(2,1)S(1)} collective-permute-done((bf16[1,1,256,2048]{3,2,1,0:T(8,128)(2,1)}, bf16[1,1,256,2048]{3,2,1,0:T(8,128)(2,1)S(1)}, u32[]{:S(2)}, u32[]{:S(2)}) %collective-permute-start) | collective-permute-done | bytes 1048608 | tf_op jit(solution)/shard_map/ppermute | solution.py:13
  33.6 2.3 broadcast_select_fusion
  36.0 1.8 collective-permute-start.5
  38.1 43.6 %collective-permute-done.5 = bf16[1,1,512,2048]{3,2,1,0:T(8,128)(2,1)S(1)} collective-permute-done((bf16[1,1,512,2048]{3,2,1,0:T(8,128)(2,1)S(1)}, bf16[1,1,512,2048]{3,2,1,0:T(8,128)(2,1)S(1)}, u32[]{:S(2)}, u32[]{:S(2)}) %collective-permute-start.5) | collective-permute-done | bytes 2097184 | tf_op jit(solution)/shard_map/ppermute | solution.py:13
  81.6 1.5 fusion.233
  83.2 1.5 collective-permute-start.3
  84.7 4.7 %constant_dynamic-update-slice_fusion.1 = bf16[2,2048,1024]{2,1,0:T(8,128)(2,1)} fusion(bf16[1,2048,1024]{2,1,0:T(8,128)(2,1)} %param.19), kind=kLoop, calls=%fused_computation.248 | loop fusion | bytes 8388608
  89.4 42.2 %collective-permute-done.6 = bf16[1,2048,1024]{2,1,0:T(8,128)(2,1)} collective-permute-done((bf16[1,2048,1024]{2,1,0:T(8,128)(2,1)}, bf16[1,2048,1024]{2,1,0:T(8,128)(2,1)}, u32[]{:S(2)}, u32[]{:S(2)}) %collective-permute-start.6) | collective-permute-done | bytes 4194336 | tf_op jit(solution)/shard_map/ppermute | solution.py:19
  131.6 4.6 %constant_dynamic-update-slice_fusion = bf16[2,2048,1024]{2,1,0:T(8,128)(2,1)} fusion(bf16[2,2048,1024]{2,1,0:T(8,128)(2,1)} %constant_dynamic-update-slice_fusion.1, bf16[1,2048,1024]{2,1,0:T(8,128)(2,1)} %collective-permute-done.6), kind=kLoop, calls=%fused_computation.247 | loop fusion | bytes 8388608 | tf_op jit(solution)/shard_map/concatenate | solution.py:51
  136.5 17.5 %collective-permute-done.3 = bf16[1,2048,256]{2,1,0:T(8,128)(2,1)S(1)} collective-permute-done((bf16[1,2048,256]{2,1,0:T(8,128)(2,1)S(1)}, bf16[1,2048,256]{2,1,0:T(8,128)(2,1)S(1)}, u32[]{:S(2)}, u32[]{:S(2)}) %collective-permute-start.3) | collective-permute-done | bytes 1048608 | tf_op jit(solution)/shard_map/ppermute | solution.py:19
  154.0 1.5 pad_maximum_fusion.2
  155.5 17.4 %collective-permute-done.1 = bf16[1,2048,256]{2,1,0:T(8,128)(2,1)S(1)} collective-permute-done((bf16[1,2048,256]{2,1,0:T(8,128)(2,1)S(1)}, bf16[1,2048,256]{2,1,0:T(8,128)(2,1)S(1)}, u32[]{:S(2)}, u32[]{:S(2)}) %collective-permute-start.1) | collective-permute-done | bytes 1048608 | tf_op jit(solution)/shard_map/ppermute | solution.py:19
  172.9 1.5 pad_maximum_fusion.1
  174.4 1.6 slice_convert_fusion
  178.7 2.6 copy.158
  181.3 2.5 copy.161
  187.1 1.9 fusion.97
  189.0 2.1 fusion.104
  191.7 2.5 multiply_reduce_fusion.2
  196.1 1.9 fusion.114
  198.0 2.1 fusion.106
  200.1 1.9 convolution_add_fusion.7
  202.0 1.9 fusion.75
  203.8 1.5 convolution_convert_fusion.9
  205.3 1.5 convolution_convert_fusion.8
  206.8 3.6 fusion.2
  210.9 1.9 fusion.4
  213.3 5.7 %fusion.37 = f32[256,1024]{1,0:T(8,128)S(1)} fusion(bf16[4096,1024]{1,0:T(8,128)(2,1)} %bitcast.27, bf16[256,2048]{1,0:T(8,128)(2,1)S(1)} %get-tuple-element.37, bf16[256,2048]{1,0:T(8,128)(2,1)S(1)} %get-tuple-element.38), kind=kOutput, calls=%fused_computation.64 | convolution fusion | flops 2151677952 | bytes 11534336 | tf_op jit(solution)/shard_map/dot_general | solution.py:165
  219.1 6.8 %fusion.64 = f32[256,1024]{1,0:T(8,128)} fusion(f32[256,1024]{1,0:T(8,128)S(1)} %fusion.37, bf16[4096,1024]{1,0:T(8,128)(2,1)} %bitcast.26, bf16[256,2048]{1,0:T(8,128)(2,1)S(1)} %get-tuple-element.39, bf16[256,2048]{1,0:T(8,128)(2,1)S(1)} %get-tuple-element.36), kind=kOutput, calls=%fused_computation.97 | convolution fusion | flops 2151940096 | bytes 12582912 | tf_op jit(solution)/shard_map/dot_general | solution.py:165
  225.9 2.7 reshape.229
  228.5 1.3 multiply_bitcast_fusion.1
  231.0 2.6 reduce_sum.99
  235.3 1.3 rsqrt.54
  236.6 3.6 fusion.235
  240.2 2.5 divide_convert_fusion.1
  247.5 32.9 %all-gather.7.cloned.1.call-done = bf16[1,1,256,8192]{3,2,1,0:T(8,128)(2,1)} async-done(((bf16[1,1,256,2048]{3,2,1,0:T(8,128)(2,1)}), bf16[1,1,256,8192]{3,2,1,0:T(8,128)(2,1)}) %all-gather.7.cloned.1.call-update) | async-done | bytes 4194320 | tf_op jit(solution)/shard_map/all_gather | solution.py:156
  280.3 3.3 fusion.5
  283.8 1.9 fusion.7
  286.2 5.7 %fusion.45 = f32[256,1024]{1,0:T(8,128)S(1)} fusion(bf16[4096,1024]{1,0:T(8,128)(2,1)} %bitcast.27, bf16[256,2048]{1,0:T(8,128)(2,1)S(1)} %get-tuple-element.33, bf16[256,2048]{1,0:T(8,128)(2,1)S(1)} %get-tuple-element.34), kind=kOutput, calls=%fused_computation.72 | convolution fusion | flops 2151677952 | bytes 11534336 | tf_op jit(solution)/shard_map/dot_general | solution.py:165
  292.0 5.7 %fusion.61 = f32[256,1024]{1,0:T(8,128)S(1)} fusion(f32[256,1024]{1,0:T(8,128)S(1)} %fusion.45, bf16[4096,1024]{1,0:T(8,128)(2,1)} %bitcast.26, bf16[256,2048]{1,0:T(8,128)(2,1)S(1)} %get-tuple-element.35, bf16[256,2048]{1,0:T(8,128)(2,1)S(1)} %get-tuple-element.32), kind=kOutput, calls=%fused_computation.96 | convolution fusion | flops 2151940096 | bytes 12582912 | tf_op jit(solution)/shard_map/dot_general | solution.py:165
  299.7 2.7 reshape.230
  302.4 2.4 copy.165
  304.8 2.2 reduce_sum.107
  309.9 3.6 fusion.240
  313.5 2.4 fusion.32
  322.3 2.5 broadcast_in_dim.96
  324.8 1.5 fusion.10
  326.8 1.7 fusion.146
  328.5 1.7 fusion.147
  330.3 1.6 fusion.12
  331.8 2.8 fusion.14
  334.6 2.8 fusion.16
  337.5 1.8 convolution_convert_fusion.4
  339.3 1.7 convolution_convert_fusion.5
  343.6 6.2 %collective-permute-done.9 = bf16[2,2048,512]{1,2,0:T(8,128)(2,1)S(1)} collective-permute-done((bf16[2,2048,512]{1,2,0:T(8,128)(2,1)S(1)}, bf16[2,2048,512]{1,2,0:T(8,128)(2,1)S(1)}, u32[]{:S(2)}, u32[]{:S(2)}) %collective-permute-start.9) | collective-permute-done | bytes 4194336 | tf_op jit(solution)/shard_map/ppermute | solution.py:19
  349.8 2.6 add_convert_fusion
  352.4 1.5 collective-permute-start.10
  360.9 52.0 %reduce-scatter.2.cloned.1.call-done = bf16[256,2048]{1,0:T(8,128)(2,1)} async-done(((bf16[256,8192]{1,0:T(8,128)(2,1)}), bf16[256,2048]{1,0:T(8,128)(2,1)}) %reduce-scatter.2.cloned.1.call-update) | async-done | bytes 1048592 | tf_op jit(solution)/shard_map/reduce_scatter | solution.py:202
  412.9 1.5 collective-permute-start.8
  414.4 3.5 fusion.8
  418.0 1.3 copy.140
  420.6 17.5 %collective-permute-done.8 = bf16[256,2048]{1,0:T(8,128)(2,1)} collective-permute-done((bf16[256,2048]{1,0:T(8,128)(2,1)}, bf16[256,2048]{1,0:T(8,128)(2,1)}, u32[]{:S(2)}, u32[]{:S(2)}) %collective-permute-start.8) | collective-permute-done | bytes 1048608 | tf_op jit(solution)/shard_map/ppermute | solution.py:13
  (172 shorter events, 38.0 us)
Async XLA Ops:
  7.2 179.9 %all-gather.9.cloned.1.call-start = ((), (), s32[]{:S(2)}) async-start(), calls=%async_computation.4 | async-start | bytes 5242880 | tf_op jit(solution)/shard_map/all_gather | solution.py:132
  7.2 26.4 %collective-permute-start = (bf16[1,1,256,2048]{3,2,1,0:T(8,128)(2,1)}, bf16[1,1,256,2048]{3,2,1,0:T(8,128)(2,1)S(1)}, u32[]{:S(2)}, u32[]{:S(2)}) collective-permute-start(bf16[1,1,256,2048]{3,2,1,0:T(8,128)(2,1)} %param.14), channel_id=1, source_target_pairs={{0,16},{16,0},{1,17},{17,1},{2,18},{18,2},{3,19},{19,3},{4,20},{20... | collective-permute-start | bytes 3145736 | tf_op jit(solution)/shard_map/ppermute | solution.py:13
  12.3 23.7 %copy-start.41 = (bf16[1,1,512,2048]{3,2,1,0:T(8,128)(2,1)S(1)}, bf16[1,1,512,2048]{3,2,1,0:T(8,128)(2,1)}, u32[]{:S(2)}) copy-start(bf16[1,1,512,2048]{3,2,1,0:T(8,128)(2,1)} %param.13) | copy-start | bytes 6291460
  35.9 47.3 %copy-start.6 = (bf16[1,2048,256]{2,1,0:T(8,128)(2,1)S(1)}, bf16[1,2048,256]{2,1,0:T(8,128)(2,1)}, u32[]{:S(2)}) copy-start(bf16[1,2048,256]{2,1,0:T(8,128)(2,1)} %param.20) | copy-start | bytes 3145732
  35.9 170.9 %all-gather.5.cloned.1.call-start = ((), (), s32[]{:S(2)}) async-start(), calls=%async_computation.1 | async-start | bytes 5242880 | tf_op jit(solution)/shard_map/all_gather | solution.py:156
  36.0 45.7 %collective-permute-start.5 = (bf16[1,1,512,2048]{3,2,1,0:T(8,128)(2,1)S(1)}, bf16[1,1,512,2048]{3,2,1,0:T(8,128)(2,1)S(1)}, u32[]{:S(2)}, u32[]{:S(2)}) collective-permute-start(bf16[1,1,512,2048]{3,2,1,0:T(8,128)(2,1)S(1)} %copy-done.41), channel_id=1, source_target_pairs={{0,16},{16,0},{1,17},{17,1},{2,18},{18,2},{3,19},{19,3},{4,20},{20... | collective-permute-start | bytes 6291464 | tf_op jit(solution)/shard_map/ppermute | solution.py:13
  37.8 93.8 %collective-permute-start.6 = (bf16[1,2048,1024]{2,1,0:T(8,128)(2,1)}, bf16[1,2048,1024]{2,1,0:T(8,128)(2,1)}, u32[]{:S(2)}, u32[]{:S(2)}) collective-permute-start(bf16[1,2048,1024]{2,1,0:T(8,128)(2,1)} %param.19), channel_id=1, source_target_pairs={{0,2},{1,3},{2,0},{3,1},{4,6},{5,7},{6,4},{7,5},{8,10},{9,11},{10,... | collective-permute-start | bytes 12582920 | tf_op jit(solution)/shard_map/ppermute | solution.py:19
  83.1 197.2 %all-gather.7.cloned.1.call-start = ((), (), s32[]{:S(2)}) async-start(), calls=%async_computation.2 | async-start | bytes 5242880 | tf_op jit(solution)/shard_map/all_gather | solution.py:156
  83.2 70.8 %collective-permute-start.3 = (bf16[1,2048,256]{2,1,0:T(8,128)(2,1)S(1)}, bf16[1,2048,256]{2,1,0:T(8,128)(2,1)S(1)}, u32[]{:S(2)}, u32[]{:S(2)}) collective-permute-start(bf16[1,2048,256]{2,1,0:T(8,128)(2,1)S(1)} %copy-done.6), channel_id=1, source_target_pairs={{0,2},{1,3},{2,0},{3,1},{4,6},{5,7},{6,4},{7,5},{8,10},{9,11},{10,... | collective-permute-start | bytes 3145736 | tf_op jit(solution)/shard_map/ppermute | solution.py:19
  89.4 46.8 %copy-start.7 = (bf16[1,2048,256]{2,1,0:T(8,128)(2,1)S(1)}, bf16[1,2048,256]{2,1,0:T(8,128)(2,1)}, u32[]{:S(2)}) copy-start(bf16[1,2048,256]{2,1,0:T(8,128)(2,1)} %param.21) | copy-start | bytes 3145732
  136.2 77.2 %collective-permute-start.7 = (bf16[2,2048,1024]{2,1,0:T(8,128)(2,1)}, bf16[2,2048,1024]{2,1,0:T(8,128)(2,1)}, u32[]{:S(2)}, u32[]{:S(2)}) collective-permute-start(bf16[2,2048,1024]{2,1,0:T(8,128)(2,1)} %constant_dynamic-update-slice_fusion), channel_id=1, source_target_pairs={{0,1},{1,0},{2,3},{3,2},{4,5},{5,4},{6,7},{7,6},{8,9},{9,8},{10,11... | collective-permute-start | bytes 25165832 | tf_op jit(solution)/shard_map/ppermute | solution.py:19
  136.2 36.7 %collective-permute-start.1 = (bf16[1,2048,256]{2,1,0:T(8,128)(2,1)S(1)}, bf16[1,2048,256]{2,1,0:T(8,128)(2,1)S(1)}, u32[]{:S(2)}, u32[]{:S(2)}) collective-permute-start(bf16[1,2048,256]{2,1,0:T(8,128)(2,1)S(1)} %copy-done.7), channel_id=1, source_target_pairs={{0,2},{1,3},{2,0},{3,1},{4,6},{5,7},{6,4},{7,5},{8,10},{9,11},{10,... | collective-permute-start | bytes 3145736 | tf_op jit(solution)/shard_map/ppermute | solution.py:19
  155.5 18.9 %copy-start.23 = (bf16[1,1,512,1024]{3,2,1,0:T(8,128)(2,1)S(1)}, bf16[1,1,512,1024]{3,2,1,0:T(8,128)(2,1)}, u32[]{:S(2)}) copy-start(bf16[1,1,512,1024]{3,2,1,0:T(8,128)(2,1)} %param.25) | copy-start | bytes 3145732
  155.5 33.5 %collective-permute-start.4 = (bf16[2,2048,256]{2,1,0:T(8,128)(2,1)}, bf16[2,2048,256]{2,1,0:T(8,128)(2,1)}, u32[]{:S(2)}, u32[]{:S(2)}) collective-permute-start(bf16[2,2048,256]{2,1,0:T(8,128)(2,1)} %pad_maximum_fusion.2), channel_id=1, source_target_pairs={{0,1},{1,0},{2,3},{3,2},{4,5},{5,4},{6,7},{7,6},{8,9},{9,8},{10,11... | collective-permute-start | bytes 6291464 | tf_op jit(solution)/shard_map/ppermute | solution.py:19
  174.4 23.6 %collective-permute-start.2 = (bf16[2,2048,256]{2,1,0:T(8,128)(2,1)}, bf16[2,2048,256]{2,1,0:T(8,128)(2,1)}, u32[]{:S(2)}, u32[]{:S(2)}) collective-permute-start(bf16[2,2048,256]{2,1,0:T(8,128)(2,1)} %pad_maximum_fusion.1), channel_id=1, source_target_pairs={{0,1},{1,0},{2,3},{3,2},{4,5},{5,4},{6,7},{7,6},{8,9},{9,8},{10,11... | collective-permute-start | bytes 6291464 | tf_op jit(solution)/shard_map/ppermute | solution.py:19
  178.7 5.8 %copy-start.42 = (s32[1,2]{1,0:T(1,128)S(1)}, s32[1,2]{1,0:T(1,128)}, u32[]{:S(2)}) copy-start(s32[1,2]{1,0:T(1,128)} %param.15) | copy-start | bytes 28
  186.8 18.5 %copy-start.36 = (pred[256]{0:T(512)(128)(4,1)}, pred[256]{0:T(512)(128)(4,1)S(1)}, u32[]{:S(2)}) copy-start(pred[256]{0:T(512)(128)(4,1)S(1)} %get-tuple-element.58) | copy-start | bytes 772
  186.8 226.1 %reduce-scatter.2.cloned.1.call-start = ((), (), s32[]{:S(2)}) async-start(), calls=%async_computation.3 | async-start | bytes 5242880 | tf_op jit(solution)/shard_map/reduce_scatter | solution.py:202
  187.1 4.0 copy-start
  191.7 3.6 copy-start.30
  196.0 4.0 copy-start.1
  200.1 3.8 copy-start.11
  200.1 3.8 copy-start.38
  201.9 3.4 copy-start.9
  206.8 4.1 copy-start.4
  240.2 2.5 copy-start.12
  240.2 2.5 copy-start.39
  240.2 3.8 copy-start.21
  242.7 3.1 copy-start.13
  242.7 1.8 copy-start.20
  242.7 2.1 copy-start.25
  242.7 2.1 copy-start.33
  242.7 2.1 copy-start.43
  242.7 2.1 copy-start.46
  244.8 0.9 copy-start.31
  280.3 3.4 copy-start.5
  297.7 1.0 copy-start.18
  302.4 7.5 %copy-start.44 = (f32[1,128]{1,0:T(1,128)S(1)}, f32[1,128]{1,0:T(1,128)}, u32[]{:S(2)}) copy-start(f32[1,128]{1,0:T(1,128)} %param.22) | copy-start | bytes 1540
  313.5 2.5 copy-start.10
  313.5 2.5 copy-start.37
  313.5 3.7 copy-start.22
  316.0 3.2 copy-start.15
  316.0 1.7 copy-start.19
  316.0 2.0 copy-start.26
  316.0 2.0 copy-start.34
  316.0 2.0 copy-start.45
  316.0 2.0 copy-start.47
  318.1 1.1 copy-start.32
  318.1 1.3 copy-start.35
  318.1 1.3 copy-start.28
  320.3 1.6 copy-start.29
  321.3 1.0 copy-start.27
  322.3 2.5 copy-start.8
  337.5 3.5 copy-start.2
  342.6 7.2 %collective-permute-start.9 = (bf16[2,2048,512]{1,2,0:T(8,128)(2,1)S(1)}, bf16[2,2048,512]{1,2,0:T(8,128)(2,1)S(1)}, u32[]{:S(2)}, u32[]{:S(2)}) collective-permute-start(bf16[2,2048,512]{1,2,0:T(8,128)(2,1)S(1)} %pad_maximum_fusion), channel_id=1, source_target_pairs={{0,1},{1,0},{2,3},{3,2},{4,5},{5,4},{6,7},{7,6},{8,9},{9,8},{10,11... | collective-permute-start | bytes 12582920 | tf_op jit(solution)/shard_map/ppermute | solution.py:19
  343.6 10.9 %copy-start.14 = (bf16[2,4,256,256]{2,3,1,0:T(8,128)(2,1)S(1)}, bf16[2,4,256,256]{2,3,1,0:T(8,128)(2,1)}, u32[]{:S(2)}) copy-start(bf16[2,4,256,256]{2,3,1,0:T(8,128)(2,1)} %copy-done.13) | copy-start | bytes 3145732
  349.8 2.6 copy-start.17
  352.4 4.4 copy-start.16
  352.4 61.9 %collective-permute-start.10 = (bf16[1,2048,512]{1,2,0:T(8,128)(2,1)}, bf16[1,2048,512]{1,2,0:T(8,128)(2,1)}, u32[]{:S(2)}, u32[]{:S(2)}) collective-permute-start(bf16[1,2048,512]{1,2,0:T(8,128)(2,1)} %add_convert_fusion), channel_id=1, source_target_pairs={{0,2},{1,3},{2,0},{3,1},{4,6},{5,7},{6,4},{7,5},{8,10},{9,11},{10,... | collective-permute-start | bytes 6291464 | tf_op jit(solution)/shard_map/ppermute | solution.py:19
  355.6 1.8 copy-start.40
  357.4 2.6 copy-start.3
  412.9 25.3 %collective-permute-start.8 = (bf16[256,2048]{1,0:T(8,128)(2,1)}, bf16[256,2048]{1,0:T(8,128)(2,1)}, u32[]{:S(2)}, u32[]{:S(2)}) collective-permute-start(bf16[256,2048]{1,0:T(8,128)(2,1)} %reduce-scatter.2.cloned.1.call-done), channel_id=1, source_target_pairs={{0,16},{16,0},{1,17},{17,1},{2,18},{18,2},{3,19},{19,3},{4,20},{20... | collective-permute-start | bytes 3145736 | tf_op jit(solution)/shard_map/ppermute | solution.py:13
  418.0 20.1 %copy-start.24 = (bf16[256,2048]{1,0:T(8,128)(2,1)S(1)}, bf16[256,2048]{1,0:T(8,128)(2,1)}, u32[]{:S(2)}) copy-start(bf16[256,2048]{1,0:T(8,128)(2,1)} %reduce-scatter.2.cloned.1.call-done) | copy-start | bytes 3145732
Sparse Core Ops, SparseCore 0:
  36.0 81.2 all-gather.8
  119.5 79.2 all-gather.4
  201.0 79.2 all-gather.6
  337.6 75.2 reduce-scatter.1

commit v13 on v3

--- a/solution.py
+++ b/solution.py
@@ -60,9 +60,11 @@
     return lax.optimization_barrier(values.astype(jnp.bfloat16)).astype(jnp.float32)
 
 
-def attend(queries, keys_raw, values_raw, key_norm, usable, present, gate_value):
-    keys = rounded(norm_rows(keys_raw, key_norm))
-    values = rounded(values_raw)
+def prepare(keys_raw, values_raw, key_norm):
+    return rounded(norm_rows(keys_raw, key_norm)), rounded(values_raw)
+
+
+def attend(queries, keys, values, usable, present, gate_value):
     text_rows, heads, depth = queries.shape
     groups = keys.shape[1]
     grouped = queries.astype(jnp.float32).reshape(text_rows, groups, heads // groups, depth)
@@ -124,6 +126,9 @@
     keys_raw = keys_raw.reshape(slot_rows, width_k // HD, HD)
     values_raw = values_raw.reshape(slot_rows, width_k // HD, HD)
     usable = jnp.arange(slot_rows) < tile_counts[0, wanted] * TILE_ROWS
+    (keys, values), prepare_back = jax.vjp(
+        lambda keys_in, values_in: prepare(keys_in, values_in, key_gain[0]), keys_raw, values_raw
+    )
 
     arrived = shifted(text_in, "section", 1)
     text_rows = text_in.shape[2]
@@ -155,9 +160,9 @@
         present = lower + jnp.arange(rows) < lengths[0, 0]
 
         def forward(keys_in, values_in):
-            return attend(queries, keys_in, values_in, key_gain[0], usable, present, cross_gate[0])
-
-        context, pullback = jax.vjp(forward, keys_raw, values_raw)
+            return attend(queries, keys_in, values_in, usable, present, cross_gate[0])
+
+        context, pullback = jax.vjp(forward, keys, values)
         contexts.append(context.astype(jnp.bfloat16))
         key_part, value_part = pullback(context_grad[0, 0, lower : lower + rows].astype(jnp.float32))
         key_back = key_part if key_back is None else key_back + key_part
@@ -167,6 +172,7 @@
                 (gathered[chunk + 1], key_back, value_back)
             )
     gated_context = jnp.concatenate(contexts, axis=0).reshape(1, 1, text_rows, width_q)
+    key_back, value_back = prepare_back((key_back, value_back))
     key_flat = key_back.reshape(slot_rows, width_k).astype(jnp.bfloat16)
     value_flat = value_back.reshape(slot_rows, width_k).astype(jnp.bfloat16)
 

time: 442 us -> 444 us (level)
  matrix products: 70.8 us -> 76.3 us
    all_gather x2, waiting for transfers between devices: 42.9 us -> 51.8 us  [per_device(): lax.all_gather(arrived[:, :, chunk * rows:(chunk + 1) * rows], 'mp', axis...]
    ppermute x8, waiting for transfers between devices: 84.5 us -> 76.7 us  [swapped(): return lax.ppermute(value, axis, pairs)]
    ppermute x3, waiting for transfers between devices: 83.8 us -> 78.9 us  [shifted(): return lax.ppermute(value, axis, pairs)]
    unnamed x110 -> x92, local copies, waits for them, and re-layouts: 10.3 us -> 11 us
  transfers between devices with their start and end apart: 15 -> 15, of which waited for: 9 -> 9; matrix products, arithmetic and copies ran while one was open for 20% -> 21% of each run, Pallas kernels for 0% -> 0%
where the time goes in v13:
time: 444 us; the launch traced here: 441 us
  waiting for transfers between devices  259 us (58%)
  matrix products  76.3 us (17%)
  other arithmetic  45.2 us (10%)
  local copies, waits for them, and re-layouts  27.3 us (6%)
  between operations  19.4 us (4%)
  starting transfers between devices  14 us (3%)
    ppermute x3, waiting for transfers between devices, shifted(): return lax.ppermute(value, axis, pairs)  78.9 us
    ppermute x8, waiting for transfers between devices, swapped(): return lax.ppermute(value, axis, pairs)  76.7 us
    all_gather x2, waiting for transfers between devices, per_device(): lax.all_gather(arrived[:, :, chunk * rows:(chunk + 1) * rows], 'mp', axis...  51.8 us
    reduce_scatter x1, waiting for transfers between devices, per_device(): lax.psum_scatter(partial_sum, 'mp', scatter_dimension=1, tiled=True)  51.2 us
    dot_general x8, matrix products, per_device(): jnp.dot(columns_of(normed, (dp_index ^ code) * block_rows, block_rows), b...  23.9 us
    another operation x3, other arithmetic, gather_blocks(): arrived = swapped(jnp.stack([held[c] for c in codes]), axis, mask)  11.8 us
    unnamed x92, local copies, waits for them, and re-layouts  11 us
  transfers between devices with their start and end apart: 15, of which 9 were waited for; matrix products, arithmetic and copies ran while one was open for 21% of the time, Pallas kernels for 0%

profile of v13, /device:TPU:0, one launch (start us, length us, event | category | flops | bytes accessed | tf_op | source)
XLA Modules:
  0.0 440.9 jit_solution(3456379352924882144)
XLA Ops:
  7.2 3.0 collective-permute-start
  12.2 21.3 %collective-permute-done = bf16[1,1,256,2048]{3,2,1,0:T(8,128)(2,1)S(1)} collective-permute-done((bf16[1,1,256,2048]{3,2,1,0:T(8,128)(2,1)}, bf16[1,1,256,2048]{3,2,1,0:T(8,128)(2,1)S(1)}, u32[]{:S(2)}, u32[]{:S(2)}) %collective-permute-start) | collective-permute-done | bytes 1048608 | tf_op jit(solution)/shard_map/ppermute | solution.py:13
  34.7 1.8 collective-permute-start.5
  36.5 2.7 collective-permute-start.6
  39.3 42.5 %collective-permute-done.5 = bf16[1,1,512,2048]{3,2,1,0:T(8,128)(2,1)S(1)} collective-permute-done((bf16[1,1,512,2048]{3,2,1,0:T(8,128)(2,1)}, bf16[1,1,512,2048]{3,2,1,0:T(8,128)(2,1)S(1)}, u32[]{:S(2)}, u32[]{:S(2)}) %collective-permute-start.5) | collective-permute-done | bytes 2097184 | tf_op jit(solution)/shard_map/ppermute | solution.py:13
  81.8 1.6 fusion.225
  83.5 1.5 collective-permute-start.3
  85.0 46.1 %collective-permute-done.6 = bf16[1,2048,1024]{2,1,0:T(8,128)(2,1)} collective-permute-done((bf16[1,2048,1024]{2,1,0:T(8,128)(2,1)}, bf16[1,2048,1024]{2,1,0:T(8,128)(2,1)}, u32[]{:S(2)}, u32[]{:S(2)}) %collective-permute-start.6) | collective-permute-done | bytes 4194336 | tf_op jit(solution)/shard_map/ppermute | solution.py:19
  131.1 7.5 %pad_maximum_fusion = bf16[2,2048,1024]{2,1,0:T(8,128)(2,1)} fusion(bf16[1,2048,1024]{2,1,0:T(8,128)(2,1)} %collective-permute-done.6, bf16[1,2048,1024]{2,1,0:T(8,128)(2,1)} %param.19), kind=kLoop, calls=%fused_computation.12 | loop fusion | flops 4194304 | bytes 16777216 | tf_op jit(solution)/shard_map/stack | solution.py:36
  138.6 11.8 %collective-permute-done.3 = bf16[1,2048,256]{2,1,0:T(8,128)(2,1)S(1)} collective-permute-done((bf16[1,2048,256]{2,1,0:T(8,128)(2,1)S(1)}, bf16[1,2048,256]{2,1,0:T(8,128)(2,1)S(1)}, u32[]{:S(2)}, u32[]{:S(2)}) %collective-permute-start.3) | collective-permute-done | bytes 1048608 | tf_op jit(solution)/shard_map/ppermute | solution.py:19
  150.4 1.5 pad_maximum_fusion.3
  151.9 1.5 collective-permute-start.1
  156.0 2.8 slice_convert_fusion
  158.8 2.6 copy.148
  161.3 2.6 copy.151
  165.1 12.5 %collective-permute-done.1 = bf16[1,2048,256]{2,1,0:T(8,128)(2,1)S(1)} collective-permute-done((bf16[1,2048,256]{2,1,0:T(8,128)(2,1)}, bf16[1,2048,256]{2,1,0:T(8,128)(2,1)S(1)}, u32[]{:S(2)}, u32[]{:S(2)}) %collective-permute-start.1) | collective-permute-done | bytes 1048608 | tf_op jit(solution)/shard_map/ppermute | solution.py:19
  177.7 2.8 pad_maximum_fusion.2
  181.5 1.9 fusion.78
  183.4 2.1 fusion.85
  186.1 1.8 multiply_reduce_fusion.1
  188.8 2.3 fusion.95
  191.1 2.2 fusion.87
  193.3 1.9 convolution_add_fusion.7
  195.2 1.8 fusion.72
  197.0 1.5 convolution_convert_fusion.9
  198.5 1.5 convolution_convert_fusion.8
  199.9 3.3 fusion.2
  206.8 3.9 fusion.11
  210.8 3.5 fusion.20
  214.2 3.5 fusion.63
  217.8 1.4 reshape.213
  220.4 3.7 fusion.227
  224.2 2.4 divide_convert_fusion.1
  227.9 1.6 fusion.64
  229.5 51.8 %all-gather.7.cloned.1.call-done = bf16[1,1,256,8192]{3,2,1,0:T(8,128)(2,1)} async-done(((bf16[1,1,256,2048]{3,2,1,0:T(8,128)(2,1)}), bf16[1,1,256,8192]{3,2,1,0:T(8,128)(2,1)}) %all-gather.7.cloned.1.call-update) | async-done | bytes 4194320 | tf_op jit(solution)/shard_map/all_gather | solution.py:142
  281.3 3.3 fusion.5
  288.2 3.5 fusion.19
  291.7 3.5 fusion.59
  295.2 3.5 fusion.62
  299.7 1.4 reshape.214
  301.2 1.4 copy.155
  303.1 3.7 fusion.232
  306.8 2.4 fusion.44
  310.6 1.9 add_convert_fusion.2
  315.1 2.5 broadcast_in_dim.91
  317.6 2.7 fusion.22
  320.8 1.7 fusion.135
  322.5 1.7 fusion.136
  324.2 1.5 fusion.24
  325.7 2.7 fusion.26
  328.4 2.7 fusion.28
  331.2 1.8 convolution_convert_fusion.2
  333.0 1.7 convolution_convert_fusion.4
  337.5 6.2 %collective-permute-done.9 = bf16[2,2048,512]{1,2,0:T(8,128)(2,1)S(1)} collective-permute-done((bf16[2,2048,512]{1,2,0:T(8,128)(2,1)S(1)}, bf16[2,2048,512]{1,2,0:T(8,128)(2,1)S(1)}, u32[]{:S(2)}, u32[]{:S(2)}) %collective-permute-start.9) | collective-permute-done | bytes 4194336 | tf_op jit(solution)/shard_map/ppermute | solution.py:19
  343.7 2.0 copy-done.18
  345.7 2.2 add_convert_fusion
  347.9 1.5 collective-permute-start.10
  354.0 1.4 convolution_convert_fusion.7
  355.4 51.2 %reduce-scatter.2.cloned.1.call-done = bf16[256,2048]{1,0:T(8,128)(2,1)} async-done(((bf16[256,8192]{1,0:T(8,128)(2,1)}), bf16[256,2048]{1,0:T(8,128)(2,1)}) %reduce-scatter.2.cloned.1.call-update) | async-done | bytes 1048592 | tf_op jit(solution)/shard_map/reduce_scatter | solution.py:189
  406.6 1.5 collective-permute-start.8
  408.1 3.9 fusion.8
  413.2 2.3 copy.130
  416.8 15.1 %collective-permute-done.8 = bf16[256,2048]{1,0:T(8,128)(2,1)} collective-permute-done((bf16[256,2048]{1,0:T(8,128)(2,1)}, bf16[256,2048]{1,0:T(8,128)(2,1)}, u32[]{:S(2)}, u32[]{:S(2)}) %collective-permute-start.8) | collective-permute-done | bytes 1048608 | tf_op jit(solution)/shard_map/ppermute | solution.py:13
  431.9 2.3 select_bitcast_fusion
  (159 shorter events, 30.2 us)
Async XLA Ops:
  7.2 174.3 %all-gather.9.cloned.1.call-start = ((), (), s32[]{:S(2)}) async-start(), calls=%async_computation.4 | async-start | bytes 5242880 | tf_op jit(solution)/shard_map/all_gather | solution.py:115
  7.2 26.4 %collective-permute-start = (bf16[1,1,256,2048]{3,2,1,0:T(8,128)(2,1)}, bf16[1,1,256,2048]{3,2,1,0:T(8,128)(2,1)S(1)}, u32[]{:S(2)}, u32[]{:S(2)}) collective-permute-start(bf16[1,1,256,2048]{3,2,1,0:T(8,128)(2,1)} %param.14), channel_id=1, source_target_pairs={{0,16},{16,0},{1,17},{17,1},{2,18},{18,2},{3,19},{19,3},{4,20},{20... | collective-permute-start | bytes 3145736 | tf_op jit(solution)/shard_map/ppermute | solution.py:13
  12.2 71.2 %copy-start.6 = (bf16[1,2048,256]{2,1,0:T(8,128)(2,1)S(1)}, bf16[1,2048,256]{2,1,0:T(8,128)(2,1)}, u32[]{:S(2)}) copy-start(bf16[1,2048,256]{2,1,0:T(8,128)(2,1)} %param.20) | copy-start | bytes 3145732
  34.7 165.2 %all-gather.5.cloned.1.call-start = ((), (), s32[]{:S(2)}) async-start(), calls=%async_computation.1 | async-start | bytes 5242880 | tf_op jit(solution)/shard_map/all_gather | solution.py:142
  34.7 47.1 %collective-permute-start.5 = (bf16[1,1,512,2048]{3,2,1,0:T(8,128)(2,1)}, bf16[1,1,512,2048]{3,2,1,0:T(8,128)(2,1)S(1)}, u32[]{:S(2)}, u32[]{:S(2)}) collective-permute-start(bf16[1,1,512,2048]{3,2,1,0:T(8,128)(2,1)} %param.13), channel_id=1, source_target_pairs={{0,16},{16,0},{1,17},{17,1},{2,18},{18,2},{3,19},{19,3},{4,20},{20... | collective-permute-start | bytes 6291464 | tf_op jit(solution)/shard_map/ppermute | solution.py:13
  36.5 94.5 %collective-permute-start.6 = (bf16[1,2048,1024]{2,1,0:T(8,128)(2,1)}, bf16[1,2048,1024]{2,1,0:T(8,128)(2,1)}, u32[]{:S(2)}, u32[]{:S(2)}) collective-permute-start(bf16[1,2048,1024]{2,1,0:T(8,128)(2,1)} %param.19), channel_id=1, source_target_pairs={{0,2},{1,3},{2,0},{3,1},{4,6},{5,7},{6,4},{7,5},{8,10},{9,11},{10,... | collective-permute-start | bytes 12582920 | tf_op jit(solution)/shard_map/ppermute | solution.py:19
  83.4 197.8 %all-gather.7.cloned.1.call-start = ((), (), s32[]{:S(2)}) async-start(), calls=%async_computation.2 | async-start | bytes 5242880 | tf_op jit(solution)/shard_map/all_gather | solution.py:142
  83.5 66.9 %collective-permute-start.3 = (bf16[1,2048,256]{2,1,0:T(8,128)(2,1)S(1)}, bf16[1,2048,256]{2,1,0:T(8,128)(2,1)S(1)}, u32[]{:S(2)}, u32[]{:S(2)}) collective-permute-start(bf16[1,2048,256]{2,1,0:T(8,128)(2,1)S(1)} %copy-done.6), channel_id=1, source_target_pairs={{0,2},{1,3},{2,0},{3,1},{4,6},{5,7},{6,4},{7,5},{8,10},{9,11},{10,... | collective-permute-start | bytes 3145736 | tf_op jit(solution)/shard_map/ppermute | solution.py:19
  138.6 72.2 %collective-permute-start.7 = (bf16[2,2048,1024]{2,1,0:T(8,128)(2,1)}, bf16[2,2048,1024]{2,1,0:T(8,128)(2,1)}, u32[]{:S(2)}, u32[]{:S(2)}) collective-permute-start(bf16[2,2048,1024]{2,1,0:T(8,128)(2,1)} %pad_maximum_fusion), channel_id=1, source_target_pairs={{0,1},{1,0},{2,3},{3,2},{4,5},{5,4},{6,7},{7,6},{8,9},{9,8},{10,11... | collective-permute-start | bytes 25165832 | tf_op jit(solution)/shard_map/ppermute | solution.py:19
  151.9 12.7 %copy-start.38 = (s32[1,2]{1,0:T(1,128)S(1)}, s32[1,2]{1,0:T(1,128)}, u32[]{:S(2)}) copy-start(s32[1,2]{1,0:T(1,128)} %param.15) | copy-start | bytes 28
  151.9 31.5 %collective-permute-start.4 = (bf16[2,2048,256]{2,1,0:T(8,128)(2,1)}, bf16[2,2048,256]{2,1,0:T(8,128)(2,1)}, u32[]{:S(2)}, u32[]{:S(2)}) collective-permute-start(bf16[2,2048,256]{2,1,0:T(8,128)(2,1)} %pad_maximum_fusion.3), channel_id=1, source_target_pairs={{0,1},{1,0},{2,3},{3,2},{4,5},{5,4},{6,7},{7,6},{8,9},{9,8},{10,11... | collective-permute-start | bytes 6291464 | tf_op jit(solution)/shard_map/ppermute | solution.py:19
  151.9 25.8 %collective-permute-start.1 = (bf16[1,2048,256]{2,1,0:T(8,128)(2,1)}, bf16[1,2048,256]{2,1,0:T(8,128)(2,1)S(1)}, u32[]{:S(2)}, u32[]{:S(2)}) collective-permute-start(bf16[1,2048,256]{2,1,0:T(8,128)(2,1)} %param.21), channel_id=1, source_target_pairs={{0,2},{1,3},{2,0},{3,1},{4,6},{5,7},{6,4},{7,5},{8,10},{9,11},{10,... | collective-permute-start | bytes 3145736 | tf_op jit(solution)/shard_map/ppermute | solution.py:19
  180.5 10.7 %collective-permute-start.2 = (bf16[2,2048,256]{2,1,0:T(8,128)(2,1)}, bf16[2,2048,256]{2,1,0:T(8,128)(2,1)}, u32[]{:S(2)}, u32[]{:S(2)}) collective-permute-start(bf16[2,2048,256]{2,1,0:T(8,128)(2,1)} %pad_maximum_fusion.2), channel_id=1, source_target_pairs={{0,1},{1,0},{2,3},{3,2},{4,5},{5,4},{6,7},{7,6},{8,9},{9,8},{10,11... | collective-permute-start | bytes 6291464 | tf_op jit(solution)/shard_map/ppermute | solution.py:19
  181.1 46.7 %copy-start.41 = (pred[256]{0:T(512)(128)(4,1)}, pred[256]{0:T(512)(128)(4,1)S(1)}, u32[]{:S(2)}) copy-start(pred[256]{0:T(512)(128)(4,1)S(1)} %iota_compare_fusion) | copy-start | bytes 772
  181.2 45.5 %copy-start.36 = (pred[256]{0:T(512)(128)(4,1)}, pred[256]{0:T(512)(128)(4,1)S(1)}, u32[]{:S(2)}) copy-start(pred[256]{0:T(512)(128)(4,1)S(1)} %iota_compare_fusion.1) | copy-start | bytes 772
  181.2 17.3 %copy-start.34 = (pred[256]{0:T(512)(128)(4,1)}, pred[256]{0:T(512)(128)(4,1)S(1)}, u32[]{:S(2)}) copy-start(pred[256]{0:T(512)(128)(4,1)S(1)} %add_compare_fusion) | copy-start | bytes 772
  181.2 225.4 %reduce-scatter.2.cloned.1.call-start = ((), (), s32[]{:S(2)}) async-start(), calls=%async_computation.3 | async-start | bytes 5242880 | tf_op jit(solution)/shard_map/reduce_scatter | solution.py:189
  181.5 4.0 copy-start
  183.4 4.6 %copy-start.32 = (f32[1,128]{1,0:T(1,128)S(1)}, f32[1,128]{1,0:T(1,128)}, u32[]{:S(2)}) copy-start(f32[1,128]{1,0:T(1,128)} %param.23) | copy-start | bytes 1540
  188.0 9.0 %copy-start.16 = (f32[256,2,128]{2,0,1:T(8,128)}, f32[256,2,128]{2,0,1:T(8,128)S(1)}, u32[]{:S(2)}) copy-start(f32[256,2,128]{2,0,1:T(8,128)S(1)} %copy.108) | copy-start | bytes 786436
  188.0 5.3 %copy-start.1 = (bf16[1,1,256,8192]{3,2,1,0:T(8,128)(2,1)S(1)}, bf16[1,1,256,8192]{3,2,1,0:T(8,128)(2,1)}, u32[]{:S(2)}) copy-start(bf16[1,1,256,8192]{3,2,1,0:T(8,128)(2,1)} %all-gather.9.cloned.1.call-done) | copy-start | bytes 12582916
  191.1 5.9 %copy-start.10 = (f32[1,1,256,1024]{2,3,1,0:T(8,128)S(1)}, f32[1,1,256,1024]{2,3,1,0:T(8,128)}, u32[]{:S(2)}) copy-start(f32[1,1,256,1024]{2,3,1,0:T(8,128)} %copy.148) | copy-start | bytes 3145732
  193.3 5.2 %copy-start.8 = (f32[1,1,256,1024]{2,3,1,0:T(8,128)S(1)}, f32[1,1,256,1024]{2,3,1,0:T(8,128)}, u32[]{:S(2)}) copy-start(f32[1,1,256,1024]{2,3,1,0:T(8,128)} %copy.151) | copy-start | bytes 3145732
  197.0 6.2 %copy-start.29 = (f32[1,8192]{1,0:T(1,128)S(1)}, f32[1,8192]{1,0:T(1,128)}, u32[]{:S(2)}) copy-start(f32[1,8192]{1,0:T(1,128)} %param.18) | copy-start | bytes 98308
  199.9 3.4 copy-start.4
  203.4 2.2 copy-start.21
  217.8 2.6 copy-start.39
  220.4 6.3 %copy-start.11 = (f32[1,1,256,1024]{2,3,1,0:T(8,128)S(1)}, f32[1,1,256,1024]{2,3,1,0:T(8,128)}, u32[]{:S(2)}) copy-start(f32[1,1,256,1024]{2,3,1,0:T(8,128)} %copy.148) | copy-start | bytes 3145732
  224.1 3.7 copy-start.20
  224.1 3.7 copy-start.24
  224.1 3.7 copy-start.28
  226.6 1.2 copy-start.12
  281.3 3.4 copy-start.5
  284.7 2.2 copy-start.22
  298.7 4.4 copy-start.30
  303.0 6.2 %copy-start.31 = (f32[256,2,4]{0,2,1:T(4,128)}, f32[256,2,4]{0,2,1:T(4,128)S(1)}, u32[]{:S(2)}) copy-start(f32[256,2,4]{0,2,1:T(4,128)S(1)} %rsqrt.54) | copy-start | bytes 24580
  303.1 6.2 %copy-start.9 = (f32[1,1,256,1024]{2,3,1,0:T(8,128)S(1)}, f32[1,1,256,1024]{2,3,1,0:T(8,128)}, u32[]{:S(2)}) copy-start(f32[1,1,256,1024]{2,3,1,0:T(8,128)} %copy.151) | copy-start | bytes 3145732
  306.8 2.5 copy-start.25
  306.8 3.8 copy-start.19
  306.8 3.8 copy-start.23
  306.8 3.8 copy-start.27
  306.8 3.8 copy-start.40
  306.8 3.8 copy-start.42
  306.8 3.8 copy-start.43
  309.3 3.2 copy-start.14
  310.6 1.9 copy-start.17
  310.6 1.9 copy-start.33
  310.6 4.0 copy-start.7
  331.2 3.5 copy-start.2
  336.4 7.2 %collective-permute-start.9 = (bf16[2,2048,512]{1,2,0:T(8,128)(2,1)S(1)}, bf16[2,2048,512]{1,2,0:T(8,128)(2,1)S(1)}, u32[]{:S(2)}, u32[]{:S(2)}) collective-permute-start(bf16[2,2048,512]{1,2,0:T(8,128)(2,1)S(1)} %pad_maximum_fusion.1), channel_id=1, source_target_pairs={{0,1},{1,0},{2,3},{3,2},{4,5},{5,4},{6,7},{7,6},{8,9},{9,8},{10,11... | collective-permute-start | bytes 12582920 | tf_op jit(solution)/shard_map/ppermute | solution.py:19
  337.0 12.9 %copy-start.13 = (bf16[2,4,256,256]{2,3,1,0:T(8,128)(2,1)S(1)}, bf16[2,4,256,256]{2,3,1,0:T(8,128)(2,1)}, u32[]{:S(2)}) copy-start(bf16[2,4,256,256]{2,3,1,0:T(8,128)(2,1)} %copy-done.12) | copy-start | bytes 3145732
  337.5 13.0 %copy-start.15 = (bf16[2,4,256,256]{2,3,1,0:T(8,128)(2,1)S(1)}, bf16[2,4,256,256]{2,3,1,0:T(8,128)(2,1)}, u32[]{:S(2)}) copy-start(bf16[2,4,256,256]{2,3,1,0:T(8,128)(2,1)} %copy-done.14) | copy-start | bytes 3145732
  343.7 2.0 copy-start.18
  347.8 3.1 copy-start.35
  347.8 3.1 copy-start.37
  347.9 60.2 %collective-permute-start.10 = (bf16[1,2048,512]{1,2,0:T(8,128)(2,1)}, bf16[1,2048,512]{1,2,0:T(8,128)(2,1)}, u32[]{:S(2)}, u32[]{:S(2)}) collective-permute-start(bf16[1,2048,512]{1,2,0:T(8,128)(2,1)} %add_convert_fusion), channel_id=1, source_target_pairs={{0,2},{1,3},{2,0},{3,1},{4,6},{5,7},{6,4},{7,5},{8,10},{9,11},{10,... | collective-permute-start | bytes 6291464 | tf_op jit(solution)/shard_map/ppermute | solution.py:19
  351.0 2.6 copy-start.3
  406.6 25.2 %collective-permute-start.8 = (bf16[256,2048]{1,0:T(8,128)(2,1)}, bf16[256,2048]{1,0:T(8,128)(2,1)}, u32[]{:S(2)}, u32[]{:S(2)}) collective-permute-start(bf16[256,2048]{1,0:T(8,128)(2,1)} %reduce-scatter.2.cloned.1.call-done), channel_id=1, source_target_pairs={{0,16},{16,0},{1,17},{17,1},{2,18},{18,2},{3,19},{19,3},{4,20},{20... | collective-permute-start | bytes 3145736 | tf_op jit(solution)/shard_map/ppermute | solution.py:13
  413.2 18.7 %copy-start.26 = (bf16[256,2048]{1,0:T(8,128)(2,1)S(1)}, bf16[256,2048]{1,0:T(8,128)(2,1)}, u32[]{:S(2)}) copy-start(bf16[256,2048]{1,0:T(8,128)(2,1)} %reduce-scatter.2.cloned.1.call-done) | copy-start | bytes 3145732
Sparse Core Ops, SparseCore 0:
  34.8 83.4 all-gather.8
  120.5 79.2 all-gather.4
  201.9 79.2 all-gather.6
  331.3 75.2 reduce-scatter.1

commit v14 on v13

--- a/solution.py
+++ b/solution.py
@@ -177,15 +177,19 @@
     value_flat = value_back.reshape(slot_rows, width_k).astype(jnp.bfloat16)
 
     contract = (((1,), (1,)), ((), ()))
-    partial_sum = jnp.zeros((slot_rows, image.shape[1]), jnp.bfloat16)
-    for code in key_blocks:
+    dp_count = lax.axis_size("dp")
+    terms = []
+    for code in range(dp_count):
         term = lax.dot_general(key_flat, key_blocks[code], contract, preferred_element_type=jnp.float32)
         term = term + lax.dot_general(
             value_flat, value_blocks[code], contract, preferred_element_type=jnp.float32
         )
-        partial_sum = lax.dynamic_update_slice_in_dim(
-            partial_sum, term.astype(jnp.bfloat16), (dp_index ^ code) * block_rows, axis=1
-        )
+        terms.append(term.astype(jnp.bfloat16))
+    in_code_order = jnp.concatenate(terms, axis=1)
+    partial_sum = jnp.concatenate(
+        [columns_of(in_code_order, (dp_index ^ block) * block_rows, block_rows) for block in range(dp_count)],
+        axis=1,
+    )
     summed = lax.psum_scatter(partial_sum, "mp", scatter_dimension=1, tiled=True)
 
     routed = summed

time: 444 us -> 442 us (level)
  local copies, waits for them, and re-layouts: 27.3 us -> 22.6 us
    all_gather x2, waiting for transfers between devices: 51.8 us -> 46.5 us  [per_device(): lax.all_gather(arrived[:, :, chunk * rows:(chunk + 1) * rows], 'mp', axis...]
    ppermute x3, waiting for transfers between devices: 78.9 us -> 84.1 us  [shifted(): return lax.ppermute(value, axis, pairs)]
    unnamed x92 -> x94, local copies, waits for them, and re-layouts: 11 us -> 10.7 us
  transfers between devices with their start and end apart: 15 -> 15, of which waited for: 9 -> 9; matrix products, arithmetic and copies ran while one was open for 21% -> 20% of each run, Pallas kernels for 0% -> 0%
where the time goes in v14:
time: 442 us; the launch traced here: 438 us
  waiting for transfers between devices  262 us (59%)
  matrix products  73 us (17%)
  other arithmetic  48.8 us (11%)
  local copies, waits for them, and re-layouts  22.6 us (5%)
  between operations  19.1 us (4%)
  starting transfers between devices  12.8 us (3%)
    ppermute x3, waiting for transfers between devices, shifted(): return lax.ppermute(value, axis, pairs)  84.1 us
    ppermute x8, waiting for transfers between devices, swapped(): return lax.ppermute(value, axis, pairs)  79.5 us
    reduce_scatter x1, waiting for transfers between devices, per_device(): lax.psum_scatter(partial_sum, 'mp', scatter_dimension=1, tiled=True)  51.8 us
    all_gather x2, waiting for transfers between devices, per_device(): lax.all_gather(arrived[:, :, chunk * rows:(chunk + 1) * rows], 'mp', axis...  46.5 us
    dot_general x8, matrix products, per_device(): jnp.dot(columns_of(normed, (dp_index ^ code) * block_rows, block_rows), b...  23.5 us
    another operation x3, other arithmetic, gather_blocks(): arrived = swapped(jnp.stack([held[c] for c in codes]), axis, mask)  12 us
    unnamed x94, local copies, waits for them, and re-layouts  10.7 us
  transfers between devices with their start and end apart: 15, of which 9 were waited for; matrix products, arithmetic and copies ran while one was open for 20% of the time, Pallas kernels for 0%

profile of v14, /device:TPU:0, one launch (start us, length us, event | category | flops | bytes accessed | tf_op | source)
XLA Modules:
  0.0 438.1 jit_solution(9696309473483703232)
XLA Ops:
  7.2 3.0 collective-permute-start
  12.1 21.5 %collective-permute-done = bf16[1,1,256,2048]{3,2,1,0:T(8,128)(2,1)S(1)} collective-permute-done((bf16[1,1,256,2048]{3,2,1,0:T(8,128)(2,1)}, bf16[1,1,256,2048]{3,2,1,0:T(8,128)(2,1)S(1)}, u32[]{:S(2)}, u32[]{:S(2)}) %collective-permute-start) | collective-permute-done | bytes 1048608 | tf_op jit(solution)/shard_map/ppermute | solution.py:13
  34.7 1.8 collective-permute-start.5
  36.5 1.5 collective-permute-start.6
  38.1 45.0 %collective-permute-done.5 = bf16[1,1,512,2048]{3,2,1,0:T(8,128)(2,1)S(1)} collective-permute-done((bf16[1,1,512,2048]{3,2,1,0:T(8,128)(2,1)}, bf16[1,1,512,2048]{3,2,1,0:T(8,128)(2,1)S(1)}, u32[]{:S(2)}, u32[]{:S(2)}) %collective-permute-start.5) | collective-permute-done | bytes 2097184 | tf_op jit(solution)/shard_map/ppermute | solution.py:13
  83.1 1.5 fusion.221
  84.6 1.5 collective-permute-start.3
  86.1 44.2 %collective-permute-done.6 = bf16[1,2048,1024]{2,1,0:T(8,128)(2,1)} collective-permute-done((bf16[1,2048,1024]{2,1,0:T(8,128)(2,1)}, bf16[1,2048,1024]{2,1,0:T(8,128)(2,1)}, u32[]{:S(2)}, u32[]{:S(2)}) %collective-permute-start.6) | collective-permute-done | bytes 4194336 | tf_op jit(solution)/shard_map/ppermute | solution.py:19
  130.3 7.5 %pad_maximum_fusion = bf16[2,2048,1024]{2,1,0:T(8,128)(2,1)} fusion(bf16[1,2048,1024]{2,1,0:T(8,128)(2,1)} %collective-permute-done.6, bf16[1,2048,1024]{2,1,0:T(8,128)(2,1)} %param.19), kind=kLoop, calls=%fused_computation.12 | loop fusion | flops 4194304 | bytes 16777216 | tf_op jit(solution)/shard_map/stack | solution.py:36
  137.9 13.7 %collective-permute-done.3 = bf16[1,2048,256]{2,1,0:T(8,128)(2,1)S(1)} collective-permute-done((bf16[1,2048,256]{2,1,0:T(8,128)(2,1)S(1)}, bf16[1,2048,256]{2,1,0:T(8,128)(2,1)S(1)}, u32[]{:S(2)}, u32[]{:S(2)}) %collective-permute-start.3) | collective-permute-done | bytes 1048608 | tf_op jit(solution)/shard_map/ppermute | solution.py:19
  151.6 1.7 pad_maximum_fusion.5
  153.3 1.6 collective-permute-start.1
  157.3 2.4 slice_convert_fusion
  159.7 1.3 copy.148
  161.0 1.6 copy.151
  163.8 15.3 %collective-permute-done.1 = bf16[1,2048,256]{2,1,0:T(8,128)(2,1)S(1)} collective-permute-done((bf16[1,2048,256]{2,1,0:T(8,128)(2,1)}, bf16[1,2048,256]{2,1,0:T(8,128)(2,1)S(1)}, u32[]{:S(2)}, u32[]{:S(2)}) %collective-permute-start.1) | collective-permute-done | bytes 1048608 | tf_op jit(solution)/shard_map/ppermute | solution.py:19
  179.1 2.8 pad_maximum_fusion.4
  183.2 2.2 fusion.74
  185.5 2.1 fusion.81
  188.1 2.5 multiply_reduce_fusion.1
  192.5 2.3 fusion.91
  194.8 2.2 fusion.83
  197.0 1.8 convolution_add_fusion.7
  198.8 1.8 fusion.68
  200.6 1.5 convolution_convert_fusion.9
  202.1 1.5 convolution_convert_fusion.8
  203.6 3.4 fusion.2
  211.3 3.5 fusion.11
  214.8 3.5 fusion.20
  218.3 3.6 fusion.59
  221.9 1.4 reshape.213
  224.5 3.8 fusion.223
  228.3 2.4 divide_convert_fusion.1
  232.0 1.6 fusion.60
  233.6 46.5 %all-gather.7.cloned.1.call-done = bf16[1,1,256,8192]{3,2,1,0:T(8,128)(2,1)} async-done(((bf16[1,1,256,2048]{3,2,1,0:T(8,128)(2,1)}), bf16[1,1,256,8192]{3,2,1,0:T(8,128)(2,1)}) %all-gather.7.cloned.1.call-update) | async-done | bytes 4194320 | tf_op jit(solution)/shard_map/all_gather | solution.py:142
  280.1 3.3 fusion.5
  287.0 3.5 fusion.19
  290.4 3.5 fusion.55
  293.9 3.5 fusion.58
  298.5 1.4 reshape.214
  299.9 1.4 copy.155
  301.8 3.7 fusion.228
  305.6 3.1 fusion.40
  308.8 2.1 add_convert_fusion.2
  313.0 1.8 add_convert_fusion.1
  315.3 1.7 fusion.21
  317.0 1.7 fusion.131
  319.2 1.8 fusion.132
  321.0 1.7 fusion.22
  323.3 1.7 fusion.24
  326.0 2.3 pad_maximum_fusion.2
  328.3 1.8 convolution_convert_fusion.3
  330.2 1.7 convolution_convert_fusion.5
  334.8 6.2 %collective-permute-done.9 = bf16[2,2048,512]{1,2,0:T(8,128)(2,1)S(1)} collective-permute-done((bf16[2,2048,512]{1,2,0:T(8,128)(2,1)S(1)}, bf16[2,2048,512]{1,2,0:T(8,128)(2,1)S(1)}, u32[]{:S(2)}, u32[]{:S(2)}) %collective-permute-start.9) | collective-permute-done | bytes 4194336 | tf_op jit(solution)/shard_map/ppermute | solution.py:19
  341.0 2.1 copy-done.18
  343.0 2.3 add_convert_fusion
  345.3 1.5 collective-permute-start.10
  352.0 51.8 %reduce-scatter.2.cloned.1.call-done = bf16[256,2048]{1,0:T(8,128)(2,1)} async-done(((bf16[256,8192]{1,0:T(8,128)(2,1)}), bf16[256,2048]{1,0:T(8,128)(2,1)}) %reduce-scatter.2.cloned.1.call-update) | async-done | bytes 1048592 | tf_op jit(solution)/shard_map/reduce_scatter | solution.py:193
  403.8 1.5 collective-permute-start.8
  405.2 3.5 fusion.8
  408.9 1.3 copy.130
  410.2 1.3 copy.131
  411.5 17.5 %collective-permute-done.8 = bf16[256,2048]{1,0:T(8,128)(2,1)} collective-permute-done((bf16[256,2048]{1,0:T(8,128)(2,1)}, bf16[256,2048]{1,0:T(8,128)(2,1)}, u32[]{:S(2)}, u32[]{:S(2)}) %collective-permute-start.8) | collective-permute-done | bytes 1048608 | tf_op jit(solution)/shard_map/ppermute | solution.py:13
  429.0 2.3 select_bitcast_fusion
  (163 shorter events, 30.7 us)
Async XLA Ops:
  7.2 176.1 %all-gather.9.cloned.1.call-start = ((), (), s32[]{:S(2)}) async-start(), calls=%async_computation.4 | async-start | bytes 5242880 | tf_op jit(solution)/shard_map/all_gather | solution.py:115
  7.2 26.4 %collective-permute-start = (bf16[1,1,256,2048]{3,2,1,0:T(8,128)(2,1)}, bf16[1,1,256,2048]{3,2,1,0:T(8,128)(2,1)S(1)}, u32[]{:S(2)}, u32[]{:S(2)}) collective-permute-start(bf16[1,1,256,2048]{3,2,1,0:T(8,128)(2,1)} %param.14), channel_id=1, source_target_pairs={{0,16},{16,0},{1,17},{17,1},{2,18},{18,2},{3,19},{19,3},{4,20},{20... | collective-permute-start | bytes 3145736 | tf_op jit(solution)/shard_map/ppermute | solution.py:13
  12.1 72.5 %copy-start.6 = (bf16[1,2048,256]{2,1,0:T(8,128)(2,1)S(1)}, bf16[1,2048,256]{2,1,0:T(8,128)(2,1)}, u32[]{:S(2)}) copy-start(bf16[1,2048,256]{2,1,0:T(8,128)(2,1)} %param.20) | copy-start | bytes 3145732
  34.7 168.9 %all-gather.5.cloned.1.call-start = ((), (), s32[]{:S(2)}) async-start(), calls=%async_computation.1 | async-start | bytes 5242880 | tf_op jit(solution)/shard_map/all_gather | solution.py:142
  34.7 48.3 %collective-permute-start.5 = (bf16[1,1,512,2048]{3,2,1,0:T(8,128)(2,1)}, bf16[1,1,512,2048]{3,2,1,0:T(8,128)(2,1)S(1)}, u32[]{:S(2)}, u32[]{:S(2)}) collective-permute-start(bf16[1,1,512,2048]{3,2,1,0:T(8,128)(2,1)} %param.13), channel_id=1, source_target_pairs={{0,16},{16,0},{1,17},{17,1},{2,18},{18,2},{3,19},{19,3},{4,20},{20... | collective-permute-start | bytes 6291464 | tf_op jit(solution)/shard_map/ppermute | solution.py:13
  36.5 93.8 %collective-permute-start.6 = (bf16[1,2048,1024]{2,1,0:T(8,128)(2,1)}, bf16[1,2048,1024]{2,1,0:T(8,128)(2,1)}, u32[]{:S(2)}, u32[]{:S(2)}) collective-permute-start(bf16[1,2048,1024]{2,1,0:T(8,128)(2,1)} %param.19), channel_id=1, source_target_pairs={{0,2},{1,3},{2,0},{3,1},{4,6},{5,7},{6,4},{7,5},{8,10},{9,11},{10,... | collective-permute-start | bytes 12582920 | tf_op jit(solution)/shard_map/ppermute | solution.py:19
  84.5 195.5 %all-gather.7.cloned.1.call-start = ((), (), s32[]{:S(2)}) async-start(), calls=%async_computation.2 | async-start | bytes 5242880 | tf_op jit(solution)/shard_map/all_gather | solution.py:142
  84.6 67.0 %collective-permute-start.3 = (bf16[1,2048,256]{2,1,0:T(8,128)(2,1)S(1)}, bf16[1,2048,256]{2,1,0:T(8,128)(2,1)S(1)}, u32[]{:S(2)}, u32[]{:S(2)}) collective-permute-start(bf16[1,2048,256]{2,1,0:T(8,128)(2,1)S(1)} %copy-done.6), channel_id=1, source_target_pairs={{0,2},{1,3},{2,0},{3,1},{4,6},{5,7},{6,4},{7,5},{8,10},{9,11},{10,... | collective-permute-start | bytes 3145736 | tf_op jit(solution)/shard_map/ppermute | solution.py:19
  137.9 76.9 %collective-permute-start.7 = (bf16[2,2048,1024]{2,1,0:T(8,128)(2,1)}, bf16[2,2048,1024]{2,1,0:T(8,128)(2,1)}, u32[]{:S(2)}, u32[]{:S(2)}) collective-permute-start(bf16[2,2048,1024]{2,1,0:T(8,128)(2,1)} %pad_maximum_fusion), channel_id=1, source_target_pairs={{0,1},{1,0},{2,3},{3,2},{4,5},{5,4},{6,7},{7,6},{8,9},{9,8},{10,11... | collective-permute-start | bytes 25165832 | tf_op jit(solution)/shard_map/ppermute | solution.py:19
  151.6 1.7 copy-start.11
  153.3 9.9 %copy-start.40 = (s32[1,2]{1,0:T(1,128)S(1)}, s32[1,2]{1,0:T(1,128)}, u32[]{:S(2)}) copy-start(s32[1,2]{1,0:T(1,128)} %param.15) | copy-start | bytes 28
  153.3 32.2 %collective-permute-start.4 = (bf16[2,2048,256]{2,1,0:T(8,128)(2,1)}, bf16[2,2048,256]{2,1,0:T(8,128)(2,1)}, u32[]{:S(2)}, u32[]{:S(2)}) collective-permute-start(bf16[2,2048,256]{2,1,0:T(8,128)(2,1)} %pad_maximum_fusion.5), channel_id=1, source_target_pairs={{0,1},{1,0},{2,3},{3,2},{4,5},{5,4},{6,7},{7,6},{8,9},{9,8},{10,11... | collective-permute-start | bytes 6291464 | tf_op jit(solution)/shard_map/ppermute | solution.py:19
  153.3 25.8 %collective-permute-start.1 = (bf16[1,2048,256]{2,1,0:T(8,128)(2,1)}, bf16[1,2048,256]{2,1,0:T(8,128)(2,1)S(1)}, u32[]{:S(2)}, u32[]{:S(2)}) collective-permute-start(bf16[1,2048,256]{2,1,0:T(8,128)(2,1)} %param.21), channel_id=1, source_target_pairs={{0,2},{1,3},{2,0},{3,1},{4,6},{5,7},{6,4},{7,5},{8,10},{9,11},{10,... | collective-permute-start | bytes 3145736 | tf_op jit(solution)/shard_map/ppermute | solution.py:19
  162.6 39.5 %copy-start.7 = (f32[1,1,256,1024]{2,3,1,0:T(8,128)}, f32[1,1,256,1024]{2,3,1,0:T(8,128)S(1)}, u32[]{:S(2)}) copy-start(f32[1,1,256,1024]{2,3,1,0:T(8,128)S(1)} %copy.151) | copy-start | bytes 3145732
  181.8 13.0 %collective-permute-start.2 = (bf16[2,2048,256]{2,1,0:T(8,128)(2,1)}, bf16[2,2048,256]{2,1,0:T(8,128)(2,1)}, u32[]{:S(2)}, u32[]{:S(2)}) collective-permute-start(bf16[2,2048,256]{2,1,0:T(8,128)(2,1)} %pad_maximum_fusion.4), channel_id=1, source_target_pairs={{0,1},{1,0},{2,3},{3,2},{4,5},{5,4},{6,7},{7,6},{8,9},{9,8},{10,11... | collective-permute-start | bytes 6291464 | tf_op jit(solution)/shard_map/ppermute | solution.py:19
  182.9 17.7 %copy-start.37 = (pred[256]{0:T(512)(128)(4,1)}, pred[256]{0:T(512)(128)(4,1)S(1)}, u32[]{:S(2)}) copy-start(pred[256]{0:T(512)(128)(4,1)S(1)} %iota_compare_fusion.1) | copy-start | bytes 772
  182.9 19.2 %copy-start.35 = (pred[256]{0:T(512)(128)(4,1)}, pred[256]{0:T(512)(128)(4,1)S(1)}, u32[]{:S(2)}) copy-start(pred[256]{0:T(512)(128)(4,1)S(1)} %add_compare_fusion) | copy-start | bytes 772
  183.0 220.8 %reduce-scatter.2.cloned.1.call-start = ((), (), s32[]{:S(2)}) async-start(), calls=%async_computation.3 | async-start | bytes 5242880 | tf_op jit(solution)/shard_map/reduce_scatter | solution.py:193
  183.2 4.3 copy-start
  185.5 6.3 %copy-start.33 = (f32[1,128]{1,0:T(1,128)S(1)}, f32[1,128]{1,0:T(1,128)}, u32[]{:S(2)}) copy-start(f32[1,128]{1,0:T(1,128)} %param.23) | copy-start | bytes 1540
  191.7 8.9 %copy-start.16 = (f32[256,2,128]{2,0,1:T(8,128)}, f32[256,2,128]{2,0,1:T(8,128)S(1)}, u32[]{:S(2)}) copy-start(f32[256,2,128]{2,0,1:T(8,128)S(1)} %copy.108) | copy-start | bytes 786436
  191.7 5.3 %copy-start.1 = (bf16[1,1,256,8192]{3,2,1,0:T(8,128)(2,1)S(1)}, bf16[1,1,256,8192]{3,2,1,0:T(8,128)(2,1)}, u32[]{:S(2)}) copy-start(bf16[1,1,256,8192]{3,2,1,0:T(8,128)(2,1)} %all-gather.9.cloned.1.call-done) | copy-start | bytes 12582916
  194.8 5.8 %copy-start.9 = (f32[1,1,256,1024]{2,3,1,0:T(8,128)S(1)}, f32[1,1,256,1024]{2,3,1,0:T(8,128)}, u32[]{:S(2)}) copy-start(f32[1,1,256,1024]{2,3,1,0:T(8,128)} %copy.148) | copy-start | bytes 3145732
  200.6 6.4 %copy-start.29 = (f32[1,8192]{1,0:T(1,128)S(1)}, f32[1,8192]{1,0:T(1,128)}, u32[]{:S(2)}) copy-start(f32[1,8192]{1,0:T(1,128)} %param.18) | copy-start | bytes 98308
  203.6 3.9 copy-start.4
  207.5 2.5 copy-start.22
  221.9 2.6 copy-start.41
  221.9 2.6 copy-start.43
  224.5 6.3 %copy-start.10 = (f32[1,1,256,1024]{2,3,1,0:T(8,128)S(1)}, f32[1,1,256,1024]{2,3,1,0:T(8,128)}, u32[]{:S(2)}) copy-start(f32[1,1,256,1024]{2,3,1,0:T(8,128)} %copy.148) | copy-start | bytes 3145732
  224.5 6.3 %copy-start.38 = (pred[256]{0:T(512)(128)(4,1)S(1)}, pred[256]{0:T(512)(128)(4,1)}, u32[]{:S(2)}) copy-start(pred[256]{0:T(512)(128)(4,1)} %copy-done.37) | copy-start | bytes 772
  228.3 3.7 copy-start.21
  228.3 3.7 copy-start.24
  228.3 3.7 copy-start.27
  230.7 1.2 copy-start.13
  280.1 3.4 copy-start.5
  283.5 2.2 copy-start.23
  297.4 4.4 copy-start.30
  301.7 3.9 copy-start.19
  301.8 3.7 copy-start.31
  305.5 3.2 copy-start.20
  305.5 3.2 copy-start.25
  305.5 3.2 copy-start.28
  305.5 3.2 copy-start.42
  305.5 3.2 copy-start.44
  305.6 3.2 copy-start.32
  308.8 2.2 copy-start.17
  308.8 2.2 copy-start.34
  308.8 4.2 copy-start.8
  319.2 3.6 copy-start.12
  328.3 3.5 copy-start.2
  333.7 7.2 %collective-permute-start.9 = (bf16[2,2048,512]{1,2,0:T(8,128)(2,1)S(1)}, bf16[2,2048,512]{1,2,0:T(8,128)(2,1)S(1)}, u32[]{:S(2)}, u32[]{:S(2)}) collective-permute-start(bf16[2,2048,512]{1,2,0:T(8,128)(2,1)S(1)} %pad_maximum_fusion.3), channel_id=1, source_target_pairs={{0,1},{1,0},{2,3},{3,2},{4,5},{5,4},{6,7},{7,6},{8,9},{9,8},{10,11... | collective-permute-start | bytes 12582920 | tf_op jit(solution)/shard_map/ppermute | solution.py:19
  334.3 13.1 %copy-start.14 = (bf16[2,4,256,256]{2,3,1,0:T(8,128)(2,1)S(1)}, bf16[2,4,256,256]{2,3,1,0:T(8,128)(2,1)}, u32[]{:S(2)}) copy-start(bf16[2,4,256,256]{2,3,1,0:T(8,128)(2,1)} %copy-done.13) | copy-start | bytes 3145732
  334.8 13.2 %copy-start.15 = (bf16[2,4,256,256]{2,3,1,0:T(8,128)(2,1)S(1)}, bf16[2,4,256,256]{2,3,1,0:T(8,128)(2,1)}, u32[]{:S(2)}) copy-start(bf16[2,4,256,256]{2,3,1,0:T(8,128)(2,1)} %get-tuple-element.37) | copy-start | bytes 3145732
  341.0 2.1 copy-start.18
  345.3 3.1 copy-start.36
  345.3 3.1 copy-start.39
  345.3 59.9 %collective-permute-start.10 = (bf16[1,2048,512]{1,2,0:T(8,128)(2,1)}, bf16[1,2048,512]{1,2,0:T(8,128)(2,1)}, u32[]{:S(2)}, u32[]{:S(2)}) collective-permute-start(bf16[1,2048,512]{1,2,0:T(8,128)(2,1)} %add_convert_fusion), channel_id=1, source_target_pairs={{0,2},{1,3},{2,0},{3,1},{4,6},{5,7},{6,4},{7,5},{8,10},{9,11},{10,... | collective-permute-start | bytes 6291464 | tf_op jit(solution)/shard_map/ppermute | solution.py:19
  348.5 2.6 copy-start.3
  403.8 25.3 %collective-permute-start.8 = (bf16[256,2048]{1,0:T(8,128)(2,1)}, bf16[256,2048]{1,0:T(8,128)(2,1)}, u32[]{:S(2)}, u32[]{:S(2)}) collective-permute-start(bf16[256,2048]{1,0:T(8,128)(2,1)} %reduce-scatter.2.cloned.1.call-done), channel_id=1, source_target_pairs={{0,16},{16,0},{1,17},{17,1},{2,18},{18,2},{3,19},{19,3},{4,20},{20... | collective-permute-start | bytes 3145736 | tf_op jit(solution)/shard_map/ppermute | solution.py:13
  408.7 20.3 %copy-start.26 = (bf16[256,2048]{1,0:T(8,128)(2,1)S(1)}, bf16[256,2048]{1,0:T(8,128)(2,1)}, u32[]{:S(2)}) copy-start(bf16[256,2048]{1,0:T(8,128)(2,1)} %reduce-scatter.2.cloned.1.call-done) | copy-start | bytes 3145732
Sparse Core Ops, SparseCore 0:
  34.8 82.2 all-gather.8
  119.3 79.2 all-gather.4
  200.7 79.2 all-gather.6
  328.4 75.2 reduce-scatter.1

commit v15 on v14

--- a/solution.py
+++ b/solution.py
@@ -57,7 +57,7 @@
 
 
 def rounded(values):
-    return lax.optimization_barrier(values.astype(jnp.bfloat16)).astype(jnp.float32)
+    return values.astype(jnp.bfloat16).astype(jnp.float32)
 
 
 def prepare(keys_raw, values_raw, key_norm):

time: 442 us -> 443 us (level)
  waiting for transfers between devices: 262 us -> 267 us
    sub x2 -> x0, matrix products: 7.44 us -> none  [attend(): weights = jnp.exp(scores - highest)]
    unnamed x94 -> x72, local copies, waits for them, and re-layouts: 10.7 us -> 10.3 us
  transfers between devices with their start and end apart: 15 -> 15, of which waited for: 9 -> 9; matrix products, arithmetic and copies ran while one was open for 20% -> 19% of each run, Pallas kernels for 0% -> 0%
where the time goes in v15:
time: 443 us; the launch traced here: 439 us
  waiting for transfers between devices  267 us (60%)
  matrix products  69.5 us (16%)
  other arithmetic  46.1 us (10%)
  local copies, waits for them, and re-layouts  24.8 us (6%)
  between operations  19.2 us (4%)
  starting transfers between devices  11.5 us (3%)
    ppermute x3, waiting for transfers between devices, shifted(): return lax.ppermute(value, axis, pairs)  82.7 us
    ppermute x8, waiting for transfers between devices, swapped(): return lax.ppermute(value, axis, pairs)  82.2 us
    reduce_scatter x1, waiting for transfers between devices, per_device(): lax.psum_scatter(partial_sum, 'mp', scatter_dimension=1, tiled=True)  51.8 us
    all_gather x2, waiting for transfers between devices, per_device(): lax.all_gather(arrived[:, :, chunk * rows:(chunk + 1) * rows], 'mp', axis...  50.7 us
    dot_general x8, matrix products, per_device(): jnp.dot(columns_of(normed, (dp_index ^ code) * block_rows, block_rows), b...  23.8 us
    another operation x3, other arithmetic, gather_blocks(): arrived = swapped(jnp.stack([held[c] for c in codes]), axis, mask)  11.9 us
    unnamed x72, local copies, waits for them, and re-layouts  10.3 us
    reduce_sum x4, other arithmetic, norm_rows(): jnp.mean(values * values, axis=-1, keepdims=True) + 1e-05  9.74 us
  transfers between devices with their start and end apart: 15, of which 9 were waited for; matrix products, arithmetic and copies ran while one was open for 19% of the time, Pallas kernels for 0%

profile of v15, /device:TPU:0, one launch (start us, length us, event | category | flops | bytes accessed | tf_op | source)
XLA Modules:
  0.0 438.5 jit_solution(8431643533026624112)
XLA Ops:
  7.2 3.0 collective-permute-start
  10.2 1.4 constant_dynamic-slice_fusion.4
  12.2 21.4 %collective-permute-done = bf16[1,1,256,2048]{3,2,1,0:T(8,128)(2,1)S(1)} collective-permute-done((bf16[1,1,256,2048]{3,2,1,0:T(8,128)(2,1)}, bf16[1,1,256,2048]{3,2,1,0:T(8,128)(2,1)S(1)}, u32[]{:S(2)}, u32[]{:S(2)}) %collective-permute-start) | collective-permute-done | bytes 1048608 | tf_op jit(solution)/shard_map/ppermute | solution.py:13
  33.6 2.3 broadcast_select_fusion
  36.0 1.8 collective-permute-start.5
  37.8 1.5 collective-permute-start.6
  39.3 43.8 %collective-permute-done.5 = bf16[1,1,512,2048]{3,2,1,0:T(8,128)(2,1)S(1)} collective-permute-done((bf16[1,1,512,2048]{3,2,1,0:T(8,128)(2,1)}, bf16[1,1,512,2048]{3,2,1,0:T(8,128)(2,1)S(1)}, u32[]{:S(2)}, u32[]{:S(2)}) %collective-permute-start.5) | collective-permute-done | bytes 2097184 | tf_op jit(solution)/shard_map/ppermute | solution.py:13
  83.1 1.5 fusion.184
  84.9 46.7 %collective-permute-done.6 = bf16[1,2048,1024]{2,1,0:T(8,128)(2,1)} collective-permute-done((bf16[1,2048,1024]{2,1,0:T(8,128)(2,1)}, bf16[1,2048,1024]{2,1,0:T(8,128)(2,1)}, u32[]{:S(2)}, u32[]{:S(2)}) %collective-permute-start.6) | collective-permute-done | bytes 4194336 | tf_op jit(solution)/shard_map/ppermute | solution.py:19
  131.6 7.5 %pad_maximum_fusion = bf16[2,2048,1024]{2,1,0:T(8,128)(2,1)} fusion(bf16[1,2048,1024]{2,1,0:T(8,128)(2,1)} %collective-permute-done.6, bf16[1,2048,1024]{2,1,0:T(8,128)(2,1)} %param.19), kind=kLoop, calls=%fused_computation.10 | loop fusion | flops 4194304 | bytes 16777216 | tf_op jit(solution)/shard_map/stack | solution.py:36
  139.1 1.5 collective-permute-start.1
  140.6 13.4 %collective-permute-done.3 = bf16[1,2048,256]{2,1,0:T(8,128)(2,1)S(1)} collective-permute-done((bf16[1,2048,256]{2,1,0:T(8,128)(2,1)S(1)}, bf16[1,2048,256]{2,1,0:T(8,128)(2,1)S(1)}, u32[]{:S(2)}, u32[]{:S(2)}) %collective-permute-start.3) | collective-permute-done | bytes 1048608 | tf_op jit(solution)/shard_map/ppermute | solution.py:19
  154.0 1.7 pad_maximum_fusion.5
  158.2 15.9 %collective-permute-done.1 = bf16[1,2048,256]{2,1,0:T(8,128)(2,1)S(1)} collective-permute-done((bf16[1,2048,256]{2,1,0:T(8,128)(2,1)}, bf16[1,2048,256]{2,1,0:T(8,128)(2,1)S(1)}, u32[]{:S(2)}, u32[]{:S(2)}) %collective-permute-start.1) | collective-permute-done | bytes 1048608 | tf_op jit(solution)/shard_map/ppermute | solution.py:19
  174.1 2.8 pad_maximum_fusion.4
  176.9 1.6 slice_convert_fusion
  178.5 2.5 copy.148
  181.0 2.5 copy.152
  187.3 1.9 fusion.68
  189.2 2.1 fusion.75
  191.9 1.8 multiply_reduce_fusion.1
  193.8 1.9 fusion.85
  195.8 2.1 fusion.77
  197.9 1.8 convolution_add_fusion.7
  199.6 1.8 fusion.62
  201.5 3.3 fusion
  207.2 1.3 fusion.13
  208.5 3.7 fusion.9
  212.2 3.5 fusion.18
  215.7 3.6 fusion.53
  219.3 1.3 copy.147
  222.9 1.8 bitcast_reduce_fusion.1
  225.0 2.7 divide_convert_fusion.1
  229.0 1.7 fusion.54
  230.6 50.7 %all-gather.7.cloned.1.call-done = bf16[1,1,256,8192]{3,2,1,0:T(8,128)(2,1)} async-done(((bf16[1,1,256,2048]{3,2,1,0:T(8,128)(2,1)}), bf16[1,1,256,8192]{3,2,1,0:T(8,128)(2,1)}) %all-gather.7.cloned.1.call-update) | async-done | bytes 4194320 | tf_op jit(solution)/shard_map/all_gather | solution.py:142
  281.3 3.3 fusion.3
  284.7 2.1 fusion.5
  288.2 3.5 fusion.17
  291.7 3.5 fusion.49
  295.2 3.5 fusion.52
  299.7 1.3 copy.151
  301.0 2.5 copy.157
  303.5 2.2 reduce_sum.108
  308.0 1.8 bitcast_reduce_fusion
  310.2 2.6 fusion.38
  314.9 2.2 add_convert_fusion.1
  317.1 1.7 fusion.19
  318.8 1.7 fusion.117
  321.0 1.8 fusion.118
  322.8 1.7 fusion.20
  325.1 1.7 fusion.22
  327.8 2.2 pad_maximum_fusion.2
  330.0 1.8 convolution_convert_fusion.3
  331.8 1.7 convolution_convert_fusion.5
  336.4 6.2 %collective-permute-done.9 = bf16[2,2048,512]{1,2,0:T(8,128)(2,1)S(1)} collective-permute-done((bf16[2,2048,512]{1,2,0:T(8,128)(2,1)S(1)}, bf16[2,2048,512]{1,2,0:T(8,128)(2,1)S(1)}, u32[]{:S(2)}, u32[]{:S(2)}) %collective-permute-start.9) | collective-permute-done | bytes 4194336 | tf_op jit(solution)/shard_map/ppermute | solution.py:19
  342.6 2.0 copy-done.12
  344.6 2.3 add_convert_fusion
  346.9 1.5 collective-permute-start.10
  353.7 51.8 %reduce-scatter.2.cloned.1.call-done = bf16[256,2048]{1,0:T(8,128)(2,1)} async-done(((bf16[256,8192]{1,0:T(8,128)(2,1)}), bf16[256,2048]{1,0:T(8,128)(2,1)}) %reduce-scatter.2.cloned.1.call-update) | async-done | bytes 1048592 | tf_op jit(solution)/shard_map/reduce_scatter | solution.py:193
  405.4 1.5 collective-permute-start.8
  406.9 3.5 fusion.6
  410.6 1.3 copy.130
  411.9 1.3 copy.131
  413.2 17.5 %collective-permute-done.8 = bf16[256,2048]{1,0:T(8,128)(2,1)} collective-permute-done((bf16[256,2048]{1,0:T(8,128)(2,1)}, bf16[256,2048]{1,0:T(8,128)(2,1)}, u32[]{:S(2)}, u32[]{:S(2)}) %collective-permute-start.8) | collective-permute-done | bytes 1048608 | tf_op jit(solution)/shard_map/ppermute | solution.py:13
  (139 shorter events, 28.4 us)
Async XLA Ops:
  7.2 180.1 %all-gather.9.cloned.1.call-start = ((), (), s32[]{:S(2)}) async-start(), calls=%async_computation.4 | async-start | bytes 5242880 | tf_op jit(solution)/shard_map/all_gather | solution.py:115
  7.2 26.4 %collective-permute-start = (bf16[1,1,256,2048]{3,2,1,0:T(8,128)(2,1)}, bf16[1,1,256,2048]{3,2,1,0:T(8,128)(2,1)S(1)}, u32[]{:S(2)}, u32[]{:S(2)}) collective-permute-start(bf16[1,1,256,2048]{3,2,1,0:T(8,128)(2,1)} %param.14), channel_id=1, source_target_pairs={{0,16},{16,0},{1,17},{17,1},{2,18},{18,2},{3,19},{19,3},{4,20},{20... | collective-permute-start | bytes 3145736 | tf_op jit(solution)/shard_map/ppermute | solution.py:13
  12.2 72.4 %copy-start.6 = (bf16[1,2048,256]{2,1,0:T(8,128)(2,1)S(1)}, bf16[1,2048,256]{2,1,0:T(8,128)(2,1)}, u32[]{:S(2)}) copy-start(bf16[1,2048,256]{2,1,0:T(8,128)(2,1)} %param.20) | copy-start | bytes 3145732
  35.9 165.5 %all-gather.5.cloned.1.call-start = ((), (), s32[]{:S(2)}) async-start(), calls=%async_computation.1 | async-start | bytes 5242880 | tf_op jit(solution)/shard_map/all_gather | solution.py:142
  36.0 47.1 %collective-permute-start.5 = (bf16[1,1,512,2048]{3,2,1,0:T(8,128)(2,1)}, bf16[1,1,512,2048]{3,2,1,0:T(8,128)(2,1)S(1)}, u32[]{:S(2)}, u32[]{:S(2)}) collective-permute-start(bf16[1,1,512,2048]{3,2,1,0:T(8,128)(2,1)} %param.13), channel_id=1, source_target_pairs={{0,16},{16,0},{1,17},{17,1},{2,18},{18,2},{3,19},{19,3},{4,20},{20... | collective-permute-start | bytes 6291464 | tf_op jit(solution)/shard_map/ppermute | solution.py:13
  37.8 93.8 %collective-permute-start.6 = (bf16[1,2048,1024]{2,1,0:T(8,128)(2,1)}, bf16[1,2048,1024]{2,1,0:T(8,128)(2,1)}, u32[]{:S(2)}, u32[]{:S(2)}) collective-permute-start(bf16[1,2048,1024]{2,1,0:T(8,128)(2,1)} %param.19), channel_id=1, source_target_pairs={{0,2},{1,3},{2,0},{3,1},{4,6},{5,7},{6,4},{7,5},{8,10},{9,11},{10,... | collective-permute-start | bytes 12582920 | tf_op jit(solution)/shard_map/ppermute | solution.py:19
  84.5 196.7 %all-gather.7.cloned.1.call-start = ((), (), s32[]{:S(2)}) async-start(), calls=%async_computation.2 | async-start | bytes 5242880 | tf_op jit(solution)/shard_map/all_gather | solution.py:142
  84.6 69.4 %collective-permute-start.3 = (bf16[1,2048,256]{2,1,0:T(8,128)(2,1)S(1)}, bf16[1,2048,256]{2,1,0:T(8,128)(2,1)S(1)}, u32[]{:S(2)}, u32[]{:S(2)}) collective-permute-start(bf16[1,2048,256]{2,1,0:T(8,128)(2,1)S(1)} %copy-done.6), channel_id=1, source_target_pairs={{0,2},{1,3},{2,0},{3,1},{4,6},{5,7},{6,4},{7,5},{8,10},{9,11},{10,... | collective-permute-start | bytes 3145736 | tf_op jit(solution)/shard_map/ppermute | solution.py:19
  139.1 73.2 %collective-permute-start.7 = (bf16[2,2048,1024]{2,1,0:T(8,128)(2,1)}, bf16[2,2048,1024]{2,1,0:T(8,128)(2,1)}, u32[]{:S(2)}, u32[]{:S(2)}) collective-permute-start(bf16[2,2048,1024]{2,1,0:T(8,128)(2,1)} %pad_maximum_fusion), channel_id=1, source_target_pairs={{0,1},{1,0},{2,3},{3,2},{4,5},{5,4},{6,7},{7,6},{8,9},{9,8},{10,11... | collective-permute-start | bytes 25165832 | tf_op jit(solution)/shard_map/ppermute | solution.py:19
  139.1 35.0 %collective-permute-start.1 = (bf16[1,2048,256]{2,1,0:T(8,128)(2,1)}, bf16[1,2048,256]{2,1,0:T(8,128)(2,1)S(1)}, u32[]{:S(2)}, u32[]{:S(2)}) collective-permute-start(bf16[1,2048,256]{2,1,0:T(8,128)(2,1)} %param.21), channel_id=1, source_target_pairs={{0,2},{1,3},{2,0},{3,1},{4,6},{5,7},{6,4},{7,5},{8,10},{9,11},{10,... | collective-permute-start | bytes 3145736 | tf_op jit(solution)/shard_map/ppermute | solution.py:19
  154.0 33.4 %copy-start.7 = (bf16[1,2048,256]{2,1,0:T(8,128)(2,1)}, bf16[1,2048,256]{2,1,0:T(8,128)(2,1)S(1)}, u32[]{:S(2)}) copy-start(bf16[1,2048,256]{2,1,0:T(8,128)(2,1)S(1)} %collective-permute-done.3) | copy-start | bytes 3145732
  155.6 33.6 %collective-permute-start.4 = (bf16[2,2048,256]{2,1,0:T(8,128)(2,1)}, bf16[2,2048,256]{2,1,0:T(8,128)(2,1)}, u32[]{:S(2)}, u32[]{:S(2)}) collective-permute-start(bf16[2,2048,256]{2,1,0:T(8,128)(2,1)} %pad_maximum_fusion.5), channel_id=1, source_target_pairs={{0,1},{1,0},{2,3},{3,2},{4,5},{5,4},{6,7},{7,6},{8,9},{9,8},{10,11... | collective-permute-start | bytes 6291464 | tf_op jit(solution)/shard_map/ppermute | solution.py:19
  156.8 20.1 %copy-start.19 = (bf16[1,1,512,1024]{3,2,1,0:T(8,128)(2,1)S(1)}, bf16[1,1,512,1024]{3,2,1,0:T(8,128)(2,1)}, u32[]{:S(2)}) copy-start(bf16[1,1,512,1024]{3,2,1,0:T(8,128)(2,1)} %param.25) | copy-start | bytes 3145732
  176.9 7.2 %copy-start.32 = (s32[1,2]{1,0:T(1,128)S(1)}, s32[1,2]{1,0:T(1,128)}, u32[]{:S(2)}) copy-start(s32[1,2]{1,0:T(1,128)} %param.15) | copy-start | bytes 28
  176.9 18.9 %collective-permute-start.2 = (bf16[2,2048,256]{2,1,0:T(8,128)(2,1)}, bf16[2,2048,256]{2,1,0:T(8,128)(2,1)}, u32[]{:S(2)}, u32[]{:S(2)}) collective-permute-start(bf16[2,2048,256]{2,1,0:T(8,128)(2,1)} %pad_maximum_fusion.4), channel_id=1, source_target_pairs={{0,1},{1,0},{2,3},{3,2},{4,5},{5,4},{6,7},{7,6},{8,9},{9,8},{10,11... | collective-permute-start | bytes 6291464 | tf_op jit(solution)/shard_map/ppermute | solution.py:19
  187.1 218.4 %reduce-scatter.2.cloned.1.call-start = ((), (), s32[]{:S(2)}) async-start(), calls=%async_computation.3 | async-start | bytes 5242880 | tf_op jit(solution)/shard_map/reduce_scatter | solution.py:193
  187.3 4.0 copy-start
  193.8 4.0 copy-start.1
  197.9 6.9 %copy-start.22 = (f32[1,8192]{1,0:T(1,128)S(1)}, f32[1,8192]{1,0:T(1,128)}, u32[]{:S(2)}) copy-start(f32[1,8192]{1,0:T(1,128)} %param.18) | copy-start | bytes 98308
  201.5 3.5 copy-start.4
  204.9 2.3 copy-start.17
  224.9 2.7 copy-start.14
  225.0 2.7 copy-start.30
  225.0 4.0 copy-start.16
  225.0 4.0 copy-start.24
  225.0 4.0 copy-start.26
  227.7 2.9 copy-start.9
  281.3 3.4 copy-start.5
  284.7 2.2 copy-start.18
  301.0 9.1 %copy-start.13 = (f32[1,1,256,1024]{2,3,1,0:T(8,128)S(1)}, f32[1,1,256,1024]{2,3,1,0:T(8,128)}, u32[]{:S(2)}) copy-start(f32[1,1,256,1024]{2,3,1,0:T(8,128)} %copy.152) | copy-start | bytes 3145732
  310.1 2.7 copy-start.15
  310.1 2.7 copy-start.23
  310.2 2.7 copy-start.25
  310.2 2.7 copy-start.27
  310.2 2.7 copy-start.33
  312.8 1.9 copy-start.28
  313.9 1.0 copy-start.20
  321.0 3.5 copy-start.8
  330.0 3.5 copy-start.2
  335.4 7.2 %collective-permute-start.9 = (bf16[2,2048,512]{1,2,0:T(8,128)(2,1)S(1)}, bf16[2,2048,512]{1,2,0:T(8,128)(2,1)S(1)}, u32[]{:S(2)}, u32[]{:S(2)}) collective-permute-start(bf16[2,2048,512]{1,2,0:T(8,128)(2,1)S(1)} %pad_maximum_fusion.3), channel_id=1, source_target_pairs={{0,1},{1,0},{2,3},{3,2},{4,5},{5,4},{6,7},{7,6},{8,9},{9,8},{10,11... | collective-permute-start | bytes 12582920 | tf_op jit(solution)/shard_map/ppermute | solution.py:19
  336.0 13.1 %copy-start.11 = (bf16[2,4,256,256]{2,3,1,0:T(8,128)(2,1)S(1)}, bf16[2,4,256,256]{2,3,1,0:T(8,128)(2,1)}, u32[]{:S(2)}) copy-start(bf16[2,4,256,256]{2,3,1,0:T(8,128)(2,1)} %get-tuple-element.37) | copy-start | bytes 3145732
  336.4 13.2 %copy-start.10 = (bf16[2,4,256,256]{2,3,1,0:T(8,128)(2,1)S(1)}, bf16[2,4,256,256]{2,3,1,0:T(8,128)(2,1)}, u32[]{:S(2)}) copy-start(bf16[2,4,256,256]{2,3,1,0:T(8,128)(2,1)} %copy-done.9) | copy-start | bytes 3145732
  342.6 2.0 copy-start.12
  346.9 3.3 copy-start.29
  346.9 3.3 copy-start.31
  346.9 60.0 %collective-permute-start.10 = (bf16[1,2048,512]{1,2,0:T(8,128)(2,1)}, bf16[1,2048,512]{1,2,0:T(8,128)(2,1)}, u32[]{:S(2)}, u32[]{:S(2)}) collective-permute-start(bf16[1,2048,512]{1,2,0:T(8,128)(2,1)} %add_convert_fusion), channel_id=1, source_target_pairs={{0,2},{1,3},{2,0},{3,1},{4,6},{5,7},{6,4},{7,5},{8,10},{9,11},{10,... | collective-permute-start | bytes 6291464 | tf_op jit(solution)/shard_map/ppermute | solution.py:19
  350.2 2.6 copy-start.3
  405.4 25.3 %collective-permute-start.8 = (bf16[256,2048]{1,0:T(8,128)(2,1)}, bf16[256,2048]{1,0:T(8,128)(2,1)}, u32[]{:S(2)}, u32[]{:S(2)}) collective-permute-start(bf16[256,2048]{1,0:T(8,128)(2,1)} %reduce-scatter.2.cloned.1.call-done), channel_id=1, source_target_pairs={{0,16},{16,0},{1,17},{17,1},{2,18},{18,2},{3,19},{19,3},{4,20},{20... | collective-permute-start | bytes 3145736 | tf_op jit(solution)/shard_map/ppermute | solution.py:13
  410.4 20.3 %copy-start.21 = (bf16[256,2048]{1,0:T(8,128)(2,1)S(1)}, bf16[256,2048]{1,0:T(8,128)(2,1)}, u32[]{:S(2)}) copy-start(bf16[256,2048]{1,0:T(8,128)(2,1)} %reduce-scatter.2.cloned.1.call-done) | copy-start | bytes 3145732
Sparse Core Ops, SparseCore 0:
  36.0 82.2 all-gather.8
  120.5 79.2 all-gather.4
  201.9 79.2 all-gather.6
  330.1 75.2 reduce-scatter.1
